TPU v7x, 512 devices: a whole 4x8x8 slice. The times are simulated.
512 devices in a mesh: section: 4 (over x_lo, core), batch: 128 (over z, y, x_hi).
Axes of the slice: x: 4 (x_hi: 2, x_lo: 2; x = x_hi * 2 + x_lo), y: 8, z: 8, core: 2. Of those that a mesh axis runs over, the one named last changes fastest.
Arguments:
- latents: bfloat16 [4096, 512], P('batch'), may hold values from -6 to 6
- token_slot: int32 [4096], P('batch'), may hold values from 0 to 4095, as said below
- cache_keys: bfloat16 [4096, 128, 512], P('batch', None, 'section'), may hold values from -320 to 320
- cache_values: bfloat16 [4096, 128, 512], P('batch', None, 'section'), may hold values from -6 to 6
- up_state: bfloat16 [4096, 512], P('batch'), may hold values from -6 to 6
- conv_state: bfloat16 [4096, 512], P('batch'), may hold values from -1 to 3
- cache_slot: int32 [4096], P('batch'), may hold values from 0 to 4095, as said below
- positions: int32 [4096], P('batch'), may hold values from 0 to 512
- up_kernel: float32 [4, 512], replicated, may hold values from -4 to 4
- norm_gain_one: float32 [512], replicated, may hold values from 0.1 to 1.9
- qkv_weight: bfloat16 [3, 512, 512], P(None, None, 'section'), may hold values from -0.25 to 0.25
- out_weight: bfloat16 [512, 512], P('section'), may hold values from -0.25 to 0.25
- scale_attention: float32 [512], replicated, may hold values from 0.1 to 1.9
- norm_gain_two: float32 [512], replicated, may hold values from 0.1 to 1.9
- in_weight: bfloat16 [512, 2048], P(None, 'section'), may hold values from -0.25 to 0.25
- down_weight: bfloat16 [2048, 512], P('section'), may hold values from -0.125 to 0.125
- scale_feedforward: float32 [512], replicated, may hold values from 0.1 to 1.9
- conv_weight: bfloat16 [16, 256, 512], P(None, 'section'), may hold values from -0.1875 to 0.1875
- conv_bias: float32 [256], P('section'), may hold values from -3 to 3
Outputs:
- audio_out: float32 [256, 65536], P('section', 'batch')
- new_keys: bfloat16 [4096, 128, 512], P('batch', None, 'section')
- new_values: bfloat16 [4096, 128, 512], P('batch', None, 'section')
- new_up_state: bfloat16 [4096, 512], P('batch')
- new_conv_state: bfloat16 [4096, 512], P('batch')
Inputs may be any that keep to these rules, and one draw needn't show every extreme that they name: `token_slot`: every slot receives exactly one token row. The 32 rows of one transformer owner go in groups of exactly 2 rows to 16 different decoder owners; the decoder owner of slot n is n // 32. `cache_slot`: A permutation of the slots. Each batch index keeps all but 2 * 1 of its streams and hands exactly 1 to the index one higher and 1 to the index one lower, cyclically.
All inputs are finite; a program needn't handle non-finite values.
Results may differ from a plain program's by a relative error of at most 0.017.
Values may be sent and summed in bfloat16 or wider, within the bound.
No kernel may reach another device: no remote copies, remote signals or barrier semaphores. Data moves between devices by JAX's collectives and lax.ppermute only.
A program may use at most 64 MiB of HBM per device.

v0:
```python
import jax
import jax.numpy as jnp
from jax import lax
from jax.sharding import PartitionSpec as P

HEAD_DIM = 64
MOVE = 1


EPSILON = 1e-05
MAX_PERIOD = 10000.0


def for_sending(array):

    def short(part):
        return part.astype(jnp.bfloat16) if part.dtype == jnp.float32 else part

    return jax.tree.map(short, array)


def passed_along(block, axis, distance):
    devices = range(lax.axis_size(axis))
    route = [((i - distance) % len(devices), i) for i in devices]
    return lax.ppermute(block, axis, route)


def layer_norm(hidden, weight_gain):
    average = jnp.mean(hidden, axis=-1, keepdims=True)
    centred = hidden - average
    variance = jnp.mean(centred * centred, axis=-1, keepdims=True)
    return centred * lax.rsqrt(variance + EPSILON) * weight_gain


def rotate(features, times, head_width):
    streams = features.shape[0]
    half = head_width // 2
    freqs = MAX_PERIOD ** (-2.0 * jnp.arange(half, dtype=jnp.float32) / head_width)
    angle = times.astype(jnp.float32)[:, :, None] * freqs[None, None, :]
    cosine = jnp.cos(angle)[:, :, None, :]
    sine = jnp.sin(angle)[:, :, None, :]
    paired = features.reshape(streams, 2, -1, half, 2)
    first = paired[..., 0]
    second = paired[..., 1]
    turned = jnp.stack([first * cosine - second * sine, first * sine + second * cosine], axis=-1)
    return turned.reshape(features.shape)


def attend(
    queries, fresh_keys, fresh_values, old_keys, old_values, starts, local_heads, head_width
):
    streams = old_keys.shape[0]
    window = old_keys.shape[1]
    query_heads = queries.reshape(streams, 2, local_heads, head_width)
    cache_heads = old_keys.reshape(streams, window, local_heads, head_width)
    fresh_heads = fresh_keys.reshape(streams, 2, local_heads, head_width)
    score_scale = head_width ** (-0.5)
    cache_scores = (
        jnp.einsum("sfhe,swhe->shfw", query_heads, cache_heads, preferred_element_type=jnp.float32)
        * score_scale
    )
    fresh_scores = (
        jnp.einsum("sfhe,sghe->shfg", query_heads, fresh_heads, preferred_element_type=jnp.float32)
        * score_scale
    )
    cycle_slots = jnp.arange(window, dtype=jnp.int32)
    held_time = starts[:, None] - window + jnp.mod(cycle_slots[None, :] - starts[:, None], window)
    query_times = starts[:, None] + jnp.arange(2, dtype=jnp.int32)[None, :]
    cache_ok = (held_time[:, None, :] >= 0) & (
        held_time[:, None, :] > query_times[:, :, None] - window
    )
    frame_ids = jnp.arange(2, dtype=jnp.int32)
    fresh_ok = frame_ids[None, :] <= frame_ids[:, None]
    allowed = jnp.concatenate(
        [
            jnp.broadcast_to(cache_ok[:, None], (streams, local_heads, 2, window)),
            jnp.broadcast_to(fresh_ok, (streams, local_heads, 2, 2)),
        ],
        axis=-1,
    )
    scores = jnp.concatenate([cache_scores, fresh_scores], axis=-1)
    scores = jnp.where(allowed, scores, -jnp.inf)
    score_max = jnp.max(scores, axis=-1, keepdims=True)
    weights = jnp.where(allowed, jnp.exp(scores - score_max), 0.0)
    denominator = jnp.sum(weights, axis=-1, keepdims=True)
    rounded = weights.astype(jnp.bfloat16)
    value_heads = old_values.reshape(streams, window, local_heads, head_width)
    fresh_value_heads = fresh_values.reshape(streams, 2, local_heads, head_width)
    attended = jnp.einsum(
        "shfw,swhe->sfhe", rounded[..., :window], value_heads, preferred_element_type=jnp.float32
    )
    attended = attended + jnp.einsum(
        "shfg,sghe->sfhe",
        rounded[..., window:],
        fresh_value_heads,
        preferred_element_type=jnp.float32,
    )
    attended = attended / jnp.transpose(denominator, (0, 2, 1, 3))
    return attended.astype(jnp.bfloat16).reshape(streams, 2, local_heads * head_width)


def pack_side(direction_owner, leaving, dest_owner, slot_ids, outgoing):
    chosen = leaving & (dest_owner == direction_owner)
    before = chosen[None, :] & (slot_ids[None, :] < slot_ids[:, None])
    box_place = jnp.where(chosen, jnp.sum(before.astype(jnp.int32), axis=1), MOVE)
    return tuple(
        (
            jnp.zeros((MOVE,) + source_array.shape[1:], source_array.dtype)
            .at[box_place]
            .set(source_array, mode="drop")
            for source_array in outgoing
        )
    )


def local(
    latents,
    token_slot,
    cache_keys,
    cache_values,
    up_state,
    conv_state,
    cache_slot,
    positions,
    up_kernel,
    norm_gain_one,
    qkv_weight,
    out_weight,
    scale_attention,
    norm_gain_two,
    in_weight,
    down_weight,
    scale_feedforward,
    conv_weight,
    conv_bias,
):
    owners = lax.axis_size("batch")
    own_index = lax.axis_index("batch")
    streams = latents.shape[0]
    model_width = latents.shape[1]
    window = cache_keys.shape[1]
    head_share = cache_keys.shape[2]
    capacity = max(2, streams // owners)
    slot_ids = jnp.arange(streams, dtype=jnp.int32)
    target = token_slot // streams
    landing = token_slot % streams
    same_before = (target[None, :] == target[:, None]) & (slot_ids[None, :] < slot_ids[:, None])
    arrival_rank = jnp.sum(same_before.astype(jnp.int32), axis=1)
    send_rows = (
        jnp.zeros((owners, capacity, model_width), jnp.bfloat16)
        .at[target, arrival_rank]
        .set(latents)
    )
    send_codes = (
        jnp.zeros((owners, capacity), jnp.bfloat16)
        .at[target, arrival_rank]
        .set((landing + 1).astype(jnp.bfloat16))
    )
    got_rows, got_codes = (
        lax.all_to_all(send_rows, "batch", split_axis=0, concat_axis=0, tiled=True),
        lax.all_to_all(send_codes, "batch", split_axis=0, concat_axis=0, tiled=True),
    )
    selector = got_codes.reshape(-1).astype(jnp.int32)[None, :] - 1 == slot_ids[:, None]
    arrived = jnp.dot(
        selector.astype(jnp.bfloat16),
        got_rows.reshape(owners * capacity, model_width),
        preferred_element_type=jnp.float32,
    ).astype(jnp.bfloat16)
    dest_owner = cache_slot // streams
    dest_local = cache_slot % streams
    leaving = dest_owner != own_index
    stay_codes = jnp.where(leaving, 0, dest_local + 1).astype(jnp.bfloat16)
    code_values = (dest_local + 1).astype(jnp.bfloat16)
    outgoing = (cache_keys, cache_values, up_state, conv_state, code_values)
    right_owner = jnp.mod(own_index + 1, owners)
    left_owner = jnp.mod(own_index + owners - 1, owners)
    right_parts = pack_side(right_owner, leaving, dest_owner, slot_ids, outgoing)
    left_parts = pack_side(left_owner, leaving, dest_owner, slot_ids, outgoing)
    from_left = jax.tree.map(
        lambda part, own: part.astype(own.dtype),
        passed_along(for_sending(right_parts), "batch", 1),
        right_parts,
    )
    from_right = jax.tree.map(
        lambda part, own: part.astype(own.dtype),
        passed_along(for_sending(left_parts), "batch", -1),
        left_parts,
    )
    incoming = tuple(
        (
            jnp.concatenate([lower_part, upper_part], axis=0)
            for lower_part, upper_part in zip(from_left, from_right)
        )
    )
    candidate = tuple(
        (
            jnp.concatenate([own_array, extra_array], axis=0)
            for own_array, extra_array in zip(
                (cache_keys, cache_values, up_state, conv_state, stay_codes), incoming
            )
        )
    )
    candidate_codes = candidate[4].astype(jnp.int32) - 1
    matches = candidate_codes[None, :] == slot_ids[:, None]
    picked = jnp.sum(
        jnp.where(matches, jnp.arange(candidate_codes.shape[0], dtype=jnp.int32)[None, :], 0),
        axis=1,
    )
    keys_old = jnp.take(candidate[0], picked, axis=0)
    values_old = jnp.take(candidate[1], picked, axis=0)
    up_prev = jnp.take(candidate[2], picked, axis=0)
    conv_prev = jnp.take(candidate[3], picked, axis=0)
    latent_f = arrived.astype(jnp.float32)
    prior_f = up_prev.astype(jnp.float32)
    residual_zero = jnp.stack(
        [
            latent_f * up_kernel[0] + prior_f * up_kernel[2],
            latent_f * up_kernel[1] + prior_f * up_kernel[3],
        ],
        axis=1,
    )
    normed_one = layer_norm(residual_zero, norm_gain_one).astype(jnp.bfloat16)
    projections = jnp.einsum(
        "sfd,kde->ksfe", normed_one, qkv_weight, preferred_element_type=jnp.float32
    )
    times = positions[:, None] + jnp.arange(2, dtype=jnp.int32)[None, :]
    queries = rotate(projections[0], times, HEAD_DIM).astype(jnp.bfloat16)
    fresh_keys = rotate(projections[1], times, HEAD_DIM).astype(jnp.bfloat16)
    fresh_values = projections[2].astype(jnp.bfloat16)
    attended = attend(
        queries,
        fresh_keys,
        fresh_values,
        keys_old,
        values_old,
        positions,
        head_share // HEAD_DIM,
        HEAD_DIM,
    )
    partial_heads = jnp.dot(
        attended.reshape(2 * streams, head_share), out_weight, preferred_element_type=jnp.float32
    )
    mixing = lax.psum(partial_heads.astype(jnp.bfloat16), "section").astype(jnp.float32)
    residual_one = residual_zero + scale_attention * mixing.reshape(streams, 2, model_width)
    normed_two = (
        layer_norm(residual_one, norm_gain_two)
        .astype(jnp.bfloat16)
        .reshape(2 * streams, model_width)
    )
    inner_units = jax.nn.gelu(
        jnp.dot(normed_two, in_weight, preferred_element_type=jnp.float32), approximate=False
    ).astype(jnp.bfloat16)
    partial_units = jnp.dot(inner_units, down_weight, preferred_element_type=jnp.float32)
    feed_forward = lax.psum(partial_units.astype(jnp.bfloat16), "section").astype(jnp.float32)
    residual_two = residual_one + scale_feedforward * feed_forward.reshape(streams, 2, model_width)
    excited = jax.nn.elu(residual_two).astype(jnp.bfloat16)
    earlier = jnp.stack([conv_prev, excited[:, 0]], axis=1)
    stride = conv_weight.shape[0] // 2
    audio_out = jnp.einsum(
        "sfi,rci->csfr", excited, conv_weight[:stride], preferred_element_type=jnp.float32
    )
    audio_out = audio_out + jnp.einsum(
        "sfi,rci->csfr", earlier, conv_weight[stride:], preferred_element_type=jnp.float32
    )
    audio_out = audio_out + conv_bias[:, None, None, None]
    audio_out = audio_out.reshape(conv_bias.shape[0], streams * 2 * stride)
    slot_first = jnp.mod(positions, window)
    slot_second = jnp.mod(positions + 1, window)
    new_keys = (
        keys_old.at[slot_ids, slot_first]
        .set(fresh_keys[:, 0])
        .at[slot_ids, slot_second]
        .set(fresh_keys[:, 1])
    )
    new_values = (
        values_old.at[slot_ids, slot_first]
        .set(fresh_values[:, 0])
        .at[slot_ids, slot_second]
        .set(fresh_values[:, 1])
    )
    return (audio_out, new_keys, new_values, arrived, excited[:, 1])


def solution(mesh):
    placed = (
        P("batch", None),
        P("batch"),
        P("batch", None, "section"),
        P("batch", None, "section"),
        P("batch", None),
        P("batch", None),
        P("batch"),
        P("batch"),
        P(),
        P(),
        P(None, None, "section"),
        P("section", None),
        P(),
        P(),
        P(None, "section"),
        P("section", None),
        P(),
        P(None, "section", None),
        P("section"),
    )
    return jax.shard_map(
        local,
        mesh=mesh,
        in_specs=placed,
        out_specs=(
            P("section", "batch"),
            P("batch", None, "section"),
            P("batch", None, "section"),
            P("batch", None),
            P("batch", None),
        ),
        check_vma=False,
    )
```

profile of v0, /device:TPU:1, one launch (start us, length us, event | category | flops | bytes accessed | tf_op | source)
XLA Modules:
  0.0 243.6 jit_solution(4903698463168684158)
XLA Ops:
  8.1 2.0 scatter_fusion
  10.9 20.8 %all-to-all-start = ((bf16[128,1,2]{2,1,0:T(2,128)(2,1)}), bf16[128,1,2]{2,1,0:T(2,128)(2,1)S(1)}, u32[]{:S(2)}, u32[]{:S(2)}) async-start(bf16[128,1,2]{2,1,0:T(2,128)(2,1)} %copy.94), calls=%async_computation | async-start | bytes 131072 | tf_op jit(solution)/shard_map/all_to_all | solution.py:161
  32.7 9.0 %collective-permute-start.1 = (bf16[1,512]{1,0:T(2,128)(2,1)S(1)}, bf16[1,512]{1,0:T(2,128)(2,1)S(1)}, u32[]{:S(2)}, u32[]{:S(2)}) collective-permute-start(bf16[1,512]{1,0:T(2,128)(2,1)S(1)} %bitcast.138), channel_id=1, source_target_pairs={{1,0},{2,1},{3,2},{4,3},{5,4},{6,5},{7,6},{8,7},{9,8},{10,9},{11,1... | collective-permute-start | bytes 3080 | tf_op jit(solution)/shard_map/ppermute | solution.py:25
  42.5 1.9 collective-permute-start
  44.4 1.8 scatter_fusion.3
  46.2 9.1 %collective-permute-start.3 = (bf16[1]{0:T(256)(128)(2,1)}, bf16[1]{0:T(256)(128)(2,1)}, u32[]{:S(2)}, u32[]{:S(2)}) collective-permute-start(bf16[1]{0:T(256)(128)(2,1)} %scatter_fusion.3), channel_id=1, source_target_pairs={{1,0},{2,1},{3,2},{4,3},{5,4},{6,5},{7,6},{8,7},{9,8},{10,9},{11,1... | collective-permute-start | bytes 14 | tf_op jit(solution)/shard_map/ppermute | solution.py:25
  55.3 1.8 scatter_fusion.2
  57.0 1.9 collective-permute-start.2
  59.0 1.7 scatter_fusion.5
  60.7 9.1 %collective-permute-start.5 = (bf16[1,128,128]{2,1,0:T(8,128)(2,1)S(1)}, bf16[1,128,128]{2,1,0:T(8,128)(2,1)S(1)}, u32[]{:S(2)}, u32[]{:S(2)}) collective-permute-start(bf16[1,128,128]{2,1,0:T(8,128)(2,1)S(1)} %bitcast.120), channel_id=1, source_target_pairs={{1,0},{2,1},{3,2},{4,3},{5,4},{6,5},{7,6},{8,7},{9,8},{10,9},{11,1... | collective-permute-start | bytes 98312 | tf_op jit(solution)/shard_map/ppermute | solution.py:25
  70.2 1.7 scatter_fusion.4
  71.9 1.7 scatter_fusion.7
  73.7 1.7 scatter_fusion.6
  77.6 4.4 %scatter_fusion.1 = bf16[128,2,512]{2,1,0:T(2,128)(2,1)} fusion(bf16[128,2,512]{2,1,0:T(2,128)(2,1)} %broadcast_in_dim.65, s32[32]{0:T(128)S(1)} %fusion.115, bf16[32,512]{1,0:T(8,128)(2,1)S(1)} %copy-done.10), kind=kCustom, calls=%fused_computation.5 | custom fusion | bytes 98560 | tf_op jit(solution)/shard_map/scatter | solution.py:152
  82.3 1.9 collective-permute-start.9
  84.3 4.9 %collective-permute-start.8 = (bf16[1,512]{1,0:T(2,128)(2,1)S(1)}, bf16[1,512]{1,0:T(2,128)(2,1)S(1)}, u32[]{:S(2)}, u32[]{:S(2)}) collective-permute-start(bf16[1,512]{1,0:T(2,128)(2,1)S(1)} %bitcast.140), channel_id=1, source_target_pairs={{127,0},{0,1},{1,2},{2,3},{3,4},{4,5},{5,6},{6,7},{7,8},{8,9},{9,1... | collective-permute-start | bytes 3080 | tf_op jit(solution)/shard_map/ppermute | solution.py:25
  90.6 8.0 %all-to-all-start.1 = ((bf16[128,2,512]{2,1,0:T(2,128)(2,1)}), bf16[128,2,512]{2,1,0:T(2,128)(2,1)S(1)}, u32[]{:S(2)}, u32[]{:S(2)}) async-start(bf16[128,2,512]{2,1,0:T(2,128)(2,1)} %scatter_fusion.1), calls=%async_computation.1 | async-start | bytes 524288 | tf_op jit(solution)/shard_map/all_to_all | solution.py:160
  99.0 4.0 %collective-permute-start.4 = (bf16[1,128,128]{2,1,0:T(8,128)(2,1)S(1)}, bf16[1,128,128]{2,1,0:T(8,128)(2,1)S(1)}, u32[]{:S(2)}, u32[]{:S(2)}) collective-permute-start(bf16[1,128,128]{2,1,0:T(8,128)(2,1)S(1)} %bitcast.121), channel_id=1, source_target_pairs={{127,0},{0,1},{1,2},{2,3},{3,4},{4,5},{5,6},{6,7},{7,8},{8,9},{9,1... | collective-permute-start | bytes 98312 | tf_op jit(solution)/shard_map/ppermute | solution.py:25
  103.0 7.0 %collective-permute-start.7 = (bf16[1,128,128]{2,1,0:T(8,128)(2,1)S(1)}, bf16[1,128,128]{2,1,0:T(8,128)(2,1)S(1)}, u32[]{:S(2)}, u32[]{:S(2)}) collective-permute-start(bf16[1,128,128]{2,1,0:T(8,128)(2,1)S(1)} %bitcast.122), channel_id=1, source_target_pairs={{1,0},{2,1},{3,2},{4,3},{5,4},{6,5},{7,6},{8,7},{9,8},{10,9},{11,1... | collective-permute-start | bytes 98312 | tf_op jit(solution)/shard_map/ppermute | solution.py:25
  110.8 2.1 collective-permute-start.6
  114.7 2.9 %gather_fusion.1 = bf16[32,128,128]{2,1,0:T(8,128)(2,1)} fusion(bf16[34,128,128]{2,1,0:T(8,128)(2,1)} %pad_maximum_fusion, s32[1024]{0:T(1024)S(1)} %pad_clamp_fusion), kind=kCustom, calls=%fused_computation.1.clone | custom fusion | bytes 2097280 | tf_op jit(solution)/shard_map/jit(_take)/gather | solution.py:210
  117.6 3.6 %collective-permute-done.6 = bf16[1,128,128]{2,1,0:T(8,128)(2,1)S(1)} collective-permute-done((bf16[1,128,128]{2,1,0:T(8,128)(2,1)S(1)}, bf16[1,128,128]{2,1,0:T(8,128)(2,1)S(1)}, u32[]{:S(2)}, u32[]{:S(2)}) %collective-permute-start.6) | collective-permute-done | bytes 32800 | tf_op jit(solution)/shard_map/ppermute | solution.py:25
  121.3 1.7 gather_fusion.2
  123.0 1.8 broadcast_select_fusion.1
  130.7 1.6 convolution_multiply_fusion.1
  135.8 44.9 %all-reduce.3.cloned.1.call-done = bf16[64,512]{1,0:T(8,128)(2,1)} async-done(((bf16[64,512]{1,0:T(8,128)(2,1)}), bf16[64,512]{1,0:T(8,128)(2,1)}) %all-reduce.3.cloned.1.call-update) | async-done | bytes 65552 | tf_op jit(solution)/shard_map/psum | solution.py:243
  182.7 1.8 convolution_convert_fusion
  185.3 2.1 scatter_fusion.8
  187.5 2.1 scatter_fusion.10
  189.6 2.1 scatter_fusion.9
  191.8 2.1 scatter_fusion.11
  194.0 38.3 %all-reduce.5.cloned.1.call-done = bf16[32,2,512]{2,0,1:T(8,128)(2,1)} async-done(((bf16[32,2,512]{2,0,1:T(8,128)(2,1)}), bf16[32,2,512]{2,0,1:T(8,128)(2,1)}) %all-reduce.5.cloned.1.call-update) | async-done | bytes 65552 | tf_op jit(solution)/shard_map/psum | solution.py:254
  (156 shorter events, 27.3 us)
Async XLA Ops:
  7.2 175.5 %copy-start = (bf16[512,512]{1,0:T(8,128)(2,1)S(1)}, bf16[512,512]{1,0:T(8,128)(2,1)}, u32[]{:S(2)}) copy-start(bf16[512,512]{1,0:T(8,128)(2,1)} %param.38) | copy-start | bytes 1572868
  7.2 24.6 %copy-start.19 = (s32[32]{0:T(128)S(1)}, s32[32]{0:T(128)}, u32[]{:S(2)}) copy-start(s32[32]{0:T(128)} %param.29) | copy-start | bytes 388
  7.2 24.8 %copy-start.12 = (bf16[32,512]{1,0:T(8,128)(2,1)S(1)}, bf16[32,512]{1,0:T(8,128)(2,1)}, u32[]{:S(2)}) copy-start(bf16[32,512]{1,0:T(8,128)(2,1)} %param.27) | copy-start | bytes 98308
  10.9 79.7 %all-to-all-start = ((bf16[128,1,2]{2,1,0:T(2,128)(2,1)}), bf16[128,1,2]{2,1,0:T(2,128)(2,1)S(1)}, u32[]{:S(2)}, u32[]{:S(2)}) async-start(bf16[128,1,2]{2,1,0:T(2,128)(2,1)} %copy.94), calls=%async_computation | async-start | bytes 131072 | tf_op jit(solution)/shard_map/all_to_all | solution.py:161
  31.8 27.2 %copy-start.1 = (bf16[32,128,128]{2,1,0:T(8,128)(2,1)S(1)}, bf16[32,128,128]{2,1,0:T(8,128)(2,1)}, u32[]{:S(2)}) copy-start(bf16[32,128,128]{2,1,0:T(8,128)(2,1)} %param.26) | copy-start | bytes 3145732
  32.7 78.1 %collective-permute-start.1 = (bf16[1,512]{1,0:T(2,128)(2,1)S(1)}, bf16[1,512]{1,0:T(2,128)(2,1)S(1)}, u32[]{:S(2)}, u32[]{:S(2)}) collective-permute-start(bf16[1,512]{1,0:T(2,128)(2,1)S(1)} %bitcast.138), channel_id=1, source_target_pairs={{1,0},{2,1},{3,2},{4,3},{5,4},{6,5},{7,6},{8,7},{9,8},{10,9},{11,1... | collective-permute-start | bytes 3080 | tf_op jit(solution)/shard_map/ppermute | solution.py:25
  42.5 70.4 %collective-permute-start = (bf16[1,512]{1,0:T(2,128)(2,1)S(1)}, bf16[1,512]{1,0:T(2,128)(2,1)S(1)}, u32[]{:S(2)}, u32[]{:S(2)}) collective-permute-start(bf16[1,512]{1,0:T(2,128)(2,1)S(1)} %bitcast.139), channel_id=1, source_target_pairs={{127,0},{0,1},{1,2},{2,3},{3,4},{4,5},{5,6},{6,7},{7,8},{8,9},{9,1... | collective-permute-start | bytes 3080 | tf_op jit(solution)/shard_map/ppermute | solution.py:25
  46.2 38.1 %collective-permute-start.3 = (bf16[1]{0:T(256)(128)(2,1)}, bf16[1]{0:T(256)(128)(2,1)}, u32[]{:S(2)}, u32[]{:S(2)}) collective-permute-start(bf16[1]{0:T(256)(128)(2,1)} %scatter_fusion.3), channel_id=1, source_target_pairs={{1,0},{2,1},{3,2},{4,3},{5,4},{6,5},{7,6},{8,7},{9,8},{10,9},{11,1... | collective-permute-start | bytes 14 | tf_op jit(solution)/shard_map/ppermute | solution.py:25
  57.0 25.3 %collective-permute-start.2 = (bf16[1]{0:T(256)(128)(2,1)}, bf16[1]{0:T(256)(128)(2,1)}, u32[]{:S(2)}, u32[]{:S(2)}) collective-permute-start(bf16[1]{0:T(256)(128)(2,1)} %scatter_fusion.2), channel_id=1, source_target_pairs={{127,0},{0,1},{1,2},{2,3},{3,4},{4,5},{5,6},{6,7},{7,8},{8,9},{9,1... | collective-permute-start | bytes 14 | tf_op jit(solution)/shard_map/ppermute | solution.py:25
  59.0 10.8 %copy-start.15 = (s32[32]{0:T(128)S(1)}, s32[32]{0:T(128)}, u32[]{:S(2)}) copy-start(s32[32]{0:T(128)} %param.30) | copy-start | bytes 388
  59.0 11.2 %copy-start.14 = (f32[4,512]{1,0:T(4,128)S(1)}, f32[4,512]{1,0:T(4,128)}, u32[]{:S(2)}) copy-start(f32[4,512]{1,0:T(4,128)} %param.31) | copy-start | bytes 24580
  60.7 52.9 %collective-permute-start.5 = (bf16[1,128,128]{2,1,0:T(8,128)(2,1)S(1)}, bf16[1,128,128]{2,1,0:T(8,128)(2,1)S(1)}, u32[]{:S(2)}, u32[]{:S(2)}) collective-permute-start(bf16[1,128,128]{2,1,0:T(8,128)(2,1)S(1)} %bitcast.120), channel_id=1, source_target_pairs={{1,0},{2,1},{3,2},{4,3},{5,4},{6,5},{7,6},{8,7},{9,8},{10,9},{11,1... | collective-permute-start | bytes 98312 | tf_op jit(solution)/shard_map/ppermute | solution.py:25
  70.2 1.7 copy-start.2
  73.7 4.0 %copy-start.10 = (bf16[32,512]{1,0:T(8,128)(2,1)S(1)}, bf16[32,512]{1,0:T(8,128)(2,1)}, u32[]{:S(2)}) copy-start(bf16[32,512]{1,0:T(8,128)(2,1)} %param.23) | copy-start | bytes 98308
  82.3 16.7 %collective-permute-start.9 = (bf16[1,512]{1,0:T(2,128)(2,1)S(1)}, bf16[1,512]{1,0:T(2,128)(2,1)S(1)}, u32[]{:S(2)}, u32[]{:S(2)}) collective-permute-start(bf16[1,512]{1,0:T(2,128)(2,1)S(1)} %bitcast.141), channel_id=1, source_target_pairs={{1,0},{2,1},{3,2},{4,3},{5,4},{6,5},{7,6},{8,7},{9,8},{10,9},{11,1... | collective-permute-start | bytes 3080 | tf_op jit(solution)/shard_map/ppermute | solution.py:25
  84.3 18.7 %collective-permute-start.8 = (bf16[1,512]{1,0:T(2,128)(2,1)S(1)}, bf16[1,512]{1,0:T(2,128)(2,1)S(1)}, u32[]{:S(2)}, u32[]{:S(2)}) collective-permute-start(bf16[1,512]{1,0:T(2,128)(2,1)S(1)} %bitcast.140), channel_id=1, source_target_pairs={{127,0},{0,1},{1,2},{2,3},{3,4},{4,5},{5,6},{6,7},{7,8},{8,9},{9,1... | collective-permute-start | bytes 3080 | tf_op jit(solution)/shard_map/ppermute | solution.py:25
  90.6 36.8 %all-to-all-start.1 = ((bf16[128,2,512]{2,1,0:T(2,128)(2,1)}), bf16[128,2,512]{2,1,0:T(2,128)(2,1)S(1)}, u32[]{:S(2)}, u32[]{:S(2)}) async-start(bf16[128,2,512]{2,1,0:T(2,128)(2,1)} %scatter_fusion.1), calls=%async_computation.1 | async-start | bytes 524288 | tf_op jit(solution)/shard_map/all_to_all | solution.py:160
  98.6 82.1 %all-reduce.3.cloned.1.call-start = ((), (), s32[]{:S(2)}) async-start(), calls=%async_computation.2 | async-start | bytes 131072 | tf_op jit(solution)/shard_map/psum | solution.py:243
  99.0 14.5 %collective-permute-start.4 = (bf16[1,128,128]{2,1,0:T(8,128)(2,1)S(1)}, bf16[1,128,128]{2,1,0:T(8,128)(2,1)S(1)}, u32[]{:S(2)}, u32[]{:S(2)}) collective-permute-start(bf16[1,128,128]{2,1,0:T(8,128)(2,1)S(1)} %bitcast.121), channel_id=1, source_target_pairs={{127,0},{0,1},{1,2},{2,3},{3,4},{4,5},{5,6},{6,7},{7,8},{8,9},{9,1... | collective-permute-start | bytes 98312 | tf_op jit(solution)/shard_map/ppermute | solution.py:25
  103.0 14.6 %collective-permute-start.7 = (bf16[1,128,128]{2,1,0:T(8,128)(2,1)S(1)}, bf16[1,128,128]{2,1,0:T(8,128)(2,1)S(1)}, u32[]{:S(2)}, u32[]{:S(2)}) collective-permute-start(bf16[1,128,128]{2,1,0:T(8,128)(2,1)S(1)} %bitcast.122), channel_id=1, source_target_pairs={{1,0},{2,1},{3,2},{4,3},{5,4},{6,5},{7,6},{8,7},{9,8},{10,9},{11,1... | collective-permute-start | bytes 98312 | tf_op jit(solution)/shard_map/ppermute | solution.py:25
  110.8 10.4 %collective-permute-start.6 = (bf16[1,128,128]{2,1,0:T(8,128)(2,1)S(1)}, bf16[1,128,128]{2,1,0:T(8,128)(2,1)S(1)}, u32[]{:S(2)}, u32[]{:S(2)}) collective-permute-start(bf16[1,128,128]{2,1,0:T(8,128)(2,1)S(1)} %bitcast.123), channel_id=1, source_target_pairs={{127,0},{0,1},{1,2},{2,3},{3,4},{4,5},{5,6},{6,7},{7,8},{8,9},{9,1... | collective-permute-start | bytes 98312 | tf_op jit(solution)/shard_map/ppermute | solution.py:25
  127.7 2.4 copy-start.8
  132.9 1.8 copy-start.9
  133.7 47.0 %copy-start.13 = (f32[512]{0:T(512)S(1)}, f32[512]{0:T(512)}, u32[]{:S(2)}) copy-start(f32[512]{0:T(512)} %param.35) | copy-start | bytes 6148
  134.3 48.4 %copy-start.20 = (f32[512]{0:T(512)S(1)}, f32[512]{0:T(512)}, u32[]{:S(2)}) copy-start(f32[512]{0:T(512)} %param.36) | copy-start | bytes 6148
  135.5 96.9 %all-reduce.5.cloned.1.call-start = ((), (), s32[]{:S(2)}) async-start(), calls=%async_computation.3 | async-start | bytes 131072 | tf_op jit(solution)/shard_map/psum | solution.py:254
  184.5 9.4 %copy-start.7 = (bf16[64,512]{1,0:T(8,128)(2,1)S(1)}, bf16[64,512]{1,0:T(8,128)(2,1)}, u32[]{:S(2)}) copy-start(bf16[64,512]{1,0:T(8,128)(2,1)} %all-reduce.3.cloned.1.call-done) | copy-start | bytes 196612
  184.5 47.9 %copy-start.17 = (f32[512]{0:T(512)S(1)}, f32[512]{0:T(512)}, u32[]{:S(2)}) copy-start(f32[512]{0:T(512)} %param.39) | copy-start | bytes 6148
  185.3 50.1 %copy-start.18 = (f32[64]{0:T(128)S(1)}, f32[64]{0:T(128)}, u32[]{:S(2)}) copy-start(f32[64]{0:T(128)} %param.41) | copy-start | bytes 772
  191.8 44.0 %copy-start.4 = (bf16[32,128,128]{2,1,0:T(8,128)(2,1)}, bf16[32,128,128]{2,1,0:T(8,128)(2,1)S(1)}, u32[]{:S(2)}) copy-start(bf16[32,128,128]{2,1,0:T(8,128)(2,1)S(1)} %scatter_fusion.9) | copy-start | bytes 3145732
  193.9 41.9 %copy-start.3 = (bf16[32,128,128]{2,1,0:T(8,128)(2,1)}, bf16[32,128,128]{2,1,0:T(8,128)(2,1)S(1)}, u32[]{:S(2)}) copy-start(bf16[32,128,128]{2,1,0:T(8,128)(2,1)S(1)} %scatter_fusion.11) | copy-start | bytes 3145732
  232.4 3.1 %copy-start.6 = (bf16[16,64,512]{2,1,0:T(8,128)(2,1)S(1)}, bf16[16,64,512]{2,1,0:T(8,128)(2,1)}, u32[]{:S(2)}) copy-start(bf16[16,64,512]{2,1,0:T(8,128)(2,1)} %param.40) | copy-start | bytes 3145732
  (3 other events, 3.6 us)
Sparse Core Ops, SparseCore 0:
  135.6 45.0 all-reduce.2
  185.3 47.0 all-reduce.4
where the time goes:
time: 245 us; the launch traced here: 244 us
  waiting for transfers between devices  86.8 us (35%)
  starting transfers between devices  79.7 us (33%)
  local copies, waits for them, and re-layouts  42.6 us (17%)
  between operations  15 us (6%)
  other arithmetic  11.2 us (5%)
  matrix products  8.35 us (3%)
    ppermute x10, starting transfers between devices, passed_along(): return lax.ppermute(block, axis, route)  50.8 us
    psum x1, waiting for transfers between devices, local(): lax.psum(partial_heads.astype(jnp.bfloat16), 'section').astype(jnp.float32)  44.9 us
    psum x1, waiting for transfers between devices, local(): lax.psum(partial_units.astype(jnp.bfloat16), 'section').astype(jnp.float32)  38.3 us
    all_to_all x1, starting transfers between devices, local(): lax.all_to_all(send_codes, 'batch', split_axis=0, concat_axis=0, tiled=True)  20.8 us
    scatter x10, local copies, waits for them, and re-layouts, pack_side(): return tuple((jnp.zeros((MOVE,) + source_array.shape[1:], source_array.dt...  13.1 us
    all_to_all x1, starting transfers between devices, local(): lax.all_to_all(send_rows, 'batch', split_axis=0, concat_axis=0, tiled=True)  7.95 us
  transfers between devices with their start and end apart: 14, of which 3 were waited for; matrix products, arithmetic and copies ran while one was open for 17% of the time, Pallas kernels for 0%

commit v1 on v0

--- a/solution.py
+++ b/solution.py
@@ -4,25 +4,12 @@
 from jax.sharding import PartitionSpec as P
 
 HEAD_DIM = 64
-MOVE = 1
+CAP = 2
+CODE_LANES = 128
 
 
 EPSILON = 1e-05
 MAX_PERIOD = 10000.0
-
-
-def for_sending(array):
-
-    def short(part):
-        return part.astype(jnp.bfloat16) if part.dtype == jnp.float32 else part
-
-    return jax.tree.map(short, array)
-
-
-def passed_along(block, axis, distance):
-    devices = range(lax.axis_size(axis))
-    route = [((i - distance) % len(devices), i) for i in devices]
-    return lax.ppermute(block, axis, route)
 
 
 def layer_norm(hidden, weight_gain):
@@ -99,18 +86,22 @@
     return attended.astype(jnp.bfloat16).reshape(streams, 2, local_heads * head_width)
 
 
-def pack_side(direction_owner, leaving, dest_owner, slot_ids, outgoing):
-    chosen = leaving & (dest_owner == direction_owner)
-    before = chosen[None, :] & (slot_ids[None, :] < slot_ids[:, None])
-    box_place = jnp.where(chosen, jnp.sum(before.astype(jnp.int32), axis=1), MOVE)
-    return tuple(
-        (
-            jnp.zeros((MOVE,) + source_array.shape[1:], source_array.dtype)
-            .at[box_place]
-            .set(source_array, mode="drop")
-            for source_array in outgoing
-        )
-    )
+def section_sum(partial):
+    size = lax.axis_size("section")
+    if size & (size - 1):
+        return lax.psum(partial.astype(jnp.bfloat16), "section").astype(jnp.float32)
+    total = partial.astype(jnp.bfloat16)
+    bit = size // 2
+    while bit >= 1:
+        route = [(i, i ^ bit) for i in range(size)]
+        other = lax.ppermute(total, "section", route)
+        total = total.astype(jnp.float32) + other.astype(jnp.float32)
+        bit //= 2
+    return total
+
+
+def one_hot(rows, columns):
+    return (rows[:, None] == columns[None, :]).astype(jnp.bfloat16)
 
 
 def local(
@@ -140,76 +131,91 @@
     model_width = latents.shape[1]
     window = cache_keys.shape[1]
     head_share = cache_keys.shape[2]
-    capacity = max(2, streams // owners)
+    capacity = max(CAP, streams // owners)
     slot_ids = jnp.arange(streams, dtype=jnp.int32)
+
+    dest_owner = cache_slot // streams
+    dest_local = cache_slot % streams
+    right_owner = jnp.mod(own_index + 1, owners)
+    left_owner = jnp.mod(own_index + owners - 1, owners)
+    state_rows = model_width // head_share
+
+    def pack(direction_owner):
+        chosen = jnp.sum(jnp.where(dest_owner == direction_owner, slot_ids, 0))
+        code = lax.dynamic_index_in_dim(dest_local, chosen, 0, keepdims=False) + 1
+        pieces = [
+            lax.dynamic_index_in_dim(cache_keys, chosen, 0, keepdims=False),
+            lax.dynamic_index_in_dim(cache_values, chosen, 0, keepdims=False),
+            lax.dynamic_index_in_dim(up_state, chosen, 0, keepdims=False).reshape(
+                state_rows, head_share
+            ),
+            lax.dynamic_index_in_dim(conv_state, chosen, 0, keepdims=False).reshape(
+                state_rows, head_share
+            ),
+            jnp.full((8, head_share), code, jnp.int32).astype(jnp.bfloat16),
+        ]
+        return jnp.concatenate(pieces, axis=0)
+
+    def unpack(box):
+        keys = box[:window]
+        values = box[window : 2 * window]
+        up = box[2 * window : 2 * window + state_rows].reshape(model_width)
+        conv = box[2 * window + state_rows : 2 * window + 2 * state_rows].reshape(model_width)
+        code = box[2 * window + 2 * state_rows, 0].astype(jnp.int32) - 1
+        return keys, values, up, conv, code
+
+    from_left = unpack(
+        lax.ppermute(pack(right_owner), "batch", [(i, (i + 1) % owners) for i in range(owners)])
+    )
+    from_right = unpack(
+        lax.ppermute(pack(left_owner), "batch", [(i, (i - 1) % owners) for i in range(owners)])
+    )
+
     target = token_slot // streams
     landing = token_slot % streams
     same_before = (target[None, :] == target[:, None]) & (slot_ids[None, :] < slot_ids[:, None])
     arrival_rank = jnp.sum(same_before.astype(jnp.int32), axis=1)
-    send_rows = (
-        jnp.zeros((owners, capacity, model_width), jnp.bfloat16)
-        .at[target, arrival_rank]
-        .set(latents)
-    )
-    send_codes = (
-        jnp.zeros((owners, capacity), jnp.bfloat16)
-        .at[target, arrival_rank]
-        .set((landing + 1).astype(jnp.bfloat16))
-    )
-    got_rows, got_codes = (
-        lax.all_to_all(send_rows, "batch", split_axis=0, concat_axis=0, tiled=True),
-        lax.all_to_all(send_codes, "batch", split_axis=0, concat_axis=0, tiled=True),
-    )
-    selector = got_codes.reshape(-1).astype(jnp.int32)[None, :] - 1 == slot_ids[:, None]
+    box_ids = target * capacity + arrival_rank
+    payload = jnp.concatenate(
+        [
+            latents,
+            jnp.broadcast_to((landing + 1).astype(jnp.bfloat16)[:, None], (streams, CODE_LANES)),
+        ],
+        axis=1,
+    )
+    placing = one_hot(jnp.arange(owners * capacity, dtype=jnp.int32), box_ids)
+    send_rows = jnp.dot(placing, payload, preferred_element_type=jnp.float32).astype(jnp.bfloat16)
+    got = lax.all_to_all(
+        send_rows.reshape(owners, capacity, model_width + CODE_LANES),
+        "batch",
+        split_axis=0,
+        concat_axis=0,
+        tiled=True,
+    ).reshape(owners * capacity, model_width + CODE_LANES)
+    got_codes = got[:, model_width].astype(jnp.int32) - 1
     arrived = jnp.dot(
-        selector.astype(jnp.bfloat16),
-        got_rows.reshape(owners * capacity, model_width),
-        preferred_element_type=jnp.float32,
+        one_hot(slot_ids, got_codes), got[:, :model_width], preferred_element_type=jnp.float32
     ).astype(jnp.bfloat16)
-    dest_owner = cache_slot // streams
-    dest_local = cache_slot % streams
-    leaving = dest_owner != own_index
-    stay_codes = jnp.where(leaving, 0, dest_local + 1).astype(jnp.bfloat16)
-    code_values = (dest_local + 1).astype(jnp.bfloat16)
-    outgoing = (cache_keys, cache_values, up_state, conv_state, code_values)
-    right_owner = jnp.mod(own_index + 1, owners)
-    left_owner = jnp.mod(own_index + owners - 1, owners)
-    right_parts = pack_side(right_owner, leaving, dest_owner, slot_ids, outgoing)
-    left_parts = pack_side(left_owner, leaving, dest_owner, slot_ids, outgoing)
-    from_left = jax.tree.map(
-        lambda part, own: part.astype(own.dtype),
-        passed_along(for_sending(right_parts), "batch", 1),
-        right_parts,
-    )
-    from_right = jax.tree.map(
-        lambda part, own: part.astype(own.dtype),
-        passed_along(for_sending(left_parts), "batch", -1),
-        left_parts,
-    )
-    incoming = tuple(
-        (
-            jnp.concatenate([lower_part, upper_part], axis=0)
-            for lower_part, upper_part in zip(from_left, from_right)
-        )
-    )
-    candidate = tuple(
-        (
-            jnp.concatenate([own_array, extra_array], axis=0)
-            for own_array, extra_array in zip(
-                (cache_keys, cache_values, up_state, conv_state, stay_codes), incoming
-            )
-        )
-    )
-    candidate_codes = candidate[4].astype(jnp.int32) - 1
-    matches = candidate_codes[None, :] == slot_ids[:, None]
-    picked = jnp.sum(
-        jnp.where(matches, jnp.arange(candidate_codes.shape[0], dtype=jnp.int32)[None, :], 0),
-        axis=1,
-    )
-    keys_old = jnp.take(candidate[0], picked, axis=0)
-    values_old = jnp.take(candidate[1], picked, axis=0)
-    up_prev = jnp.take(candidate[2], picked, axis=0)
-    conv_prev = jnp.take(candidate[3], picked, axis=0)
+
+    staying = dest_owner == own_index
+    source_of = (dest_local[None, :] == slot_ids[:, None]) & staying[None, :]
+    picking = source_of.astype(jnp.bfloat16)
+    from_l = slot_ids == from_left[4]
+    from_r = slot_ids == from_right[4]
+
+    def gathered(own_rows, left_row, right_row):
+        flat = own_rows.reshape(streams, -1)
+        rows = jnp.dot(picking, flat, preferred_element_type=jnp.float32).astype(own_rows.dtype)
+        rows = rows.reshape(own_rows.shape)
+        shape = (streams,) + (1,) * (own_rows.ndim - 1)
+        rows = jnp.where(from_l.reshape(shape), left_row[None], rows)
+        return jnp.where(from_r.reshape(shape), right_row[None], rows)
+
+    keys_old = gathered(cache_keys, from_left[0], from_right[0])
+    values_old = gathered(cache_values, from_left[1], from_right[1])
+    up_prev = gathered(up_state, from_left[2], from_right[2])
+    conv_prev = gathered(conv_state, from_left[3], from_right[3])
+
     latent_f = arrived.astype(jnp.float32)
     prior_f = up_prev.astype(jnp.float32)
     residual_zero = jnp.stack(
@@ -240,7 +246,7 @@
     partial_heads = jnp.dot(
         attended.reshape(2 * streams, head_share), out_weight, preferred_element_type=jnp.float32
     )
-    mixing = lax.psum(partial_heads.astype(jnp.bfloat16), "section").astype(jnp.float32)
+    mixing = section_sum(partial_heads)
     residual_one = residual_zero + scale_attention * mixing.reshape(streams, 2, model_width)
     normed_two = (
         layer_norm(residual_one, norm_gain_two)
@@ -251,7 +257,7 @@
         jnp.dot(normed_two, in_weight, preferred_element_type=jnp.float32), approximate=False
     ).astype(jnp.bfloat16)
     partial_units = jnp.dot(inner_units, down_weight, preferred_element_type=jnp.float32)
-    feed_forward = lax.psum(partial_units.astype(jnp.bfloat16), "section").astype(jnp.float32)
+    feed_forward = section_sum(partial_units)
     residual_two = residual_one + scale_feedforward * feed_forward.reshape(streams, 2, model_width)
     excited = jax.nn.elu(residual_two).astype(jnp.bfloat16)
     earlier = jnp.stack([conv_prev, excited[:, 0]], axis=1)
@@ -264,23 +270,20 @@
     )
     audio_out = audio_out + conv_bias[:, None, None, None]
     audio_out = audio_out.reshape(conv_bias.shape[0], streams * 2 * stride)
-    slot_first = jnp.mod(positions, window)
-    slot_second = jnp.mod(positions + 1, window)
-    new_keys = (
-        keys_old.at[slot_ids, slot_first]
-        .set(fresh_keys[:, 0])
-        .at[slot_ids, slot_second]
-        .set(fresh_keys[:, 1])
-    )
-    new_values = (
-        values_old.at[slot_ids, slot_first]
-        .set(fresh_values[:, 0])
-        .at[slot_ids, slot_second]
-        .set(fresh_values[:, 1])
+    cycle = jnp.arange(window, dtype=jnp.int32)
+    hit_first = (cycle[None, :] == jnp.mod(positions, window)[:, None])[..., None]
+    hit_second = (cycle[None, :] == jnp.mod(positions + 1, window)[:, None])[..., None]
+    new_keys = jnp.where(
+        hit_second,
+        fresh_keys[:, 1][:, None, :],
+        jnp.where(hit_first, fresh_keys[:, 0][:, None, :], keys_old),
+    )
+    new_values = jnp.where(
+        hit_second,
+        fresh_values[:, 1][:, None, :],
+        jnp.where(hit_first, fresh_values[:, 0][:, None, :], values_old),
     )
     return (audio_out, new_keys, new_values, arrived, excited[:, 1])
-
-
 def solution(mesh):
     placed = (
         P("batch", None),

time: 245 us -> 113 us (0.46)
  waiting for transfers between devices: 86.8 us -> 6.13 us
  starting transfers between devices: 79.7 us -> 44.6 us
  local copies, waits for them, and re-layouts: 42.6 us -> 22.1 us
  between operations: 15 us -> 7.95 us
  other arithmetic: 11.2 us -> 18 us
  matrix products: 8.35 us -> 13.5 us
    psum x2 -> x0, waiting for transfers between devices: 83.2 us -> none  [the longest x1 44.9 us: local(): lax.psum(partial_heads.astype(jnp.bfloat16), 'section').astype(jnp.float32)]
    scatter x16 -> x0, local copies, waits for them, and re-layouts: 28 us -> none  [the longest x10 13.1 us: pack_side(): return tuple((jnp.zeros((MOVE,) + source_array.shape[1:], source_array.dt...]
    ppermute x10 -> x6, starting transfers between devices: 50.8 us -> 23.6 us  [the longest x4 12.4 us: section_sum(): other = lax.ppermute(total, 'section', route)]
    select_n x2 -> x4, other arithmetic: 1.8 us -> 11.4 us  [the longest x1 7.17 us: gathered(): return jnp.where(from_r.reshape(shape), right_row[None], rows)]
    reshape x1 -> x8, local copies, waits for them, and re-layouts: 0.1 us -> 8.11 us  [the longest x2 6.58 us: gathered(): rows = rows.reshape(own_rows.shape)]
    all_to_all x2 -> x1, starting transfers between devices: 28.8 us -> 20.9 us  [local(): lax.all_to_all(send_rows.reshape(owners, capacity, model_width + CODE_LAN...]
    dot_general x1 -> x6, matrix products: 0.14 us -> 6.28 us  [the longest x4 5.15 us: gathered(): jnp.dot(picking, flat, preferred_element_type=jnp.float32)]
    gather x4 -> x0, local copies, waits for them, and re-layouts: 5.8 us -> none  [the longest x1 2.9 us: local(): values_old = jnp.take(candidate[1], picked, axis=0)]
  transfers between devices with their start and end apart: 14 -> 7, of which waited for: 3 -> 3; matrix products, arithmetic and copies ran while one was open for 17% -> 32% of each run, Pallas kernels for 0% -> 0%
where the time goes in v1:
time: 113 us; the launch traced here: 112 us
  starting transfers between devices  44.6 us (39%)
  local copies, waits for them, and re-layouts  22.1 us (20%)
  other arithmetic  18 us (16%)
  matrix products  13.5 us (12%)
  between operations  7.95 us (7%)
  waiting for transfers between devices  6.13 us (5%)
    all_to_all x1, starting transfers between devices, local(): lax.all_to_all(send_rows.reshape(owners, capacity, model_width + CODE_LAN...  20.9 us
    ppermute x4, starting transfers between devices, section_sum(): other = lax.ppermute(total, 'section', route)  12.4 us
    ppermute x1, starting transfers between devices, local(): lax.ppermute(pack(left_owner), 'batch', [(i, (i - 1) % owners) for i in r...  7.2 us
    select_n x1, other arithmetic, gathered(): return jnp.where(from_r.reshape(shape), right_row[None], rows)  7.17 us
    reshape x2, local copies, waits for them, and re-layouts, gathered(): rows = rows.reshape(own_rows.shape)  6.58 us
    ppermute x4, waiting for transfers between devices, section_sum(): other = lax.ppermute(total, 'section', route)  6.13 us
    dot_general x4, matrix products, gathered(): jnp.dot(picking, flat, preferred_element_type=jnp.float32)  5.15 us
    unnamed x55, local copies, waits for them, and re-layouts  4.11 us
  transfers between devices with their start and end apart: 7, of which 3 were waited for; matrix products, arithmetic and copies ran while one was open for 32% of the time, Pallas kernels for 0%

profile of v1, /device:TPU:1, one launch (start us, length us, event | category | flops | bytes accessed | tf_op | source)
XLA Modules:
  0.0 112.3 jit_solution(10363761653061969011)
XLA Ops:
  0.7 0.7 and_select_fusion.1
  1.7 1.0 convolution_convert_fusion.2
  2.7 0.9 reshape.343
  3.5 20.9 %all-to-all-start = ((bf16[128,2,640]{2,1,0:T(2,128)(2,1)}), bf16[128,2,640]{2,1,0:T(2,128)(2,1)S(1)}, u32[]{:S(2)}, u32[]{:S(2)}) async-start(bf16[128,2,640]{2,1,0:T(2,128)(2,1)} %reshape.343), calls=%async_computation | async-start | bytes 655360 | tf_op jit(solution)/shard_map/all_to_all | solution.py:188
  30.4 0.8 constant_dynamic-slice_fusion.2
  31.4 0.8 dynamic-slice_reduce_fusion.2
  33.9 4.0 %collective-permute-start.1 = (bf16[272,128]{0,1:T(8,128)(2,1)S(1)}, bf16[272,128]{0,1:T(8,128)(2,1)S(1)}, u32[]{:S(2)}, u32[]{:S(2)}) collective-permute-start(bf16[272,128]{0,1:T(8,128)(2,1)S(1)} %concatenate.17), channel_id=1, source_target_pairs={{0,1},{1,2},{2,3},{3,4},{4,5},{5,6},{6,7},{7,8},{8,9},{9,10},{10,1... | collective-permute-start | bytes 208904 | tf_op jit(solution)/shard_map/ppermute | solution.py:168
  39.2 7.2 %collective-permute-start = (bf16[272,128]{0,1:T(8,128)(2,1)S(1)}, bf16[272,128]{0,1:T(8,128)(2,1)S(1)}, u32[]{:S(2)}, u32[]{:S(2)}) collective-permute-start(bf16[272,128]{0,1:T(8,128)(2,1)S(1)} %concatenate.16), channel_id=1, source_target_pairs={{0,127},{1,0},{2,1},{3,2},{4,3},{5,4},{6,5},{7,6},{8,7},{9,8},{10,... | collective-permute-start | bytes 208904 | tf_op jit(solution)/shard_map/ppermute | solution.py:171
  48.1 3.3 %reshape.350 = bf16[32,128,2,64]{3,2,1,0:T(2,128)(2,1)} reshape(bf16[32,16384]{1,0:T(8,128)(2,1)S(1)} %convolution_convert_fusion.1) | data formatting | bytes 2097152 | tf_op jit(solution)/shard_map/reshape | solution.py:209
  51.4 2.0 %convolution_convert_fusion = bf16[32,16384]{1,0:T(8,128)(2,1)S(1)} fusion(bf16[4,8,128,128]{3,2,1,0:T(8,128)(2,1)} %bitcast.128, s32[32]{0:T(128)S(1)} %and_select_fusion.2, pred[32]{0:T(512)(128)(4,1)S(1)} %get-tuple-element.39), kind=kOutput, calls=%fused_computation.1 | convolution fusion | flops 34080768 | bytes 2097312 | tf_op jit(solution)/shard_map/dot_general | solution.py:208
  53.4 3.3 %reshape.352 = bf16[32,128,2,64]{3,2,1,0:T(2,128)(2,1)} reshape(bf16[32,16384]{1,0:T(8,128)(2,1)S(1)} %convolution_convert_fusion) | data formatting | bytes 2097152 | tf_op jit(solution)/shard_map/reshape | solution.py:209
  56.7 1.2 %copy.234 = bf16[4,8,128,128]{3,2,1,0:T(8,128)(2,1)} copy(bf16[4,8,128,128]{3,1,2,0:T(8,128)(2,1)S(1)} %bitcast.126) | data formatting | bytes 2097152
  59.2 1.2 %copy.233 = bf16[4,8,128,128]{3,2,1,0:T(8,128)(2,1)} copy(bf16[4,8,128,128]{3,1,2,0:T(8,128)(2,1)S(1)} %bitcast.125) | data formatting | bytes 2097152
  64.3 7.2 %broadcast_select_fusion.3 = (bf16[32,128,2,64]{3,2,1,0:T(2,128)(2,1)}, bf16[32,128,2,64]{3,2,1,0:T(2,128)(2,1)S(1)}) fusion(pred[32]{0:T(512)(128)(4,1)S(1)} %iota_compare_fusion.10, bf16[32,128,2,64]{3,2,1,0:T(2,128)(2,1)} %reshape.350, pred[32]{0:T(512)(128)(4,1)S(1)} %iota_compare_fusion.9, bf16[128,2,64]{2,1,0:T(2,128)(2,1)S(1)} %copy.198, ...), kind=kLoop, calls=%fused_computation.6 | loop fusion | flops 2097152 | bytes 4325440 | tf_op jit(solution)/shard_map/jit(_where)/select_n | solution.py:212
  71.9 0.7 copy.223
  72.8 0.9 fusion.173
  74.0 1.5 %select_bitcast_fusion = bf16[32,1,512]{2,0,1:T(8,128)(2,1)} fusion(pred[32]{0:T(512)(128)(4,1)} %copy-done.19, pred[32]{0:T(512)(128)(4,1)} %copy-done.21, bf16[512]{0:T(512)(128)(2,1)S(1)} %bitcast.155, bf16[512]{0:T(512)(128)(2,1)S(1)} %bitcast.156, bf16[32,512]{1,0:T(8,128)(2,1)} %param.24, s32[32]{0:T(128)} %copy-done.16, pred[32]{0:T(512)(128)(4,1)} %copy-done.17), kind=kOutput, calls=%fused_computation.155 | convolution fusion | flops 1099776 | bytes 67808 | tf_op jit(solution)/shard_map/dot_general | solution.py:208
  75.9 0.9 fusion.46
  77.1 1.3 %convolution_bitcast_fusion = f32[3,32,2,128]{3,1,0,2:T(8,128)S(1)} fusion(bf16[3,512,128]{2,1,0:T(8,128)(2,1)} %param.29, f32[512]{0:T(512)} %param.28, f32[32,2]{0,1:T(2,128)S(1)} %add_rsqrt_fusion, f32[32,2]{0,1:T(2,128)S(1)} %broadcast_multiply_fusion, f32[32,1,512]{2,0,1:T(8,128)S(1)} %get-tuple-element.68, f32[32,1,512]{2,0,1:T(8,128)S(1)} %get-tuple-element.67), kind=kOutput, calls=%fused_computation.20 | convolution fusion | flops 25329664 | bytes 625152 | tf_op jit(solution)/shard_map/sfd,kde->ksfe/dot_general | solution.py:229
  79.8 1.2 %fusion.10 = f32[32,2,2,128]{3,2,1,0:T(2,128)S(1)} fusion(bf16[32,2,2,64]{3,1,2,0:T(2,128)(2,1)S(1)} %copy.203, bf16[32,128,2,64]{3,2,1,0:T(2,128)(2,1)S(1)} %get-tuple-element.80), kind=kOutput, calls=%fused_computation.21 | convolution fusion | flops 2113536 | bytes 1130496 | tf_op jit(solution)/shard_map/sfhe,swhe->shfw/dot_general | solution.py:46
  81.8 0.8 copy-done.3
  83.7 2.2 %collective-permute-start.2 = (bf16[64,512]{1,0:T(8,128)(2,1)S(1)}, bf16[64,512]{1,0:T(8,128)(2,1)S(1)}, u32[]{:S(2)}, u32[]{:S(2)}) collective-permute-start(bf16[64,512]{1,0:T(8,128)(2,1)S(1)} %convolution_convert_fusion.4), channel_id=1, source_target_pairs={{0,256},{128,384},{256,0},{384,128},{1,257},{129,385},{257,1},{385... | collective-permute-start | bytes 196616 | tf_op jit(solution)/shard_map/ppermute | solution.py:97
  86.2 2.6 %collective-permute-done.2 = bf16[64,512]{1,0:T(8,128)(2,1)S(1)} collective-permute-done((bf16[64,512]{1,0:T(8,128)(2,1)S(1)}, bf16[64,512]{1,0:T(8,128)(2,1)S(1)}, u32[]{:S(2)}, u32[]{:S(2)}) %collective-permute-start.2) | collective-permute-done | bytes 65568 | tf_op jit(solution)/shard_map/ppermute | solution.py:97
  88.7 4.6 %collective-permute-start.3 = (f32[64,512]{1,0:T(8,128)S(1)}, f32[64,512]{1,0:T(8,128)S(1)}, u32[]{:S(2)}, u32[]{:S(2)}) collective-permute-start(f32[64,512]{1,0:T(8,128)S(1)} %convert_add_fusion.1), channel_id=1, source_target_pairs={{0,128},{128,0},{256,384},{384,256},{1,129},{129,1},{257,385},{385... | collective-permute-start | bytes 393224 | tf_op jit(solution)/shard_map/ppermute | solution.py:97
  93.3 1.0 collective-permute-done.3
  94.7 1.8 %convolution_convert_fusion.3 = bf16[64,512]{1,0:T(8,128)(2,1)S(1)} fusion(bf16[512,512]{1,0:T(8,128)(2,1)S(1)} %copy-done, bf16[512,512]{1,0:T(8,128)(2,1)} %param.33, f32[64,512]{1,0:T(8,128)S(1)} %get-tuple-element.37, f32[512]{0:T(512)S(1)} %copy-done.25, f32[64]{0:T(128)S(1)} %add_rsqrt_fusion.1, f32[64]{0:T(128)S(1)} %broadcast_multiply_fusion.1), kind=kOutput, calls=%fused_computation.18 | convolution fusion | flops 69402624 | bytes 1247744 | tf_op jit(solution)/shard_map/dot_general | solution.py:259
  96.6 2.2 %collective-permute-start.4 = (bf16[64,512]{1,0:T(8,128)(2,1)S(1)}, bf16[64,512]{1,0:T(8,128)(2,1)S(1)}, u32[]{:S(2)}, u32[]{:S(2)}) collective-permute-start(bf16[64,512]{1,0:T(8,128)(2,1)S(1)} %convolution_convert_fusion.3), channel_id=1, source_target_pairs={{0,256},{128,384},{256,0},{384,128},{1,257},{129,385},{257,1},{385... | collective-permute-start | bytes 196616 | tf_op jit(solution)/shard_map/ppermute | solution.py:97
  99.0 2.6 %collective-permute-done.4 = bf16[64,512]{1,0:T(8,128)(2,1)S(1)} collective-permute-done((bf16[64,512]{1,0:T(8,128)(2,1)S(1)}, bf16[64,512]{1,0:T(8,128)(2,1)S(1)}, u32[]{:S(2)}, u32[]{:S(2)}) %collective-permute-start.4) | collective-permute-done | bytes 65568 | tf_op jit(solution)/shard_map/ppermute | solution.py:97
  102.3 3.4 %collective-permute-start.5 = (f32[64,512]{1,0:T(8,128)}, f32[64,512]{1,0:T(8,128)S(1)}, u32[]{:S(2)}, u32[]{:S(2)}) collective-permute-start(f32[64,512]{1,0:T(8,128)} %convert_add_fusion), channel_id=1, source_target_pairs={{0,128},{128,0},{256,384},{384,256},{1,129},{129,1},{257,385},{385... | collective-permute-start | bytes 393224 | tf_op jit(solution)/shard_map/ppermute | solution.py:97
  105.8 2.8 %fusion.15 = (bf16[32,128,128]{2,1,0:T(8,128)(2,1)}, bf16[32,128,128]{2,1,0:T(8,128)(2,1)}) fusion(bf16[4,8,128,128]{3,2,1,0:T(8,128)(2,1)S(1)} %copy-done.1, pred[32]{0:T(512)(128)(4,1)S(1)} %copy-done.20, pred[32]{0:T(512)(128)(4,1)S(1)} %copy-done.22, pred[32,128]{1,0:T(8,128)(4,1)S(1)} %copy-done.11, pred[32,128]{1,0:T(8,128)(4,1)S(1)} %copy-done.12, ...), kind=kLoop, calls=%fused_computation.29 | loop fusion | flops 4194304 | bytes 4366400 | tf_op jit(solution)/shard_map/jit(_where)/select_n | solution.py:281
  109.5 1.4 %fusion.24 = f32[32,2,8,64]{3,0,2,1:T(8,128)S(1)} fusion(bf16[16,64,512]{2,1,0:T(8,128)(2,1)} %param.36, bf16[32,2,512]{2,0,1:T(8,128)(2,1)S(1)} %fusion.34), kind=kOutput, calls=%fused_computation.39 | convolution fusion | flops 33554432 | bytes 720896 | tf_op jit(solution)/shard_map/sfi,rci->csfr/dot_general | solution.py:265
  111.5 0.8 copy.227
  (154 shorter events, 17.0 us)
Async XLA Ops:
  0.6 94.1 %copy-start = (bf16[512,512]{1,0:T(8,128)(2,1)S(1)}, bf16[512,512]{1,0:T(8,128)(2,1)}, u32[]{:S(2)}) copy-start(bf16[512,512]{1,0:T(8,128)(2,1)} %param.34) | copy-start | bytes 1572868
  0.6 45.8 %copy-start.14 = (s32[32]{0:T(128)S(1)}, s32[32]{0:T(128)}, u32[]{:S(2)}) copy-start(s32[32]{0:T(128)} %param.26) | copy-start | bytes 388
  0.7 46.0 %copy-start.15 = (f32[4,512]{1,0:T(4,128)S(1)}, f32[4,512]{1,0:T(4,128)}, u32[]{:S(2)}) copy-start(f32[4,512]{1,0:T(4,128)} %param.27) | copy-start | bytes 24580
  3.5 43.8 %copy-start.4 = (bf16[32,128,128]{2,1,0:T(8,128)(2,1)S(1)}, bf16[32,128,128]{2,1,0:T(8,128)(2,1)}, u32[]{:S(2)}) copy-start(bf16[32,128,128]{2,1,0:T(8,128)(2,1)} %param.22) | copy-start | bytes 3145732
  3.5 72.0 %all-to-all-start = ((bf16[128,2,640]{2,1,0:T(2,128)(2,1)}), bf16[128,2,640]{2,1,0:T(2,128)(2,1)S(1)}, u32[]{:S(2)}, u32[]{:S(2)}) async-start(bf16[128,2,640]{2,1,0:T(2,128)(2,1)} %reshape.343), calls=%async_computation | async-start | bytes 655360 | tf_op jit(solution)/shard_map/all_to_all | solution.py:188
  25.2 26.2 %copy-start.16 = (s32[32]{0:T(128)}, s32[32]{0:T(128)S(1)}, u32[]{:S(2)}) copy-start(s32[32]{0:T(128)S(1)} %and_select_fusion.2) | copy-start | bytes 388
  25.8 25.6 %copy-start.17 = (pred[32]{0:T(512)(128)(4,1)}, pred[32]{0:T(512)(128)(4,1)S(1)}, u32[]{:S(2)}) copy-start(pred[32]{0:T(512)(128)(4,1)S(1)} %get-tuple-element.39) | copy-start | bytes 100
  33.9 27.3 %collective-permute-start.1 = (bf16[272,128]{0,1:T(8,128)(2,1)S(1)}, bf16[272,128]{0,1:T(8,128)(2,1)S(1)}, u32[]{:S(2)}, u32[]{:S(2)}) collective-permute-start(bf16[272,128]{0,1:T(8,128)(2,1)S(1)} %concatenate.17), channel_id=1, source_target_pairs={{0,1},{1,2},{2,3},{3,4},{4,5},{5,6},{6,7},{7,8},{8,9},{9,10},{10,1... | collective-permute-start | bytes 208904 | tf_op jit(solution)/shard_map/ppermute | solution.py:168
  39.2 23.3 %collective-permute-start = (bf16[272,128]{0,1:T(8,128)(2,1)S(1)}, bf16[272,128]{0,1:T(8,128)(2,1)S(1)}, u32[]{:S(2)}, u32[]{:S(2)}) collective-permute-start(bf16[272,128]{0,1:T(8,128)(2,1)S(1)} %concatenate.16), channel_id=1, source_target_pairs={{0,127},{1,0},{2,1},{3,2},{4,3},{5,4},{6,5},{7,6},{8,7},{9,8},{10,... | collective-permute-start | bytes 208904 | tf_op jit(solution)/shard_map/ppermute | solution.py:171
  62.5 9.0 %copy-start.19 = (pred[32]{0:T(512)(128)(4,1)}, pred[32]{0:T(512)(128)(4,1)S(1)}, u32[]{:S(2)}) copy-start(pred[32]{0:T(512)(128)(4,1)S(1)} %iota_compare_fusion.9) | copy-start | bytes 100
  62.5 1.4 %copy-start.6 = (bf16[272,128]{0,1:T(8,128)(2,1)}, bf16[272,128]{0,1:T(8,128)(2,1)S(1)}, u32[]{:S(2)}) copy-start(bf16[272,128]{0,1:T(8,128)(2,1)S(1)} %collective-permute-done) | copy-start | bytes 208900
  63.8 7.7 %copy-start.21 = (pred[32]{0:T(512)(128)(4,1)}, pred[32]{0:T(512)(128)(4,1)S(1)}, u32[]{:S(2)}) copy-start(pred[32]{0:T(512)(128)(4,1)S(1)} %iota_compare_fusion.10) | copy-start | bytes 100
  78.4 2.7 %copy-start.24 = (pred[2,2]{1,0:T(4,128)(4,1)S(1)}, pred[2,2]{1,0:T(4,128)(4,1)}, u32[]{:S(2)}) copy-start(pred[2,2]{1,0:T(4,128)(4,1)} %iota_compare_fusion.8) | copy-start | bytes 16
  81.0 1.6 %copy-start.3 = (bf16[32,128,2,64]{3,2,1,0:T(2,128)(2,1)S(1)}, bf16[32,128,2,64]{3,2,1,0:T(2,128)(2,1)}, u32[]{:S(2)}) copy-start(bf16[32,128,2,64]{3,2,1,0:T(2,128)(2,1)} %get-tuple-element.79) | copy-start | bytes 3145732
  81.6 2.0 %copy-start.8 = (bf16[128,512]{1,0:T(8,128)(2,1)S(1)}, bf16[128,512]{1,0:T(8,128)(2,1)}, u32[]{:S(2)}) copy-start(bf16[128,512]{1,0:T(8,128)(2,1)} %param.30) | copy-start | bytes 393220
  82.6 11.7 %copy-start.13 = (f32[512]{0:T(512)S(1)}, f32[512]{0:T(512)}, u32[]{:S(2)}) copy-start(f32[512]{0:T(512)} %param.31) | copy-start | bytes 6148
  82.6 12.1 %copy-start.25 = (f32[512]{0:T(512)S(1)}, f32[512]{0:T(512)}, u32[]{:S(2)}) copy-start(f32[512]{0:T(512)} %param.32) | copy-start | bytes 6148
  83.7 5.0 %collective-permute-start.2 = (bf16[64,512]{1,0:T(8,128)(2,1)S(1)}, bf16[64,512]{1,0:T(8,128)(2,1)S(1)}, u32[]{:S(2)}, u32[]{:S(2)}) collective-permute-start(bf16[64,512]{1,0:T(8,128)(2,1)S(1)} %convolution_convert_fusion.4), channel_id=1, source_target_pairs={{0,256},{128,384},{256,0},{384,128},{1,257},{129,385},{257,1},{385... | collective-permute-start | bytes 196616 | tf_op jit(solution)/shard_map/ppermute | solution.py:97
  88.7 5.5 %collective-permute-start.3 = (f32[64,512]{1,0:T(8,128)S(1)}, f32[64,512]{1,0:T(8,128)S(1)}, u32[]{:S(2)}, u32[]{:S(2)}) collective-permute-start(f32[64,512]{1,0:T(8,128)S(1)} %convert_add_fusion.1), channel_id=1, source_target_pairs={{0,128},{128,0},{256,384},{384,256},{1,129},{129,1},{257,385},{385... | collective-permute-start | bytes 393224 | tf_op jit(solution)/shard_map/ppermute | solution.py:97
  94.6 11.1 %copy-start.1 = (bf16[4,8,128,128]{3,2,1,0:T(8,128)(2,1)S(1)}, bf16[4,8,128,128]{3,2,1,0:T(8,128)(2,1)}, u32[]{:S(2)}) copy-start(bf16[4,8,128,128]{3,2,1,0:T(8,128)(2,1)} %copy.234) | copy-start | bytes 3145732
  94.6 11.1 %copy-start.2 = (bf16[4,8,128,128]{3,2,1,0:T(8,128)(2,1)S(1)}, bf16[4,8,128,128]{3,2,1,0:T(8,128)(2,1)}, u32[]{:S(2)}) copy-start(bf16[4,8,128,128]{3,2,1,0:T(8,128)(2,1)} %copy.233) | copy-start | bytes 3145732
  94.6 11.1 %copy-start.7 = (bf16[128,128]{1,0:T(8,128)(2,1)S(1)}, bf16[128,128]{1,0:T(8,128)(2,1)}, u32[]{:S(2)}) copy-start(bf16[128,128]{1,0:T(8,128)(2,1)} %copy.223) | copy-start | bytes 98308
  94.6 11.1 %copy-start.11 = (pred[32,128]{1,0:T(8,128)(4,1)S(1)}, pred[32,128]{1,0:T(8,128)(4,1)}, u32[]{:S(2)}) copy-start(pred[32,128]{1,0:T(8,128)(4,1)} %iota_compare_fusion.4) | copy-start | bytes 12292
  94.7 11.1 %copy-start.12 = (pred[32,128]{1,0:T(8,128)(4,1)S(1)}, pred[32,128]{1,0:T(8,128)(4,1)}, u32[]{:S(2)}) copy-start(pred[32,128]{1,0:T(8,128)(4,1)} %iota_compare_fusion.5) | copy-start | bytes 12292
  94.7 11.1 %copy-start.20 = (pred[32]{0:T(512)(128)(4,1)S(1)}, pred[32]{0:T(512)(128)(4,1)}, u32[]{:S(2)}) copy-start(pred[32]{0:T(512)(128)(4,1)} %copy-done.19) | copy-start | bytes 100
  94.7 11.1 %copy-start.22 = (pred[32]{0:T(512)(128)(4,1)S(1)}, pred[32]{0:T(512)(128)(4,1)}, u32[]{:S(2)}) copy-start(pred[32]{0:T(512)(128)(4,1)} %copy-done.21) | copy-start | bytes 100
  96.6 5.0 %collective-permute-start.4 = (bf16[64,512]{1,0:T(8,128)(2,1)S(1)}, bf16[64,512]{1,0:T(8,128)(2,1)S(1)}, u32[]{:S(2)}, u32[]{:S(2)}) collective-permute-start(bf16[64,512]{1,0:T(8,128)(2,1)S(1)} %convolution_convert_fusion.3), channel_id=1, source_target_pairs={{0,256},{128,384},{256,0},{384,128},{1,257},{129,385},{257,1},{385... | collective-permute-start | bytes 196616 | tf_op jit(solution)/shard_map/ppermute | solution.py:97
  102.3 6.4 %collective-permute-start.5 = (f32[64,512]{1,0:T(8,128)}, f32[64,512]{1,0:T(8,128)S(1)}, u32[]{:S(2)}, u32[]{:S(2)}) collective-permute-start(f32[64,512]{1,0:T(8,128)} %convert_add_fusion), channel_id=1, source_target_pairs={{0,128},{128,0},{256,384},{384,256},{1,129},{129,1},{257,385},{385... | collective-permute-start | bytes 393224 | tf_op jit(solution)/shard_map/ppermute | solution.py:97
  105.7 3.0 %copy-start.18 = (f32[512]{0:T(512)S(1)}, f32[512]{0:T(512)}, u32[]{:S(2)}) copy-start(f32[512]{0:T(512)} %param.35) | copy-start | bytes 6148
  108.6 2.3 %copy-start.5 = (bf16[16,64,512]{2,1,0:T(8,128)(2,1)S(1)}, bf16[16,64,512]{2,1,0:T(8,128)(2,1)}, u32[]{:S(2)}) copy-start(bf16[16,64,512]{2,1,0:T(8,128)(2,1)} %param.36) | copy-start | bytes 3145732
  108.6 2.3 %copy-start.10 = (bf16[32,1,512]{2,0,1:T(8,128)(2,1)S(1)}, bf16[32,1,512]{2,0,1:T(8,128)(2,1)}, u32[]{:S(2)}) copy-start(bf16[32,1,512]{2,0,1:T(8,128)(2,1)} %select_bitcast_fusion) | copy-start | bytes 98308
  108.6 2.4 %copy-start.23 = (f32[64]{0:T(128)S(1)}, f32[64]{0:T(128)}, u32[]{:S(2)}) copy-start(f32[64]{0:T(128)} %param.37) | copy-start | bytes 772
  (1 other events, 1.2 us)

commit v2 on v1

--- a/solution.py
+++ b/solution.py
@@ -33,21 +33,21 @@
     return turned.reshape(features.shape)
 
 
-def attend(
-    queries, fresh_keys, fresh_values, old_keys, old_values, starts, local_heads, head_width
-):
-    streams = old_keys.shape[0]
-    window = old_keys.shape[1]
-    query_heads = queries.reshape(streams, 2, local_heads, head_width)
-    cache_heads = old_keys.reshape(streams, window, local_heads, head_width)
-    fresh_heads = fresh_keys.reshape(streams, 2, local_heads, head_width)
+def attend(queries, fresh_keys, fresh_values, old_keys, old_values, starts, local_heads, head_width):
+    streams, window, share = old_keys.shape
+    head_of = jnp.arange(share, dtype=jnp.int32) // head_width
+    head_ids = jnp.arange(local_heads, dtype=jnp.int32)
+    in_head = head_of[None, :] == head_ids[:, None]
+    lanes = in_head[None, :, None, :]
+    masked = jnp.where(lanes, queries[:, None], jnp.zeros((), queries.dtype))
+    masked = masked.reshape(streams, local_heads * 2, share)
     score_scale = head_width ** (-0.5)
     cache_scores = (
-        jnp.einsum("sfhe,swhe->shfw", query_heads, cache_heads, preferred_element_type=jnp.float32)
+        jnp.einsum("sxd,swd->sxw", masked, old_keys, preferred_element_type=jnp.float32)
         * score_scale
     )
     fresh_scores = (
-        jnp.einsum("sfhe,sghe->shfg", query_heads, fresh_heads, preferred_element_type=jnp.float32)
+        jnp.einsum("sxd,sgd->sxg", masked, fresh_keys, preferred_element_type=jnp.float32)
         * score_scale
     )
     cycle_slots = jnp.arange(window, dtype=jnp.int32)
@@ -56,34 +56,36 @@
     cache_ok = (held_time[:, None, :] >= 0) & (
         held_time[:, None, :] > query_times[:, :, None] - window
     )
+    cache_ok = jnp.broadcast_to(cache_ok[:, None], (streams, local_heads, 2, window)).reshape(
+        streams, local_heads * 2, window
+    )
     frame_ids = jnp.arange(2, dtype=jnp.int32)
-    fresh_ok = frame_ids[None, :] <= frame_ids[:, None]
-    allowed = jnp.concatenate(
-        [
-            jnp.broadcast_to(cache_ok[:, None], (streams, local_heads, 2, window)),
-            jnp.broadcast_to(fresh_ok, (streams, local_heads, 2, 2)),
-        ],
-        axis=-1,
-    )
-    scores = jnp.concatenate([cache_scores, fresh_scores], axis=-1)
-    scores = jnp.where(allowed, scores, -jnp.inf)
-    score_max = jnp.max(scores, axis=-1, keepdims=True)
-    weights = jnp.where(allowed, jnp.exp(scores - score_max), 0.0)
-    denominator = jnp.sum(weights, axis=-1, keepdims=True)
-    rounded = weights.astype(jnp.bfloat16)
-    value_heads = old_values.reshape(streams, window, local_heads, head_width)
-    fresh_value_heads = fresh_values.reshape(streams, 2, local_heads, head_width)
-    attended = jnp.einsum(
-        "shfw,swhe->sfhe", rounded[..., :window], value_heads, preferred_element_type=jnp.float32
-    )
-    attended = attended + jnp.einsum(
-        "shfg,sghe->sfhe",
-        rounded[..., window:],
-        fresh_value_heads,
+    fresh_ok = jnp.tile(frame_ids[None, :] <= frame_ids[:, None], (local_heads, 1))[None]
+    cache_scores = jnp.where(cache_ok, cache_scores, -jnp.inf)
+    fresh_scores = jnp.where(fresh_ok, fresh_scores, -jnp.inf)
+    score_max = jnp.maximum(
+        jnp.max(cache_scores, axis=-1, keepdims=True), jnp.max(fresh_scores, axis=-1, keepdims=True)
+    )
+    cache_weights = jnp.where(cache_ok, jnp.exp(cache_scores - score_max), 0.0)
+    fresh_weights = jnp.where(fresh_ok, jnp.exp(fresh_scores - score_max), 0.0)
+    denominator = jnp.sum(cache_weights, axis=-1, keepdims=True) + jnp.sum(
+        fresh_weights, axis=-1, keepdims=True
+    )
+    spread = jnp.einsum(
+        "sxw,swd->sxd",
+        cache_weights.astype(jnp.bfloat16),
+        old_values,
         preferred_element_type=jnp.float32,
     )
-    attended = attended / jnp.transpose(denominator, (0, 2, 1, 3))
-    return attended.astype(jnp.bfloat16).reshape(streams, 2, local_heads * head_width)
+    spread = spread + jnp.einsum(
+        "sxg,sgd->sxd",
+        fresh_weights.astype(jnp.bfloat16),
+        fresh_values,
+        preferred_element_type=jnp.float32,
+    )
+    spread = (spread / denominator).reshape(streams, local_heads, 2, share)
+    attended = jnp.sum(jnp.where(lanes, spread, 0.0), axis=1)
+    return attended.astype(jnp.bfloat16)
 
 
 def section_sum(partial):
@@ -141,17 +143,18 @@
     state_rows = model_width // head_share
 
     def pack(direction_owner):
-        chosen = jnp.sum(jnp.where(dest_owner == direction_owner, slot_ids, 0))
-        code = lax.dynamic_index_in_dim(dest_local, chosen, 0, keepdims=False) + 1
+        chosen = dest_owner == direction_owner
+        code = jnp.sum(jnp.where(chosen, dest_local + 1, 0))
+
+        def pick(rows):
+            shape = (streams,) + (1,) * (rows.ndim - 1)
+            return jnp.sum(jnp.where(chosen.reshape(shape), rows, jnp.zeros((), rows.dtype)), axis=0)
+
         pieces = [
-            lax.dynamic_index_in_dim(cache_keys, chosen, 0, keepdims=False),
-            lax.dynamic_index_in_dim(cache_values, chosen, 0, keepdims=False),
-            lax.dynamic_index_in_dim(up_state, chosen, 0, keepdims=False).reshape(
-                state_rows, head_share
-            ),
-            lax.dynamic_index_in_dim(conv_state, chosen, 0, keepdims=False).reshape(
-                state_rows, head_share
-            ),
+            pick(cache_keys),
+            pick(cache_values),
+            pick(up_state).reshape(state_rows, head_share),
+            pick(conv_state).reshape(state_rows, head_share),
             jnp.full((8, head_share), code, jnp.int32).astype(jnp.bfloat16),
         ]
         return jnp.concatenate(pieces, axis=0)
@@ -204,9 +207,8 @@
     from_r = slot_ids == from_right[4]
 
     def gathered(own_rows, left_row, right_row):
-        flat = own_rows.reshape(streams, -1)
-        rows = jnp.dot(picking, flat, preferred_element_type=jnp.float32).astype(own_rows.dtype)
-        rows = rows.reshape(own_rows.shape)
+        rows = jnp.tensordot(picking, own_rows, axes=1, preferred_element_type=jnp.float32)
+        rows = rows.astype(own_rows.dtype)
         shape = (streams,) + (1,) * (own_rows.ndim - 1)
         rows = jnp.where(from_l.reshape(shape), left_row[None], rows)
         return jnp.where(from_r.reshape(shape), right_row[None], rows)

time: 113 us -> 93.6 us (0.83)
  local copies, waits for them, and re-layouts: 22.1 us -> 8.34 us
  other arithmetic: 18 us -> 7.3 us
  waiting for transfers between devices: 6.13 us -> 15.9 us
  between operations: 7.95 us -> 3.95 us
    select_n x3 -> x1, other arithmetic: 10.7 us -> 0.01 us  [attend(): head_of = jnp.arange(share, dtype=jnp.int32) // head_width]
    all_to_all x1, starting transfers between devices: 20.9 us -> 10.7 us  [local(): lax.all_to_all(send_rows.reshape(owners, capacity, model_width + CODE_LAN...]
    ppermute x1, starting transfers between devices: 7.2 us -> 16.9 us  [local(): lax.ppermute(pack(left_owner), 'batch', [(i, (i - 1) % owners) for i in r...]
    all_to_all x1, waiting for transfers between devices: 0.01 us -> 9.54 us  [local(): lax.all_to_all(send_rows.reshape(owners, capacity, model_width + CODE_LAN...]
    reshape x6 -> x0, local copies, waits for them, and re-layouts: 7.12 us -> none  [the longest x2 6.58 us: gathered(): rows = rows.reshape(own_rows.shape)]
    reduce_sum x1 -> x6, other arithmetic: 0.64 us -> 4.26 us  [the longest x2 2.65 us: pick(): jnp.sum(jnp.where(chosen.reshape(shape), rows, jnp.zeros((), rows.dtype))...]
    dot_general x8, matrix products: 7.39 us -> 10.2 us  [the longest x4 7.18 us: gathered(): jnp.tensordot(picking, own_rows, axes=1, preferred_element_type=jnp.float32)]
    dynamic_slice x7 -> x0, local copies, waits for them, and re-layouts: 2.7 us -> none  [the longest x3 1.07 us: pack(): lax.dynamic_index_in_dim(cache_values, chosen, 0, keepdims=False)]
  transfers between devices with their start and end apart: 7 -> 7, of which waited for: 3 -> 4; matrix products, arithmetic and copies ran while one was open for 32% -> 9% of each run, Pallas kernels for 0% -> 0%
where the time goes in v2:
time: 93.6 us; the launch traced here: 93 us
  starting transfers between devices  44.1 us (47%)
  waiting for transfers between devices  15.9 us (17%)
  matrix products  13.5 us (14%)
  local copies, waits for them, and re-layouts  8.34 us (9%)
  other arithmetic  7.3 us (8%)
  between operations  3.95 us (4%)
    ppermute x1, starting transfers between devices, local(): lax.ppermute(pack(left_owner), 'batch', [(i, (i - 1) % owners) for i in r...  16.9 us
    ppermute x4, starting transfers between devices, section_sum(): other = lax.ppermute(total, 'section', route)  14.6 us
    all_to_all x1, starting transfers between devices, local(): lax.all_to_all(send_rows.reshape(owners, capacity, model_width + CODE_LAN...  10.7 us
    all_to_all x1, waiting for transfers between devices, local(): lax.all_to_all(send_rows.reshape(owners, capacity, model_width + CODE_LAN...  9.54 us
    dot_general x4, matrix products, gathered(): jnp.tensordot(picking, own_rows, axes=1, preferred_element_type=jnp.float32)  7.18 us
    ppermute x4, waiting for transfers between devices, section_sum(): other = lax.ppermute(total, 'section', route)  6.33 us
    unnamed x41, local copies, waits for them, and re-layouts  4.23 us
    reduce_sum x2, other arithmetic, pick(): jnp.sum(jnp.where(chosen.reshape(shape), rows, jnp.zeros((), rows.dtype))...  2.65 us
  transfers between devices with their start and end apart: 7, of which 4 were waited for; matrix products, arithmetic and copies ran while one was open for 9% of the time, Pallas kernels for 0%

profile of v2, /device:TPU:1, one launch (start us, length us, event | category | flops | bytes accessed | tf_op | source)
XLA Modules:
  0.0 93.0 jit_solution(14176546364779821583)
XLA Ops:
  0.7 0.7 broadcast_compare_fusion.1
  1.4 1.3 %select_reduce_fusion.10 = (s32[]{:T(128)}, s32[]{:T(128)}, s32[32]{0:T(128)S(1)}, pred[32]{0:T(512)(128)(4,1)S(1)}, pred[32]{0:T(512)(128)(4,1)S(1)}) fusion(s32[32]{0:T(128)} %param.25, s32[32]{0:T(128)S(1)} %get-tuple-element.43, s32[]{:T(128)S(6)} %select_n.176, s32[]{:T(128)S(6)} %select_n.169), kind=kLoop, calls=%fused_computation.226 | loop fusion | flops 574 | bytes 464 | tf_op jit(solution)/shard_map/reduce_sum | solution.py:147
  3.4 2.5 %select_reduce_fusion.3 = (bf16[128,128]{1,0:T(8,128)(2,1)S(1)}, bf16[128,128]{1,0:T(8,128)(2,1)S(1)}, bf16[128,128]{1,0:T(8,128)(2,1)S(1)}, bf16[128,128]{1,0:T(8,128)(2,1)S(1)}) fusion(bf16[32,128,128]{2,1,0:T(8,128)(2,1)} %param.21, pred[32]{0:T(512)(128)(4,1)S(1)} %get-tuple-element.46, pred[32]{0:T(512)(128)(4,1)S(1)} %get-tuple-element.45, ...), kind=kLoop, calls=%fused_computation.29 | loop fusion | flops 4128768 | bytes 2228288 | tf_op jit(solution)/shard_map/reduce_sum | solution.py:151
  6.2 16.9 %collective-permute-start = (bf16[272,128]{1,0:T(8,128)(2,1)S(1)}, bf16[272,128]{1,0:T(8,128)(2,1)S(1)}, u32[]{:S(2)}, u32[]{:S(2)}) collective-permute-start(bf16[272,128]{1,0:T(8,128)(2,1)S(1)} %concatenate.10), channel_id=1, source_target_pairs={{0,127},{1,0},{2,1},{3,2},{4,3},{5,4},{6,5},{7,6},{8,7},{9,8},{10,... | collective-permute-start | bytes 208904 | tf_op jit(solution)/shard_map/ppermute | solution.py:174
  23.8 1.9 %collective-permute-start.1 = (bf16[272,128]{1,0:T(8,128)(2,1)S(1)}, bf16[272,128]{1,0:T(8,128)(2,1)S(1)}, u32[]{:S(2)}, u32[]{:S(2)}) collective-permute-start(bf16[272,128]{1,0:T(8,128)(2,1)S(1)} %concatenate.11), channel_id=1, source_target_pairs={{0,1},{1,2},{2,3},{3,4},{4,5},{5,6},{6,7},{7,8},{8,9},{9,10},{10,1... | collective-permute-start | bytes 208904 | tf_op jit(solution)/shard_map/ppermute | solution.py:171
  26.2 0.8 reshape.387
  27.1 10.7 %all-to-all-start = ((bf16[128,2,640]{2,1,0:T(2,128)(2,1)}), bf16[128,2,640]{2,1,0:T(2,128)(2,1)S(1)}, u32[]{:S(2)}, u32[]{:S(2)}) async-start(bf16[128,2,640]{2,1,0:T(2,128)(2,1)} %reshape.387), calls=%async_computation | async-start | bytes 655360 | tf_op jit(solution)/shard_map/all_to_all | solution.py:191
  38.6 0.5 slice.127
  39.8 0.5 slice.129
  41.0 1.7 %select_select_fusion.3 = bf16[32,128,128]{2,0,1:T(8,128)(2,1)} fusion(pred[32]{0:T(512)(128)(4,1)S(1)} %iota_compare_fusion.10, pred[32]{0:T(512)(128)(4,1)S(1)} %iota_compare_fusion.11, bf16[128,128]{1,0:T(8,128)(2,1)S(1)} %get-tuple-element.62, bf16[128,128]{1,0:T(8,128)(2,1)S(1)} %get-tuple-element.60, bf16[32,128,128]{2,1,0:T(8,128)(2,1)S(1)} %copy-done.1, ...), kind=kOutput, calls=%fused_computation.25 | convolution fusion | flops 35129344 | bytes 2162912 | tf_op jit(solution)/shard_map/dot_general | solution.py:210
  42.7 9.5 %all-to-all-done = bf16[128,2,640]{2,1,0:T(2,128)(2,1)S(1)} async-done(((bf16[128,2,640]{2,1,0:T(2,128)(2,1)}), bf16[128,2,640]{2,1,0:T(2,128)(2,1)S(1)}, u32[]{:S(2)}, u32[]{:S(2)}) %all-to-all-start) | async-done | bytes 327712 | tf_op jit(solution)/shard_map/all_to_all | solution.py:191
  53.6 0.4 subtract_convert_fusion.1
  54.0 0.4 pad_maximum_fusion.1
  54.6 2.0 %fusion.178 = (f32[32,4]{1,0:T(8,128)S(1)}, f32[32,4,128]{2,1,0:T(4,128)S(1)}) fusion(bf16[32,128,128]{2,0,1:T(8,128)(2,1)} %select_select_fusion.3, bf16[32,4,128]{2,1,0:T(4,128)(2,1)S(1)} %bitcast.99, pred[4,128]{1,0:T(4,128)(4,1)S(1)} %broadcast_in_dim.359, pred[32,4,128]{2,0,1:T(32,128)(4,1)S(1)} %bitcast.95), kind=kOutput, calls=%fused_computation.279 | convolution fusion | flops 4259712 | bytes 1164288 | tf_op jit(solution)/shard_map/sxd,swd->sxw/dot_general | solution.py:46
  57.5 5.2 %select_select_fusion = (bf16[32,128,128]{2,0,1:T(8,128)(2,1)S(1)}, bf16[32,128,128]{2,0,1:T(8,128)(2,1)}, bf16[32,128,128]{2,0,1:T(8,128)(2,1)S(1)}) fusion(pred[32,128]{0,1:T(8,128)(4,1)S(1)} %get-tuple-element.95, pred[32,128]{0,1:T(8,128)(4,1)S(1)} %get-tuple-element.96, bf16[32,128]{1,0:T(8,128)(2,1)S(1)} %get-tuple-element.74, ...), kind=kOutput, calls=%fused_computation.22 | convolution fusion | flops 37226496 | bytes 5349600 | tf_op jit(solution)/shard_map/dot_general | solution.py:210
  62.7 0.5 fusion.2
  63.3 0.3 copy-done.6
  63.8 2.2 %collective-permute-start.2 = (bf16[64,512]{1,0:T(8,128)(2,1)S(1)}, bf16[64,512]{1,0:T(8,128)(2,1)S(1)}, u32[]{:S(2)}, u32[]{:S(2)}) collective-permute-start(bf16[64,512]{1,0:T(8,128)(2,1)S(1)} %convolution_convert_fusion.4), channel_id=1, source_target_pairs={{0,256},{128,384},{256,0},{384,128},{1,257},{129,385},{257,1},{385... | collective-permute-start | bytes 196616 | tf_op jit(solution)/shard_map/ppermute | solution.py:99
  66.0 2.8 %collective-permute-done.2 = bf16[64,512]{1,0:T(8,128)(2,1)S(1)} collective-permute-done((bf16[64,512]{1,0:T(8,128)(2,1)S(1)}, bf16[64,512]{1,0:T(8,128)(2,1)S(1)}, u32[]{:S(2)}, u32[]{:S(2)}) %collective-permute-start.2) | collective-permute-done | bytes 65568 | tf_op jit(solution)/shard_map/ppermute | solution.py:99
  68.8 6.8 %collective-permute-start.3 = (f32[64,512]{1,0:T(8,128)S(1)}, f32[64,512]{1,0:T(8,128)S(1)}, u32[]{:S(2)}, u32[]{:S(2)}) collective-permute-start(f32[64,512]{1,0:T(8,128)S(1)} %convert_add_fusion.1), channel_id=1, source_target_pairs={{0,128},{128,0},{256,384},{384,256},{1,129},{129,1},{257,385},{385... | collective-permute-start | bytes 393224 | tf_op jit(solution)/shard_map/ppermute | solution.py:99
  75.8 0.8 collective-permute-done.3
  76.9 1.8 %convolution_convert_fusion.3 = bf16[64,512]{1,0:T(8,128)(2,1)S(1)} fusion(bf16[512,512]{1,0:T(8,128)(2,1)S(1)} %copy-done, bf16[512,512]{1,0:T(8,128)(2,1)} %param.33, f32[64,512]{1,0:T(8,128)S(1)} %get-tuple-element.40, f32[512]{0:T(512)S(1)} %copy-done.17, f32[64]{0:T(128)S(1)} %add_rsqrt_fusion.1, f32[64]{0:T(128)S(1)} %broadcast_multiply_fusion.1), kind=kOutput, calls=%fused_computation.6 | convolution fusion | flops 69402624 | bytes 1247744 | tf_op jit(solution)/shard_map/dot_general | solution.py:261
  78.7 2.2 %collective-permute-start.4 = (bf16[64,512]{1,0:T(8,128)(2,1)S(1)}, bf16[64,512]{1,0:T(8,128)(2,1)S(1)}, u32[]{:S(2)}, u32[]{:S(2)}) collective-permute-start(bf16[64,512]{1,0:T(8,128)(2,1)S(1)} %convolution_convert_fusion.3), channel_id=1, source_target_pairs={{0,256},{128,384},{256,0},{384,128},{1,257},{129,385},{257,1},{385... | collective-permute-start | bytes 196616 | tf_op jit(solution)/shard_map/ppermute | solution.py:99
  81.0 2.8 %collective-permute-done.4 = bf16[64,512]{1,0:T(8,128)(2,1)S(1)} collective-permute-done((bf16[64,512]{1,0:T(8,128)(2,1)S(1)}, bf16[64,512]{1,0:T(8,128)(2,1)S(1)}, u32[]{:S(2)}, u32[]{:S(2)}) %collective-permute-start.4) | collective-permute-done | bytes 65568 | tf_op jit(solution)/shard_map/ppermute | solution.py:99
  83.8 3.4 %collective-permute-start.5 = (f32[64,512]{1,0:T(8,128)S(1)}, f32[64,512]{1,0:T(8,128)S(1)}, u32[]{:S(2)}, u32[]{:S(2)}) collective-permute-start(f32[64,512]{1,0:T(8,128)S(1)} %convert_add_fusion), channel_id=1, source_target_pairs={{0,128},{128,0},{256,384},{384,256},{1,129},{129,1},{257,385},{385... | collective-permute-start | bytes 393224 | tf_op jit(solution)/shard_map/ppermute | solution.py:99
  87.3 1.4 %copy.97 = bf16[32,128,128]{2,1,0:T(8,128)(2,1)} copy(bf16[32,128,128]{2,0,1:T(8,128)(2,1)S(1)} %copy-done.3) | data formatting | bytes 2097152
  88.7 1.4 %copy.98 = bf16[32,128,128]{2,1,0:T(8,128)(2,1)} copy(bf16[32,128,128]{2,0,1:T(8,128)(2,1)S(1)} %get-tuple-element.71) | data formatting | bytes 2097152
  90.4 0.6 slice_bitcast_fusion
  91.0 0.3 copy-done.4
  91.3 0.4 fusion.10
  91.7 0.4 fusion.1
  92.2 0.8 copy.96
  (115 shorter events, 5.2 us)
Async XLA Ops:
  0.6 76.3 %copy-start = (bf16[512,512]{1,0:T(8,128)(2,1)S(1)}, bf16[512,512]{1,0:T(8,128)(2,1)}, u32[]{:S(2)}) copy-start(bf16[512,512]{1,0:T(8,128)(2,1)} %param.34) | copy-start | bytes 1572868
  3.3 2.6 %copy-start.9 = (bf16[32,512]{1,0:T(8,128)(2,1)S(1)}, bf16[32,512]{1,0:T(8,128)(2,1)}, u32[]{:S(2)}) copy-start(bf16[32,512]{1,0:T(8,128)(2,1)} %param.23) | copy-start | bytes 98308
  3.4 2.6 %copy-start.10 = (bf16[32,512]{1,0:T(8,128)(2,1)S(1)}, bf16[32,512]{1,0:T(8,128)(2,1)}, u32[]{:S(2)}) copy-start(bf16[32,512]{1,0:T(8,128)(2,1)} %param.24) | copy-start | bytes 98308
  3.4 22.3 %copy-start.18 = (s32[32]{0:T(128)S(1)}, s32[32]{0:T(128)}, u32[]{:S(2)}) copy-start(s32[32]{0:T(128)} %param.20) | copy-start | bytes 388
  3.4 22.6 %copy-start.7 = (bf16[32,512]{1,0:T(8,128)(2,1)S(1)}, bf16[32,512]{1,0:T(8,128)(2,1)}, u32[]{:S(2)}) copy-start(bf16[32,512]{1,0:T(8,128)(2,1)} %param.19) | copy-start | bytes 98308
  6.0 31.8 %copy-start.12 = (s32[32]{0:T(128)S(1)}, s32[32]{0:T(128)}, u32[]{:S(2)}) copy-start(s32[32]{0:T(128)} %param.26) | copy-start | bytes 388
  6.0 32.0 %copy-start.13 = (f32[4,512]{1,0:T(4,128)S(1)}, f32[4,512]{1,0:T(4,128)}, u32[]{:S(2)}) copy-start(f32[4,512]{1,0:T(4,128)} %param.27) | copy-start | bytes 24580
  6.2 32.4 %collective-permute-start = (bf16[272,128]{1,0:T(8,128)(2,1)S(1)}, bf16[272,128]{1,0:T(8,128)(2,1)S(1)}, u32[]{:S(2)}, u32[]{:S(2)}) collective-permute-start(bf16[272,128]{1,0:T(8,128)(2,1)S(1)} %concatenate.10), channel_id=1, source_target_pairs={{0,127},{1,0},{2,1},{3,2},{4,3},{5,4},{6,5},{7,6},{8,7},{9,8},{10,... | collective-permute-start | bytes 208904 | tf_op jit(solution)/shard_map/ppermute | solution.py:174
  23.8 16.0 %collective-permute-start.1 = (bf16[272,128]{1,0:T(8,128)(2,1)S(1)}, bf16[272,128]{1,0:T(8,128)(2,1)S(1)}, u32[]{:S(2)}, u32[]{:S(2)}) collective-permute-start(bf16[272,128]{1,0:T(8,128)(2,1)S(1)} %concatenate.11), channel_id=1, source_target_pairs={{0,1},{1,2},{2,3},{3,4},{4,5},{5,6},{6,7},{7,8},{8,9},{9,10},{10,1... | collective-permute-start | bytes 208904 | tf_op jit(solution)/shard_map/ppermute | solution.py:171
  26.0 15.0 %copy-start.1 = (bf16[32,128,128]{2,1,0:T(8,128)(2,1)S(1)}, bf16[32,128,128]{2,1,0:T(8,128)(2,1)}, u32[]{:S(2)}) copy-start(bf16[32,128,128]{2,1,0:T(8,128)(2,1)} %param.21) | copy-start | bytes 3145732
  27.1 25.2 %all-to-all-start = ((bf16[128,2,640]{2,1,0:T(2,128)(2,1)}), bf16[128,2,640]{2,1,0:T(2,128)(2,1)S(1)}, u32[]{:S(2)}, u32[]{:S(2)}) async-start(bf16[128,2,640]{2,1,0:T(2,128)(2,1)} %reshape.387), calls=%async_computation | async-start | bytes 655360 | tf_op jit(solution)/shard_map/all_to_all | solution.py:191
  42.7 10.4 %copy-start.5 = (bf16[3,512,128]{2,1,0:T(8,128)(2,1)S(1)}, bf16[3,512,128]{2,1,0:T(8,128)(2,1)}, u32[]{:S(2)}) copy-start(bf16[3,512,128]{2,1,0:T(8,128)(2,1)} %param.29) | copy-start | bytes 1179652
  42.7 10.4 %copy-start.14 = (f32[512]{0:T(512)S(1)}, f32[512]{0:T(512)}, u32[]{:S(2)}) copy-start(f32[512]{0:T(512)} %param.28) | copy-start | bytes 6148
  52.6 1.3 %copy-start.8 = (bf16[32,512]{1,0:T(8,128)(2,1)}, bf16[32,512]{1,0:T(8,128)(2,1)S(1)}, u32[]{:S(2)}) copy-start(bf16[32,512]{1,0:T(8,128)(2,1)S(1)} %convolution_convert_fusion.7) | copy-start | bytes 98308
  54.6 3.0 %copy-start.2 = (bf16[32,128,128]{2,1,0:T(8,128)(2,1)S(1)}, bf16[32,128,128]{2,1,0:T(8,128)(2,1)}, u32[]{:S(2)}) copy-start(bf16[32,128,128]{2,1,0:T(8,128)(2,1)} %param.22) | copy-start | bytes 3145732
  62.7 0.9 copy-start.6
  62.7 13.8 %copy-start.11 = (f32[512]{0:T(512)S(1)}, f32[512]{0:T(512)}, u32[]{:S(2)}) copy-start(f32[512]{0:T(512)} %param.31) | copy-start | bytes 6148
  63.3 13.7 %copy-start.17 = (f32[512]{0:T(512)S(1)}, f32[512]{0:T(512)}, u32[]{:S(2)}) copy-start(f32[512]{0:T(512)} %param.32) | copy-start | bytes 6148
  63.8 5.0 %collective-permute-start.2 = (bf16[64,512]{1,0:T(8,128)(2,1)S(1)}, bf16[64,512]{1,0:T(8,128)(2,1)S(1)}, u32[]{:S(2)}, u32[]{:S(2)}) collective-permute-start(bf16[64,512]{1,0:T(8,128)(2,1)S(1)} %convolution_convert_fusion.4), channel_id=1, source_target_pairs={{0,256},{128,384},{256,0},{384,128},{1,257},{129,385},{257,1},{385... | collective-permute-start | bytes 196616 | tf_op jit(solution)/shard_map/ppermute | solution.py:99
  68.8 7.8 %collective-permute-start.3 = (f32[64,512]{1,0:T(8,128)S(1)}, f32[64,512]{1,0:T(8,128)S(1)}, u32[]{:S(2)}, u32[]{:S(2)}) collective-permute-start(f32[64,512]{1,0:T(8,128)S(1)} %convert_add_fusion.1), channel_id=1, source_target_pairs={{0,128},{128,0},{256,384},{384,256},{1,129},{129,1},{257,385},{385... | collective-permute-start | bytes 393224 | tf_op jit(solution)/shard_map/ppermute | solution.py:99
  76.9 10.4 %copy-start.3 = (bf16[32,128,128]{2,0,1:T(8,128)(2,1)S(1)}, bf16[32,128,128]{2,0,1:T(8,128)(2,1)}, u32[]{:S(2)}) copy-start(bf16[32,128,128]{2,0,1:T(8,128)(2,1)} %get-tuple-element.72) | copy-start | bytes 3145732
  78.7 5.0 %collective-permute-start.4 = (bf16[64,512]{1,0:T(8,128)(2,1)S(1)}, bf16[64,512]{1,0:T(8,128)(2,1)S(1)}, u32[]{:S(2)}, u32[]{:S(2)}) collective-permute-start(bf16[64,512]{1,0:T(8,128)(2,1)S(1)} %convolution_convert_fusion.3), channel_id=1, source_target_pairs={{0,256},{128,384},{256,0},{384,128},{1,257},{129,385},{257,1},{385... | collective-permute-start | bytes 196616 | tf_op jit(solution)/shard_map/ppermute | solution.py:99
  83.8 6.4 %collective-permute-start.5 = (f32[64,512]{1,0:T(8,128)S(1)}, f32[64,512]{1,0:T(8,128)S(1)}, u32[]{:S(2)}, u32[]{:S(2)}) collective-permute-start(f32[64,512]{1,0:T(8,128)S(1)} %convert_add_fusion), channel_id=1, source_target_pairs={{0,128},{128,0},{256,384},{384,256},{1,129},{129,1},{257,385},{385... | collective-permute-start | bytes 393224 | tf_op jit(solution)/shard_map/ppermute | solution.py:99
  88.7 1.6 %copy-start.15 = (f32[512]{0:T(512)S(1)}, f32[512]{0:T(512)}, u32[]{:S(2)}) copy-start(f32[512]{0:T(512)} %param.35) | copy-start | bytes 6148
  90.1 1.2 %copy-start.4 = (bf16[16,64,512]{2,1,0:T(8,128)(2,1)S(1)}, bf16[16,64,512]{2,1,0:T(8,128)(2,1)}, u32[]{:S(2)}) copy-start(bf16[16,64,512]{2,1,0:T(8,128)(2,1)} %param.36) | copy-start | bytes 3145732
  90.2 1.5 %copy-start.16 = (f32[64]{0:T(128)S(1)}, f32[64]{0:T(128)}, u32[]{:S(2)}) copy-start(f32[64]{0:T(128)} %param.37) | copy-start | bytes 772

commit v3 on v2

--- a/solution.py
+++ b/solution.py
@@ -90,16 +90,14 @@
 
 def section_sum(partial):
     size = lax.axis_size("section")
-    if size & (size - 1):
-        return lax.psum(partial.astype(jnp.bfloat16), "section").astype(jnp.float32)
-    total = partial.astype(jnp.bfloat16)
-    bit = size // 2
-    while bit >= 1:
-        route = [(i, i ^ bit) for i in range(size)]
-        other = lax.ppermute(total, "section", route)
-        total = total.astype(jnp.float32) + other.astype(jnp.float32)
-        bit //= 2
-    return total
+    rounded = partial.astype(jnp.bfloat16)
+    copies = jnp.broadcast_to(rounded[None], (size,) + rounded.shape)
+    every = lax.all_to_all(copies, "section", 0, 0, tiled=False).astype(jnp.float32)
+    terms = [every[i] for i in range(size)]
+    while len(terms) > 1:
+        paired = [terms[i] + terms[i + 1] for i in range(0, len(terms) - 1, 2)]
+        terms = paired + ([terms[-1]] if len(terms) % 2 else [])
+    return terms[0]
 
 
 def one_hot(rows, columns):
@@ -179,25 +177,24 @@
     same_before = (target[None, :] == target[:, None]) & (slot_ids[None, :] < slot_ids[:, None])
     arrival_rank = jnp.sum(same_before.astype(jnp.int32), axis=1)
     box_ids = target * capacity + arrival_rank
-    payload = jnp.concatenate(
-        [
-            latents,
-            jnp.broadcast_to((landing + 1).astype(jnp.bfloat16)[:, None], (streams, CODE_LANES)),
-        ],
-        axis=1,
-    )
     placing = one_hot(jnp.arange(owners * capacity, dtype=jnp.int32), box_ids)
-    send_rows = jnp.dot(placing, payload, preferred_element_type=jnp.float32).astype(jnp.bfloat16)
-    got = lax.all_to_all(
-        send_rows.reshape(owners, capacity, model_width + CODE_LANES),
-        "batch",
-        split_axis=0,
-        concat_axis=0,
-        tiled=True,
-    ).reshape(owners * capacity, model_width + CODE_LANES)
-    got_codes = got[:, model_width].astype(jnp.int32) - 1
+    send_rows = jnp.dot(placing, latents, preferred_element_type=jnp.float32).astype(jnp.bfloat16)
+    send_codes = jnp.dot(
+        placing,
+        jnp.broadcast_to((landing + 1).astype(jnp.bfloat16)[:, None], (streams, CODE_LANES)),
+        preferred_element_type=jnp.float32,
+    ).astype(jnp.bfloat16)
+    code_block = send_codes.reshape(owners, capacity, CODE_LANES)[:, :, 0]
+    code_block = jnp.pad(code_block, ((0, 0), (0, CODE_LANES - capacity)))
+    send = jnp.concatenate(
+        [send_rows.reshape(owners, capacity * model_width), code_block], axis=1
+    )
+    got = lax.all_to_all(send, "batch", split_axis=0, concat_axis=0, tiled=True)
+    got_codes = got[:, capacity * model_width : capacity * model_width + capacity]
+    got_codes = got_codes.reshape(owners * capacity).astype(jnp.int32) - 1
+    got_rows = got[:, : capacity * model_width].reshape(owners * capacity, model_width)
     arrived = jnp.dot(
-        one_hot(slot_ids, got_codes), got[:, :model_width], preferred_element_type=jnp.float32
+        one_hot(slot_ids, got_codes), got_rows, preferred_element_type=jnp.float32
     ).astype(jnp.bfloat16)
 
     staying = dest_owner == own_index

time: 93.6 us -> 96 us (1.026)
  local copies, waits for them, and re-layouts: 8.34 us -> 12 us
  starting transfers between devices: 44.1 us -> 40.9 us
    ppermute x4 -> x0, starting transfers between devices: 14.6 us -> none  [section_sum(): other = lax.ppermute(total, 'section', route)]
    all_to_all x1 -> x3, starting transfers between devices: 10.7 us -> 22.2 us  [the longest x2 11.5 us: section_sum(): lax.all_to_all(copies, 'section', 0, 0, tiled=False).astype(jnp.float32)]
    all_to_all x1 -> x3, waiting for transfers between devices: 9.54 us -> 16.6 us  [the longest x1 9.54 us: local(): got = lax.all_to_all(send, 'batch', split_axis=0, concat_axis=0, tiled=True)]
    ppermute x4 -> x0, waiting for transfers between devices: 6.33 us -> none  [section_sum(): other = lax.ppermute(total, 'section', route)]
    unnamed x41 -> x45, local copies, waits for them, and re-layouts: 4.23 us -> 6.52 us
    broadcast_in_dim x1 -> x2, local copies, waits for them, and re-layouts: 0.07 us -> 1.45 us  [section_sum(): copies = jnp.broadcast_to(rounded[None], (size,) + rounded.shape)]
  transfers between devices with their start and end apart: 7 -> 5, of which waited for: 4 -> 3; matrix products, arithmetic and copies ran while one was open for 9% -> 11% of each run, Pallas kernels for 0% -> 0%
where the time goes in v3:
time: 96 us; the launch traced here: 95.3 us
  starting transfers between devices  40.9 us (43%)
  waiting for transfers between devices  16.6 us (17%)
  matrix products  13.7 us (14%)
  local copies, waits for them, and re-layouts  12 us (12%)
  other arithmetic  8.17 us (9%)
  between operations  4 us (4%)
    ppermute x1, starting transfers between devices, local(): lax.ppermute(pack(left_owner), 'batch', [(i, (i - 1) % owners) for i in r...  16.9 us
    all_to_all x2, starting transfers between devices, section_sum(): lax.all_to_all(copies, 'section', 0, 0, tiled=False).astype(jnp.float32)  11.5 us
    all_to_all x1, starting transfers between devices, local(): got = lax.all_to_all(send, 'batch', split_axis=0, concat_axis=0, tiled=True)  10.7 us
    all_to_all x1, waiting for transfers between devices, local(): got = lax.all_to_all(send, 'batch', split_axis=0, concat_axis=0, tiled=True)  9.54 us
    dot_general x4, matrix products, gathered(): jnp.tensordot(picking, own_rows, axes=1, preferred_element_type=jnp.float32)  7.18 us
    all_to_all x2, waiting for transfers between devices, section_sum(): lax.all_to_all(copies, 'section', 0, 0, tiled=False).astype(jnp.float32)  7.05 us
    unnamed x45, local copies, waits for them, and re-layouts  6.52 us
    reduce_sum x2, other arithmetic, pick(): jnp.sum(jnp.where(chosen.reshape(shape), rows, jnp.zeros((), rows.dtype))...  2.65 us
  transfers between devices with their start and end apart: 5, of which 3 were waited for; matrix products, arithmetic and copies ran while one was open for 11% of the time, Pallas kernels for 0%

profile of v3, /device:TPU:1, one launch (start us, length us, event | category | flops | bytes accessed | tf_op | source)
XLA Modules:
  0.0 95.3 jit_solution(3678047370477839583)
XLA Ops:
  0.7 0.7 broadcast_compare_fusion.1
  1.4 1.3 %select_reduce_fusion.10 = (s32[]{:T(128)}, s32[]{:T(128)}, s32[32]{0:T(128)S(1)}, pred[32]{0:T(512)(128)(4,1)S(1)}, pred[32]{0:T(512)(128)(4,1)S(1)}) fusion(s32[32]{0:T(128)} %param.25, s32[32]{0:T(128)S(1)} %get-tuple-element.47, s32[]{:T(128)S(6)} %select_n.176, s32[]{:T(128)S(6)} %select_n.169), kind=kLoop, calls=%fused_computation.241 | loop fusion | flops 574 | bytes 464 | tf_op jit(solution)/shard_map/reduce_sum | solution.py:145
  3.4 2.5 %select_reduce_fusion.3 = (bf16[128,128]{1,0:T(8,128)(2,1)S(1)}, bf16[128,128]{1,0:T(8,128)(2,1)S(1)}, bf16[128,128]{1,0:T(8,128)(2,1)S(1)}, bf16[128,128]{1,0:T(8,128)(2,1)S(1)}) fusion(bf16[32,128,128]{2,1,0:T(8,128)(2,1)} %param.21, pred[32]{0:T(512)(128)(4,1)S(1)} %get-tuple-element.50, pred[32]{0:T(512)(128)(4,1)S(1)} %get-tuple-element.49, ...), kind=kLoop, calls=%fused_computation.30 | loop fusion | flops 4128768 | bytes 2228288 | tf_op jit(solution)/shard_map/reduce_sum | solution.py:149
  6.2 16.9 %collective-permute-start = (bf16[272,128]{1,0:T(8,128)(2,1)S(1)}, bf16[272,128]{1,0:T(8,128)(2,1)S(1)}, u32[]{:S(2)}, u32[]{:S(2)}) collective-permute-start(bf16[272,128]{1,0:T(8,128)(2,1)S(1)} %concatenate.10), channel_id=1, source_target_pairs={{0,127},{1,0},{2,1},{3,2},{4,3},{5,4},{6,5},{7,6},{8,7},{9,8},{10,... | collective-permute-start | bytes 208904 | tf_op jit(solution)/shard_map/ppermute | solution.py:172
  23.7 1.9 %collective-permute-start.1 = (bf16[272,128]{1,0:T(8,128)(2,1)S(1)}, bf16[272,128]{1,0:T(8,128)(2,1)S(1)}, u32[]{:S(2)}, u32[]{:S(2)}) collective-permute-start(bf16[272,128]{1,0:T(8,128)(2,1)S(1)} %concatenate.11), channel_id=1, source_target_pairs={{0,1},{1,2},{2,3},{3,4},{4,5},{5,6},{6,7},{7,8},{8,9},{9,10},{10,1... | collective-permute-start | bytes 208904 | tf_op jit(solution)/shard_map/ppermute | solution.py:169
  26.1 0.9 copy.134
  27.3 0.5 broadcast.459
  27.9 0.9 reduce.10
  28.7 1.1 %reshape.429 = bf16[128,2,576]{2,1,0:T(2,128)(2,1)} reshape(bf16[128,1152]{1,0:T(8,128)(2,1)S(1)} %reduce.10) | data formatting | bytes 589824
  29.8 10.7 %all-to-all-start = ((bf16[128,2,576]{2,1,0:T(2,128)(2,1)}), bf16[128,2,576]{2,1,0:T(2,128)(2,1)S(1)}, u32[]{:S(2)}, u32[]{:S(2)}) async-start(bf16[128,2,576]{2,1,0:T(2,128)(2,1)} %reshape.429), calls=%async_computation | async-start | bytes 655360 | tf_op jit(solution)/shard_map/all_to_all | solution.py:192
  41.3 0.5 slice.166
  42.4 0.5 slice.164
  43.7 1.7 %select_select_fusion.3 = bf16[32,128,128]{2,0,1:T(8,128)(2,1)} fusion(pred[32]{0:T(512)(128)(4,1)S(1)} %iota_compare_fusion.12, pred[32]{0:T(512)(128)(4,1)S(1)} %iota_compare_fusion.13, bf16[128,128]{1,0:T(8,128)(2,1)S(1)} %get-tuple-element.66, bf16[128,128]{1,0:T(8,128)(2,1)S(1)} %get-tuple-element.64, bf16[32,128,128]{2,1,0:T(8,128)(2,1)S(1)} %copy-done.1, ...), kind=kOutput, calls=%fused_computation.26 | convolution fusion | flops 35129344 | bytes 2162912 | tf_op jit(solution)/shard_map/dot_general | solution.py:207
  45.4 9.5 %all-to-all-done = bf16[128,2,576]{2,1,0:T(2,128)(2,1)S(1)} async-done(((bf16[128,2,576]{2,1,0:T(2,128)(2,1)}), bf16[128,2,576]{2,1,0:T(2,128)(2,1)S(1)}, u32[]{:S(2)}, u32[]{:S(2)}) %all-to-all-start) | async-done | bytes 294944 | tf_op jit(solution)/shard_map/all_to_all | solution.py:192
  55.0 0.5 reshape.430
  57.3 0.4 pad_maximum_fusion.1
  58.0 2.0 %fusion.190 = (f32[32,4]{1,0:T(8,128)S(1)}, f32[32,4,128]{2,1,0:T(4,128)S(1)}) fusion(bf16[32,128,128]{2,0,1:T(8,128)(2,1)} %select_select_fusion.3, bf16[32,4,128]{2,1,0:T(4,128)(2,1)S(1)} %bitcast.130, pred[4,128]{1,0:T(4,128)(4,1)S(1)} %broadcast_in_dim.371, pred[32,4,128]{2,0,1:T(32,128)(4,1)S(1)} %bitcast.125), kind=kOutput, calls=%fused_computation.290 | convolution fusion | flops 4259712 | bytes 1164288 | tf_op jit(solution)/shard_map/sxd,swd->sxw/dot_general | solution.py:46
  60.9 5.2 %select_select_fusion = (bf16[32,128,128]{2,0,1:T(8,128)(2,1)S(1)}, bf16[32,128,128]{2,0,1:T(8,128)(2,1)}, bf16[32,128,128]{2,0,1:T(8,128)(2,1)S(1)}) fusion(pred[32,128]{0,1:T(8,128)(4,1)S(1)} %get-tuple-element.99, pred[32,128]{0,1:T(8,128)(4,1)S(1)} %get-tuple-element.100, bf16[32,128]{1,0:T(8,128)(2,1)S(1)} %get-tuple-element.78, ...), kind=kOutput, calls=%fused_computation.23 | convolution fusion | flops 37226496 | bytes 5349600 | tf_op jit(solution)/shard_map/dot_general | solution.py:207
  66.1 0.5 fusion.2
  67.2 0.7 broadcast_in_dim.388
  67.9 7.2 %all-to-all-start.1 = ((bf16[4,64,512]{2,1,0:T(8,128)(2,1)}), bf16[4,64,512]{2,1,0:T(8,128)(2,1)S(1)}, u32[]{:S(2)}, u32[]{:S(2)}) async-start(bf16[4,64,512]{2,1,0:T(8,128)(2,1)} %broadcast_in_dim.388), calls=%async_computation.1 | async-start | bytes 524288 | tf_op jit(solution)/shard_map/all_to_all | solution.py:95
  75.5 4.9 %all-to-all-done.1 = bf16[4,64,512]{2,1,0:T(8,128)(2,1)S(1)} async-done(((bf16[4,64,512]{2,1,0:T(8,128)(2,1)}), bf16[4,64,512]{2,1,0:T(8,128)(2,1)S(1)}, u32[]{:S(2)}, u32[]{:S(2)}) %all-to-all-start.1) | async-done | bytes 262176 | tf_op jit(solution)/shard_map/all_to_all | solution.py:95
  80.8 1.8 %convolution_convert_fusion.3 = bf16[64,512]{1,0:T(8,128)(2,1)S(1)} fusion(bf16[512,512]{1,0:T(8,128)(2,1)S(1)} %copy-done, bf16[512,512]{1,0:T(8,128)(2,1)} %param.33, f32[64,512]{1,0:T(8,128)S(1)} %stack.36, f32[1,64,512]{2,1,0:T(8,128)S(1)} %get-tuple-element.45, f32[512]{0:T(512)S(1)} %copy-done.17, f32[64]{0:T(128)S(1)} %add_rsqrt_fusion.1, ...), kind=kOutput, calls=%fused_computation.6 | convolution fusion | flops 69468160 | bytes 1380864 | tf_op jit(solution)/shard_map/dot_general | solution.py:258
  82.6 0.7 broadcast_in_dim.389
  83.3 4.2 %all-to-all-start.2 = ((bf16[4,64,512]{2,1,0:T(8,128)(2,1)}), bf16[4,64,512]{2,1,0:T(8,128)(2,1)S(1)}, u32[]{:S(2)}, u32[]{:S(2)}) async-start(bf16[4,64,512]{2,1,0:T(8,128)(2,1)} %broadcast_in_dim.389), calls=%async_computation.2 | async-start | bytes 524288 | tf_op jit(solution)/shard_map/all_to_all | solution.py:95
  87.7 1.4 %copy.128 = bf16[32,128,128]{2,1,0:T(8,128)(2,1)} copy(bf16[32,128,128]{2,0,1:T(8,128)(2,1)S(1)} %copy-done.3) | data formatting | bytes 2097152
  89.1 1.4 %copy.129 = bf16[32,128,128]{2,1,0:T(8,128)(2,1)} copy(bf16[32,128,128]{2,0,1:T(8,128)(2,1)S(1)} %get-tuple-element.75) | data formatting | bytes 2097152
  90.5 2.2 %all-to-all-done.2 = bf16[4,64,512]{2,1,0:T(8,128)(2,1)S(1)} async-done(((bf16[4,64,512]{2,1,0:T(8,128)(2,1)}), bf16[4,64,512]{2,1,0:T(8,128)(2,1)S(1)}, u32[]{:S(2)}, u32[]{:S(2)}) %all-to-all-start.2) | async-done | bytes 262176 | tf_op jit(solution)/shard_map/all_to_all | solution.py:95
  93.0 0.6 slice_bitcast_fusion
  93.6 0.4 fusion.11
  94.0 0.4 fusion.1
  94.6 0.8 copy.127
  (123 shorter events, 6.5 us)
Async XLA Ops:
  0.6 80.1 %copy-start = (bf16[512,512]{1,0:T(8,128)(2,1)S(1)}, bf16[512,512]{1,0:T(8,128)(2,1)}, u32[]{:S(2)}) copy-start(bf16[512,512]{1,0:T(8,128)(2,1)} %param.34) | copy-start | bytes 1572868
  3.3 2.6 %copy-start.9 = (bf16[32,512]{1,0:T(8,128)(2,1)S(1)}, bf16[32,512]{1,0:T(8,128)(2,1)}, u32[]{:S(2)}) copy-start(bf16[32,512]{1,0:T(8,128)(2,1)} %param.23) | copy-start | bytes 98308
  3.4 2.6 %copy-start.10 = (bf16[32,512]{1,0:T(8,128)(2,1)S(1)}, bf16[32,512]{1,0:T(8,128)(2,1)}, u32[]{:S(2)}) copy-start(bf16[32,512]{1,0:T(8,128)(2,1)} %param.24) | copy-start | bytes 98308
  3.4 22.3 %copy-start.18 = (s32[32]{0:T(128)S(1)}, s32[32]{0:T(128)}, u32[]{:S(2)}) copy-start(s32[32]{0:T(128)} %param.20) | copy-start | bytes 388
  3.4 23.6 %copy-start.7 = (bf16[32,512]{1,0:T(8,128)(2,1)S(1)}, bf16[32,512]{1,0:T(8,128)(2,1)}, u32[]{:S(2)}) copy-start(bf16[32,512]{1,0:T(8,128)(2,1)} %param.19) | copy-start | bytes 98308
  6.2 36.3 %collective-permute-start = (bf16[272,128]{1,0:T(8,128)(2,1)S(1)}, bf16[272,128]{1,0:T(8,128)(2,1)S(1)}, u32[]{:S(2)}, u32[]{:S(2)}) collective-permute-start(bf16[272,128]{1,0:T(8,128)(2,1)S(1)} %concatenate.10), channel_id=1, source_target_pairs={{0,127},{1,0},{2,1},{3,2},{4,3},{5,4},{6,5},{7,6},{8,7},{9,8},{10,... | collective-permute-start | bytes 208904 | tf_op jit(solution)/shard_map/ppermute | solution.py:172
  23.7 17.5 %collective-permute-start.1 = (bf16[272,128]{1,0:T(8,128)(2,1)S(1)}, bf16[272,128]{1,0:T(8,128)(2,1)S(1)}, u32[]{:S(2)}, u32[]{:S(2)}) collective-permute-start(bf16[272,128]{1,0:T(8,128)(2,1)S(1)} %concatenate.11), channel_id=1, source_target_pairs={{0,1},{1,2},{2,3},{3,4},{4,5},{5,6},{6,7},{7,8},{8,9},{9,10},{10,1... | collective-permute-start | bytes 208904 | tf_op jit(solution)/shard_map/ppermute | solution.py:169
  27.3 13.2 %copy-start.12 = (s32[32]{0:T(128)S(1)}, s32[32]{0:T(128)}, u32[]{:S(2)}) copy-start(s32[32]{0:T(128)} %param.26) | copy-start | bytes 388
  27.3 13.4 %copy-start.13 = (f32[4,512]{1,0:T(4,128)S(1)}, f32[4,512]{1,0:T(4,128)}, u32[]{:S(2)}) copy-start(f32[4,512]{1,0:T(4,128)} %param.27) | copy-start | bytes 24580
  27.8 15.8 %copy-start.1 = (bf16[32,128,128]{2,1,0:T(8,128)(2,1)S(1)}, bf16[32,128,128]{2,1,0:T(8,128)(2,1)}, u32[]{:S(2)}) copy-start(bf16[32,128,128]{2,1,0:T(8,128)(2,1)} %param.21) | copy-start | bytes 3145732
  29.8 25.2 %all-to-all-start = ((bf16[128,2,576]{2,1,0:T(2,128)(2,1)}), bf16[128,2,576]{2,1,0:T(2,128)(2,1)S(1)}, u32[]{:S(2)}, u32[]{:S(2)}) async-start(bf16[128,2,576]{2,1,0:T(2,128)(2,1)} %reshape.429), calls=%async_computation | async-start | bytes 655360 | tf_op jit(solution)/shard_map/all_to_all | solution.py:192
  55.5 1.0 %copy-start.5 = (bf16[3,512,128]{2,1,0:T(8,128)(2,1)S(1)}, bf16[3,512,128]{2,1,0:T(8,128)(2,1)}, u32[]{:S(2)}) copy-start(bf16[3,512,128]{2,1,0:T(8,128)(2,1)} %param.29) | copy-start | bytes 1179652
  55.5 1.0 %copy-start.14 = (f32[512]{0:T(512)S(1)}, f32[512]{0:T(512)}, u32[]{:S(2)}) copy-start(f32[512]{0:T(512)} %param.28) | copy-start | bytes 6148
  56.0 1.4 %copy-start.8 = (bf16[32,512]{1,0:T(8,128)(2,1)}, bf16[32,512]{1,0:T(8,128)(2,1)S(1)}, u32[]{:S(2)}) copy-start(bf16[32,512]{1,0:T(8,128)(2,1)S(1)} %convolution_convert_fusion.8) | copy-start | bytes 98308
  58.0 3.0 %copy-start.2 = (bf16[32,128,128]{2,1,0:T(8,128)(2,1)S(1)}, bf16[32,128,128]{2,1,0:T(8,128)(2,1)}, u32[]{:S(2)}) copy-start(bf16[32,128,128]{2,1,0:T(8,128)(2,1)} %param.22) | copy-start | bytes 3145732
  66.1 0.9 copy-start.6
  67.9 12.5 %copy-start.11 = (f32[512]{0:T(512)S(1)}, f32[512]{0:T(512)}, u32[]{:S(2)}) copy-start(f32[512]{0:T(512)} %param.31) | copy-start | bytes 6148
  67.9 12.4 %all-to-all-start.1 = ((bf16[4,64,512]{2,1,0:T(8,128)(2,1)}), bf16[4,64,512]{2,1,0:T(8,128)(2,1)S(1)}, u32[]{:S(2)}, u32[]{:S(2)}) async-start(bf16[4,64,512]{2,1,0:T(8,128)(2,1)} %broadcast_in_dim.388), calls=%async_computation.1 | async-start | bytes 524288 | tf_op jit(solution)/shard_map/all_to_all | solution.py:95
  75.3 5.4 %copy-start.17 = (f32[512]{0:T(512)S(1)}, f32[512]{0:T(512)}, u32[]{:S(2)}) copy-start(f32[512]{0:T(512)} %param.32) | copy-start | bytes 6148
  80.8 6.9 %copy-start.3 = (bf16[32,128,128]{2,0,1:T(8,128)(2,1)S(1)}, bf16[32,128,128]{2,0,1:T(8,128)(2,1)}, u32[]{:S(2)}) copy-start(bf16[32,128,128]{2,0,1:T(8,128)(2,1)} %get-tuple-element.76) | copy-start | bytes 3145732
  83.3 9.4 %all-to-all-start.2 = ((bf16[4,64,512]{2,1,0:T(8,128)(2,1)}), bf16[4,64,512]{2,1,0:T(8,128)(2,1)S(1)}, u32[]{:S(2)}, u32[]{:S(2)}) async-start(bf16[4,64,512]{2,1,0:T(8,128)(2,1)} %broadcast_in_dim.389), calls=%async_computation.2 | async-start | bytes 524288 | tf_op jit(solution)/shard_map/all_to_all | solution.py:95
  90.4 2.5 %copy-start.15 = (f32[512]{0:T(512)S(1)}, f32[512]{0:T(512)}, u32[]{:S(2)}) copy-start(f32[512]{0:T(512)} %param.35) | copy-start | bytes 6148
  90.5 3.1 %copy-start.4 = (bf16[16,64,512]{2,1,0:T(8,128)(2,1)S(1)}, bf16[16,64,512]{2,1,0:T(8,128)(2,1)}, u32[]{:S(2)}) copy-start(bf16[16,64,512]{2,1,0:T(8,128)(2,1)} %param.36) | copy-start | bytes 3145732
  92.8 1.2 %copy-start.16 = (f32[64]{0:T(128)S(1)}, f32[64]{0:T(128)}, u32[]{:S(2)}) copy-start(f32[64]{0:T(128)} %param.37) | copy-start | bytes 772

commit v4 on v3

--- a/solution.py
+++ b/solution.py
@@ -2,6 +2,8 @@
 import jax.numpy as jnp
 from jax import lax
 from jax.sharding import PartitionSpec as P
+from jax.experimental import pallas as pl
+from jax.experimental.pallas import tpu as pltpu
 
 HEAD_DIM = 64
 CAP = 2
@@ -90,14 +92,54 @@
 
 def section_sum(partial):
     size = lax.axis_size("section")
-    rounded = partial.astype(jnp.bfloat16)
-    copies = jnp.broadcast_to(rounded[None], (size,) + rounded.shape)
-    every = lax.all_to_all(copies, "section", 0, 0, tiled=False).astype(jnp.float32)
-    terms = [every[i] for i in range(size)]
-    while len(terms) > 1:
-        paired = [terms[i] + terms[i + 1] for i in range(0, len(terms) - 1, 2)]
-        terms = paired + ([terms[-1]] if len(terms) % 2 else [])
-    return terms[0]
+    if size & (size - 1):
+        return lax.psum(partial.astype(jnp.bfloat16), "section").astype(jnp.float32)
+    total = partial.astype(jnp.bfloat16)
+    bit = size // 2
+    while bit >= 1:
+        route = [(i, i ^ bit) for i in range(size)]
+        other = lax.ppermute(total, "section", route)
+        total = total.astype(jnp.float32) + other.astype(jnp.float32)
+        bit //= 2
+    return total
+
+
+def cache_kernel(src_ref, take_ref, keys_ref, values_ref, lbox_ref, rbox_ref, ok_ref, ov_ref):
+    streams, window, _ = keys_ref.shape
+
+    def body(n, carry):
+        src = src_ref[n]
+        take = take_ref[n]
+        ok_ref[n] = keys_ref[src]
+        ov_ref[n] = values_ref[src]
+
+        @pl.when(take == 1)
+        def _():
+            ok_ref[n] = lbox_ref[0:window]
+            ov_ref[n] = lbox_ref[window : 2 * window]
+
+        @pl.when(take == 2)
+        def _():
+            ok_ref[n] = rbox_ref[0:window]
+            ov_ref[n] = rbox_ref[window : 2 * window]
+
+        return carry
+
+    lax.fori_loop(0, streams, body, 0)
+
+
+def route_caches(src, take, keys, values, lbox, rbox):
+    smem = pl.BlockSpec(memory_space=pltpu.SMEM)
+    vmem = pl.BlockSpec(memory_space=pltpu.VMEM)
+    shape = jax.ShapeDtypeStruct(keys.shape, keys.dtype)
+    moved = 4 * keys.size * keys.dtype.itemsize
+    return pl.pallas_call(
+        cache_kernel,
+        out_shape=(shape, shape),
+        in_specs=[smem] * 2 + [vmem] * 4,
+        out_specs=(vmem, vmem),
+        cost_estimate=pl.CostEstimate(flops=0, transcendentals=0, bytes_accessed=moved),
+    )(src, take, keys, values, lbox, rbox)
 
 
 def one_hot(rows, columns):
@@ -165,12 +207,14 @@
         code = box[2 * window + 2 * state_rows, 0].astype(jnp.int32) - 1
         return keys, values, up, conv, code
 
-    from_left = unpack(
-        lax.ppermute(pack(right_owner), "batch", [(i, (i + 1) % owners) for i in range(owners)])
-    )
-    from_right = unpack(
-        lax.ppermute(pack(left_owner), "batch", [(i, (i - 1) % owners) for i in range(owners)])
-    )
+    left_box = lax.ppermute(
+        pack(right_owner), "batch", [(i, (i + 1) % owners) for i in range(owners)]
+    )
+    right_box = lax.ppermute(
+        pack(left_owner), "batch", [(i, (i - 1) % owners) for i in range(owners)]
+    )
+    from_left = unpack(left_box)
+    from_right = unpack(right_box)
 
     target = token_slot // streams
     landing = token_slot % streams
@@ -199,19 +243,21 @@
 
     staying = dest_owner == own_index
     source_of = (dest_local[None, :] == slot_ids[:, None]) & staying[None, :]
-    picking = source_of.astype(jnp.bfloat16)
+    source = jnp.sum(jnp.where(source_of, slot_ids[None, :], 0), axis=1)
     from_l = slot_ids == from_left[4]
     from_r = slot_ids == from_right[4]
+    take = jnp.where(from_l, 1, jnp.where(from_r, 2, 0)).astype(jnp.int32)
+    keys_old, values_old = route_caches(
+        source, take, cache_keys, cache_values, left_box, right_box
+    )
+    picking = source_of.astype(jnp.bfloat16)
 
     def gathered(own_rows, left_row, right_row):
-        rows = jnp.tensordot(picking, own_rows, axes=1, preferred_element_type=jnp.float32)
+        rows = jnp.dot(picking, own_rows, preferred_element_type=jnp.float32)
         rows = rows.astype(own_rows.dtype)
-        shape = (streams,) + (1,) * (own_rows.ndim - 1)
-        rows = jnp.where(from_l.reshape(shape), left_row[None], rows)
-        return jnp.where(from_r.reshape(shape), right_row[None], rows)
-
-    keys_old = gathered(cache_keys, from_left[0], from_right[0])
-    values_old = gathered(cache_values, from_left[1], from_right[1])
+        rows = jnp.where(from_l[:, None], left_row[None], rows)
+        return jnp.where(from_r[:, None], right_row[None], rows)
+
     up_prev = gathered(up_state, from_left[2], from_right[2])
     conv_prev = gathered(conv_state, from_left[3], from_right[3])
 

time: 96 us -> 87 us (0.906)
  waiting for transfers between devices: 16.6 us -> 6.02 us
  matrix products: 13.7 us -> 5.24 us
  Pallas kernels: 0 us -> 3.5 us
  starting transfers between devices: 40.9 us -> 44.2 us
  other arithmetic: 8.17 us -> 9.77 us
  local copies, waits for them, and re-layouts: 12 us -> 13.5 us
    ppermute x0 -> x4, starting transfers between devices: none -> 12.4 us  [section_sum(): other = lax.ppermute(total, 'section', route)]
    all_to_all x2 -> x0, starting transfers between devices: 11.5 us -> none  [section_sum(): lax.all_to_all(copies, 'section', 0, 0, tiled=False).astype(jnp.float32)]
    all_to_all x1, starting transfers between devices: 10.7 us -> 20.8 us  [local(): got = lax.all_to_all(send, 'batch', split_axis=0, concat_axis=0, tiled=True)]
    ppermute x1, starting transfers between devices: 16.9 us -> 7.01 us  [local(): lax.ppermute(pack(left_owner), 'batch', [(i, (i - 1) % owners) for i in r...]
    all_to_all x1, waiting for transfers between devices: 9.54 us -> 0.01 us  [local(): got = lax.all_to_all(send, 'batch', split_axis=0, concat_axis=0, tiled=True)]
    all_to_all x2 -> x0, waiting for transfers between devices: 7.05 us -> none  [section_sum(): lax.all_to_all(copies, 'section', 0, 0, tiled=False).astype(jnp.float32)]
    dot_general x4 -> x2, matrix products: 7.18 us -> 0.27 us  [gathered(): rows = jnp.dot(picking, own_rows, preferred_element_type=jnp.float32)]
    ppermute x0 -> x4, waiting for transfers between devices: none -> 6.01 us  [section_sum(): other = lax.ppermute(total, 'section', route)]
  transfers between devices with their start and end apart: 5 -> 7, of which waited for: 3 -> 3; matrix products, arithmetic and copies ran while one was open for 11% -> 11% of each run, Pallas kernels for 0% -> 4%
where the time goes in v4:
time: 87 us; the launch traced here: 86.3 us
  starting transfers between devices  44.2 us (51%)
  local copies, waits for them, and re-layouts  13.5 us (16%)
  other arithmetic  9.77 us (11%)
  waiting for transfers between devices  6.02 us (7%)
  matrix products  5.24 us (6%)
  between operations  3.97 us (5%)
  Pallas kernels  3.5 us (4%)
    all_to_all x1, starting transfers between devices, local(): got = lax.all_to_all(send, 'batch', split_axis=0, concat_axis=0, tiled=True)  20.8 us
    ppermute x4, starting transfers between devices, section_sum(): other = lax.ppermute(total, 'section', route)  12.4 us
    unnamed x49, local copies, waits for them, and re-layouts  8.12 us
    ppermute x1, starting transfers between devices, local(): lax.ppermute(pack(left_owner), 'batch', [(i, (i - 1) % owners) for i in r...  7.01 us
    ppermute x4, waiting for transfers between devices, section_sum(): other = lax.ppermute(total, 'section', route)  6.01 us
    ppermute x1, starting transfers between devices, local(): lax.ppermute(pack(right_owner), 'batch', [(i, (i + 1) % owners) for i in...  3.97 us
    pallas_call x1, Pallas kernels, route_caches(): pl.pallas_call(cache_kernel, out_shape=(shape, shape), in_specs=[smem] *...  3.5 us
    select_n x1, other arithmetic, local(): jnp.where(hit_second, fresh_values[:, 1][:, None, :], jnp.where(hit_first...  2.63 us
  transfers between devices with their start and end apart: 7, of which 3 were waited for; matrix products, arithmetic and copies ran while one was open for 11% of the time, Pallas kernels for 4%

profile of v4, /device:TPU:1, one launch (start us, length us, event | category | flops | bytes accessed | tf_op | source)
XLA Modules:
  0.0 86.3 jit_solution(1134757256919519795)
XLA Ops:
  0.6 0.7 fusion.111
  1.8 0.9 %copy.100 = bf16[128,2,1]{1,0,2:T(8,128)(2,1)S(1)} copy(bf16[128,2,1]{2,1,0:T(2,128)(2,1)S(1)} %bitcast.105) | data formatting | bytes 1024
  3.5 0.8 reduce.10
  4.4 1.0 %reshape.391 = bf16[128,2,576]{2,1,0:T(2,128)(2,1)} reshape(bf16[128,1152]{1,0:T(8,128)(2,1)S(1)} %reduce.10) | data formatting | bytes 589824
  5.4 20.8 %all-to-all-start = ((bf16[128,2,576]{2,1,0:T(2,128)(2,1)}), bf16[128,2,576]{2,1,0:T(2,128)(2,1)S(1)}, u32[]{:S(2)}, u32[]{:S(2)}) async-start(bf16[128,2,576]{2,1,0:T(2,128)(2,1)} %reshape.391), calls=%async_computation | async-start | bytes 655360 | tf_op jit(solution)/shard_map/all_to_all | solution.py:236
  26.3 0.6 copy-done.19
  27.0 0.6 select_reduce_fusion.11
  28.3 1.0 %select_reduce_fusion.3 = (bf16[128,128]{1,0:T(8,128)(2,1)S(1)}, bf16[128,128]{1,0:T(8,128)(2,1)S(1)}, bf16[128,128]{1,0:T(8,128)(2,1)S(1)}, bf16[128,128]{1,0:T(8,128)(2,1)S(1)}) fusion(bf16[32,128,128]{2,1,0:T(8,128)(2,1)S(1)} %copy-done.1, pred[32]{0:T(512)(128)(4,1)S(1)} %get-tuple-element.50, pred[32]{0:T(512)(128)(4,1)S(1)} %get-tuple-element.49, ...), kind=kLoop, calls=%fused_computation.22 | loop fusion | flops 4128768 | bytes 2228288 | tf_op jit(solution)/shard_map/reduce_sum | solution.py:191
  29.5 4.0 %collective-permute-start.1 = (bf16[272,128]{1,0:T(8,128)(2,1)S(1)}, bf16[272,128]{1,0:T(8,128)(2,1)S(1)}, u32[]{:S(2)}, u32[]{:S(2)}) collective-permute-start(bf16[272,128]{1,0:T(8,128)(2,1)S(1)} %concatenate.11), channel_id=1, source_target_pairs={{0,1},{1,2},{2,3},{3,4},{4,5},{5,6},{6,7},{7,8},{8,9},{9,10},{10,1... | collective-permute-start | bytes 208904 | tf_op jit(solution)/shard_map/ppermute | solution.py:210
  34.2 7.0 %collective-permute-start = (bf16[272,128]{1,0:T(8,128)(2,1)S(1)}, bf16[272,128]{1,0:T(8,128)(2,1)S(1)}, u32[]{:S(2)}, u32[]{:S(2)}) collective-permute-start(bf16[272,128]{1,0:T(8,128)(2,1)S(1)} %concatenate.10), channel_id=1, source_target_pairs={{0,127},{1,0},{2,1},{3,2},{4,3},{5,4},{6,5},{7,6},{8,7},{9,8},{10,... | collective-permute-start | bytes 208904 | tf_op jit(solution)/shard_map/ppermute | solution.py:213
  41.3 0.6 copy-done.15
  43.2 0.6 select_reduce_fusion.9.src_ref
  43.8 0.5 slice.118
  45.1 0.5 slice.116
  46.2 0.6 select_select_fusion.3.take_ref
  46.9 3.5 %shard_map.218 = (bf16[32,128,128]{2,1,0:T(8,128)(2,1)}, bf16[32,128,128]{2,1,0:T(8,128)(2,1)}) custom-call(s32[32]{0:T(128)} %select_reduce_fusion.9.src_ref, s32[32]{0:T(128)} %select_select_fusion.3.take_ref, bf16[32,128,128]{2,1,0:T(8,128)(2,1)} %keys_ref.1, bf16[32,128,128]{2,1,0:T(8,128)(2,1)} %values_ref.1, bf16[272,128]{1,0:T(8,128)(2,1)} %copy-done.8, ...), custom_call_target="tpu_custom_call" | custom-call | bytes 4194304 | tf_op jit(solution)/shard_map/pallas_call | solution.py:136
  50.4 0.8 slice_bitcast_fusion.3
  51.1 0.7 slice_bitcast_fusion.4
  53.9 0.6 copy-done.17
  56.1 0.7 fusion.157
  58.5 2.2 %collective-permute-start.2 = (bf16[64,512]{1,0:T(8,128)(2,1)S(1)}, bf16[64,512]{1,0:T(8,128)(2,1)S(1)}, u32[]{:S(2)}, u32[]{:S(2)}) collective-permute-start(bf16[64,512]{1,0:T(8,128)(2,1)S(1)} %convolution_convert_fusion.3), channel_id=1, source_target_pairs={{0,256},{128,384},{256,0},{384,128},{1,257},{129,385},{257,1},{385... | collective-permute-start | bytes 196616 | tf_op jit(solution)/shard_map/ppermute | solution.py:101
  61.0 2.4 %collective-permute-done.2 = bf16[64,512]{1,0:T(8,128)(2,1)S(1)} collective-permute-done((bf16[64,512]{1,0:T(8,128)(2,1)S(1)}, bf16[64,512]{1,0:T(8,128)(2,1)S(1)}, u32[]{:S(2)}, u32[]{:S(2)}) %collective-permute-start.2) | collective-permute-done | bytes 65568 | tf_op jit(solution)/shard_map/ppermute | solution.py:101
  63.5 4.6 %collective-permute-start.3 = (f32[64,512]{1,0:T(8,128)S(1)}, f32[64,512]{1,0:T(8,128)S(1)}, u32[]{:S(2)}, u32[]{:S(2)}) collective-permute-start(f32[64,512]{1,0:T(8,128)S(1)} %convert_add_fusion.1), channel_id=1, source_target_pairs={{0,128},{128,0},{256,384},{384,256},{1,129},{129,1},{257,385},{385... | collective-permute-start | bytes 393224 | tf_op jit(solution)/shard_map/ppermute | solution.py:101
  68.1 0.9 %collective-permute-done.3 = f32[64,512]{1,0:T(8,128)S(1)} collective-permute-done((f32[64,512]{1,0:T(8,128)S(1)}, f32[64,512]{1,0:T(8,128)S(1)}, u32[]{:S(2)}, u32[]{:S(2)}) %collective-permute-start.3) | collective-permute-done | bytes 131104 | tf_op jit(solution)/shard_map/ppermute | solution.py:101
  69.9 1.7 %convolution_convert_fusion.1 = bf16[64,512]{1,0:T(8,128)(2,1)S(1)} fusion(bf16[512,512]{1,0:T(8,128)(2,1)S(1)} %copy-done, bf16[512,512]{1,0:T(8,128)(2,1)} %param.33, f32[64,512]{1,0:T(8,128)S(1)} %get-tuple-element.44, f32[512]{0:T(512)S(1)} %copy-done.21, f32[64]{0:T(128)S(1)} %add_rsqrt_fusion.1, f32[64]{0:T(128)S(1)} %broadcast_multiply_fusion.1), kind=kOutput, calls=%fused_computation.4 | convolution fusion | flops 69402624 | bytes 1247744 | tf_op jit(solution)/shard_map/dot_general | solution.py:304
  71.6 2.2 %collective-permute-start.4 = (bf16[64,512]{1,0:T(8,128)(2,1)S(1)}, bf16[64,512]{1,0:T(8,128)(2,1)S(1)}, u32[]{:S(2)}, u32[]{:S(2)}) collective-permute-start(bf16[64,512]{1,0:T(8,128)(2,1)S(1)} %convolution_convert_fusion.1), channel_id=1, source_target_pairs={{0,256},{128,384},{256,0},{384,128},{1,257},{129,385},{257,1},{385... | collective-permute-start | bytes 196616 | tf_op jit(solution)/shard_map/ppermute | solution.py:101
  74.0 2.6 %collective-permute-done.4 = bf16[64,512]{1,0:T(8,128)(2,1)S(1)} collective-permute-done((bf16[64,512]{1,0:T(8,128)(2,1)S(1)}, bf16[64,512]{1,0:T(8,128)(2,1)S(1)}, u32[]{:S(2)}, u32[]{:S(2)}) %collective-permute-start.4) | collective-permute-done | bytes 65568 | tf_op jit(solution)/shard_map/ppermute | solution.py:101
  76.6 3.4 %collective-permute-start.5 = (f32[64,512]{1,0:T(8,128)S(1)}, f32[64,512]{1,0:T(8,128)S(1)}, u32[]{:S(2)}, u32[]{:S(2)}) collective-permute-start(f32[64,512]{1,0:T(8,128)S(1)} %convert_add_fusion), channel_id=1, source_target_pairs={{0,128},{128,0},{256,384},{384,256},{1,129},{129,1},{257,385},{385... | collective-permute-start | bytes 393224 | tf_op jit(solution)/shard_map/ppermute | solution.py:101
  80.1 2.6 %select_select_fusion = (bf16[32,128,128]{2,1,0:T(8,128)(2,1)}, bf16[32,128,128]{2,1,0:T(8,128)(2,1)}) fusion(bf16[32,128,128]{2,1,0:T(8,128)(2,1)S(1)} %copy-done.5, pred[32,128]{1,0:T(8,128)(4,1)S(1)} %get-tuple-element.94, pred[32,128]{1,0:T(8,128)(4,1)S(1)} %get-tuple-element.95, bf16[32,128]{1,0:T(8,128)(2,1)S(1)} %get-tuple-element.72, ...), kind=kLoop, calls=%fused_computation.17 | loop fusion | flops 2097152 | bytes 4235264 | tf_op jit(solution)/shard_map/jit(_where)/select_n | solution.py:326
  83.0 0.6 slice_bitcast_fusion
  84.3 0.7 copy-done.20
  85.5 0.8 copy.95
  (128 shorter events, 10.7 us)
Async XLA Ops:
  0.6 68.8 %copy-start = (bf16[512,512]{1,0:T(8,128)(2,1)S(1)}, bf16[512,512]{1,0:T(8,128)(2,1)}, u32[]{:S(2)}) copy-start(bf16[512,512]{1,0:T(8,128)(2,1)} %param.34) | copy-start | bytes 1572868
  1.8 0.9 %copy-start.10 = (bf16[32,512]{1,0:T(8,128)(2,1)S(1)}, bf16[32,512]{1,0:T(8,128)(2,1)}, u32[]{:S(2)}) copy-start(bf16[32,512]{1,0:T(8,128)(2,1)} %param.19) | copy-start | bytes 98308
  3.0 25.3 %copy-start.2 = (bf16[32,128,128]{2,1,0:T(8,128)(2,1)S(1)}, bf16[32,128,128]{2,1,0:T(8,128)(2,1)}, u32[]{:S(2)}) copy-start(bf16[32,128,128]{2,1,0:T(8,128)(2,1)} %values_ref.1) | copy-start | bytes 3145732
  3.0 25.3 %copy-start.1 = (bf16[32,128,128]{2,1,0:T(8,128)(2,1)S(1)}, bf16[32,128,128]{2,1,0:T(8,128)(2,1)}, u32[]{:S(2)}) copy-start(bf16[32,128,128]{2,1,0:T(8,128)(2,1)} %keys_ref.1) | copy-start | bytes 3145732
  5.4 46.4 %all-to-all-start = ((bf16[128,2,576]{2,1,0:T(2,128)(2,1)}), bf16[128,2,576]{2,1,0:T(2,128)(2,1)S(1)}, u32[]{:S(2)}, u32[]{:S(2)}) async-start(bf16[128,2,576]{2,1,0:T(2,128)(2,1)} %reshape.391), calls=%async_computation | async-start | bytes 655360 | tf_op jit(solution)/shard_map/all_to_all | solution.py:236
  26.3 0.7 copy-start.19
  28.3 1.0 %copy-start.12 = (bf16[32,512]{1,0:T(8,128)(2,1)S(1)}, bf16[32,512]{1,0:T(8,128)(2,1)}, u32[]{:S(2)}) copy-start(bf16[32,512]{1,0:T(8,128)(2,1)} %param.23) | copy-start | bytes 98308
  28.3 1.0 %copy-start.13 = (bf16[32,512]{1,0:T(8,128)(2,1)S(1)}, bf16[32,512]{1,0:T(8,128)(2,1)}, u32[]{:S(2)}) copy-start(bf16[32,512]{1,0:T(8,128)(2,1)} %param.24) | copy-start | bytes 98308
  29.5 14.3 %collective-permute-start.1 = (bf16[272,128]{1,0:T(8,128)(2,1)S(1)}, bf16[272,128]{1,0:T(8,128)(2,1)S(1)}, u32[]{:S(2)}, u32[]{:S(2)}) collective-permute-start(bf16[272,128]{1,0:T(8,128)(2,1)S(1)} %concatenate.11), channel_id=1, source_target_pairs={{0,1},{1,2},{2,3},{3,4},{4,5},{5,6},{6,7},{7,8},{8,9},{9,10},{10,1... | collective-permute-start | bytes 208904 | tf_op jit(solution)/shard_map/ppermute | solution.py:210
  34.2 10.8 %collective-permute-start = (bf16[272,128]{1,0:T(8,128)(2,1)S(1)}, bf16[272,128]{1,0:T(8,128)(2,1)S(1)}, u32[]{:S(2)}, u32[]{:S(2)}) collective-permute-start(bf16[272,128]{1,0:T(8,128)(2,1)S(1)} %concatenate.10), channel_id=1, source_target_pairs={{0,127},{1,0},{2,1},{3,2},{4,3},{5,4},{6,5},{7,6},{8,7},{9,8},{10,... | collective-permute-start | bytes 208904 | tf_op jit(solution)/shard_map/ppermute | solution.py:213
  41.3 0.7 copy-start.15
  41.9 0.7 copy-start.16
  43.8 3.0 %copy-start.8 = (bf16[272,128]{1,0:T(8,128)(2,1)}, bf16[272,128]{1,0:T(8,128)(2,1)S(1)}, u32[]{:S(2)}) copy-start(bf16[272,128]{1,0:T(8,128)(2,1)S(1)} %collective-permute-done.1.lbox_ref) | copy-start | bytes 208900
  45.1 1.8 %copy-start.9 = (bf16[272,128]{1,0:T(8,128)(2,1)}, bf16[272,128]{1,0:T(8,128)(2,1)S(1)}, u32[]{:S(2)}) copy-start(bf16[272,128]{1,0:T(8,128)(2,1)S(1)} %collective-permute-done.rbox_ref) | copy-start | bytes 208900
  52.8 0.6 copy-start.11
  52.8 1.0 %copy-start.6 = (bf16[3,512,128]{2,1,0:T(8,128)(2,1)S(1)}, bf16[3,512,128]{2,1,0:T(8,128)(2,1)}, u32[]{:S(2)}) copy-start(bf16[3,512,128]{2,1,0:T(8,128)(2,1)} %param.29) | copy-start | bytes 1179652
  53.7 0.7 copy-start.17
  54.7 1.4 %copy-start.3 = (bf16[32,128,128]{2,1,0:T(8,128)(2,1)S(1)}, bf16[32,128,128]{2,1,0:T(8,128)(2,1)}, u32[]{:S(2)}) copy-start(bf16[32,128,128]{2,1,0:T(8,128)(2,1)} %get-tuple-element.7) | copy-start | bytes 3145732
  55.8 1.6 %copy-start.5 = (bf16[32,128,128]{2,1,0:T(8,128)(2,1)S(1)}, bf16[32,128,128]{2,1,0:T(8,128)(2,1)}, u32[]{:S(2)}) copy-start(bf16[32,128,128]{2,1,0:T(8,128)(2,1)} %get-tuple-element.8) | copy-start | bytes 3145732
  57.4 0.9 %copy-start.7 = (bf16[128,512]{1,0:T(8,128)(2,1)S(1)}, bf16[128,512]{1,0:T(8,128)(2,1)}, u32[]{:S(2)}) copy-start(bf16[128,512]{1,0:T(8,128)(2,1)} %param.30) | copy-start | bytes 393220
  58.5 5.0 %collective-permute-start.2 = (bf16[64,512]{1,0:T(8,128)(2,1)S(1)}, bf16[64,512]{1,0:T(8,128)(2,1)S(1)}, u32[]{:S(2)}, u32[]{:S(2)}) collective-permute-start(bf16[64,512]{1,0:T(8,128)(2,1)S(1)} %convolution_convert_fusion.3), channel_id=1, source_target_pairs={{0,256},{128,384},{256,0},{384,128},{1,257},{129,385},{257,1},{385... | collective-permute-start | bytes 196616 | tf_op jit(solution)/shard_map/ppermute | solution.py:101
  63.5 5.6 %copy-start.14 = (f32[512]{0:T(512)S(1)}, f32[512]{0:T(512)}, u32[]{:S(2)}) copy-start(f32[512]{0:T(512)} %param.31) | copy-start | bytes 6148
  63.5 5.5 %collective-permute-start.3 = (f32[64,512]{1,0:T(8,128)S(1)}, f32[64,512]{1,0:T(8,128)S(1)}, u32[]{:S(2)}, u32[]{:S(2)}) collective-permute-start(f32[64,512]{1,0:T(8,128)S(1)} %convert_add_fusion.1), channel_id=1, source_target_pairs={{0,128},{128,0},{256,384},{384,256},{1,129},{129,1},{257,385},{385... | collective-permute-start | bytes 393224 | tf_op jit(solution)/shard_map/ppermute | solution.py:101
  69.2 0.7 copy-start.21
  71.6 5.0 %collective-permute-start.4 = (bf16[64,512]{1,0:T(8,128)(2,1)S(1)}, bf16[64,512]{1,0:T(8,128)(2,1)S(1)}, u32[]{:S(2)}, u32[]{:S(2)}) collective-permute-start(bf16[64,512]{1,0:T(8,128)(2,1)S(1)} %convolution_convert_fusion.1), channel_id=1, source_target_pairs={{0,256},{128,384},{256,0},{384,128},{1,257},{129,385},{257,1},{385... | collective-permute-start | bytes 196616 | tf_op jit(solution)/shard_map/ppermute | solution.py:101
  76.6 6.2 %collective-permute-start.5 = (f32[64,512]{1,0:T(8,128)S(1)}, f32[64,512]{1,0:T(8,128)S(1)}, u32[]{:S(2)}, u32[]{:S(2)}) collective-permute-start(f32[64,512]{1,0:T(8,128)S(1)} %convert_add_fusion), channel_id=1, source_target_pairs={{0,128},{128,0},{256,384},{384,256},{1,129},{129,1},{257,385},{385... | collective-permute-start | bytes 393224 | tf_op jit(solution)/shard_map/ppermute | solution.py:101
  80.1 2.8 %copy-start.18 = (f32[512]{0:T(512)S(1)}, f32[512]{0:T(512)}, u32[]{:S(2)}) copy-start(f32[512]{0:T(512)} %param.35) | copy-start | bytes 6148
  82.7 1.2 %copy-start.4 = (bf16[16,64,512]{2,1,0:T(8,128)(2,1)S(1)}, bf16[16,64,512]{2,1,0:T(8,128)(2,1)}, u32[]{:S(2)}) copy-start(bf16[16,64,512]{2,1,0:T(8,128)(2,1)} %param.36) | copy-start | bytes 3145732
  84.3 0.7 copy-start.20

commit v5 on v4

--- a/solution.py
+++ b/solution.py
@@ -220,26 +220,29 @@
     landing = token_slot % streams
     same_before = (target[None, :] == target[:, None]) & (slot_ids[None, :] < slot_ids[:, None])
     arrival_rank = jnp.sum(same_before.astype(jnp.int32), axis=1)
-    box_ids = target * capacity + arrival_rank
-    placing = one_hot(jnp.arange(owners * capacity, dtype=jnp.int32), box_ids)
-    send_rows = jnp.dot(placing, latents, preferred_element_type=jnp.float32).astype(jnp.bfloat16)
-    send_codes = jnp.dot(
-        placing,
-        jnp.broadcast_to((landing + 1).astype(jnp.bfloat16)[:, None], (streams, CODE_LANES)),
-        preferred_element_type=jnp.float32,
-    ).astype(jnp.bfloat16)
-    code_block = send_codes.reshape(owners, capacity, CODE_LANES)[:, :, 0]
-    code_block = jnp.pad(code_block, ((0, 0), (0, CODE_LANES - capacity)))
-    send = jnp.concatenate(
-        [send_rows.reshape(owners, capacity * model_width), code_block], axis=1
-    )
+    owner_ids = jnp.arange(owners, dtype=jnp.int32)
+    lane_ids = jnp.arange(CODE_LANES, dtype=jnp.int32)
+    blocks = []
+    code_block = jnp.zeros((owners, CODE_LANES), jnp.int32)
+    for rank in range(capacity):
+        chosen = (owner_ids[:, None] == target[None, :]) & (arrival_rank == rank)[None, :]
+        blocks.append(
+            jnp.dot(chosen.astype(jnp.bfloat16), latents, preferred_element_type=jnp.float32)
+        )
+        code = jnp.sum(jnp.where(chosen, landing[None, :] + 1, 0), axis=1)
+        code_block = jnp.where(lane_ids[None, :] == rank, code[:, None], code_block)
+    blocks.append(code_block.astype(jnp.float32))
+    send = jnp.concatenate(blocks, axis=1).astype(jnp.bfloat16)
     got = lax.all_to_all(send, "batch", split_axis=0, concat_axis=0, tiled=True)
-    got_codes = got[:, capacity * model_width : capacity * model_width + capacity]
-    got_codes = got_codes.reshape(owners * capacity).astype(jnp.int32) - 1
-    got_rows = got[:, : capacity * model_width].reshape(owners * capacity, model_width)
-    arrived = jnp.dot(
-        one_hot(slot_ids, got_codes), got_rows, preferred_element_type=jnp.float32
-    ).astype(jnp.bfloat16)
+    arrived = jnp.zeros((streams, model_width), jnp.float32)
+    for rank in range(capacity):
+        got_code = got[:, capacity * model_width + rank].astype(jnp.int32) - 1
+        arrived = arrived + jnp.dot(
+            one_hot(slot_ids, got_code),
+            got[:, rank * model_width : (rank + 1) * model_width],
+            preferred_element_type=jnp.float32,
+        )
+    arrived = arrived.astype(jnp.bfloat16)
 
     staying = dest_owner == own_index
     source_of = (dest_local[None, :] == slot_ids[:, None]) & staying[None, :]

time: 87 us -> 87.4 us (level)
  matrix products: 5.24 us -> 6.37 us
    dot_general x3 -> x4, matrix products: 0.56 us -> 1.69 us  [the longest x2 1.41 us: local(): jnp.dot(chosen.astype(jnp.bfloat16), latents, preferred_element_type=jnp....]
    concatenate x0 -> x3, other arithmetic: none -> 0.97 us  [local(): send = jnp.concatenate(blocks, axis=1).astype(jnp.bfloat16)]
    unnamed x49 -> x50, local copies, waits for them, and re-layouts: 8.12 us -> 7.91 us
where the time goes in v5:
time: 87.4 us; the launch traced here: 86.6 us
  starting transfers between devices  44.2 us (51%)
  local copies, waits for them, and re-layouts  13 us (15%)
  other arithmetic  9.46 us (11%)
  matrix products  6.37 us (7%)
  waiting for transfers between devices  6.02 us (7%)
  between operations  3.98 us (5%)
  Pallas kernels  3.5 us (4%)
    all_to_all x1, starting transfers between devices, local(): got = lax.all_to_all(send, 'batch', split_axis=0, concat_axis=0, tiled=True)  20.8 us
    ppermute x4, starting transfers between devices, section_sum(): other = lax.ppermute(total, 'section', route)  12.4 us
    unnamed x50, local copies, waits for them, and re-layouts  7.91 us
    ppermute x1, starting transfers between devices, local(): lax.ppermute(pack(left_owner), 'batch', [(i, (i - 1) % owners) for i in r...  7.01 us
    ppermute x4, waiting for transfers between devices, section_sum(): other = lax.ppermute(total, 'section', route)  6.01 us
    ppermute x1, starting transfers between devices, local(): lax.ppermute(pack(right_owner), 'batch', [(i, (i + 1) % owners) for i in...  3.97 us
    pallas_call x1, Pallas kernels, route_caches(): pl.pallas_call(cache_kernel, out_shape=(shape, shape), in_specs=[smem] *...  3.5 us
    select_n x1, other arithmetic, local(): jnp.where(hit_second, fresh_values[:, 1][:, None, :], jnp.where(hit_first...  2.63 us
  transfers between devices with their start and end apart: 7, of which 3 were waited for; matrix products, arithmetic and copies ran while one was open for 11% of the time, Pallas kernels for 4%

profile of v5, /device:TPU:1, one launch (start us, length us, event | category | flops | bytes accessed | tf_op | source)
XLA Modules:
  0.0 86.6 jit_solution(13790445841769320860)
XLA Ops:
  0.7 0.7 copy-done.22
  1.6 1.1 %fusion.3 = bf16[128,1,512]{2,0,1:T(8,128)(2,1)S(1)} fusion(bf16[32,512]{1,0:T(8,128)(2,1)} %param.19, s32[32]{0:T(128)S(1)} %get-tuple-element.92, pred[32]{0:T(512)(128)(4,1)S(1)} %get-tuple-element.91), kind=kOutput, calls=%fused_computation.6 | convolution fusion | flops 4268032 | bytes 164000 | tf_op jit(solution)/shard_map/dot_general | solution.py:230
  3.8 0.8 reduce.14
  4.6 1.0 %reshape.506 = bf16[128,2,576]{2,1,0:T(2,128)(2,1)} reshape(bf16[128,1152]{1,0:T(8,128)(2,1)S(1)} %reduce.14) | data formatting | bytes 589824
  5.7 20.8 %all-to-all-start = ((bf16[128,2,576]{2,1,0:T(2,128)(2,1)}), bf16[128,2,576]{2,1,0:T(2,128)(2,1)S(1)}, u32[]{:S(2)}, u32[]{:S(2)}) async-start(bf16[128,2,576]{2,1,0:T(2,128)(2,1)} %reshape.506), calls=%async_computation | async-start | bytes 655360 | tf_op jit(solution)/shard_map/all_to_all | solution.py:236
  26.5 0.6 copy-done.19
  27.2 0.6 select_reduce_fusion.13
  28.6 1.0 %select_reduce_fusion.3 = (bf16[128,128]{1,0:T(8,128)(2,1)S(1)}, bf16[128,128]{1,0:T(8,128)(2,1)S(1)}, bf16[128,128]{1,0:T(8,128)(2,1)S(1)}, bf16[128,128]{1,0:T(8,128)(2,1)S(1)}) fusion(bf16[32,128,128]{2,1,0:T(8,128)(2,1)S(1)} %copy-done.1, pred[32]{0:T(512)(128)(4,1)S(1)} %get-tuple-element.54, pred[32]{0:T(512)(128)(4,1)S(1)} %get-tuple-element.53, ...), kind=kLoop, calls=%fused_computation.25 | loop fusion | flops 4128768 | bytes 2228288 | tf_op jit(solution)/shard_map/reduce_sum | solution.py:191
  29.8 4.0 %collective-permute-start.1 = (bf16[272,128]{1,0:T(8,128)(2,1)S(1)}, bf16[272,128]{1,0:T(8,128)(2,1)S(1)}, u32[]{:S(2)}, u32[]{:S(2)}) collective-permute-start(bf16[272,128]{1,0:T(8,128)(2,1)S(1)} %concatenate.28), channel_id=1, source_target_pairs={{0,1},{1,2},{2,3},{3,4},{4,5},{5,6},{6,7},{7,8},{8,9},{9,10},{10,1... | collective-permute-start | bytes 208904 | tf_op jit(solution)/shard_map/ppermute | solution.py:210
  34.5 7.0 %collective-permute-start = (bf16[272,128]{1,0:T(8,128)(2,1)S(1)}, bf16[272,128]{1,0:T(8,128)(2,1)S(1)}, u32[]{:S(2)}, u32[]{:S(2)}) collective-permute-start(bf16[272,128]{1,0:T(8,128)(2,1)S(1)} %concatenate.27), channel_id=1, source_target_pairs={{0,127},{1,0},{2,1},{3,2},{4,3},{5,4},{6,5},{7,6},{8,7},{9,8},{10,... | collective-permute-start | bytes 208904 | tf_op jit(solution)/shard_map/ppermute | solution.py:213
  41.6 0.6 copy-done.15
  43.5 0.6 select_reduce_fusion.9.src_ref
  44.1 0.5 slice.123
  45.3 0.5 slice.121
  46.5 0.6 select_select_fusion.3.take_ref
  47.1 3.5 %shard_map.218 = (bf16[32,128,128]{2,1,0:T(8,128)(2,1)}, bf16[32,128,128]{2,1,0:T(8,128)(2,1)}) custom-call(s32[32]{0:T(128)} %select_reduce_fusion.9.src_ref, s32[32]{0:T(128)} %select_select_fusion.3.take_ref, bf16[32,128,128]{2,1,0:T(8,128)(2,1)} %keys_ref.1, bf16[32,128,128]{2,1,0:T(8,128)(2,1)} %values_ref.1, bf16[272,128]{1,0:T(8,128)(2,1)} %copy-done.9, ...), custom_call_target="tpu_custom_call" | custom-call | bytes 4194304 | tf_op jit(solution)/shard_map/pallas_call | solution.py:136
  50.6 0.8 slice_bitcast_fusion.3
  51.4 0.7 slice_bitcast_fusion.4
  54.1 0.7 copy-done.17
  56.4 0.7 fusion.166
  58.7 2.2 %collective-permute-start.2 = (bf16[64,512]{1,0:T(8,128)(2,1)S(1)}, bf16[64,512]{1,0:T(8,128)(2,1)S(1)}, u32[]{:S(2)}, u32[]{:S(2)}) collective-permute-start(bf16[64,512]{1,0:T(8,128)(2,1)S(1)} %convolution_convert_fusion.3), channel_id=1, source_target_pairs={{0,256},{128,384},{256,0},{384,128},{1,257},{129,385},{257,1},{385... | collective-permute-start | bytes 196616 | tf_op jit(solution)/shard_map/ppermute | solution.py:101
  61.3 2.4 %collective-permute-done.2 = bf16[64,512]{1,0:T(8,128)(2,1)S(1)} collective-permute-done((bf16[64,512]{1,0:T(8,128)(2,1)S(1)}, bf16[64,512]{1,0:T(8,128)(2,1)S(1)}, u32[]{:S(2)}, u32[]{:S(2)}) %collective-permute-start.2) | collective-permute-done | bytes 65568 | tf_op jit(solution)/shard_map/ppermute | solution.py:101
  63.8 4.6 %collective-permute-start.3 = (f32[64,512]{1,0:T(8,128)S(1)}, f32[64,512]{1,0:T(8,128)S(1)}, u32[]{:S(2)}, u32[]{:S(2)}) collective-permute-start(f32[64,512]{1,0:T(8,128)S(1)} %convert_add_fusion.1), channel_id=1, source_target_pairs={{0,128},{128,0},{256,384},{384,256},{1,129},{129,1},{257,385},{385... | collective-permute-start | bytes 393224 | tf_op jit(solution)/shard_map/ppermute | solution.py:101
  68.4 0.9 %collective-permute-done.3 = f32[64,512]{1,0:T(8,128)S(1)} collective-permute-done((f32[64,512]{1,0:T(8,128)S(1)}, f32[64,512]{1,0:T(8,128)S(1)}, u32[]{:S(2)}, u32[]{:S(2)}) %collective-permute-start.3) | collective-permute-done | bytes 131104 | tf_op jit(solution)/shard_map/ppermute | solution.py:101
  70.2 1.7 %convolution_convert_fusion.2 = bf16[64,512]{1,0:T(8,128)(2,1)S(1)} fusion(bf16[512,512]{1,0:T(8,128)(2,1)S(1)} %copy-done, bf16[512,512]{1,0:T(8,128)(2,1)} %param.33, f32[64,512]{1,0:T(8,128)S(1)} %get-tuple-element.48, f32[512]{0:T(512)S(1)} %copy-done.21, f32[64]{0:T(128)S(1)} %add_rsqrt_fusion.1, f32[64]{0:T(128)S(1)} %broadcast_multiply_fusion.1), kind=kOutput, calls=%fused_computation.7 | convolution fusion | flops 69402624 | bytes 1247744 | tf_op jit(solution)/shard_map/dot_general | solution.py:307
  71.9 2.2 %collective-permute-start.4 = (bf16[64,512]{1,0:T(8,128)(2,1)S(1)}, bf16[64,512]{1,0:T(8,128)(2,1)S(1)}, u32[]{:S(2)}, u32[]{:S(2)}) collective-permute-start(bf16[64,512]{1,0:T(8,128)(2,1)S(1)} %convolution_convert_fusion.2), channel_id=1, source_target_pairs={{0,256},{128,384},{256,0},{384,128},{1,257},{129,385},{257,1},{385... | collective-permute-start | bytes 196616 | tf_op jit(solution)/shard_map/ppermute | solution.py:101
  74.3 2.6 %collective-permute-done.4 = bf16[64,512]{1,0:T(8,128)(2,1)S(1)} collective-permute-done((bf16[64,512]{1,0:T(8,128)(2,1)S(1)}, bf16[64,512]{1,0:T(8,128)(2,1)S(1)}, u32[]{:S(2)}, u32[]{:S(2)}) %collective-permute-start.4) | collective-permute-done | bytes 65568 | tf_op jit(solution)/shard_map/ppermute | solution.py:101
  76.9 3.4 %collective-permute-start.5 = (f32[64,512]{1,0:T(8,128)S(1)}, f32[64,512]{1,0:T(8,128)S(1)}, u32[]{:S(2)}, u32[]{:S(2)}) collective-permute-start(f32[64,512]{1,0:T(8,128)S(1)} %convert_add_fusion), channel_id=1, source_target_pairs={{0,128},{128,0},{256,384},{384,256},{1,129},{129,1},{257,385},{385... | collective-permute-start | bytes 393224 | tf_op jit(solution)/shard_map/ppermute | solution.py:101
  80.4 2.6 %select_select_fusion = (bf16[32,128,128]{2,1,0:T(8,128)(2,1)}, bf16[32,128,128]{2,1,0:T(8,128)(2,1)}) fusion(bf16[32,128,128]{2,1,0:T(8,128)(2,1)S(1)} %copy-done.5, pred[32,128]{1,0:T(8,128)(4,1)S(1)} %get-tuple-element.100, pred[32,128]{1,0:T(8,128)(4,1)S(1)} %get-tuple-element.101, bf16[32,128]{1,0:T(8,128)(2,1)S(1)} %get-tuple-element.76, ...), kind=kLoop, calls=%fused_computation.20 | loop fusion | flops 2097152 | bytes 4235264 | tf_op jit(solution)/shard_map/jit(_where)/select_n | solution.py:329
  83.3 0.6 slice_bitcast_fusion
  84.6 0.7 copy-done.20
  85.8 0.8 copy.91
  (130 shorter events, 10.6 us)
Async XLA Ops:
  0.6 69.1 %copy-start = (bf16[512,512]{1,0:T(8,128)(2,1)S(1)}, bf16[512,512]{1,0:T(8,128)(2,1)}, u32[]{:S(2)}) copy-start(bf16[512,512]{1,0:T(8,128)(2,1)} %param.34) | copy-start | bytes 1572868
  0.6 0.7 copy-start.22
  1.6 1.1 %copy-start.7 = (bf16[32,512]{1,0:T(8,128)(2,1)S(1)}, bf16[32,512]{1,0:T(8,128)(2,1)}, u32[]{:S(2)}) copy-start(bf16[32,512]{1,0:T(8,128)(2,1)} %param.19) | copy-start | bytes 98308
  3.2 25.3 %copy-start.2 = (bf16[32,128,128]{2,1,0:T(8,128)(2,1)S(1)}, bf16[32,128,128]{2,1,0:T(8,128)(2,1)}, u32[]{:S(2)}) copy-start(bf16[32,128,128]{2,1,0:T(8,128)(2,1)} %values_ref.1) | copy-start | bytes 3145732
  3.3 25.3 %copy-start.1 = (bf16[32,128,128]{2,1,0:T(8,128)(2,1)S(1)}, bf16[32,128,128]{2,1,0:T(8,128)(2,1)}, u32[]{:S(2)}) copy-start(bf16[32,128,128]{2,1,0:T(8,128)(2,1)} %keys_ref.1) | copy-start | bytes 3145732
  5.7 46.4 %all-to-all-start = ((bf16[128,2,576]{2,1,0:T(2,128)(2,1)}), bf16[128,2,576]{2,1,0:T(2,128)(2,1)S(1)}, u32[]{:S(2)}, u32[]{:S(2)}) async-start(bf16[128,2,576]{2,1,0:T(2,128)(2,1)} %reshape.506), calls=%async_computation | async-start | bytes 655360 | tf_op jit(solution)/shard_map/all_to_all | solution.py:236
  26.5 0.7 copy-start.19
  28.5 1.0 %copy-start.12 = (bf16[32,512]{1,0:T(8,128)(2,1)S(1)}, bf16[32,512]{1,0:T(8,128)(2,1)}, u32[]{:S(2)}) copy-start(bf16[32,512]{1,0:T(8,128)(2,1)} %param.23) | copy-start | bytes 98308
  28.6 1.0 %copy-start.13 = (bf16[32,512]{1,0:T(8,128)(2,1)S(1)}, bf16[32,512]{1,0:T(8,128)(2,1)}, u32[]{:S(2)}) copy-start(bf16[32,512]{1,0:T(8,128)(2,1)} %param.24) | copy-start | bytes 98308
  29.8 14.3 %collective-permute-start.1 = (bf16[272,128]{1,0:T(8,128)(2,1)S(1)}, bf16[272,128]{1,0:T(8,128)(2,1)S(1)}, u32[]{:S(2)}, u32[]{:S(2)}) collective-permute-start(bf16[272,128]{1,0:T(8,128)(2,1)S(1)} %concatenate.28), channel_id=1, source_target_pairs={{0,1},{1,2},{2,3},{3,4},{4,5},{5,6},{6,7},{7,8},{8,9},{9,10},{10,1... | collective-permute-start | bytes 208904 | tf_op jit(solution)/shard_map/ppermute | solution.py:210
  34.5 10.8 %collective-permute-start = (bf16[272,128]{1,0:T(8,128)(2,1)S(1)}, bf16[272,128]{1,0:T(8,128)(2,1)S(1)}, u32[]{:S(2)}, u32[]{:S(2)}) collective-permute-start(bf16[272,128]{1,0:T(8,128)(2,1)S(1)} %concatenate.27), channel_id=1, source_target_pairs={{0,127},{1,0},{2,1},{3,2},{4,3},{5,4},{6,5},{7,6},{8,7},{9,8},{10,... | collective-permute-start | bytes 208904 | tf_op jit(solution)/shard_map/ppermute | solution.py:213
  41.5 0.7 copy-start.15
  42.2 0.7 copy-start.16
  44.1 3.0 %copy-start.9 = (bf16[272,128]{1,0:T(8,128)(2,1)}, bf16[272,128]{1,0:T(8,128)(2,1)S(1)}, u32[]{:S(2)}) copy-start(bf16[272,128]{1,0:T(8,128)(2,1)S(1)} %collective-permute-done.1.lbox_ref) | copy-start | bytes 208900
  45.3 1.8 %copy-start.10 = (bf16[272,128]{1,0:T(8,128)(2,1)}, bf16[272,128]{1,0:T(8,128)(2,1)S(1)}, u32[]{:S(2)}) copy-start(bf16[272,128]{1,0:T(8,128)(2,1)S(1)} %collective-permute-done.rbox_ref) | copy-start | bytes 208900
  53.0 1.1 %copy-start.6 = (bf16[3,512,128]{2,1,0:T(8,128)(2,1)S(1)}, bf16[3,512,128]{2,1,0:T(8,128)(2,1)}, u32[]{:S(2)}) copy-start(bf16[3,512,128]{2,1,0:T(8,128)(2,1)} %param.29) | copy-start | bytes 1179652
  53.2 0.6 copy-start.11
  54.0 0.7 copy-start.17
  55.0 1.4 %copy-start.3 = (bf16[32,128,128]{2,1,0:T(8,128)(2,1)S(1)}, bf16[32,128,128]{2,1,0:T(8,128)(2,1)}, u32[]{:S(2)}) copy-start(bf16[32,128,128]{2,1,0:T(8,128)(2,1)} %get-tuple-element.7) | copy-start | bytes 3145732
  56.1 1.6 %copy-start.5 = (bf16[32,128,128]{2,1,0:T(8,128)(2,1)S(1)}, bf16[32,128,128]{2,1,0:T(8,128)(2,1)}, u32[]{:S(2)}) copy-start(bf16[32,128,128]{2,1,0:T(8,128)(2,1)} %get-tuple-element.8) | copy-start | bytes 3145732
  57.7 0.9 %copy-start.8 = (bf16[128,512]{1,0:T(8,128)(2,1)S(1)}, bf16[128,512]{1,0:T(8,128)(2,1)}, u32[]{:S(2)}) copy-start(bf16[128,512]{1,0:T(8,128)(2,1)} %param.30) | copy-start | bytes 393220
  58.7 5.0 %collective-permute-start.2 = (bf16[64,512]{1,0:T(8,128)(2,1)S(1)}, bf16[64,512]{1,0:T(8,128)(2,1)S(1)}, u32[]{:S(2)}, u32[]{:S(2)}) collective-permute-start(bf16[64,512]{1,0:T(8,128)(2,1)S(1)} %convolution_convert_fusion.3), channel_id=1, source_target_pairs={{0,256},{128,384},{256,0},{384,128},{1,257},{129,385},{257,1},{385... | collective-permute-start | bytes 196616 | tf_op jit(solution)/shard_map/ppermute | solution.py:101
  63.8 5.6 %copy-start.14 = (f32[512]{0:T(512)S(1)}, f32[512]{0:T(512)}, u32[]{:S(2)}) copy-start(f32[512]{0:T(512)} %param.31) | copy-start | bytes 6148
  63.8 5.5 %collective-permute-start.3 = (f32[64,512]{1,0:T(8,128)S(1)}, f32[64,512]{1,0:T(8,128)S(1)}, u32[]{:S(2)}, u32[]{:S(2)}) collective-permute-start(f32[64,512]{1,0:T(8,128)S(1)} %convert_add_fusion.1), channel_id=1, source_target_pairs={{0,128},{128,0},{256,384},{384,256},{1,129},{129,1},{257,385},{385... | collective-permute-start | bytes 393224 | tf_op jit(solution)/shard_map/ppermute | solution.py:101
  69.5 0.7 copy-start.21
  71.9 5.0 %collective-permute-start.4 = (bf16[64,512]{1,0:T(8,128)(2,1)S(1)}, bf16[64,512]{1,0:T(8,128)(2,1)S(1)}, u32[]{:S(2)}, u32[]{:S(2)}) collective-permute-start(bf16[64,512]{1,0:T(8,128)(2,1)S(1)} %convolution_convert_fusion.2), channel_id=1, source_target_pairs={{0,256},{128,384},{256,0},{384,128},{1,257},{129,385},{257,1},{385... | collective-permute-start | bytes 196616 | tf_op jit(solution)/shard_map/ppermute | solution.py:101
  76.9 6.2 %collective-permute-start.5 = (f32[64,512]{1,0:T(8,128)S(1)}, f32[64,512]{1,0:T(8,128)S(1)}, u32[]{:S(2)}, u32[]{:S(2)}) collective-permute-start(f32[64,512]{1,0:T(8,128)S(1)} %convert_add_fusion), channel_id=1, source_target_pairs={{0,128},{128,0},{256,384},{384,256},{1,129},{129,1},{257,385},{385... | collective-permute-start | bytes 393224 | tf_op jit(solution)/shard_map/ppermute | solution.py:101
  80.3 2.8 %copy-start.18 = (f32[512]{0:T(512)S(1)}, f32[512]{0:T(512)}, u32[]{:S(2)}) copy-start(f32[512]{0:T(512)} %param.35) | copy-start | bytes 6148
  83.0 1.2 %copy-start.4 = (bf16[16,64,512]{2,1,0:T(8,128)(2,1)S(1)}, bf16[16,64,512]{2,1,0:T(8,128)(2,1)}, u32[]{:S(2)}) copy-start(bf16[16,64,512]{2,1,0:T(8,128)(2,1)} %param.36) | copy-start | bytes 3145732
  84.6 0.7 copy-start.20

commit v6 on v5

--- a/solution.py
+++ b/solution.py
@@ -92,16 +92,14 @@
 
 def section_sum(partial):
     size = lax.axis_size("section")
-    if size & (size - 1):
+    if size != 4:
         return lax.psum(partial.astype(jnp.bfloat16), "section").astype(jnp.float32)
-    total = partial.astype(jnp.bfloat16)
-    bit = size // 2
-    while bit >= 1:
-        route = [(i, i ^ bit) for i in range(size)]
-        other = lax.ppermute(total, "section", route)
-        total = total.astype(jnp.float32) + other.astype(jnp.float32)
-        bit //= 2
-    return total
+    rounded = partial.astype(jnp.bfloat16)
+    got = [
+        lax.ppermute(rounded, "section", [(i, i ^ mask) for i in range(size)]).astype(jnp.float32)
+        for mask in (1, 2, 3)
+    ]
+    return (rounded.astype(jnp.float32) + got[0]) + (got[1] + got[2])
 
 
 def cache_kernel(src_ref, take_ref, keys_ref, values_ref, lbox_ref, rbox_ref, ok_ref, ov_ref):

time: 87.4 us -> 88.2 us (level)
  waiting for transfers between devices: 6.02 us -> 0.84 us
  starting transfers between devices: 44.2 us -> 48.3 us
    ppermute x4 -> x6, waiting for transfers between devices: 6.01 us -> 0.83 us  [section_sum(): lax.ppermute(rounded, 'section', [(i, i ^ mask) for i in range(size)])]
    ppermute x4 -> x6, starting transfers between devices: 12.4 us -> 16.5 us  [section_sum(): lax.ppermute(rounded, 'section', [(i, i ^ mask) for i in range(size)])]
    unnamed x50 -> x56, local copies, waits for them, and re-layouts: 7.91 us -> 8.55 us
  transfers between devices with their start and end apart: 7 -> 9, of which waited for: 3 -> 2; matrix products, arithmetic and copies ran while one was open for 11% -> 12% of each run, Pallas kernels for 4% -> 4%
where the time goes in v6:
time: 88.2 us; the launch traced here: 87.2 us
  starting transfers between devices  48.3 us (55%)
  local copies, waits for them, and re-layouts  13.6 us (15%)
  other arithmetic  9.99 us (11%)
  matrix products  6.99 us (8%)
  between operations  4.01 us (5%)
  Pallas kernels  3.5 us (4%)
    all_to_all x1, starting transfers between devices, local(): got = lax.all_to_all(send, 'batch', split_axis=0, concat_axis=0, tiled=True)  20.8 us
    ppermute x6, starting transfers between devices, section_sum(): lax.ppermute(rounded, 'section', [(i, i ^ mask) for i in range(size)])  16.5 us
    unnamed x56, local copies, waits for them, and re-layouts  8.55 us
    ppermute x1, starting transfers between devices, local(): lax.ppermute(pack(left_owner), 'batch', [(i, (i - 1) % owners) for i in r...  7.01 us
    ppermute x1, starting transfers between devices, local(): lax.ppermute(pack(right_owner), 'batch', [(i, (i + 1) % owners) for i in...  3.97 us
    pallas_call x1, Pallas kernels, route_caches(): pl.pallas_call(cache_kernel, out_shape=(shape, shape), in_specs=[smem] *...  3.5 us
    select_n x1, other arithmetic, local(): jnp.where(hit_second, fresh_values[:, 1][:, None, :], jnp.where(hit_first...  2.61 us
  transfers between devices with their start and end apart: 9, of which 2 were waited for; matrix products, arithmetic and copies ran while one was open for 12% of the time, Pallas kernels for 4%

profile of v6, /device:TPU:1, one launch (start us, length us, event | category | flops | bytes accessed | tf_op | source)
XLA Modules:
  0.0 87.2 jit_solution(6545300078546493961)
XLA Ops:
  0.7 0.7 copy-done.25
  1.6 1.1 %fusion.3 = bf16[128,1,512]{2,0,1:T(8,128)(2,1)S(1)} fusion(bf16[32,512]{1,0:T(8,128)(2,1)} %param.19, s32[32]{0:T(128)S(1)} %get-tuple-element.92, pred[32]{0:T(512)(128)(4,1)S(1)} %get-tuple-element.91), kind=kOutput, calls=%fused_computation.6 | convolution fusion | flops 4268032 | bytes 164000 | tf_op jit(solution)/shard_map/dot_general | solution.py:228
  3.8 0.8 reduce.14
  4.6 1.0 %reshape.506 = bf16[128,2,576]{2,1,0:T(2,128)(2,1)} reshape(bf16[128,1152]{1,0:T(8,128)(2,1)S(1)} %reduce.14) | data formatting | bytes 589824
  5.7 20.8 %all-to-all-start = ((bf16[128,2,576]{2,1,0:T(2,128)(2,1)}), bf16[128,2,576]{2,1,0:T(2,128)(2,1)S(1)}, u32[]{:S(2)}, u32[]{:S(2)}) async-start(bf16[128,2,576]{2,1,0:T(2,128)(2,1)} %reshape.506), calls=%async_computation | async-start | bytes 655360 | tf_op jit(solution)/shard_map/all_to_all | solution.py:234
  26.5 0.6 copy-done.22
  27.2 0.6 select_reduce_fusion.13
  28.6 1.0 %select_reduce_fusion.3 = (bf16[128,128]{1,0:T(8,128)(2,1)S(1)}, bf16[128,128]{1,0:T(8,128)(2,1)S(1)}, bf16[128,128]{1,0:T(8,128)(2,1)S(1)}, bf16[128,128]{1,0:T(8,128)(2,1)S(1)}) fusion(bf16[32,128,128]{2,1,0:T(8,128)(2,1)S(1)} %copy-done.1, pred[32]{0:T(512)(128)(4,1)S(1)} %get-tuple-element.54, pred[32]{0:T(512)(128)(4,1)S(1)} %get-tuple-element.53, ...), kind=kLoop, calls=%fused_computation.25 | loop fusion | flops 4128768 | bytes 2228288 | tf_op jit(solution)/shard_map/reduce_sum | solution.py:189
  29.7 4.0 %collective-permute-start.1 = (bf16[272,128]{1,0:T(8,128)(2,1)S(1)}, bf16[272,128]{1,0:T(8,128)(2,1)S(1)}, u32[]{:S(2)}, u32[]{:S(2)}) collective-permute-start(bf16[272,128]{1,0:T(8,128)(2,1)S(1)} %concatenate.28), channel_id=1, source_target_pairs={{0,1},{1,2},{2,3},{3,4},{4,5},{5,6},{6,7},{7,8},{8,9},{9,10},{10,1... | collective-permute-start | bytes 208904 | tf_op jit(solution)/shard_map/ppermute | solution.py:208
  34.5 7.0 %collective-permute-start = (bf16[272,128]{1,0:T(8,128)(2,1)S(1)}, bf16[272,128]{1,0:T(8,128)(2,1)S(1)}, u32[]{:S(2)}, u32[]{:S(2)}) collective-permute-start(bf16[272,128]{1,0:T(8,128)(2,1)S(1)} %concatenate.27), channel_id=1, source_target_pairs={{0,127},{1,0},{2,1},{3,2},{4,3},{5,4},{6,5},{7,6},{8,7},{9,8},{10,... | collective-permute-start | bytes 208904 | tf_op jit(solution)/shard_map/ppermute | solution.py:211
  41.5 0.6 copy-done.18
  43.3 0.7 iota_compare_fusion
  44.0 0.7 select_reduce_fusion.9.src_ref
  44.7 0.5 slice.123
  46.0 0.5 slice.121
  47.7 3.5 %shard_map.218 = (bf16[32,128,128]{2,1,0:T(8,128)(2,1)}, bf16[32,128,128]{2,1,0:T(8,128)(2,1)}) custom-call(s32[32]{0:T(128)} %select_reduce_fusion.9.src_ref, s32[32]{0:T(128)} %select_select_fusion.3.take_ref, bf16[32,128,128]{2,1,0:T(8,128)(2,1)} %keys_ref.1, bf16[32,128,128]{2,1,0:T(8,128)(2,1)} %values_ref.1, bf16[272,128]{1,0:T(8,128)(2,1)} %copy-done.9, ...), custom_call_target="tpu_custom_call" | custom-call | bytes 4194304 | tf_op jit(solution)/shard_map/pallas_call | solution.py:134
  51.2 0.8 slice_bitcast_fusion.3
  51.9 0.7 slice_bitcast_fusion.4
  52.7 0.7 select_bitcast_fusion
  55.4 0.7 copy-done.20
  57.7 0.7 fusion.163
  60.1 3.6 %collective-permute-start.4 = (bf16[64,512]{1,0:T(8,128)(2,1)S(1)}, bf16[64,512]{1,0:T(8,128)(2,1)S(1)}, u32[]{:S(2)}, u32[]{:S(2)}) collective-permute-start(bf16[64,512]{1,0:T(8,128)(2,1)S(1)} %convolution_convert_fusion.3), channel_id=1, source_target_pairs={{0,384},{128,256},{256,128},{384,0},{1,385},{129,257},{257,129},{3... | collective-permute-start | bytes 196616 | tf_op jit(solution)/shard_map/ppermute | solution.py:99
  63.7 3.1 %collective-permute-start.3 = (bf16[64,512]{1,0:T(8,128)(2,1)S(1)}, bf16[64,512]{1,0:T(8,128)(2,1)S(1)}, u32[]{:S(2)}, u32[]{:S(2)}) collective-permute-start(bf16[64,512]{1,0:T(8,128)(2,1)S(1)} %convolution_convert_fusion.3), channel_id=1, source_target_pairs={{0,256},{128,384},{256,0},{384,128},{1,257},{129,385},{257,1},{385... | collective-permute-start | bytes 196616 | tf_op jit(solution)/shard_map/ppermute | solution.py:99
  66.8 1.9 %collective-permute-start.2 = (bf16[64,512]{1,0:T(8,128)(2,1)S(1)}, bf16[64,512]{1,0:T(8,128)(2,1)S(1)}, u32[]{:S(2)}, u32[]{:S(2)}) collective-permute-start(bf16[64,512]{1,0:T(8,128)(2,1)S(1)} %convolution_convert_fusion.3), channel_id=1, source_target_pairs={{0,128},{128,0},{256,384},{384,256},{1,129},{129,1},{257,385},{385... | collective-permute-start | bytes 196616 | tf_op jit(solution)/shard_map/ppermute | solution.py:99
  70.7 1.7 %convolution_convert_fusion.2 = bf16[64,512]{1,0:T(8,128)(2,1)S(1)} fusion(bf16[512,512]{1,0:T(8,128)(2,1)S(1)} %copy-done, bf16[512,512]{1,0:T(8,128)(2,1)} %param.33, f32[64,512]{1,0:T(8,128)S(1)} %get-tuple-element.48, f32[512]{0:T(512)S(1)} %copy-done.24, f32[64]{0:T(128)S(1)} %add_rsqrt_fusion.1, f32[64]{0:T(128)S(1)} %broadcast_multiply_fusion.1), kind=kOutput, calls=%fused_computation.7 | convolution fusion | flops 69402624 | bytes 1247744 | tf_op jit(solution)/shard_map/dot_general | solution.py:305
  72.5 2.4 %collective-permute-start.7 = (bf16[64,512]{1,0:T(8,128)(2,1)S(1)}, bf16[64,512]{1,0:T(8,128)(2,1)S(1)}, u32[]{:S(2)}, u32[]{:S(2)}) collective-permute-start(bf16[64,512]{1,0:T(8,128)(2,1)S(1)} %convolution_convert_fusion.2), channel_id=1, source_target_pairs={{0,384},{128,256},{256,128},{384,0},{1,385},{129,257},{257,129},{3... | collective-permute-start | bytes 196616 | tf_op jit(solution)/shard_map/ppermute | solution.py:99
  74.9 3.1 %collective-permute-start.6 = (bf16[64,512]{1,0:T(8,128)(2,1)S(1)}, bf16[64,512]{1,0:T(8,128)(2,1)S(1)}, u32[]{:S(2)}, u32[]{:S(2)}) collective-permute-start(bf16[64,512]{1,0:T(8,128)(2,1)S(1)} %convolution_convert_fusion.2), channel_id=1, source_target_pairs={{0,256},{128,384},{256,0},{384,128},{1,257},{129,385},{257,1},{385... | collective-permute-start | bytes 196616 | tf_op jit(solution)/shard_map/ppermute | solution.py:99
  77.9 2.4 %collective-permute-start.5 = (bf16[64,512]{1,0:T(8,128)(2,1)S(1)}, bf16[64,512]{1,0:T(8,128)(2,1)S(1)}, u32[]{:S(2)}, u32[]{:S(2)}) collective-permute-start(bf16[64,512]{1,0:T(8,128)(2,1)S(1)} %convolution_convert_fusion.2), channel_id=1, source_target_pairs={{0,128},{128,0},{256,384},{384,256},{1,129},{129,1},{257,385},{385... | collective-permute-start | bytes 196616 | tf_op jit(solution)/shard_map/ppermute | solution.py:99
  80.4 0.7 copy-done.16
  81.0 2.6 %select_select_fusion = (bf16[32,128,128]{2,1,0:T(8,128)(2,1)}, bf16[32,128,128]{2,1,0:T(8,128)(2,1)}) fusion(bf16[32,128,128]{2,1,0:T(8,128)(2,1)S(1)} %copy-done.5, pred[32,128]{1,0:T(8,128)(4,1)S(1)} %copy-done.15, pred[32,128]{1,0:T(8,128)(4,1)S(1)} %copy-done.16, bf16[32,128]{1,0:T(8,128)(2,1)S(1)} %get-tuple-element.76, ...), kind=kLoop, calls=%fused_computation.20 | loop fusion | flops 2097152 | bytes 4235264 | tf_op jit(solution)/shard_map/jit(_where)/select_n | solution.py:327
  84.0 0.6 slice_bitcast_fusion
  86.5 0.8 copy.91
  (138 shorter events, 12.4 us)
Async XLA Ops:
  0.6 69.6 %copy-start = (bf16[512,512]{1,0:T(8,128)(2,1)S(1)}, bf16[512,512]{1,0:T(8,128)(2,1)}, u32[]{:S(2)}) copy-start(bf16[512,512]{1,0:T(8,128)(2,1)} %param.34) | copy-start | bytes 1572868
  0.6 0.7 copy-start.25
  1.6 1.1 %copy-start.7 = (bf16[32,512]{1,0:T(8,128)(2,1)S(1)}, bf16[32,512]{1,0:T(8,128)(2,1)}, u32[]{:S(2)}) copy-start(bf16[32,512]{1,0:T(8,128)(2,1)} %param.19) | copy-start | bytes 98308
  3.2 25.3 %copy-start.2 = (bf16[32,128,128]{2,1,0:T(8,128)(2,1)S(1)}, bf16[32,128,128]{2,1,0:T(8,128)(2,1)}, u32[]{:S(2)}) copy-start(bf16[32,128,128]{2,1,0:T(8,128)(2,1)} %values_ref.1) | copy-start | bytes 3145732
  3.3 25.3 %copy-start.1 = (bf16[32,128,128]{2,1,0:T(8,128)(2,1)S(1)}, bf16[32,128,128]{2,1,0:T(8,128)(2,1)}, u32[]{:S(2)}) copy-start(bf16[32,128,128]{2,1,0:T(8,128)(2,1)} %keys_ref.1) | copy-start | bytes 3145732
  5.7 47.8 %all-to-all-start = ((bf16[128,2,576]{2,1,0:T(2,128)(2,1)}), bf16[128,2,576]{2,1,0:T(2,128)(2,1)S(1)}, u32[]{:S(2)}, u32[]{:S(2)}) async-start(bf16[128,2,576]{2,1,0:T(2,128)(2,1)} %reshape.506), calls=%async_computation | async-start | bytes 655360 | tf_op jit(solution)/shard_map/all_to_all | solution.py:234
  28.5 1.0 %copy-start.13 = (bf16[32,512]{1,0:T(8,128)(2,1)S(1)}, bf16[32,512]{1,0:T(8,128)(2,1)}, u32[]{:S(2)}) copy-start(bf16[32,512]{1,0:T(8,128)(2,1)} %param.24) | copy-start | bytes 98308
  28.5 1.0 %copy-start.14 = (bf16[32,512]{1,0:T(8,128)(2,1)S(1)}, bf16[32,512]{1,0:T(8,128)(2,1)}, u32[]{:S(2)}) copy-start(bf16[32,512]{1,0:T(8,128)(2,1)} %param.23) | copy-start | bytes 98308
  29.7 15.0 %collective-permute-start.1 = (bf16[272,128]{1,0:T(8,128)(2,1)S(1)}, bf16[272,128]{1,0:T(8,128)(2,1)S(1)}, u32[]{:S(2)}, u32[]{:S(2)}) collective-permute-start(bf16[272,128]{1,0:T(8,128)(2,1)S(1)} %concatenate.28), channel_id=1, source_target_pairs={{0,1},{1,2},{2,3},{3,4},{4,5},{5,6},{6,7},{7,8},{8,9},{9,10},{10,1... | collective-permute-start | bytes 208904 | tf_op jit(solution)/shard_map/ppermute | solution.py:208
  34.5 11.5 %collective-permute-start = (bf16[272,128]{1,0:T(8,128)(2,1)S(1)}, bf16[272,128]{1,0:T(8,128)(2,1)S(1)}, u32[]{:S(2)}, u32[]{:S(2)}) collective-permute-start(bf16[272,128]{1,0:T(8,128)(2,1)S(1)} %concatenate.27), channel_id=1, source_target_pairs={{0,127},{1,0},{2,1},{3,2},{4,3},{5,4},{6,5},{7,6},{8,7},{9,8},{10,... | collective-permute-start | bytes 208904 | tf_op jit(solution)/shard_map/ppermute | solution.py:211
  42.2 0.7 copy-start.19
  44.7 3.0 %copy-start.9 = (bf16[272,128]{1,0:T(8,128)(2,1)}, bf16[272,128]{1,0:T(8,128)(2,1)S(1)}, u32[]{:S(2)}) copy-start(bf16[272,128]{1,0:T(8,128)(2,1)S(1)} %collective-permute-done.1.lbox_ref) | copy-start | bytes 208900
  46.0 1.7 %copy-start.10 = (bf16[272,128]{1,0:T(8,128)(2,1)}, bf16[272,128]{1,0:T(8,128)(2,1)S(1)}, u32[]{:S(2)}) copy-start(bf16[272,128]{1,0:T(8,128)(2,1)S(1)} %collective-permute-done.rbox_ref) | copy-start | bytes 208900
  54.3 1.1 %copy-start.6 = (bf16[3,512,128]{2,1,0:T(8,128)(2,1)S(1)}, bf16[3,512,128]{2,1,0:T(8,128)(2,1)}, u32[]{:S(2)}) copy-start(bf16[3,512,128]{2,1,0:T(8,128)(2,1)} %param.29) | copy-start | bytes 1179652
  55.4 0.7 copy-start.20
  56.3 1.4 %copy-start.3 = (bf16[32,128,128]{2,1,0:T(8,128)(2,1)S(1)}, bf16[32,128,128]{2,1,0:T(8,128)(2,1)}, u32[]{:S(2)}) copy-start(bf16[32,128,128]{2,1,0:T(8,128)(2,1)} %get-tuple-element.7) | copy-start | bytes 3145732
  57.4 1.6 %copy-start.5 = (bf16[32,128,128]{2,1,0:T(8,128)(2,1)S(1)}, bf16[32,128,128]{2,1,0:T(8,128)(2,1)}, u32[]{:S(2)}) copy-start(bf16[32,128,128]{2,1,0:T(8,128)(2,1)} %get-tuple-element.8) | copy-start | bytes 3145732
  59.0 0.9 %copy-start.8 = (bf16[128,512]{1,0:T(8,128)(2,1)S(1)}, bf16[128,512]{1,0:T(8,128)(2,1)}, u32[]{:S(2)}) copy-start(bf16[128,512]{1,0:T(8,128)(2,1)} %param.30) | copy-start | bytes 393220
  60.1 9.0 %collective-permute-start.4 = (bf16[64,512]{1,0:T(8,128)(2,1)S(1)}, bf16[64,512]{1,0:T(8,128)(2,1)S(1)}, u32[]{:S(2)}, u32[]{:S(2)}) collective-permute-start(bf16[64,512]{1,0:T(8,128)(2,1)S(1)} %convolution_convert_fusion.3), channel_id=1, source_target_pairs={{0,384},{128,256},{256,128},{384,0},{1,385},{129,257},{257,129},{3... | collective-permute-start | bytes 196616 | tf_op jit(solution)/shard_map/ppermute | solution.py:99
  63.7 5.7 %collective-permute-start.3 = (bf16[64,512]{1,0:T(8,128)(2,1)S(1)}, bf16[64,512]{1,0:T(8,128)(2,1)S(1)}, u32[]{:S(2)}, u32[]{:S(2)}) collective-permute-start(bf16[64,512]{1,0:T(8,128)(2,1)S(1)} %convolution_convert_fusion.3), channel_id=1, source_target_pairs={{0,256},{128,384},{256,0},{384,128},{1,257},{129,385},{257,1},{385... | collective-permute-start | bytes 196616 | tf_op jit(solution)/shard_map/ppermute | solution.py:99
  66.8 3.1 %collective-permute-start.2 = (bf16[64,512]{1,0:T(8,128)(2,1)S(1)}, bf16[64,512]{1,0:T(8,128)(2,1)S(1)}, u32[]{:S(2)}, u32[]{:S(2)}) collective-permute-start(bf16[64,512]{1,0:T(8,128)(2,1)S(1)} %convolution_convert_fusion.3), channel_id=1, source_target_pairs={{0,128},{128,0},{256,384},{384,256},{1,129},{129,1},{257,385},{385... | collective-permute-start | bytes 196616 | tf_op jit(solution)/shard_map/ppermute | solution.py:99
  69.0 0.9 %copy-start.17 = (f32[512]{0:T(512)S(1)}, f32[512]{0:T(512)}, u32[]{:S(2)}) copy-start(f32[512]{0:T(512)} %param.31) | copy-start | bytes 6148
  70.1 0.7 copy-start.24
  72.5 11.3 %collective-permute-start.7 = (bf16[64,512]{1,0:T(8,128)(2,1)S(1)}, bf16[64,512]{1,0:T(8,128)(2,1)S(1)}, u32[]{:S(2)}, u32[]{:S(2)}) collective-permute-start(bf16[64,512]{1,0:T(8,128)(2,1)S(1)} %convolution_convert_fusion.2), channel_id=1, source_target_pairs={{0,384},{128,256},{256,128},{384,0},{1,385},{129,257},{257,129},{3... | collective-permute-start | bytes 196616 | tf_op jit(solution)/shard_map/ppermute | solution.py:99
  74.9 8.9 %collective-permute-start.6 = (bf16[64,512]{1,0:T(8,128)(2,1)S(1)}, bf16[64,512]{1,0:T(8,128)(2,1)S(1)}, u32[]{:S(2)}, u32[]{:S(2)}) collective-permute-start(bf16[64,512]{1,0:T(8,128)(2,1)S(1)} %convolution_convert_fusion.2), channel_id=1, source_target_pairs={{0,256},{128,384},{256,0},{384,128},{1,257},{129,385},{257,1},{385... | collective-permute-start | bytes 196616 | tf_op jit(solution)/shard_map/ppermute | solution.py:99
  77.9 5.8 %collective-permute-start.5 = (bf16[64,512]{1,0:T(8,128)(2,1)S(1)}, bf16[64,512]{1,0:T(8,128)(2,1)S(1)}, u32[]{:S(2)}, u32[]{:S(2)}) collective-permute-start(bf16[64,512]{1,0:T(8,128)(2,1)S(1)} %convolution_convert_fusion.2), channel_id=1, source_target_pairs={{0,128},{128,0},{256,384},{384,256},{1,129},{129,1},{257,385},{385... | collective-permute-start | bytes 196616 | tf_op jit(solution)/shard_map/ppermute | solution.py:99
  80.3 0.7 copy-start.16
  80.4 0.7 copy-start.15
  81.0 2.8 %copy-start.21 = (f32[512]{0:T(512)S(1)}, f32[512]{0:T(512)}, u32[]{:S(2)}) copy-start(f32[512]{0:T(512)} %param.35) | copy-start | bytes 6148
  83.7 1.2 %copy-start.4 = (bf16[16,64,512]{2,1,0:T(8,128)(2,1)S(1)}, bf16[16,64,512]{2,1,0:T(8,128)(2,1)}, u32[]{:S(2)}) copy-start(bf16[16,64,512]{2,1,0:T(8,128)(2,1)} %param.36) | copy-start | bytes 3145732
  84.9 0.8 copy-start.12
  85.3 0.7 copy-start.23
  (3 other events, 1.9 us)

commit v7 on v4

--- a/solution.py
+++ b/solution.py
@@ -221,24 +221,25 @@
     same_before = (target[None, :] == target[:, None]) & (slot_ids[None, :] < slot_ids[:, None])
     arrival_rank = jnp.sum(same_before.astype(jnp.int32), axis=1)
     box_ids = target * capacity + arrival_rank
+    payload = jnp.concatenate(
+        [
+            latents,
+            jnp.broadcast_to((landing + 1).astype(jnp.bfloat16)[:, None], (streams, CODE_LANES)),
+        ],
+        axis=1,
+    )
     placing = one_hot(jnp.arange(owners * capacity, dtype=jnp.int32), box_ids)
-    send_rows = jnp.dot(placing, latents, preferred_element_type=jnp.float32).astype(jnp.bfloat16)
-    send_codes = jnp.dot(
-        placing,
-        jnp.broadcast_to((landing + 1).astype(jnp.bfloat16)[:, None], (streams, CODE_LANES)),
-        preferred_element_type=jnp.float32,
-    ).astype(jnp.bfloat16)
-    code_block = send_codes.reshape(owners, capacity, CODE_LANES)[:, :, 0]
-    code_block = jnp.pad(code_block, ((0, 0), (0, CODE_LANES - capacity)))
-    send = jnp.concatenate(
-        [send_rows.reshape(owners, capacity * model_width), code_block], axis=1
-    )
-    got = lax.all_to_all(send, "batch", split_axis=0, concat_axis=0, tiled=True)
-    got_codes = got[:, capacity * model_width : capacity * model_width + capacity]
-    got_codes = got_codes.reshape(owners * capacity).astype(jnp.int32) - 1
-    got_rows = got[:, : capacity * model_width].reshape(owners * capacity, model_width)
+    send_rows = jnp.dot(placing, payload, preferred_element_type=jnp.float32).astype(jnp.bfloat16)
+    got = lax.all_to_all(
+        send_rows.reshape(owners, capacity, model_width + CODE_LANES),
+        "batch",
+        split_axis=0,
+        concat_axis=0,
+        tiled=True,
+    ).reshape(owners * capacity, model_width + CODE_LANES)
+    got_codes = got[:, model_width].astype(jnp.int32) - 1
     arrived = jnp.dot(
-        one_hot(slot_ids, got_codes), got_rows, preferred_element_type=jnp.float32
+        one_hot(slot_ids, got_codes), got[:, :model_width], preferred_element_type=jnp.float32
     ).astype(jnp.bfloat16)
 
     staying = dest_owner == own_index
@@ -278,15 +279,40 @@
     queries = rotate(projections[0], times, HEAD_DIM).astype(jnp.bfloat16)
     fresh_keys = rotate(projections[1], times, HEAD_DIM).astype(jnp.bfloat16)
     fresh_values = projections[2].astype(jnp.bfloat16)
-    attended = attend(
-        queries,
-        fresh_keys,
-        fresh_values,
-        keys_old,
-        values_old,
-        positions,
-        head_share // HEAD_DIM,
+    to_source = jnp.transpose(picking)
+    arrivals = jnp.stack([from_l, from_r]).astype(jnp.bfloat16)
+
+    def reorder(order, rows):
+        return jnp.einsum(
+            "gn,nfd->gfd", order, rows, preferred_element_type=jnp.float32
+        ).astype(rows.dtype)
+
+    def reorder_positions(order):
+        return jnp.sum(jnp.where(order > 0, positions[None, :], 0), axis=1)
+
+    local_heads = head_share // HEAD_DIM
+    staying_attended = attend(
+        reorder(to_source, queries),
+        reorder(to_source, fresh_keys),
+        reorder(to_source, fresh_values),
+        cache_keys,
+        cache_values,
+        reorder_positions(to_source),
+        local_heads,
         HEAD_DIM,
+    )
+    arriving_attended = attend(
+        reorder(arrivals, queries),
+        reorder(arrivals, fresh_keys),
+        reorder(arrivals, fresh_values),
+        jnp.stack([from_left[0], from_right[0]]),
+        jnp.stack([from_left[1], from_right[1]]),
+        reorder_positions(arrivals),
+        local_heads,
+        HEAD_DIM,
+    )
+    attended = reorder(picking, staying_attended) + reorder(
+        jnp.transpose(arrivals), arriving_attended
     )
     partial_heads = jnp.dot(
         attended.reshape(2 * streams, head_share), out_weight, preferred_element_type=jnp.float32

time: 87 us -> 89.1 us (1.024)
  waiting for transfers between devices: 6.02 us -> 8.09 us
  matrix products: 5.24 us -> 7.24 us
  local copies, waits for them, and re-layouts: 13.5 us -> 11.7 us
  starting transfers between devices: 44.2 us -> 43.3 us
    all_to_all x1, starting transfers between devices: 20.8 us -> 8.82 us  [local(): lax.all_to_all(send_rows.reshape(owners, capacity, model_width + CODE_LAN...]
    ppermute x1, starting transfers between devices: 7.01 us -> 13.3 us  [local(): lax.ppermute(pack(left_owner), 'batch', [(i, (i - 1) % owners) for i in r...]
    ppermute x4, starting transfers between devices: 12.4 us -> 15.7 us  [section_sum(): other = lax.ppermute(total, 'section', route)]
    all_to_all x1, waiting for transfers between devices: 0.01 us -> 3.17 us  [local(): lax.all_to_all(send_rows.reshape(owners, capacity, model_width + CODE_LAN...]
    unnamed x49, local copies, waits for them, and re-layouts: 8.12 us -> 6.07 us
    reduce_sum x2, other arithmetic: 1.1 us -> 2.63 us  [pick(): jnp.sum(jnp.where(chosen.reshape(shape), rows, jnp.zeros((), rows.dtype))...]
    ppermute x1, starting transfers between devices: 3.97 us -> 5.47 us  [local(): lax.ppermute(pack(right_owner), 'batch', [(i, (i + 1) % owners) for i in...]
    ppermute x4, waiting for transfers between devices: 6.01 us -> 4.91 us  [section_sum(): other = lax.ppermute(total, 'section', route)]
  transfers between devices with their start and end apart: 7 -> 7, of which waited for: 3 -> 4; matrix products, arithmetic and copies ran while one was open for 11% -> 11% of each run, Pallas kernels for 4% -> 4%
where the time goes in v7:
time: 89.1 us; the launch traced here: 88.3 us
  starting transfers between devices  43.3 us (49%)
  local copies, waits for them, and re-layouts  11.7 us (13%)
  other arithmetic  10.5 us (12%)
  waiting for transfers between devices  8.09 us (9%)
  matrix products  7.24 us (8%)
  between operations  3.99 us (4%)
  Pallas kernels  3.5 us (4%)
    ppermute x4, starting transfers between devices, section_sum(): other = lax.ppermute(total, 'section', route)  15.7 us
    ppermute x1, starting transfers between devices, local(): lax.ppermute(pack(left_owner), 'batch', [(i, (i - 1) % owners) for i in r...  13.3 us
    all_to_all x1, starting transfers between devices, local(): lax.all_to_all(send_rows.reshape(owners, capacity, model_width + CODE_LAN...  8.82 us
    unnamed x49, local copies, waits for them, and re-layouts  6.07 us
    ppermute x1, starting transfers between devices, local(): lax.ppermute(pack(right_owner), 'batch', [(i, (i + 1) % owners) for i in...  5.47 us
    ppermute x4, waiting for transfers between devices, section_sum(): other = lax.ppermute(total, 'section', route)  4.91 us
    pallas_call x1, Pallas kernels, route_caches(): pl.pallas_call(cache_kernel, out_shape=(shape, shape), in_specs=[smem] *...  3.5 us
    all_to_all x1, waiting for transfers between devices, local(): lax.all_to_all(send_rows.reshape(owners, capacity, model_width + CODE_LAN...  3.17 us
  transfers between devices with their start and end apart: 7, of which 4 were waited for; matrix products, arithmetic and copies ran while one was open for 11% of the time, Pallas kernels for 4%

profile of v7, /device:TPU:1, one launch (start us, length us, event | category | flops | bytes accessed | tf_op | source)
XLA Modules:
  0.0 88.3 jit_solution(12580575793980630404)
XLA Ops:
  0.7 0.7 copy-done.20
  1.4 0.6 select_reduce_fusion.13
  2.8 2.5 %select_reduce_fusion.3 = (bf16[128,128]{1,0:T(8,128)(2,1)S(1)}, bf16[128,128]{1,0:T(8,128)(2,1)S(1)}, bf16[128,128]{1,0:T(8,128)(2,1)S(1)}, bf16[128,128]{1,0:T(8,128)(2,1)S(1)}) fusion(bf16[32,128,128]{2,1,0:T(8,128)(2,1)} %keys_ref.1, pred[32]{0:T(512)(128)(4,1)S(1)} %get-tuple-element.54, pred[32]{0:T(512)(128)(4,1)S(1)} %get-tuple-element.53, ...), kind=kLoop, calls=%fused_computation.36 | loop fusion | flops 4128768 | bytes 2228288 | tf_op jit(solution)/shard_map/reduce_sum | solution.py:191
  5.4 5.5 %collective-permute-start.1 = (bf16[272,128]{1,0:T(8,128)(2,1)S(1)}, bf16[272,128]{1,0:T(8,128)(2,1)S(1)}, u32[]{:S(2)}, u32[]{:S(2)}) collective-permute-start(bf16[272,128]{1,0:T(8,128)(2,1)S(1)} %concatenate.11), channel_id=1, source_target_pairs={{0,1},{1,2},{2,3},{3,4},{4,5},{5,6},{6,7},{7,8},{8,9},{9,10},{10,1... | collective-permute-start | bytes 208904 | tf_op jit(solution)/shard_map/ppermute | solution.py:210
  11.7 13.3 %collective-permute-start = (bf16[272,128]{1,0:T(8,128)(2,1)S(1)}, bf16[272,128]{1,0:T(8,128)(2,1)S(1)}, u32[]{:S(2)}, u32[]{:S(2)}) collective-permute-start(bf16[272,128]{1,0:T(8,128)(2,1)S(1)} %concatenate.10), channel_id=1, source_target_pairs={{0,127},{1,0},{2,1},{3,2},{4,3},{5,4},{6,5},{7,6},{8,7},{9,8},{10,... | collective-permute-start | bytes 208904 | tf_op jit(solution)/shard_map/ppermute | solution.py:213
  25.5 0.8 reshape.502
  26.3 8.8 %all-to-all-start = ((bf16[128,2,640]{2,1,0:T(2,128)(2,1)}), bf16[128,2,640]{2,1,0:T(2,128)(2,1)S(1)}, u32[]{:S(2)}, u32[]{:S(2)}) async-start(bf16[128,2,640]{2,1,0:T(2,128)(2,1)} %reshape.502), calls=%async_computation | async-start | bytes 655360 | tf_op jit(solution)/shard_map/all_to_all | solution.py:233
  35.2 0.6 copy-done.19
  35.8 0.7 select_reduce_fusion.9
  36.7 0.6 copy-done.16
  37.9 0.5 slice.129
  39.1 0.5 slice.127
  40.3 0.6 select_select_fusion.3.take_ref
  41.4 3.5 %shard_map.218 = (bf16[32,128,128]{2,1,0:T(8,128)(2,1)}, bf16[32,128,128]{2,1,0:T(8,128)(2,1)}) custom-call(s32[32]{0:T(128)} %get-tuple-element.41.src_ref, s32[32]{0:T(128)} %select_select_fusion.3.take_ref, bf16[32,128,128]{2,1,0:T(8,128)(2,1)} %keys_ref.1, bf16[32,128,128]{2,1,0:T(8,128)(2,1)} %values_ref.1, bf16[272,128]{1,0:T(8,128)(2,1)} %copy-done.7, ...), custom_call_target="tpu_custom_call" | custom-call | bytes 4194304 | tf_op jit(solution)/shard_map/pallas_call | solution.py:136
  44.9 0.8 slice_bitcast_fusion.10
  45.7 0.8 slice_bitcast_fusion.4
  46.5 3.2 %all-to-all-done = bf16[128,2,640]{2,1,0:T(2,128)(2,1)S(1)} async-done(((bf16[128,2,640]{2,1,0:T(2,128)(2,1)}), bf16[128,2,640]{2,1,0:T(2,128)(2,1)S(1)}, u32[]{:S(2)}, u32[]{:S(2)}) %all-to-all-start) | async-done | bytes 327712 | tf_op jit(solution)/shard_map/all_to_all | solution.py:233
  51.1 0.6 copy-done.17
  54.0 0.7 fusion.202
  57.3 0.7 copy-done.10
  58.1 2.8 %collective-permute-start.2 = (bf16[64,512]{1,0:T(8,128)(2,1)S(1)}, bf16[64,512]{1,0:T(8,128)(2,1)S(1)}, u32[]{:S(2)}, u32[]{:S(2)}) collective-permute-start(bf16[64,512]{1,0:T(8,128)(2,1)S(1)} %convolution_convert_fusion.2), channel_id=1, source_target_pairs={{0,256},{128,384},{256,0},{384,128},{1,257},{129,385},{257,1},{385... | collective-permute-start | bytes 196616 | tf_op jit(solution)/shard_map/ppermute | solution.py:101
  61.2 1.9 %collective-permute-done.2 = bf16[64,512]{1,0:T(8,128)(2,1)S(1)} collective-permute-done((bf16[64,512]{1,0:T(8,128)(2,1)S(1)}, bf16[64,512]{1,0:T(8,128)(2,1)S(1)}, u32[]{:S(2)}, u32[]{:S(2)}) %collective-permute-start.2) | collective-permute-done | bytes 65568 | tf_op jit(solution)/shard_map/ppermute | solution.py:101
  63.2 6.8 %collective-permute-start.3 = (f32[64,512]{1,0:T(8,128)S(1)}, f32[64,512]{1,0:T(8,128)S(1)}, u32[]{:S(2)}, u32[]{:S(2)}) collective-permute-start(f32[64,512]{1,0:T(8,128)S(1)} %convert_add_fusion.1), channel_id=1, source_target_pairs={{0,128},{128,0},{256,384},{384,256},{1,129},{129,1},{257,385},{385... | collective-permute-start | bytes 393224 | tf_op jit(solution)/shard_map/ppermute | solution.py:101
  70.0 0.9 %collective-permute-done.3 = f32[64,512]{1,0:T(8,128)S(1)} collective-permute-done((f32[64,512]{1,0:T(8,128)S(1)}, f32[64,512]{1,0:T(8,128)S(1)}, u32[]{:S(2)}, u32[]{:S(2)}) %collective-permute-start.3) | collective-permute-done | bytes 131104 | tf_op jit(solution)/shard_map/ppermute | solution.py:101
  71.8 1.9 %convolution_convert_fusion.1 = bf16[64,512]{1,0:T(8,128)(2,1)S(1)} fusion(bf16[512,512]{1,0:T(8,128)(2,1)S(1)} %copy-done, bf16[512,512]{1,0:T(8,128)(2,1)} %param.33, f32[64,512]{1,0:T(8,128)S(1)} %get-tuple-element.46, f32[512]{0:T(512)S(1)} %copy-done.22, f32[64]{0:T(128)S(1)} %add_rsqrt_fusion.1, f32[64]{0:T(128)S(1)} %broadcast_multiply_fusion.1), kind=kOutput, calls=%fused_computation.4 | convolution fusion | flops 69402624 | bytes 1247744 | tf_op jit(solution)/shard_map/dot_general | solution.py:330
  73.6 2.8 %collective-permute-start.4 = (bf16[64,512]{1,0:T(8,128)(2,1)S(1)}, bf16[64,512]{1,0:T(8,128)(2,1)S(1)}, u32[]{:S(2)}, u32[]{:S(2)}) collective-permute-start(bf16[64,512]{1,0:T(8,128)(2,1)S(1)} %convolution_convert_fusion.1), channel_id=1, source_target_pairs={{0,256},{128,384},{256,0},{384,128},{1,257},{129,385},{257,1},{385... | collective-permute-start | bytes 196616 | tf_op jit(solution)/shard_map/ppermute | solution.py:101
  76.6 2.1 %collective-permute-done.4 = bf16[64,512]{1,0:T(8,128)(2,1)S(1)} collective-permute-done((bf16[64,512]{1,0:T(8,128)(2,1)S(1)}, bf16[64,512]{1,0:T(8,128)(2,1)S(1)}, u32[]{:S(2)}, u32[]{:S(2)}) %collective-permute-start.4) | collective-permute-done | bytes 65568 | tf_op jit(solution)/shard_map/ppermute | solution.py:101
  78.6 3.4 %collective-permute-start.5 = (f32[64,512]{1,0:T(8,128)S(1)}, f32[64,512]{1,0:T(8,128)S(1)}, u32[]{:S(2)}, u32[]{:S(2)}) collective-permute-start(f32[64,512]{1,0:T(8,128)S(1)} %convert_add_fusion), channel_id=1, source_target_pairs={{0,128},{128,0},{256,384},{384,256},{1,129},{129,1},{257,385},{385... | collective-permute-start | bytes 393224 | tf_op jit(solution)/shard_map/ppermute | solution.py:101
  82.1 2.6 %select_select_fusion = (bf16[32,128,128]{2,1,0:T(8,128)(2,1)}, bf16[32,128,128]{2,1,0:T(8,128)(2,1)}) fusion(bf16[32,128,128]{2,1,0:T(8,128)(2,1)S(1)} %copy-done.5, pred[32,128]{1,0:T(8,128)(4,1)S(1)} %get-tuple-element.105, pred[32,128]{1,0:T(8,128)(4,1)S(1)} %get-tuple-element.106, bf16[32,128]{1,0:T(8,128)(2,1)S(1)} %get-tuple-element.80, ...), kind=kLoop, calls=%fused_computation.31 | loop fusion | flops 2097152 | bytes 4235264 | tf_op jit(solution)/shard_map/jit(_where)/select_n | solution.py:352
  85.0 0.6 slice_bitcast_fusion
  86.3 0.7 copy-done.21
  87.5 0.8 copy.133
  (155 shorter events, 11.1 us)
Async XLA Ops:
  0.6 70.6 %copy-start = (bf16[512,512]{1,0:T(8,128)(2,1)S(1)}, bf16[512,512]{1,0:T(8,128)(2,1)}, u32[]{:S(2)}) copy-start(bf16[512,512]{1,0:T(8,128)(2,1)} %param.34) | copy-start | bytes 1572868
  0.6 0.7 copy-start.20
  0.7 2.0 %copy-start.14 = (bf16[32,512]{1,0:T(8,128)(2,1)S(1)}, bf16[32,512]{1,0:T(8,128)(2,1)}, u32[]{:S(2)}) copy-start(bf16[32,512]{1,0:T(8,128)(2,1)} %param.24) | copy-start | bytes 98308
  0.7 2.0 %copy-start.13 = (bf16[32,512]{1,0:T(8,128)(2,1)S(1)}, bf16[32,512]{1,0:T(8,128)(2,1)}, u32[]{:S(2)}) copy-start(bf16[32,512]{1,0:T(8,128)(2,1)} %param.23) | copy-start | bytes 98308
  5.4 32.4 %collective-permute-start.1 = (bf16[272,128]{1,0:T(8,128)(2,1)S(1)}, bf16[272,128]{1,0:T(8,128)(2,1)S(1)}, u32[]{:S(2)}, u32[]{:S(2)}) collective-permute-start(bf16[272,128]{1,0:T(8,128)(2,1)S(1)} %concatenate.11), channel_id=1, source_target_pairs={{0,1},{1,2},{2,3},{3,4},{4,5},{5,6},{6,7},{7,8},{8,9},{9,10},{10,1... | collective-permute-start | bytes 208904 | tf_op jit(solution)/shard_map/ppermute | solution.py:210
  11.6 13.4 %copy-start.23 = (s32[32]{0:T(128)S(1)}, s32[32]{0:T(128)}, u32[]{:S(2)}) copy-start(s32[32]{0:T(128)} %param.20) | copy-start | bytes 388
  11.6 13.7 %copy-start.11 = (bf16[32,512]{1,0:T(8,128)(2,1)S(1)}, bf16[32,512]{1,0:T(8,128)(2,1)}, u32[]{:S(2)}) copy-start(bf16[32,512]{1,0:T(8,128)(2,1)} %param.19) | copy-start | bytes 98308
  11.7 27.4 %collective-permute-start = (bf16[272,128]{1,0:T(8,128)(2,1)S(1)}, bf16[272,128]{1,0:T(8,128)(2,1)S(1)}, u32[]{:S(2)}, u32[]{:S(2)}) collective-permute-start(bf16[272,128]{1,0:T(8,128)(2,1)S(1)} %concatenate.10), channel_id=1, source_target_pairs={{0,127},{1,0},{2,1},{3,2},{4,3},{5,4},{6,5},{7,6},{8,7},{9,8},{10,... | collective-permute-start | bytes 208904 | tf_op jit(solution)/shard_map/ppermute | solution.py:213
  26.3 23.3 %all-to-all-start = ((bf16[128,2,640]{2,1,0:T(2,128)(2,1)}), bf16[128,2,640]{2,1,0:T(2,128)(2,1)S(1)}, u32[]{:S(2)}, u32[]{:S(2)}) async-start(bf16[128,2,640]{2,1,0:T(2,128)(2,1)} %reshape.502), calls=%async_computation | async-start | bytes 655360 | tf_op jit(solution)/shard_map/all_to_all | solution.py:233
  35.2 0.7 copy-start.19
  36.6 0.7 copy-start.16
  37.9 3.5 %copy-start.7 = (bf16[272,128]{1,0:T(8,128)(2,1)}, bf16[272,128]{1,0:T(8,128)(2,1)S(1)}, u32[]{:S(2)}) copy-start(bf16[272,128]{1,0:T(8,128)(2,1)S(1)} %collective-permute-done.1.lbox_ref) | copy-start | bytes 208900
  39.1 2.3 %copy-start.8 = (bf16[272,128]{1,0:T(8,128)(2,1)}, bf16[272,128]{1,0:T(8,128)(2,1)S(1)}, u32[]{:S(2)}) copy-start(bf16[272,128]{1,0:T(8,128)(2,1)S(1)} %collective-permute-done.rbox_ref) | copy-start | bytes 208900
  44.9 1.6 %copy-start.9 = (bf16[272,128]{1,0:T(8,128)(2,1)S(1)}, bf16[272,128]{1,0:T(8,128)(2,1)}, u32[]{:S(2)}) copy-start(bf16[272,128]{1,0:T(8,128)(2,1)} %copy-done.8) | copy-start | bytes 208900
  50.0 0.6 copy-start.12
  50.0 1.0 %copy-start.6 = (bf16[3,512,128]{2,1,0:T(8,128)(2,1)S(1)}, bf16[3,512,128]{2,1,0:T(8,128)(2,1)}, u32[]{:S(2)}) copy-start(bf16[3,512,128]{2,1,0:T(8,128)(2,1)} %param.29) | copy-start | bytes 1179652
  50.9 0.7 copy-start.17
  51.9 2.0 %copy-start.1 = (bf16[32,128,128]{2,1,0:T(8,128)(2,1)S(1)}, bf16[32,128,128]{2,1,0:T(8,128)(2,1)}, u32[]{:S(2)}) copy-start(bf16[32,128,128]{2,1,0:T(8,128)(2,1)} %keys_ref.1) | copy-start | bytes 3145732
  53.2 1.9 %copy-start.2 = (bf16[32,128,128]{2,1,0:T(8,128)(2,1)S(1)}, bf16[32,128,128]{2,1,0:T(8,128)(2,1)}, u32[]{:S(2)}) copy-start(bf16[32,128,128]{2,1,0:T(8,128)(2,1)} %values_ref.1) | copy-start | bytes 3145732
  57.1 0.9 %copy-start.10 = (bf16[128,512]{1,0:T(8,128)(2,1)S(1)}, bf16[128,512]{1,0:T(8,128)(2,1)}, u32[]{:S(2)}) copy-start(bf16[128,512]{1,0:T(8,128)(2,1)} %param.30) | copy-start | bytes 393220
  58.1 5.0 %collective-permute-start.2 = (bf16[64,512]{1,0:T(8,128)(2,1)S(1)}, bf16[64,512]{1,0:T(8,128)(2,1)S(1)}, u32[]{:S(2)}, u32[]{:S(2)}) collective-permute-start(bf16[64,512]{1,0:T(8,128)(2,1)S(1)} %convolution_convert_fusion.2), channel_id=1, source_target_pairs={{0,256},{128,384},{256,0},{384,128},{1,257},{129,385},{257,1},{385... | collective-permute-start | bytes 196616 | tf_op jit(solution)/shard_map/ppermute | solution.py:101
  63.2 7.8 %copy-start.15 = (f32[512]{0:T(512)S(1)}, f32[512]{0:T(512)}, u32[]{:S(2)}) copy-start(f32[512]{0:T(512)} %param.31) | copy-start | bytes 6148
  63.2 7.8 %collective-permute-start.3 = (f32[64,512]{1,0:T(8,128)S(1)}, f32[64,512]{1,0:T(8,128)S(1)}, u32[]{:S(2)}, u32[]{:S(2)}) collective-permute-start(f32[64,512]{1,0:T(8,128)S(1)} %convert_add_fusion.1), channel_id=1, source_target_pairs={{0,128},{128,0},{256,384},{384,256},{1,129},{129,1},{257,385},{385... | collective-permute-start | bytes 393224 | tf_op jit(solution)/shard_map/ppermute | solution.py:101
  71.1 0.7 copy-start.22
  71.7 10.3 %copy-start.4 = (bf16[32,128,128]{2,1,0:T(8,128)(2,1)S(1)}, bf16[32,128,128]{2,1,0:T(8,128)(2,1)}, u32[]{:S(2)}) copy-start(bf16[32,128,128]{2,1,0:T(8,128)(2,1)} %get-tuple-element.7) | copy-start | bytes 3145732
  71.8 10.3 %copy-start.5 = (bf16[32,128,128]{2,1,0:T(8,128)(2,1)S(1)}, bf16[32,128,128]{2,1,0:T(8,128)(2,1)}, u32[]{:S(2)}) copy-start(bf16[32,128,128]{2,1,0:T(8,128)(2,1)} %get-tuple-element.8) | copy-start | bytes 3145732
  73.6 5.0 %collective-permute-start.4 = (bf16[64,512]{1,0:T(8,128)(2,1)S(1)}, bf16[64,512]{1,0:T(8,128)(2,1)S(1)}, u32[]{:S(2)}, u32[]{:S(2)}) collective-permute-start(bf16[64,512]{1,0:T(8,128)(2,1)S(1)} %convolution_convert_fusion.1), channel_id=1, source_target_pairs={{0,256},{128,384},{256,0},{384,128},{1,257},{129,385},{257,1},{385... | collective-permute-start | bytes 196616 | tf_op jit(solution)/shard_map/ppermute | solution.py:101
  78.6 6.2 %collective-permute-start.5 = (f32[64,512]{1,0:T(8,128)S(1)}, f32[64,512]{1,0:T(8,128)S(1)}, u32[]{:S(2)}, u32[]{:S(2)}) collective-permute-start(f32[64,512]{1,0:T(8,128)S(1)} %convert_add_fusion), channel_id=1, source_target_pairs={{0,128},{128,0},{256,384},{384,256},{1,129},{129,1},{257,385},{385... | collective-permute-start | bytes 393224 | tf_op jit(solution)/shard_map/ppermute | solution.py:101
  82.1 2.8 %copy-start.18 = (f32[512]{0:T(512)S(1)}, f32[512]{0:T(512)}, u32[]{:S(2)}) copy-start(f32[512]{0:T(512)} %param.35) | copy-start | bytes 6148
  84.7 1.2 %copy-start.3 = (bf16[16,64,512]{2,1,0:T(8,128)(2,1)S(1)}, bf16[16,64,512]{2,1,0:T(8,128)(2,1)}, u32[]{:S(2)}) copy-start(bf16[16,64,512]{2,1,0:T(8,128)(2,1)} %param.36) | copy-start | bytes 3145732
  86.3 0.7 copy-start.21

commit v8 on v7

--- a/solution.py
+++ b/solution.py
@@ -176,46 +176,6 @@
     capacity = max(CAP, streams // owners)
     slot_ids = jnp.arange(streams, dtype=jnp.int32)
 
-    dest_owner = cache_slot // streams
-    dest_local = cache_slot % streams
-    right_owner = jnp.mod(own_index + 1, owners)
-    left_owner = jnp.mod(own_index + owners - 1, owners)
-    state_rows = model_width // head_share
-
-    def pack(direction_owner):
-        chosen = dest_owner == direction_owner
-        code = jnp.sum(jnp.where(chosen, dest_local + 1, 0))
-
-        def pick(rows):
-            shape = (streams,) + (1,) * (rows.ndim - 1)
-            return jnp.sum(jnp.where(chosen.reshape(shape), rows, jnp.zeros((), rows.dtype)), axis=0)
-
-        pieces = [
-            pick(cache_keys),
-            pick(cache_values),
-            pick(up_state).reshape(state_rows, head_share),
-            pick(conv_state).reshape(state_rows, head_share),
-            jnp.full((8, head_share), code, jnp.int32).astype(jnp.bfloat16),
-        ]
-        return jnp.concatenate(pieces, axis=0)
-
-    def unpack(box):
-        keys = box[:window]
-        values = box[window : 2 * window]
-        up = box[2 * window : 2 * window + state_rows].reshape(model_width)
-        conv = box[2 * window + state_rows : 2 * window + 2 * state_rows].reshape(model_width)
-        code = box[2 * window + 2 * state_rows, 0].astype(jnp.int32) - 1
-        return keys, values, up, conv, code
-
-    left_box = lax.ppermute(
-        pack(right_owner), "batch", [(i, (i + 1) % owners) for i in range(owners)]
-    )
-    right_box = lax.ppermute(
-        pack(left_owner), "batch", [(i, (i - 1) % owners) for i in range(owners)]
-    )
-    from_left = unpack(left_box)
-    from_right = unpack(right_box)
-
     target = token_slot // streams
     landing = token_slot % streams
     same_before = (target[None, :] == target[:, None]) & (slot_ids[None, :] < slot_ids[:, None])
@@ -237,10 +197,56 @@
         concat_axis=0,
         tiled=True,
     ).reshape(owners * capacity, model_width + CODE_LANES)
+
+    got, cache_keys, cache_values, up_state, conv_state, cache_slot = lax.optimization_barrier(
+        (got, cache_keys, cache_values, up_state, conv_state, cache_slot)
+    )
+
     got_codes = got[:, model_width].astype(jnp.int32) - 1
     arrived = jnp.dot(
         one_hot(slot_ids, got_codes), got[:, :model_width], preferred_element_type=jnp.float32
     ).astype(jnp.bfloat16)
+
+    dest_owner = cache_slot // streams
+    dest_local = cache_slot % streams
+    right_owner = jnp.mod(own_index + 1, owners)
+    left_owner = jnp.mod(own_index + owners - 1, owners)
+    state_rows = model_width // head_share
+
+    def pack(direction_owner):
+        chosen = dest_owner == direction_owner
+        code = jnp.sum(jnp.where(chosen, dest_local + 1, 0))
+
+        def pick(rows):
+            shape = (streams,) + (1,) * (rows.ndim - 1)
+            return jnp.sum(jnp.where(chosen.reshape(shape), rows, jnp.zeros((), rows.dtype)), axis=0)
+
+        pieces = [
+            pick(cache_keys),
+            pick(cache_values),
+            pick(up_state).reshape(state_rows, head_share),
+            pick(conv_state).reshape(state_rows, head_share),
+            jnp.full((8, head_share), code, jnp.int32).astype(jnp.bfloat16),
+        ]
+        return jnp.concatenate(pieces, axis=0)
+
+    def unpack(box):
+        keys = box[:window]
+        values = box[window : 2 * window]
+        up = box[2 * window : 2 * window + state_rows].reshape(model_width)
+        conv = box[2 * window + state_rows : 2 * window + 2 * state_rows].reshape(model_width)
+        code = box[2 * window + 2 * state_rows, 0].astype(jnp.int32) - 1
+        return keys, values, up, conv, code
+
+    left_box = lax.ppermute(
+        pack(right_owner), "batch", [(i, (i + 1) % owners) for i in range(owners)]
+    )
+    right_box = lax.ppermute(
+        pack(left_owner), "batch", [(i, (i - 1) % owners) for i in range(owners)]
+    )
+    from_left = unpack(left_box)
+    from_right = unpack(right_box)
+
 
     staying = dest_owner == own_index
     source_of = (dest_local[None, :] == slot_ids[:, None]) & staying[None, :]

time: 89.1 us -> 102 us (1.14)
  waiting for transfers between devices: 8.09 us -> 17.1 us
  starting transfers between devices: 43.3 us -> 46.6 us
  other arithmetic: 10.5 us -> 12.5 us
  local copies, waits for them, and re-layouts: 11.7 us -> 10.2 us
    all_to_all x1, starting transfers between devices: 8.82 us -> 20.9 us  [local(): lax.all_to_all(send_rows.reshape(owners, capacity, model_width + CODE_LAN...]
    all_to_all x1, waiting for transfers between devices: 3.17 us -> 13.7 us  [local(): lax.all_to_all(send_rows.reshape(owners, capacity, model_width + CODE_LAN...]
    ppermute x1, starting transfers between devices: 13.3 us -> 7.82 us  [local(): lax.ppermute(pack(left_owner), 'batch', [(i, (i - 1) % owners) for i in r...]
    ppermute x1, starting transfers between devices: 5.47 us -> 3.29 us  [local(): lax.ppermute(pack(right_owner), 'batch', [(i, (i + 1) % owners) for i in...]
    select_n x1, other arithmetic: 2.63 us -> 4.37 us  [local(): jnp.where(hit_second, fresh_values[:, 1][:, None, :], jnp.where(hit_first...]
    unnamed x49 -> x59, local copies, waits for them, and re-layouts: 6.07 us -> 4.4 us
    ppermute x4, waiting for transfers between devices: 4.91 us -> 3.32 us  [section_sum(): other = lax.ppermute(total, 'section', route)]
    reduce_sum x2, other arithmetic: 2.63 us -> 1.08 us  [pick(): jnp.sum(jnp.where(chosen.reshape(shape), rows, jnp.zeros((), rows.dtype))...]
  transfers between devices with their start and end apart: 7 -> 7, of which waited for: 4 -> 3; matrix products, arithmetic and copies ran while one was open for 11% -> 7% of each run, Pallas kernels for 4% -> 3%
where the time goes in v8:
time: 102 us; the launch traced here: 101 us
  starting transfers between devices  46.6 us (46%)
  waiting for transfers between devices  17.1 us (17%)
  other arithmetic  12.5 us (12%)
  local copies, waits for them, and re-layouts  10.2 us (10%)
  matrix products  6.8 us (7%)
  between operations  4.11 us (4%)
  Pallas kernels  3.49 us (3%)
    all_to_all x1, starting transfers between devices, local(): lax.all_to_all(send_rows.reshape(owners, capacity, model_width + CODE_LAN...  20.9 us
    ppermute x4, starting transfers between devices, section_sum(): other = lax.ppermute(total, 'section', route)  14.6 us
    all_to_all x1, waiting for transfers between devices, local(): lax.all_to_all(send_rows.reshape(owners, capacity, model_width + CODE_LAN...  13.7 us
    ppermute x1, starting transfers between devices, local(): lax.ppermute(pack(left_owner), 'batch', [(i, (i - 1) % owners) for i in r...  7.82 us
    unnamed x59, local copies, waits for them, and re-layouts  4.4 us
    select_n x1, other arithmetic, local(): jnp.where(hit_second, fresh_values[:, 1][:, None, :], jnp.where(hit_first...  4.37 us
    pallas_call x1, Pallas kernels, route_caches(): pl.pallas_call(cache_kernel, out_shape=(shape, shape), in_specs=[smem] *...  3.49 us
    ppermute x4, waiting for transfers between devices, section_sum(): other = lax.ppermute(total, 'section', route)  3.32 us
  transfers between devices with their start and end apart: 7, of which 3 were waited for; matrix products, arithmetic and copies ran while one was open for 7% of the time, Pallas kernels for 3%

profile of v8, /device:TPU:1, one launch (start us, length us, event | category | flops | bytes accessed | tf_op | source)
XLA Modules:
  0.0 100.8 jit_solution(7831609098012740358)
XLA Ops:
  0.6 0.7 fusion.144
  1.6 1.0 convolution_convert_fusion
  2.7 0.8 reshape.502
  3.5 20.9 %all-to-all-start = ((bf16[128,2,640]{2,1,0:T(2,128)(2,1)}), bf16[128,2,640]{2,1,0:T(2,128)(2,1)S(1)}, u32[]{:S(2)}, u32[]{:S(2)}) async-start(bf16[128,2,640]{2,1,0:T(2,128)(2,1)} %reshape.502), calls=%async_computation | async-start | bytes 655360 | tf_op jit(solution)/shard_map/all_to_all | solution.py:193
  24.7 0.6 broadcast_in_dim.445
  25.6 13.7 %all-to-all-done = bf16[128,2,640]{2,1,0:T(2,128)(2,1)S(1)} async-done(((bf16[128,2,640]{2,1,0:T(2,128)(2,1)}), bf16[128,2,640]{2,1,0:T(2,128)(2,1)S(1)}, u32[]{:S(2)}, u32[]{:S(2)}) %all-to-all-start) | async-done | bytes 327712 | tf_op jit(solution)/shard_map/all_to_all | solution.py:193
  39.5 0.6 select_reduce_fusion.13
  40.2 0.6 select_reduce_fusion.9
  42.8 1.0 select_reduce_fusion.3
  43.8 3.3 %collective-permute-start.1 = (bf16[272,128]{1,0:T(8,128)(2,1)S(1)}, bf16[272,128]{1,0:T(8,128)(2,1)S(1)}, u32[]{:S(2)}, u32[]{:S(2)}) collective-permute-start(bf16[272,128]{1,0:T(8,128)(2,1)S(1)} %concatenate.11), channel_id=1, source_target_pairs={{0,1},{1,2},{2,3},{3,4},{4,5},{5,6},{6,7},{7,8},{8,9},{9,10},{10,1... | collective-permute-start | bytes 208904 | tf_op jit(solution)/shard_map/ppermute | solution.py:241
  47.2 7.8 %collective-permute-start = (bf16[272,128]{1,0:T(8,128)(2,1)S(1)}, bf16[272,128]{1,0:T(8,128)(2,1)S(1)}, u32[]{:S(2)}, u32[]{:S(2)}) collective-permute-start(bf16[272,128]{1,0:T(8,128)(2,1)S(1)} %concatenate.10), channel_id=1, source_target_pairs={{0,127},{1,0},{2,1},{3,2},{4,3},{5,4},{6,5},{7,6},{8,7},{9,8},{10,... | collective-permute-start | bytes 208904 | tf_op jit(solution)/shard_map/ppermute | solution.py:244
  57.8 0.6 broadcast_compare_fusion.1
  58.5 0.6 add_add_fusion
  59.1 0.6 slice_bitcast_fusion.9
  59.7 0.5 slice_bitcast_fusion.10
  60.7 0.7 copy-done.13
  63.6 0.7 copy-done.21
  64.3 0.7 fusion.202
  68.0 0.7 copy-done.7
  68.8 2.2 %collective-permute-start.2 = (bf16[64,512]{1,0:T(8,128)(2,1)S(1)}, bf16[64,512]{1,0:T(8,128)(2,1)S(1)}, u32[]{:S(2)}, u32[]{:S(2)}) collective-permute-start(bf16[64,512]{1,0:T(8,128)(2,1)S(1)} %convolution_convert_fusion.2), channel_id=1, source_target_pairs={{0,256},{128,384},{256,0},{384,128},{1,257},{129,385},{257,1},{385... | collective-permute-start | bytes 196616 | tf_op jit(solution)/shard_map/ppermute | solution.py:101
  71.4 2.4 %collective-permute-done.2 = bf16[64,512]{1,0:T(8,128)(2,1)S(1)} collective-permute-done((bf16[64,512]{1,0:T(8,128)(2,1)S(1)}, bf16[64,512]{1,0:T(8,128)(2,1)S(1)}, u32[]{:S(2)}, u32[]{:S(2)}) %collective-permute-start.2) | collective-permute-done | bytes 65568 | tf_op jit(solution)/shard_map/ppermute | solution.py:101
  73.8 7.6 %collective-permute-start.3 = (f32[64,512]{1,0:T(8,128)S(1)}, f32[64,512]{1,0:T(8,128)S(1)}, u32[]{:S(2)}, u32[]{:S(2)}) collective-permute-start(f32[64,512]{1,0:T(8,128)S(1)} %convert_add_fusion.1), channel_id=1, source_target_pairs={{0,128},{128,0},{256,384},{384,256},{1,129},{129,1},{257,385},{385... | collective-permute-start | bytes 393224 | tf_op jit(solution)/shard_map/ppermute | solution.py:101
  81.4 1.0 collective-permute-done.3
  83.2 0.7 convolution_convert_fusion.1
  83.9 2.2 %collective-permute-start.4 = (bf16[64,512]{1,0:T(8,128)(2,1)S(1)}, bf16[64,512]{1,0:T(8,128)(2,1)S(1)}, u32[]{:S(2)}, u32[]{:S(2)}) collective-permute-start(bf16[64,512]{1,0:T(8,128)(2,1)S(1)} %convolution_convert_fusion.1), channel_id=1, source_target_pairs={{0,256},{128,384},{256,0},{384,128},{1,257},{129,385},{257,1},{385... | collective-permute-start | bytes 196616 | tf_op jit(solution)/shard_map/ppermute | solution.py:101
  86.1 0.6 select_select_fusion.3.take_ref
  86.7 3.5 %shard_map.218 = (bf16[32,128,128]{2,1,0:T(8,128)(2,1)}, bf16[32,128,128]{2,1,0:T(8,128)(2,1)}) custom-call(s32[32]{0:T(128)} %get-tuple-element.53.src_ref, s32[32]{0:T(128)} %select_select_fusion.3.take_ref, bf16[32,128,128]{2,1,0:T(8,128)(2,1)} %keys_ref, bf16[32,128,128]{2,1,0:T(8,128)(2,1)} %values_ref, bf16[272,128]{1,0:T(8,128)(2,1)} %copy-done.5, ...), custom_call_target="tpu_custom_call" | custom-call | bytes 4194304 | tf_op jit(solution)/shard_map/pallas_call | solution.py:136
  90.2 2.6 %collective-permute-start.5 = (f32[64,512]{1,0:T(8,128)S(1)}, f32[64,512]{1,0:T(8,128)S(1)}, u32[]{:S(2)}, u32[]{:S(2)}) collective-permute-start(f32[64,512]{1,0:T(8,128)S(1)} %convert_add_fusion), channel_id=1, source_target_pairs={{0,128},{128,0},{256,384},{384,256},{1,129},{129,1},{257,385},{385... | collective-permute-start | bytes 393224 | tf_op jit(solution)/shard_map/ppermute | solution.py:101
  92.8 4.4 %select_select_fusion = (bf16[32,128,128]{2,1,0:T(8,128)(2,1)}, bf16[32,128,128]{2,1,0:T(8,128)(2,1)}) fusion(bf16[32,128,128]{2,1,0:T(8,128)(2,1)} %get-tuple-element.20, pred[32,128]{1,0:T(8,128)(4,1)S(1)} %get-tuple-element.117, pred[32,128]{1,0:T(8,128)(4,1)S(1)} %get-tuple-element.118, bf16[32,128]{1,0:T(8,128)(2,1)S(1)} %get-tuple-element.92, ...), kind=kLoop, calls=%fused_computation.31 | loop fusion | flops 2097152 | bytes 4235264 | tf_op jit(solution)/shard_map/jit(_where)/select_n | solution.py:358
  97.7 0.6 slice_bitcast_fusion
  98.8 0.7 copy-done.20
  100.0 0.8 copy.133
  (165 shorter events, 11.3 us)
Async XLA Ops:
  0.6 82.1 %copy-start = (bf16[512,512]{1,0:T(8,128)(2,1)S(1)}, bf16[512,512]{1,0:T(8,128)(2,1)}, u32[]{:S(2)}) copy-start(bf16[512,512]{1,0:T(8,128)(2,1)} %param.34) | copy-start | bytes 1572868
  2.6 22.7 %copy-start.15 = (s32[32]{0:T(128)S(1)}, s32[32]{0:T(128)}, u32[]{:S(2)}) copy-start(s32[32]{0:T(128)} %param.26) | copy-start | bytes 388
  2.6 22.8 %copy-start.12 = (f32[4,512]{1,0:T(4,128)S(1)}, f32[4,512]{1,0:T(4,128)}, u32[]{:S(2)}) copy-start(f32[4,512]{1,0:T(4,128)} %param.27) | copy-start | bytes 24580
  2.6 40.1 %copy-start.2 = (bf16[32,128,128]{2,1,0:T(8,128)(2,1)S(1)}, bf16[32,128,128]{2,1,0:T(8,128)(2,1)}, u32[]{:S(2)}) copy-start(bf16[32,128,128]{2,1,0:T(8,128)(2,1)} %values_ref) | copy-start | bytes 3145732
  3.5 39.3 %copy-start.1 = (bf16[32,128,128]{2,1,0:T(8,128)(2,1)S(1)}, bf16[32,128,128]{2,1,0:T(8,128)(2,1)}, u32[]{:S(2)}) copy-start(bf16[32,128,128]{2,1,0:T(8,128)(2,1)} %keys_ref) | copy-start | bytes 3145732
  3.5 35.9 %all-to-all-start = ((bf16[128,2,640]{2,1,0:T(2,128)(2,1)}), bf16[128,2,640]{2,1,0:T(2,128)(2,1)S(1)}, u32[]{:S(2)}, u32[]{:S(2)}) async-start(bf16[128,2,640]{2,1,0:T(2,128)(2,1)} %reshape.502), calls=%async_computation | async-start | bytes 655360 | tf_op jit(solution)/shard_map/all_to_all | solution.py:193
  25.6 13.9 %copy-start.16 = (s32[32]{0:T(128)S(1)}, s32[32]{0:T(128)}, u32[]{:S(2)}) copy-start(s32[32]{0:T(128)} %param.25) | copy-start | bytes 388
  41.1 1.5 %copy-start.9 = (bf16[32,512]{1,0:T(8,128)(2,1)S(1)}, bf16[32,512]{1,0:T(8,128)(2,1)}, u32[]{:S(2)}) copy-start(bf16[32,512]{1,0:T(8,128)(2,1)} %param.23) | copy-start | bytes 98308
  41.1 1.5 %copy-start.10 = (bf16[32,512]{1,0:T(8,128)(2,1)S(1)}, bf16[32,512]{1,0:T(8,128)(2,1)}, u32[]{:S(2)}) copy-start(bf16[32,512]{1,0:T(8,128)(2,1)} %param.24) | copy-start | bytes 98308
  41.3 18.9 %copy-start.8 = (bf16[32,512]{1,0:T(8,128)(2,1)}, bf16[32,512]{1,0:T(8,128)(2,1)S(1)}, u32[]{:S(2)}) copy-start(bf16[32,512]{1,0:T(8,128)(2,1)S(1)} %convolution_convert_fusion.5) | copy-start | bytes 98308
  43.8 11.3 %collective-permute-start.1 = (bf16[272,128]{1,0:T(8,128)(2,1)S(1)}, bf16[272,128]{1,0:T(8,128)(2,1)S(1)}, u32[]{:S(2)}, u32[]{:S(2)}) collective-permute-start(bf16[272,128]{1,0:T(8,128)(2,1)S(1)} %concatenate.11), channel_id=1, source_target_pairs={{0,1},{1,2},{2,3},{3,4},{4,5},{5,6},{6,7},{7,8},{8,9},{9,10},{10,1... | collective-permute-start | bytes 208904 | tf_op jit(solution)/shard_map/ppermute | solution.py:241
  47.2 13.4 %copy-start.4 = (bf16[3,512,128]{2,1,0:T(8,128)(2,1)S(1)}, bf16[3,512,128]{2,1,0:T(8,128)(2,1)}, u32[]{:S(2)}) copy-start(bf16[3,512,128]{2,1,0:T(8,128)(2,1)} %param.29) | copy-start | bytes 1179652
  47.2 9.2 %collective-permute-start = (bf16[272,128]{1,0:T(8,128)(2,1)S(1)}, bf16[272,128]{1,0:T(8,128)(2,1)S(1)}, u32[]{:S(2)}, u32[]{:S(2)}) collective-permute-start(bf16[272,128]{1,0:T(8,128)(2,1)S(1)} %concatenate.10), channel_id=1, source_target_pairs={{0,127},{1,0},{2,1},{3,2},{4,3},{5,4},{6,5},{7,6},{8,7},{9,8},{10,... | collective-permute-start | bytes 208904 | tf_op jit(solution)/shard_map/ppermute | solution.py:244
  55.1 11.2 %copy-start.5 = (bf16[272,128]{1,0:T(8,128)(2,1)}, bf16[272,128]{1,0:T(8,128)(2,1)S(1)}, u32[]{:S(2)}) copy-start(bf16[272,128]{1,0:T(8,128)(2,1)S(1)} %collective-permute-done.1.lbox_ref) | copy-start | bytes 208900
  56.4 3.9 %copy-start.25 = (pred[32]{0:T(512)(128)(4,1)}, pred[32]{0:T(512)(128)(4,1)S(1)}, u32[]{:S(2)}) copy-start(pred[32]{0:T(512)(128)(4,1)S(1)} %iota_compare_fusion.13) | copy-start | bytes 100
  56.4 9.9 %copy-start.6 = (bf16[272,128]{1,0:T(8,128)(2,1)}, bf16[272,128]{1,0:T(8,128)(2,1)S(1)}, u32[]{:S(2)}) copy-start(bf16[272,128]{1,0:T(8,128)(2,1)S(1)} %collective-permute-done.rbox_ref) | copy-start | bytes 208900
  57.6 2.6 %copy-start.27 = (pred[32]{0:T(512)(128)(4,1)}, pred[32]{0:T(512)(128)(4,1)S(1)}, u32[]{:S(2)}) copy-start(pred[32]{0:T(512)(128)(4,1)S(1)} %iota_compare_fusion.14) | copy-start | bytes 100
  60.6 0.7 copy-start.13
  67.7 0.9 copy-start.7
  68.8 5.0 %collective-permute-start.2 = (bf16[64,512]{1,0:T(8,128)(2,1)S(1)}, bf16[64,512]{1,0:T(8,128)(2,1)S(1)}, u32[]{:S(2)}, u32[]{:S(2)}) collective-permute-start(bf16[64,512]{1,0:T(8,128)(2,1)S(1)} %convolution_convert_fusion.2), channel_id=1, source_target_pairs={{0,256},{128,384},{256,0},{384,128},{1,257},{129,385},{257,1},{385... | collective-permute-start | bytes 196616 | tf_op jit(solution)/shard_map/ppermute | solution.py:101
  71.3 11.4 %copy-start.23 = (bf16[512,512]{1,0:T(8,128)(2,1)S(1)}, bf16[512,512]{1,0:T(8,128)(2,1)}, u32[]{:S(2)}) copy-start(bf16[512,512]{1,0:T(8,128)(2,1)} %param.33) | copy-start | bytes 1572868
  73.8 8.6 %copy-start.11 = (f32[512]{0:T(512)S(1)}, f32[512]{0:T(512)}, u32[]{:S(2)}) copy-start(f32[512]{0:T(512)} %param.31) | copy-start | bytes 6148
  73.8 8.5 %collective-permute-start.3 = (f32[64,512]{1,0:T(8,128)S(1)}, f32[64,512]{1,0:T(8,128)S(1)}, u32[]{:S(2)}, u32[]{:S(2)}) collective-permute-start(f32[64,512]{1,0:T(8,128)S(1)} %convert_add_fusion.1), channel_id=1, source_target_pairs={{0,128},{128,0},{256,384},{384,256},{1,129},{129,1},{257,385},{385... | collective-permute-start | bytes 393224 | tf_op jit(solution)/shard_map/ppermute | solution.py:101
  82.5 0.7 copy-start.24
  83.9 6.3 %collective-permute-start.4 = (bf16[64,512]{1,0:T(8,128)(2,1)S(1)}, bf16[64,512]{1,0:T(8,128)(2,1)S(1)}, u32[]{:S(2)}, u32[]{:S(2)}) collective-permute-start(bf16[64,512]{1,0:T(8,128)(2,1)S(1)} %convolution_convert_fusion.1), channel_id=1, source_target_pairs={{0,256},{128,384},{256,0},{384,128},{1,257},{129,385},{257,1},{385... | collective-permute-start | bytes 196616 | tf_op jit(solution)/shard_map/ppermute | solution.py:101
  90.2 7.2 %collective-permute-start.5 = (f32[64,512]{1,0:T(8,128)S(1)}, f32[64,512]{1,0:T(8,128)S(1)}, u32[]{:S(2)}, u32[]{:S(2)}) collective-permute-start(f32[64,512]{1,0:T(8,128)S(1)} %convert_add_fusion), channel_id=1, source_target_pairs={{0,128},{128,0},{256,384},{384,256},{1,129},{129,1},{257,385},{385... | collective-permute-start | bytes 393224 | tf_op jit(solution)/shard_map/ppermute | solution.py:101
  92.8 4.4 %copy-start.18 = (bf16[512]{0:T(512)(128)(2,1)S(1)}, bf16[512]{0:T(512)(128)(2,1)}, u32[]{:S(2)}) copy-start(bf16[512]{0:T(512)(128)(2,1)} %get-tuple-element.77) | copy-start | bytes 3076
  92.8 4.4 %copy-start.19 = (bf16[512]{0:T(512)(128)(2,1)S(1)}, bf16[512]{0:T(512)(128)(2,1)}, u32[]{:S(2)}) copy-start(bf16[512]{0:T(512)(128)(2,1)} %get-tuple-element.75) | copy-start | bytes 3076
  92.8 4.4 %copy-start.26 = (pred[32]{0:T(512)(128)(4,1)S(1)}, pred[32]{0:T(512)(128)(4,1)}, u32[]{:S(2)}) copy-start(pred[32]{0:T(512)(128)(4,1)} %copy-done.25) | copy-start | bytes 100
  92.8 4.4 %copy-start.28 = (pred[32]{0:T(512)(128)(4,1)S(1)}, pred[32]{0:T(512)(128)(4,1)}, u32[]{:S(2)}) copy-start(pred[32]{0:T(512)(128)(4,1)} %copy-done.27) | copy-start | bytes 100
  92.8 4.7 %copy-start.14 = (f32[512]{0:T(512)S(1)}, f32[512]{0:T(512)}, u32[]{:S(2)}) copy-start(f32[512]{0:T(512)} %param.35) | copy-start | bytes 6148
  97.2 1.2 %copy-start.3 = (bf16[16,64,512]{2,1,0:T(8,128)(2,1)S(1)}, bf16[16,64,512]{2,1,0:T(8,128)(2,1)}, u32[]{:S(2)}) copy-start(bf16[16,64,512]{2,1,0:T(8,128)(2,1)} %param.36) | copy-start | bytes 3145732
  (4 other events, 2.7 us)

commit v9 on v5

--- a/solution.py
+++ b/solution.py
@@ -220,6 +220,12 @@
     landing = token_slot % streams
     same_before = (target[None, :] == target[:, None]) & (slot_ids[None, :] < slot_ids[:, None])
     arrival_rank = jnp.sum(same_before.astype(jnp.int32), axis=1)
+    members = lax.axis_size("section")
+    member = lax.axis_index("section")
+    part = model_width // members
+    quarter = jnp.zeros((streams, part), latents.dtype)
+    for k in range(members):
+        quarter = jnp.where(member == k, latents[:, k * part : (k + 1) * part], quarter)
     owner_ids = jnp.arange(owners, dtype=jnp.int32)
     lane_ids = jnp.arange(CODE_LANES, dtype=jnp.int32)
     blocks = []
@@ -227,22 +233,36 @@
     for rank in range(capacity):
         chosen = (owner_ids[:, None] == target[None, :]) & (arrival_rank == rank)[None, :]
         blocks.append(
-            jnp.dot(chosen.astype(jnp.bfloat16), latents, preferred_element_type=jnp.float32)
+            jnp.dot(chosen.astype(jnp.bfloat16), quarter, preferred_element_type=jnp.float32)
         )
         code = jnp.sum(jnp.where(chosen, landing[None, :] + 1, 0), axis=1)
         code_block = jnp.where(lane_ids[None, :] == rank, code[:, None], code_block)
     blocks.append(code_block.astype(jnp.float32))
     send = jnp.concatenate(blocks, axis=1).astype(jnp.bfloat16)
     got = lax.all_to_all(send, "batch", split_axis=0, concat_axis=0, tiled=True)
-    arrived = jnp.zeros((streams, model_width), jnp.float32)
+    mine = jnp.zeros((streams, part), jnp.float32)
     for rank in range(capacity):
-        got_code = got[:, capacity * model_width + rank].astype(jnp.int32) - 1
-        arrived = arrived + jnp.dot(
+        got_code = got[:, capacity * part + rank].astype(jnp.int32) - 1
+        mine = mine + jnp.dot(
             one_hot(slot_ids, got_code),
-            got[:, rank * model_width : (rank + 1) * model_width],
+            got[:, rank * part : (rank + 1) * part],
             preferred_element_type=jnp.float32,
         )
-    arrived = arrived.astype(jnp.bfloat16)
+    mine = mine.astype(jnp.bfloat16)
+    if members == 4:
+        pieces = [mine] + [
+            lax.ppermute(mine, "section", [(i, i ^ mask) for i in range(members)])
+            for mask in (1, 2, 3)
+        ]
+        columns = []
+        for k in range(members):
+            column = jnp.zeros_like(mine)
+            for mask in range(members):
+                column = jnp.where((member ^ mask) == k, pieces[mask], column)
+            columns.append(column)
+        arrived = jnp.concatenate(columns, axis=1)
+    else:
+        arrived = lax.all_gather(mine, "section", axis=1, tiled=True)
 
     staying = dest_owner == own_index
     source_of = (dest_local[None, :] == slot_ids[:, None]) & staying[None, :]

time: 87.4 us -> 97.9 us (1.12)
  waiting for transfers between devices: 6.02 us -> 12.2 us
  starting transfers between devices: 44.2 us -> 49.9 us
  local copies, waits for them, and re-layouts: 13 us -> 11.2 us
  other arithmetic: 9.46 us -> 10.9 us
  matrix products: 6.37 us -> 5.38 us
    all_to_all x1, starting transfers between devices: 20.8 us -> 8.82 us  [local(): got = lax.all_to_all(send, 'batch', split_axis=0, concat_axis=0, tiled=True)]
    ppermute x0 -> x3, starting transfers between devices: none -> 9.81 us  [local(): lax.ppermute(mine, 'section', [(i, i ^ mask) for i in range(members)])]
    all_to_all x1, waiting for transfers between devices: 0.01 us -> 7.25 us  [local(): got = lax.all_to_all(send, 'batch', split_axis=0, concat_axis=0, tiled=True)]
    ppermute x1, starting transfers between devices: 7.01 us -> 13.3 us  [local(): lax.ppermute(pack(left_owner), 'batch', [(i, (i - 1) % owners) for i in r...]
    reduce_sum x2, other arithmetic: 1.1 us -> 2.64 us  [pick(): jnp.sum(jnp.where(chosen.reshape(shape), rows, jnp.zeros((), rows.dtype))...]
    ppermute x1, starting transfers between devices: 3.97 us -> 5.47 us  [local(): lax.ppermute(pack(right_owner), 'batch', [(i, (i + 1) % owners) for i in...]
    ppermute x4, waiting for transfers between devices: 6.01 us -> 4.91 us  [section_sum(): other = lax.ppermute(total, 'section', route)]
    unnamed x50 -> x47, local copies, waits for them, and re-layouts: 7.91 us -> 7.57 us
  transfers between devices with their start and end apart: 7 -> 10, of which waited for: 3 -> 4; matrix products, arithmetic and copies ran while one was open for 11% -> 10% of each run, Pallas kernels for 4% -> 4%
where the time goes in v9:
time: 97.9 us; the launch traced here: 97.1 us
  starting transfers between devices  49.9 us (51%)
  waiting for transfers between devices  12.2 us (12%)
  local copies, waits for them, and re-layouts  11.2 us (11%)
  other arithmetic  10.9 us (11%)
  matrix products  5.38 us (5%)
  between operations  4.1 us (4%)
  Pallas kernels  3.49 us (4%)
    ppermute x1, starting transfers between devices, local(): lax.ppermute(pack(left_owner), 'batch', [(i, (i - 1) % owners) for i in r...  13.3 us
    ppermute x4, starting transfers between devices, section_sum(): other = lax.ppermute(total, 'section', route)  12.5 us
    ppermute x3, starting transfers between devices, local(): lax.ppermute(mine, 'section', [(i, i ^ mask) for i in range(members)])  9.81 us
    all_to_all x1, starting transfers between devices, local(): got = lax.all_to_all(send, 'batch', split_axis=0, concat_axis=0, tiled=True)  8.82 us
    unnamed x47, local copies, waits for them, and re-layouts  7.57 us
    all_to_all x1, waiting for transfers between devices, local(): got = lax.all_to_all(send, 'batch', split_axis=0, concat_axis=0, tiled=True)  7.25 us
    ppermute x1, starting transfers between devices, local(): lax.ppermute(pack(right_owner), 'batch', [(i, (i + 1) % owners) for i in...  5.47 us
    ppermute x4, waiting for transfers between devices, section_sum(): other = lax.ppermute(total, 'section', route)  4.91 us
  transfers between devices with their start and end apart: 10, of which 4 were waited for; matrix products, arithmetic and copies ran while one was open for 10% of the time, Pallas kernels for 4%

profile of v9, /device:TPU:1, one launch (start us, length us, event | category | flops | bytes accessed | tf_op | source)
XLA Modules:
  0.0 97.1 jit_solution(4302585981022725433)
XLA Ops:
  0.7 0.7 copy-done.17
  1.4 0.6 select_reduce_fusion.13
  2.7 2.5 %select_reduce_fusion.3 = (bf16[128,128]{1,0:T(8,128)(2,1)S(1)}, bf16[128,128]{1,0:T(8,128)(2,1)S(1)}, bf16[128,128]{1,0:T(8,128)(2,1)S(1)}, bf16[128,128]{1,0:T(8,128)(2,1)S(1)}) fusion(bf16[32,128,128]{2,1,0:T(8,128)(2,1)} %keys_ref.1, pred[32]{0:T(512)(128)(4,1)S(1)} %get-tuple-element.56, pred[32]{0:T(512)(128)(4,1)S(1)} %get-tuple-element.55, ...), kind=kLoop, calls=%fused_computation.25 | loop fusion | flops 4128768 | bytes 2228288 | tf_op jit(solution)/shard_map/reduce_sum | solution.py:191
  5.5 5.5 %collective-permute-start.4 = (bf16[272,128]{1,0:T(8,128)(2,1)S(1)}, bf16[272,128]{1,0:T(8,128)(2,1)S(1)}, u32[]{:S(2)}, u32[]{:S(2)}) collective-permute-start(bf16[272,128]{1,0:T(8,128)(2,1)S(1)} %concatenate.32), channel_id=1, source_target_pairs={{0,1},{1,2},{2,3},{3,4},{4,5},{5,6},{6,7},{7,8},{8,9},{9,10},{10,1... | collective-permute-start | bytes 208904 | tf_op jit(solution)/shard_map/ppermute | solution.py:210
  11.7 13.3 %collective-permute-start.3 = (bf16[272,128]{1,0:T(8,128)(2,1)S(1)}, bf16[272,128]{1,0:T(8,128)(2,1)S(1)}, u32[]{:S(2)}, u32[]{:S(2)}) collective-permute-start(bf16[272,128]{1,0:T(8,128)(2,1)S(1)} %concatenate.31), channel_id=1, source_target_pairs={{0,127},{1,0},{2,1},{3,2},{4,3},{5,4},{6,5},{7,6},{8,7},{9,8},{10,... | collective-permute-start | bytes 208904 | tf_op jit(solution)/shard_map/ppermute | solution.py:213
  25.0 0.6 copy-done.20
  27.1 0.7 reduce.14
  27.9 0.8 reshape.506
  28.7 8.8 %all-to-all-start = ((bf16[128,2,192]{2,1,0:T(2,128)(2,1)}), bf16[128,2,192]{2,1,0:T(2,128)(2,1)S(1)}, u32[]{:S(2)}, u32[]{:S(2)}) async-start(bf16[128,2,192]{2,1,0:T(2,128)(2,1)} %reshape.506), calls=%async_computation | async-start | bytes 262144 | tf_op jit(solution)/shard_map/all_to_all | solution.py:242
  37.6 0.6 copy-done.13
  39.5 0.7 select_reduce_fusion.9.src_ref
  40.2 0.5 slice.139
  42.8 7.2 %all-to-all-done = bf16[128,2,192]{2,1,0:T(2,128)(2,1)S(1)} async-done(((bf16[128,2,192]{2,1,0:T(2,128)(2,1)}), bf16[128,2,192]{2,1,0:T(2,128)(2,1)S(1)}, u32[]{:S(2)}, u32[]{:S(2)}) %all-to-all-start) | async-done | bytes 98336 | tf_op jit(solution)/shard_map/all_to_all | solution.py:242
  50.7 5.4 %collective-permute-start = (bf16[32,128]{1,0:T(8,128)(2,1)S(1)}, bf16[32,128]{1,0:T(8,128)(2,1)S(1)}, u32[]{:S(2)}, u32[]{:S(2)}) collective-permute-start(bf16[32,128]{1,0:T(8,128)(2,1)S(1)} %fusion.7), channel_id=1, source_target_pairs={{0,384},{128,256},{256,128},{384,0},{1,385},{129,257},{257,129},{3... | collective-permute-start | bytes 24584 | tf_op jit(solution)/shard_map/ppermute | solution.py:254
  56.1 2.5 %collective-permute-start.1 = (bf16[32,128]{1,0:T(8,128)(2,1)S(1)}, bf16[32,128]{1,0:T(8,128)(2,1)S(1)}, u32[]{:S(2)}, u32[]{:S(2)}) collective-permute-start(bf16[32,128]{1,0:T(8,128)(2,1)S(1)} %fusion.7), channel_id=1, source_target_pairs={{0,256},{128,384},{256,0},{384,128},{1,257},{129,385},{257,1},{385... | collective-permute-start | bytes 24584 | tf_op jit(solution)/shard_map/ppermute | solution.py:254
  58.6 1.9 %collective-permute-start.2 = (bf16[32,128]{1,0:T(8,128)(2,1)S(1)}, bf16[32,128]{1,0:T(8,128)(2,1)S(1)}, u32[]{:S(2)}, u32[]{:S(2)}) collective-permute-start(bf16[32,128]{1,0:T(8,128)(2,1)S(1)} %fusion.7), channel_id=1, source_target_pairs={{0,128},{128,0},{256,384},{384,256},{1,129},{129,1},{257,385},{385... | collective-permute-start | bytes 24584 | tf_op jit(solution)/shard_map/ppermute | solution.py:254
  61.1 3.5 %shard_map.218 = (bf16[32,128,128]{2,1,0:T(8,128)(2,1)}, bf16[32,128,128]{2,1,0:T(8,128)(2,1)}) custom-call(s32[32]{0:T(128)} %select_reduce_fusion.9.src_ref, s32[32]{0:T(128)} %select_select_fusion.8.take_ref, bf16[32,128,128]{2,1,0:T(8,128)(2,1)} %keys_ref.1, bf16[32,128,128]{2,1,0:T(8,128)(2,1)} %values_ref.1, bf16[272,128]{1,0:T(8,128)(2,1)} %copy-done.7, ...), custom_call_target="tpu_custom_call" | custom-call | bytes 4194304 | tf_op jit(solution)/shard_map/pallas_call | solution.py:136
  64.7 0.6 copy-done.6
  65.6 0.6 copy-done.15
  68.0 0.7 fusion.166
  70.3 2.8 %collective-permute-start.5 = (bf16[64,512]{1,0:T(8,128)(2,1)S(1)}, bf16[64,512]{1,0:T(8,128)(2,1)S(1)}, u32[]{:S(2)}, u32[]{:S(2)}) collective-permute-start(bf16[64,512]{1,0:T(8,128)(2,1)S(1)} %convolution_convert_fusion.1), channel_id=1, source_target_pairs={{0,256},{128,384},{256,0},{384,128},{1,257},{129,385},{257,1},{385... | collective-permute-start | bytes 196616 | tf_op jit(solution)/shard_map/ppermute | solution.py:101
  73.4 1.9 %collective-permute-done.5 = bf16[64,512]{1,0:T(8,128)(2,1)S(1)} collective-permute-done((bf16[64,512]{1,0:T(8,128)(2,1)S(1)}, bf16[64,512]{1,0:T(8,128)(2,1)S(1)}, u32[]{:S(2)}, u32[]{:S(2)}) %collective-permute-start.5) | collective-permute-done | bytes 65568 | tf_op jit(solution)/shard_map/ppermute | solution.py:101
  75.3 3.6 %collective-permute-start.6 = (f32[64,512]{1,0:T(8,128)S(1)}, f32[64,512]{1,0:T(8,128)S(1)}, u32[]{:S(2)}, u32[]{:S(2)}) collective-permute-start(f32[64,512]{1,0:T(8,128)S(1)} %convert_add_fusion.1), channel_id=1, source_target_pairs={{0,128},{128,0},{256,384},{384,256},{1,129},{129,1},{257,385},{385... | collective-permute-start | bytes 393224 | tf_op jit(solution)/shard_map/ppermute | solution.py:101
  78.9 0.9 collective-permute-done.6
  80.7 1.7 %convolution_convert_fusion = bf16[64,512]{1,0:T(8,128)(2,1)S(1)} fusion(bf16[512,512]{1,0:T(8,128)(2,1)S(1)} %copy-done, bf16[512,512]{1,0:T(8,128)(2,1)} %param.33, f32[64,512]{1,0:T(8,128)S(1)} %get-tuple-element.48, f32[512]{0:T(512)S(1)} %copy-done.19, f32[64]{0:T(128)S(1)} %add_rsqrt_fusion.1, f32[64]{0:T(128)S(1)} %broadcast_multiply_fusion.1), kind=kOutput, calls=%fused_computation.3 | convolution fusion | flops 69402624 | bytes 1247744 | tf_op jit(solution)/shard_map/dot_general | solution.py:327
  82.4 2.8 %collective-permute-start.7 = (bf16[64,512]{1,0:T(8,128)(2,1)S(1)}, bf16[64,512]{1,0:T(8,128)(2,1)S(1)}, u32[]{:S(2)}, u32[]{:S(2)}) collective-permute-start(bf16[64,512]{1,0:T(8,128)(2,1)S(1)} %convolution_convert_fusion), channel_id=1, source_target_pairs={{0,256},{128,384},{256,0},{384,128},{1,257},{129,385},{257,1},{385... | collective-permute-start | bytes 196616 | tf_op jit(solution)/shard_map/ppermute | solution.py:101
  85.4 2.1 %collective-permute-done.7 = bf16[64,512]{1,0:T(8,128)(2,1)S(1)} collective-permute-done((bf16[64,512]{1,0:T(8,128)(2,1)S(1)}, bf16[64,512]{1,0:T(8,128)(2,1)S(1)}, u32[]{:S(2)}, u32[]{:S(2)}) %collective-permute-start.7) | collective-permute-done | bytes 65568 | tf_op jit(solution)/shard_map/ppermute | solution.py:101
  87.4 3.4 %collective-permute-start.8 = (f32[64,512]{1,0:T(8,128)S(1)}, f32[64,512]{1,0:T(8,128)S(1)}, u32[]{:S(2)}, u32[]{:S(2)}) collective-permute-start(f32[64,512]{1,0:T(8,128)S(1)} %convert_add_fusion), channel_id=1, source_target_pairs={{0,128},{128,0},{256,384},{384,256},{1,129},{129,1},{257,385},{385... | collective-permute-start | bytes 393224 | tf_op jit(solution)/shard_map/ppermute | solution.py:101
  90.9 2.6 %select_select_fusion = (bf16[32,128,128]{2,1,0:T(8,128)(2,1)}, bf16[32,128,128]{2,1,0:T(8,128)(2,1)}) fusion(bf16[32,128,128]{2,1,0:T(8,128)(2,1)S(1)} %copy-done.3, pred[32,128]{1,0:T(8,128)(4,1)S(1)} %get-tuple-element.103, pred[32,128]{1,0:T(8,128)(4,1)S(1)} %get-tuple-element.104, bf16[32,128]{1,0:T(8,128)(2,1)S(1)} %get-tuple-element.79, ...), kind=kLoop, calls=%fused_computation.20 | loop fusion | flops 2097152 | bytes 4235264 | tf_op jit(solution)/shard_map/jit(_where)/select_n | solution.py:349
  93.8 0.6 slice_bitcast_fusion
  95.1 0.7 copy-done.18
  96.3 0.8 copy.91
  (138 shorter events, 11.3 us)
Async XLA Ops:
  0.6 79.6 %copy-start = (bf16[512,512]{1,0:T(8,128)(2,1)S(1)}, bf16[512,512]{1,0:T(8,128)(2,1)}, u32[]{:S(2)}) copy-start(bf16[512,512]{1,0:T(8,128)(2,1)} %param.34) | copy-start | bytes 1572868
  0.7 0.7 copy-start.17
  2.7 2.6 %copy-start.10 = (bf16[32,512]{1,0:T(8,128)(2,1)S(1)}, bf16[32,512]{1,0:T(8,128)(2,1)}, u32[]{:S(2)}) copy-start(bf16[32,512]{1,0:T(8,128)(2,1)} %param.23) | copy-start | bytes 98308
  2.7 2.6 %copy-start.11 = (bf16[32,512]{1,0:T(8,128)(2,1)S(1)}, bf16[32,512]{1,0:T(8,128)(2,1)}, u32[]{:S(2)}) copy-start(bf16[32,512]{1,0:T(8,128)(2,1)} %param.24) | copy-start | bytes 98308
  5.5 34.7 %collective-permute-start.4 = (bf16[272,128]{1,0:T(8,128)(2,1)S(1)}, bf16[272,128]{1,0:T(8,128)(2,1)S(1)}, u32[]{:S(2)}, u32[]{:S(2)}) collective-permute-start(bf16[272,128]{1,0:T(8,128)(2,1)S(1)} %concatenate.32), channel_id=1, source_target_pairs={{0,1},{1,2},{2,3},{3,4},{4,5},{5,6},{6,7},{7,8},{8,9},{9,10},{10,1... | collective-permute-start | bytes 208904 | tf_op jit(solution)/shard_map/ppermute | solution.py:210
  11.6 14.3 %copy-start.9 = (bf16[32,512]{1,0:T(8,128)(2,1)S(1)}, bf16[32,512]{1,0:T(8,128)(2,1)}, u32[]{:S(2)}) copy-start(bf16[32,512]{1,0:T(8,128)(2,1)} %param.19) | copy-start | bytes 98308
  11.7 29.7 %collective-permute-start.3 = (bf16[272,128]{1,0:T(8,128)(2,1)S(1)}, bf16[272,128]{1,0:T(8,128)(2,1)S(1)}, u32[]{:S(2)}, u32[]{:S(2)}) collective-permute-start(bf16[272,128]{1,0:T(8,128)(2,1)S(1)} %concatenate.31), channel_id=1, source_target_pairs={{0,127},{1,0},{2,1},{3,2},{4,3},{5,4},{6,5},{7,6},{8,7},{9,8},{10,... | collective-permute-start | bytes 208904 | tf_op jit(solution)/shard_map/ppermute | solution.py:213
  25.0 0.7 copy-start.20
  28.7 21.3 %all-to-all-start = ((bf16[128,2,192]{2,1,0:T(2,128)(2,1)}), bf16[128,2,192]{2,1,0:T(2,128)(2,1)S(1)}, u32[]{:S(2)}, u32[]{:S(2)}) async-start(bf16[128,2,192]{2,1,0:T(2,128)(2,1)} %reshape.506), calls=%async_computation | async-start | bytes 262144 | tf_op jit(solution)/shard_map/all_to_all | solution.py:242
  37.6 0.7 copy-start.13
  38.3 0.7 copy-start.14
  40.2 2.6 %copy-start.7 = (bf16[272,128]{1,0:T(8,128)(2,1)}, bf16[272,128]{1,0:T(8,128)(2,1)S(1)}, u32[]{:S(2)}) copy-start(bf16[272,128]{1,0:T(8,128)(2,1)S(1)} %collective-permute-done.4.lbox_ref) | copy-start | bytes 208900
  41.4 1.4 %copy-start.8 = (bf16[272,128]{1,0:T(8,128)(2,1)}, bf16[272,128]{1,0:T(8,128)(2,1)S(1)}, u32[]{:S(2)}) copy-start(bf16[272,128]{1,0:T(8,128)(2,1)S(1)} %collective-permute-done.3.rbox_ref) | copy-start | bytes 208900
  50.7 13.9 %collective-permute-start = (bf16[32,128]{1,0:T(8,128)(2,1)S(1)}, bf16[32,128]{1,0:T(8,128)(2,1)S(1)}, u32[]{:S(2)}, u32[]{:S(2)}) collective-permute-start(bf16[32,128]{1,0:T(8,128)(2,1)S(1)} %fusion.7), channel_id=1, source_target_pairs={{0,384},{128,256},{256,128},{384,0},{1,385},{129,257},{257,129},{3... | collective-permute-start | bytes 24584 | tf_op jit(solution)/shard_map/ppermute | solution.py:254
  56.1 8.5 %collective-permute-start.1 = (bf16[32,128]{1,0:T(8,128)(2,1)S(1)}, bf16[32,128]{1,0:T(8,128)(2,1)S(1)}, u32[]{:S(2)}, u32[]{:S(2)}) collective-permute-start(bf16[32,128]{1,0:T(8,128)(2,1)S(1)} %fusion.7), channel_id=1, source_target_pairs={{0,256},{128,384},{256,0},{384,128},{1,257},{129,385},{257,1},{385... | collective-permute-start | bytes 24584 | tf_op jit(solution)/shard_map/ppermute | solution.py:254
  58.6 6.0 %collective-permute-start.2 = (bf16[32,128]{1,0:T(8,128)(2,1)S(1)}, bf16[32,128]{1,0:T(8,128)(2,1)S(1)}, u32[]{:S(2)}, u32[]{:S(2)}) collective-permute-start(bf16[32,128]{1,0:T(8,128)(2,1)S(1)} %fusion.7), channel_id=1, source_target_pairs={{0,128},{128,0},{256,384},{384,256},{1,129},{129,1},{257,385},{385... | collective-permute-start | bytes 24584 | tf_op jit(solution)/shard_map/ppermute | solution.py:254
  64.6 1.0 %copy-start.4 = (bf16[3,512,128]{2,1,0:T(8,128)(2,1)S(1)}, bf16[3,512,128]{2,1,0:T(8,128)(2,1)}, u32[]{:S(2)}) copy-start(bf16[3,512,128]{2,1,0:T(8,128)(2,1)} %param.29) | copy-start | bytes 1179652
  64.7 0.6 copy-start.6
  65.6 0.7 copy-start.15
  66.5 1.4 %copy-start.1 = (bf16[32,128,128]{2,1,0:T(8,128)(2,1)S(1)}, bf16[32,128,128]{2,1,0:T(8,128)(2,1)}, u32[]{:S(2)}) copy-start(bf16[32,128,128]{2,1,0:T(8,128)(2,1)} %get-tuple-element.7) | copy-start | bytes 3145732
  67.6 1.6 %copy-start.3 = (bf16[32,128,128]{2,1,0:T(8,128)(2,1)S(1)}, bf16[32,128,128]{2,1,0:T(8,128)(2,1)}, u32[]{:S(2)}) copy-start(bf16[32,128,128]{2,1,0:T(8,128)(2,1)} %get-tuple-element.8) | copy-start | bytes 3145732
  69.2 0.9 copy-start.5
  70.3 5.0 %collective-permute-start.5 = (bf16[64,512]{1,0:T(8,128)(2,1)S(1)}, bf16[64,512]{1,0:T(8,128)(2,1)S(1)}, u32[]{:S(2)}, u32[]{:S(2)}) collective-permute-start(bf16[64,512]{1,0:T(8,128)(2,1)S(1)} %convolution_convert_fusion.1), channel_id=1, source_target_pairs={{0,256},{128,384},{256,0},{384,128},{1,257},{129,385},{257,1},{385... | collective-permute-start | bytes 196616 | tf_op jit(solution)/shard_map/ppermute | solution.py:101
  75.3 4.5 %copy-start.12 = (f32[512]{0:T(512)S(1)}, f32[512]{0:T(512)}, u32[]{:S(2)}) copy-start(f32[512]{0:T(512)} %param.31) | copy-start | bytes 6148
  75.3 4.5 %collective-permute-start.6 = (f32[64,512]{1,0:T(8,128)S(1)}, f32[64,512]{1,0:T(8,128)S(1)}, u32[]{:S(2)}, u32[]{:S(2)}) collective-permute-start(f32[64,512]{1,0:T(8,128)S(1)} %convert_add_fusion.1), channel_id=1, source_target_pairs={{0,128},{128,0},{256,384},{384,256},{1,129},{129,1},{257,385},{385... | collective-permute-start | bytes 393224 | tf_op jit(solution)/shard_map/ppermute | solution.py:101
  80.0 0.7 copy-start.19
  82.4 5.0 %collective-permute-start.7 = (bf16[64,512]{1,0:T(8,128)(2,1)S(1)}, bf16[64,512]{1,0:T(8,128)(2,1)S(1)}, u32[]{:S(2)}, u32[]{:S(2)}) collective-permute-start(bf16[64,512]{1,0:T(8,128)(2,1)S(1)} %convolution_convert_fusion), channel_id=1, source_target_pairs={{0,256},{128,384},{256,0},{384,128},{1,257},{129,385},{257,1},{385... | collective-permute-start | bytes 196616 | tf_op jit(solution)/shard_map/ppermute | solution.py:101
  87.4 6.2 %collective-permute-start.8 = (f32[64,512]{1,0:T(8,128)S(1)}, f32[64,512]{1,0:T(8,128)S(1)}, u32[]{:S(2)}, u32[]{:S(2)}) collective-permute-start(f32[64,512]{1,0:T(8,128)S(1)} %convert_add_fusion), channel_id=1, source_target_pairs={{0,128},{128,0},{256,384},{384,256},{1,129},{129,1},{257,385},{385... | collective-permute-start | bytes 393224 | tf_op jit(solution)/shard_map/ppermute | solution.py:101
  90.9 2.8 %copy-start.16 = (f32[512]{0:T(512)S(1)}, f32[512]{0:T(512)}, u32[]{:S(2)}) copy-start(f32[512]{0:T(512)} %param.35) | copy-start | bytes 6148
  93.5 1.2 %copy-start.2 = (bf16[16,64,512]{2,1,0:T(8,128)(2,1)S(1)}, bf16[16,64,512]{2,1,0:T(8,128)(2,1)}, u32[]{:S(2)}) copy-start(bf16[16,64,512]{2,1,0:T(8,128)(2,1)} %param.36) | copy-start | bytes 3145732
  95.1 0.7 copy-start.18

commit v10 on v5

--- a/solution.py
+++ b/solution.py
@@ -220,6 +220,13 @@
     landing = token_slot % streams
     same_before = (target[None, :] == target[:, None]) & (slot_ids[None, :] < slot_ids[:, None])
     arrival_rank = jnp.sum(same_before.astype(jnp.int32), axis=1)
+    members = lax.axis_size("section")
+    halves = 2 if members % 2 == 0 else 1
+    half = lax.axis_index("section") % halves
+    part = model_width // halves
+    share_rows = latents[:, :part]
+    for k in range(1, halves):
+        share_rows = jnp.where(half == k, latents[:, k * part : (k + 1) * part], share_rows)
     owner_ids = jnp.arange(owners, dtype=jnp.int32)
     lane_ids = jnp.arange(CODE_LANES, dtype=jnp.int32)
     blocks = []
@@ -227,22 +234,29 @@
     for rank in range(capacity):
         chosen = (owner_ids[:, None] == target[None, :]) & (arrival_rank == rank)[None, :]
         blocks.append(
-            jnp.dot(chosen.astype(jnp.bfloat16), latents, preferred_element_type=jnp.float32)
+            jnp.dot(chosen.astype(jnp.bfloat16), share_rows, preferred_element_type=jnp.float32)
         )
         code = jnp.sum(jnp.where(chosen, landing[None, :] + 1, 0), axis=1)
         code_block = jnp.where(lane_ids[None, :] == rank, code[:, None], code_block)
     blocks.append(code_block.astype(jnp.float32))
     send = jnp.concatenate(blocks, axis=1).astype(jnp.bfloat16)
     got = lax.all_to_all(send, "batch", split_axis=0, concat_axis=0, tiled=True)
-    arrived = jnp.zeros((streams, model_width), jnp.float32)
+    mine = jnp.zeros((streams, part), jnp.float32)
     for rank in range(capacity):
-        got_code = got[:, capacity * model_width + rank].astype(jnp.int32) - 1
-        arrived = arrived + jnp.dot(
+        got_code = got[:, capacity * part + rank].astype(jnp.int32) - 1
+        mine = mine + jnp.dot(
             one_hot(slot_ids, got_code),
-            got[:, rank * model_width : (rank + 1) * model_width],
+            got[:, rank * part : (rank + 1) * part],
             preferred_element_type=jnp.float32,
         )
-    arrived = arrived.astype(jnp.bfloat16)
+    mine = mine.astype(jnp.bfloat16)
+    if halves == 2:
+        other = lax.ppermute(mine, "section", [(i, i ^ 1) for i in range(members)])
+        lower = jnp.where(half == 0, mine, other)
+        upper = jnp.where(half == 0, other, mine)
+        arrived = jnp.concatenate([lower, upper], axis=1)
+    else:
+        arrived = mine
 
     staying = dest_owner == own_index
     source_of = (dest_local[None, :] == slot_ids[:, None]) & staying[None, :]

time: 87.4 us -> 92.7 us (1.061)
  waiting for transfers between devices: 6.02 us -> 13.3 us
  local copies, waits for them, and re-layouts: 13 us -> 10.6 us
  other arithmetic: 9.46 us -> 10.8 us
    all_to_all x1, starting transfers between devices: 20.8 us -> 8.82 us  [local(): got = lax.all_to_all(send, 'batch', split_axis=0, concat_axis=0, tiled=True)]
    all_to_all x1, waiting for transfers between devices: 0.01 us -> 7.82 us  [local(): got = lax.all_to_all(send, 'batch', split_axis=0, concat_axis=0, tiled=True)]
    ppermute x1, starting transfers between devices: 7.01 us -> 13.4 us  [local(): lax.ppermute(pack(left_owner), 'batch', [(i, (i - 1) % owners) for i in r...]
    ppermute x0 -> x1, starting transfers between devices: none -> 4.79 us  [local(): other = lax.ppermute(mine, 'section', [(i, i ^ 1) for i in range(members)])]
    reduce_sum x2, other arithmetic: 1.1 us -> 2.64 us  [pick(): jnp.sum(jnp.where(chosen.reshape(shape), rows, jnp.zeros((), rows.dtype))...]
    ppermute x1, starting transfers between devices: 3.97 us -> 5.47 us  [local(): lax.ppermute(pack(right_owner), 'batch', [(i, (i + 1) % owners) for i in...]
    unnamed x50 -> x46, local copies, waits for them, and re-layouts: 7.91 us -> 6.98 us
  transfers between devices with their start and end apart: 7 -> 8, of which waited for: 3 -> 4; matrix products, arithmetic and copies ran while one was open for 11% -> 10% of each run, Pallas kernels for 4% -> 4%
where the time goes in v10:
time: 92.7 us; the launch traced here: 91.9 us
  starting transfers between devices  44.2 us (48%)
  waiting for transfers between devices  13.3 us (14%)
  other arithmetic  10.8 us (12%)
  local copies, waits for them, and re-layouts  10.6 us (11%)
  matrix products  5.51 us (6%)
  between operations  4.02 us (4%)
  Pallas kernels  3.49 us (4%)
    ppermute x1, starting transfers between devices, local(): lax.ppermute(pack(left_owner), 'batch', [(i, (i - 1) % owners) for i in r...  13.4 us
    ppermute x4, starting transfers between devices, section_sum(): other = lax.ppermute(total, 'section', route)  11.7 us
    all_to_all x1, starting transfers between devices, local(): got = lax.all_to_all(send, 'batch', split_axis=0, concat_axis=0, tiled=True)  8.82 us
    all_to_all x1, waiting for transfers between devices, local(): got = lax.all_to_all(send, 'batch', split_axis=0, concat_axis=0, tiled=True)  7.82 us
    unnamed x46, local copies, waits for them, and re-layouts  6.98 us
    ppermute x4, waiting for transfers between devices, section_sum(): other = lax.ppermute(total, 'section', route)  5.51 us
    ppermute x1, starting transfers between devices, local(): lax.ppermute(pack(right_owner), 'batch', [(i, (i + 1) % owners) for i in...  5.47 us
    ppermute x1, starting transfers between devices, local(): other = lax.ppermute(mine, 'section', [(i, i ^ 1) for i in range(members)])  4.79 us
  transfers between devices with their start and end apart: 8, of which 4 were waited for; matrix products, arithmetic and copies ran while one was open for 10% of the time, Pallas kernels for 4%

profile of v10, /device:TPU:1, one launch (start us, length us, event | category | flops | bytes accessed | tf_op | source)
XLA Modules:
  0.0 91.9 jit_solution(18417915707929982040)
XLA Ops:
  0.7 0.7 copy-done.16
  1.4 0.6 select_reduce_fusion.13
  2.7 2.5 %select_reduce_fusion.3 = (bf16[128,128]{1,0:T(8,128)(2,1)S(1)}, bf16[128,128]{1,0:T(8,128)(2,1)S(1)}, bf16[128,128]{1,0:T(8,128)(2,1)S(1)}, bf16[128,128]{1,0:T(8,128)(2,1)S(1)}) fusion(bf16[32,128,128]{2,1,0:T(8,128)(2,1)} %keys_ref.1, pred[32]{0:T(512)(128)(4,1)S(1)} %get-tuple-element.56, pred[32]{0:T(512)(128)(4,1)S(1)} %get-tuple-element.55, ...), kind=kLoop, calls=%fused_computation.25 | loop fusion | flops 4128768 | bytes 2228288 | tf_op jit(solution)/shard_map/reduce_sum | solution.py:191
  5.5 5.5 %collective-permute-start.2 = (bf16[272,128]{1,0:T(8,128)(2,1)S(1)}, bf16[272,128]{1,0:T(8,128)(2,1)S(1)}, u32[]{:S(2)}, u32[]{:S(2)}) collective-permute-start(bf16[272,128]{1,0:T(8,128)(2,1)S(1)} %concatenate.32), channel_id=1, source_target_pairs={{0,1},{1,2},{2,3},{3,4},{4,5},{5,6},{6,7},{7,8},{8,9},{9,10},{10,1... | collective-permute-start | bytes 208904 | tf_op jit(solution)/shard_map/ppermute | solution.py:210
  11.7 13.4 %collective-permute-start.1 = (bf16[272,128]{1,0:T(8,128)(2,1)S(1)}, bf16[272,128]{1,0:T(8,128)(2,1)S(1)}, u32[]{:S(2)}, u32[]{:S(2)}) collective-permute-start(bf16[272,128]{1,0:T(8,128)(2,1)S(1)} %concatenate.31), channel_id=1, source_target_pairs={{0,127},{1,0},{2,1},{3,2},{4,3},{5,4},{6,5},{7,6},{8,7},{9,8},{10,... | collective-permute-start | bytes 208904 | tf_op jit(solution)/shard_map/ppermute | solution.py:213
  26.2 0.5 broadcast.515
  26.7 0.7 reduce.14
  27.4 0.9 reshape.506
  28.3 8.8 %all-to-all-start = ((bf16[128,2,320]{2,1,0:T(2,128)(2,1)}), bf16[128,2,320]{2,1,0:T(2,128)(2,1)S(1)}, u32[]{:S(2)}, u32[]{:S(2)}) async-start(bf16[128,2,320]{2,1,0:T(2,128)(2,1)} %reshape.506), calls=%async_computation | async-start | bytes 393216 | tf_op jit(solution)/shard_map/all_to_all | solution.py:243
  37.2 0.6 copy-done.12
  38.0 0.5 copy-done.13
  39.1 0.6 select_reduce_fusion.9.src_ref
  39.7 0.5 slice.131
  41.0 0.5 slice.129
  42.3 7.8 %all-to-all-done = bf16[128,2,320]{2,1,0:T(2,128)(2,1)S(1)} async-done(((bf16[128,2,320]{2,1,0:T(2,128)(2,1)}), bf16[128,2,320]{2,1,0:T(2,128)(2,1)S(1)}, u32[]{:S(2)}, u32[]{:S(2)}) %all-to-all-start) | async-done | bytes 163872 | tf_op jit(solution)/shard_map/all_to_all | solution.py:243
  50.9 4.8 %collective-permute-start = (bf16[32,256]{1,0:T(8,128)(2,1)S(1)}, bf16[32,256]{1,0:T(8,128)(2,1)S(1)}, u32[]{:S(2)}, u32[]{:S(2)}) collective-permute-start(bf16[32,256]{1,0:T(8,128)(2,1)S(1)} %fusion.7), channel_id=1, source_target_pairs={{0,128},{128,0},{256,384},{384,256},{1,129},{129,1},{257,385},{385... | collective-permute-start | bytes 49160 | tf_op jit(solution)/shard_map/ppermute | solution.py:254
  56.2 3.5 %shard_map.218 = (bf16[32,128,128]{2,1,0:T(8,128)(2,1)}, bf16[32,128,128]{2,1,0:T(8,128)(2,1)}) custom-call(s32[32]{0:T(128)} %select_reduce_fusion.9.src_ref, s32[32]{0:T(128)} %select_select_fusion.3.take_ref, bf16[32,128,128]{2,1,0:T(8,128)(2,1)} %keys_ref.1, bf16[32,128,128]{2,1,0:T(8,128)(2,1)} %values_ref.1, bf16[272,128]{1,0:T(8,128)(2,1)} %copy-done.7, ...), custom_call_target="tpu_custom_call" | custom-call | bytes 4194304 | tf_op jit(solution)/shard_map/pallas_call | solution.py:136
  59.8 0.6 copy-done.6
  60.7 0.6 copy-done.14
  63.0 0.7 fusion.166
  65.4 2.8 %collective-permute-start.3 = (bf16[64,512]{1,0:T(8,128)(2,1)S(1)}, bf16[64,512]{1,0:T(8,128)(2,1)S(1)}, u32[]{:S(2)}, u32[]{:S(2)}) collective-permute-start(bf16[64,512]{1,0:T(8,128)(2,1)S(1)} %convolution_convert_fusion.3), channel_id=1, source_target_pairs={{0,256},{128,384},{256,0},{384,128},{1,257},{129,385},{257,1},{385... | collective-permute-start | bytes 196616 | tf_op jit(solution)/shard_map/ppermute | solution.py:101
  68.5 2.5 %collective-permute-done.3 = bf16[64,512]{1,0:T(8,128)(2,1)S(1)} collective-permute-done((bf16[64,512]{1,0:T(8,128)(2,1)S(1)}, bf16[64,512]{1,0:T(8,128)(2,1)S(1)}, u32[]{:S(2)}, u32[]{:S(2)}) %collective-permute-start.3) | collective-permute-done | bytes 65568 | tf_op jit(solution)/shard_map/ppermute | solution.py:101
  71.0 2.7 %collective-permute-start.4 = (f32[64,512]{1,0:T(8,128)S(1)}, f32[64,512]{1,0:T(8,128)S(1)}, u32[]{:S(2)}, u32[]{:S(2)}) collective-permute-start(f32[64,512]{1,0:T(8,128)S(1)} %convert_add_fusion.1), channel_id=1, source_target_pairs={{0,128},{128,0},{256,384},{384,256},{1,129},{129,1},{257,385},{385... | collective-permute-start | bytes 393224 | tf_op jit(solution)/shard_map/ppermute | solution.py:101
  73.7 0.9 %collective-permute-done.4 = f32[64,512]{1,0:T(8,128)S(1)} collective-permute-done((f32[64,512]{1,0:T(8,128)S(1)}, f32[64,512]{1,0:T(8,128)S(1)}, u32[]{:S(2)}, u32[]{:S(2)}) %collective-permute-start.4) | collective-permute-done | bytes 131104 | tf_op jit(solution)/shard_map/ppermute | solution.py:101
  75.5 1.7 %convolution_convert_fusion = bf16[64,512]{1,0:T(8,128)(2,1)S(1)} fusion(bf16[512,512]{1,0:T(8,128)(2,1)S(1)} %copy-done, bf16[512,512]{1,0:T(8,128)(2,1)} %param.33, f32[64,512]{1,0:T(8,128)S(1)} %get-tuple-element.48, f32[512]{0:T(512)S(1)} %copy-done.19, f32[64]{0:T(128)S(1)} %add_rsqrt_fusion.1, f32[64]{0:T(128)S(1)} %broadcast_multiply_fusion.1), kind=kOutput, calls=%fused_computation.3 | convolution fusion | flops 69402624 | bytes 1247744 | tf_op jit(solution)/shard_map/dot_general | solution.py:321
  77.2 2.8 %collective-permute-start.5 = (bf16[64,512]{1,0:T(8,128)(2,1)S(1)}, bf16[64,512]{1,0:T(8,128)(2,1)S(1)}, u32[]{:S(2)}, u32[]{:S(2)}) collective-permute-start(bf16[64,512]{1,0:T(8,128)(2,1)S(1)} %convolution_convert_fusion), channel_id=1, source_target_pairs={{0,256},{128,384},{256,0},{384,128},{1,257},{129,385},{257,1},{385... | collective-permute-start | bytes 196616 | tf_op jit(solution)/shard_map/ppermute | solution.py:101
  80.2 2.1 %collective-permute-done.5 = bf16[64,512]{1,0:T(8,128)(2,1)S(1)} collective-permute-done((bf16[64,512]{1,0:T(8,128)(2,1)S(1)}, bf16[64,512]{1,0:T(8,128)(2,1)S(1)}, u32[]{:S(2)}, u32[]{:S(2)}) %collective-permute-start.5) | collective-permute-done | bytes 65568 | tf_op jit(solution)/shard_map/ppermute | solution.py:101
  82.3 3.4 %collective-permute-start.6 = (f32[64,512]{1,0:T(8,128)S(1)}, f32[64,512]{1,0:T(8,128)S(1)}, u32[]{:S(2)}, u32[]{:S(2)}) collective-permute-start(f32[64,512]{1,0:T(8,128)S(1)} %convert_add_fusion), channel_id=1, source_target_pairs={{0,128},{128,0},{256,384},{384,256},{1,129},{129,1},{257,385},{385... | collective-permute-start | bytes 393224 | tf_op jit(solution)/shard_map/ppermute | solution.py:101
  85.7 2.6 %select_select_fusion = (bf16[32,128,128]{2,1,0:T(8,128)(2,1)}, bf16[32,128,128]{2,1,0:T(8,128)(2,1)}) fusion(bf16[32,128,128]{2,1,0:T(8,128)(2,1)S(1)} %copy-done.3, pred[32,128]{1,0:T(8,128)(4,1)S(1)} %get-tuple-element.102, pred[32,128]{1,0:T(8,128)(4,1)S(1)} %get-tuple-element.103, bf16[32,128]{1,0:T(8,128)(2,1)S(1)} %get-tuple-element.78, ...), kind=kLoop, calls=%fused_computation.20 | loop fusion | flops 2097152 | bytes 4235264 | tf_op jit(solution)/shard_map/jit(_where)/select_n | solution.py:343
  88.6 0.6 slice_bitcast_fusion
  89.9 0.7 copy-done.17
  91.1 0.8 copy.91
  (131 shorter events, 9.8 us)
Async XLA Ops:
  0.6 74.4 %copy-start = (bf16[512,512]{1,0:T(8,128)(2,1)S(1)}, bf16[512,512]{1,0:T(8,128)(2,1)}, u32[]{:S(2)}) copy-start(bf16[512,512]{1,0:T(8,128)(2,1)} %param.34) | copy-start | bytes 1572868
  0.7 0.7 copy-start.16
  2.7 2.6 %copy-start.9 = (bf16[32,512]{1,0:T(8,128)(2,1)S(1)}, bf16[32,512]{1,0:T(8,128)(2,1)}, u32[]{:S(2)}) copy-start(bf16[32,512]{1,0:T(8,128)(2,1)} %param.23) | copy-start | bytes 98308
  2.7 2.6 %copy-start.10 = (bf16[32,512]{1,0:T(8,128)(2,1)S(1)}, bf16[32,512]{1,0:T(8,128)(2,1)}, u32[]{:S(2)}) copy-start(bf16[32,512]{1,0:T(8,128)(2,1)} %param.24) | copy-start | bytes 98308
  5.5 34.2 %collective-permute-start.2 = (bf16[272,128]{1,0:T(8,128)(2,1)S(1)}, bf16[272,128]{1,0:T(8,128)(2,1)S(1)}, u32[]{:S(2)}, u32[]{:S(2)}) collective-permute-start(bf16[272,128]{1,0:T(8,128)(2,1)S(1)} %concatenate.32), channel_id=1, source_target_pairs={{0,1},{1,2},{2,3},{3,4},{4,5},{5,6},{6,7},{7,8},{8,9},{9,10},{10,1... | collective-permute-start | bytes 208904 | tf_op jit(solution)/shard_map/ppermute | solution.py:210
  11.6 13.5 %copy-start.20 = (s32[32]{0:T(128)S(1)}, s32[32]{0:T(128)}, u32[]{:S(2)}) copy-start(s32[32]{0:T(128)} %param.20) | copy-start | bytes 388
  11.7 13.7 %copy-start.18 = (bf16[32,512]{1,0:T(8,128)(2,1)S(1)}, bf16[32,512]{1,0:T(8,128)(2,1)}, u32[]{:S(2)}) copy-start(bf16[32,512]{1,0:T(8,128)(2,1)} %param.19) | copy-start | bytes 98308
  11.7 29.2 %collective-permute-start.1 = (bf16[272,128]{1,0:T(8,128)(2,1)S(1)}, bf16[272,128]{1,0:T(8,128)(2,1)S(1)}, u32[]{:S(2)}, u32[]{:S(2)}) collective-permute-start(bf16[272,128]{1,0:T(8,128)(2,1)S(1)} %concatenate.31), channel_id=1, source_target_pairs={{0,127},{1,0},{2,1},{3,2},{4,3},{5,4},{6,5},{7,6},{8,7},{9,8},{10,... | collective-permute-start | bytes 208904 | tf_op jit(solution)/shard_map/ppermute | solution.py:213
  28.3 21.8 %all-to-all-start = ((bf16[128,2,320]{2,1,0:T(2,128)(2,1)}), bf16[128,2,320]{2,1,0:T(2,128)(2,1)S(1)}, u32[]{:S(2)}, u32[]{:S(2)}) async-start(bf16[128,2,320]{2,1,0:T(2,128)(2,1)} %reshape.506), calls=%async_computation | async-start | bytes 393216 | tf_op jit(solution)/shard_map/all_to_all | solution.py:243
  37.2 0.7 copy-start.12
  37.8 0.7 copy-start.13
  39.7 2.6 %copy-start.7 = (bf16[272,128]{1,0:T(8,128)(2,1)}, bf16[272,128]{1,0:T(8,128)(2,1)S(1)}, u32[]{:S(2)}) copy-start(bf16[272,128]{1,0:T(8,128)(2,1)S(1)} %collective-permute-done.2.lbox_ref) | copy-start | bytes 208900
  40.9 1.4 %copy-start.8 = (bf16[272,128]{1,0:T(8,128)(2,1)}, bf16[272,128]{1,0:T(8,128)(2,1)S(1)}, u32[]{:S(2)}) copy-start(bf16[272,128]{1,0:T(8,128)(2,1)S(1)} %collective-permute-done.1.rbox_ref) | copy-start | bytes 208900
  50.9 8.8 %collective-permute-start = (bf16[32,256]{1,0:T(8,128)(2,1)S(1)}, bf16[32,256]{1,0:T(8,128)(2,1)S(1)}, u32[]{:S(2)}, u32[]{:S(2)}) collective-permute-start(bf16[32,256]{1,0:T(8,128)(2,1)S(1)} %fusion.7), channel_id=1, source_target_pairs={{0,128},{128,0},{256,384},{384,256},{1,129},{129,1},{257,385},{385... | collective-permute-start | bytes 49160 | tf_op jit(solution)/shard_map/ppermute | solution.py:254
  59.7 1.0 %copy-start.4 = (bf16[3,512,128]{2,1,0:T(8,128)(2,1)S(1)}, bf16[3,512,128]{2,1,0:T(8,128)(2,1)}, u32[]{:S(2)}) copy-start(bf16[3,512,128]{2,1,0:T(8,128)(2,1)} %param.29) | copy-start | bytes 1179652
  59.8 0.6 copy-start.6
  60.6 0.7 copy-start.14
  61.6 1.4 %copy-start.1 = (bf16[32,128,128]{2,1,0:T(8,128)(2,1)S(1)}, bf16[32,128,128]{2,1,0:T(8,128)(2,1)}, u32[]{:S(2)}) copy-start(bf16[32,128,128]{2,1,0:T(8,128)(2,1)} %get-tuple-element.7) | copy-start | bytes 3145732
  62.7 1.6 %copy-start.3 = (bf16[32,128,128]{2,1,0:T(8,128)(2,1)S(1)}, bf16[32,128,128]{2,1,0:T(8,128)(2,1)}, u32[]{:S(2)}) copy-start(bf16[32,128,128]{2,1,0:T(8,128)(2,1)} %get-tuple-element.8) | copy-start | bytes 3145732
  64.3 0.9 copy-start.5
  65.4 5.6 %collective-permute-start.3 = (bf16[64,512]{1,0:T(8,128)(2,1)S(1)}, bf16[64,512]{1,0:T(8,128)(2,1)S(1)}, u32[]{:S(2)}, u32[]{:S(2)}) collective-permute-start(bf16[64,512]{1,0:T(8,128)(2,1)S(1)} %convolution_convert_fusion.3), channel_id=1, source_target_pairs={{0,256},{128,384},{256,0},{384,128},{1,257},{129,385},{257,1},{385... | collective-permute-start | bytes 196616 | tf_op jit(solution)/shard_map/ppermute | solution.py:101
  71.0 3.7 %copy-start.11 = (f32[512]{0:T(512)S(1)}, f32[512]{0:T(512)}, u32[]{:S(2)}) copy-start(f32[512]{0:T(512)} %param.31) | copy-start | bytes 6148
  71.0 3.7 %collective-permute-start.4 = (f32[64,512]{1,0:T(8,128)S(1)}, f32[64,512]{1,0:T(8,128)S(1)}, u32[]{:S(2)}, u32[]{:S(2)}) collective-permute-start(f32[64,512]{1,0:T(8,128)S(1)} %convert_add_fusion.1), channel_id=1, source_target_pairs={{0,128},{128,0},{256,384},{384,256},{1,129},{129,1},{257,385},{385... | collective-permute-start | bytes 393224 | tf_op jit(solution)/shard_map/ppermute | solution.py:101
  74.8 0.7 copy-start.19
  77.2 5.0 %collective-permute-start.5 = (bf16[64,512]{1,0:T(8,128)(2,1)S(1)}, bf16[64,512]{1,0:T(8,128)(2,1)S(1)}, u32[]{:S(2)}, u32[]{:S(2)}) collective-permute-start(bf16[64,512]{1,0:T(8,128)(2,1)S(1)} %convolution_convert_fusion), channel_id=1, source_target_pairs={{0,256},{128,384},{256,0},{384,128},{1,257},{129,385},{257,1},{385... | collective-permute-start | bytes 196616 | tf_op jit(solution)/shard_map/ppermute | solution.py:101
  82.3 6.2 %collective-permute-start.6 = (f32[64,512]{1,0:T(8,128)S(1)}, f32[64,512]{1,0:T(8,128)S(1)}, u32[]{:S(2)}, u32[]{:S(2)}) collective-permute-start(f32[64,512]{1,0:T(8,128)S(1)} %convert_add_fusion), channel_id=1, source_target_pairs={{0,128},{128,0},{256,384},{384,256},{1,129},{129,1},{257,385},{385... | collective-permute-start | bytes 393224 | tf_op jit(solution)/shard_map/ppermute | solution.py:101
  85.7 2.8 %copy-start.15 = (f32[512]{0:T(512)S(1)}, f32[512]{0:T(512)}, u32[]{:S(2)}) copy-start(f32[512]{0:T(512)} %param.35) | copy-start | bytes 6148
  88.3 1.2 %copy-start.2 = (bf16[16,64,512]{2,1,0:T(8,128)(2,1)S(1)}, bf16[16,64,512]{2,1,0:T(8,128)(2,1)}, u32[]{:S(2)}) copy-start(bf16[16,64,512]{2,1,0:T(8,128)(2,1)} %param.36) | copy-start | bytes 3145732
  89.9 0.7 copy-start.17

commit v11 on v5

--- a/solution.py
+++ b/solution.py
@@ -125,7 +125,7 @@
 
         return carry
 
-    lax.fori_loop(0, streams, body, 0)
+    lax.fori_loop(0, streams, body, 0, unroll=True)
 
 
 def route_caches(src, take, keys, values, lbox, rbox):

time: 87.4 us -> 87.2 us (level)
  no operation moved by 1% of the time
where the time goes in v11:
time: 87.2 us; the launch traced here: 86.4 us
  starting transfers between devices  44.2 us (51%)
  local copies, waits for them, and re-layouts  13 us (15%)
  other arithmetic  9.46 us (11%)
  matrix products  6.37 us (7%)
  waiting for transfers between devices  6.02 us (7%)
  between operations  3.98 us (5%)
  Pallas kernels  3.31 us (4%)
    all_to_all x1, starting transfers between devices, local(): got = lax.all_to_all(send, 'batch', split_axis=0, concat_axis=0, tiled=True)  20.8 us
    ppermute x4, starting transfers between devices, section_sum(): other = lax.ppermute(total, 'section', route)  12.4 us
    unnamed x50, local copies, waits for them, and re-layouts  7.91 us
    ppermute x1, starting transfers between devices, local(): lax.ppermute(pack(left_owner), 'batch', [(i, (i - 1) % owners) for i in r...  7.01 us
    ppermute x4, waiting for transfers between devices, section_sum(): other = lax.ppermute(total, 'section', route)  6.01 us
    ppermute x1, starting transfers between devices, local(): lax.ppermute(pack(right_owner), 'batch', [(i, (i + 1) % owners) for i in...  3.97 us
    pallas_call x1, Pallas kernels, route_caches(): pl.pallas_call(cache_kernel, out_shape=(shape, shape), in_specs=[smem] *...  3.31 us
    select_n x1, other arithmetic, local(): jnp.where(hit_second, fresh_values[:, 1][:, None, :], jnp.where(hit_first...  2.63 us
  transfers between devices with their start and end apart: 7, of which 3 were waited for; matrix products, arithmetic and copies ran while one was open for 11% of the time, Pallas kernels for 4%

profile of v11, /device:TPU:1, one launch (start us, length us, event | category | flops | bytes accessed | tf_op | source)
XLA Modules:
  0.0 86.4 jit_solution(7151279079986989573)
XLA Ops:
  0.7 0.7 copy-done.22
  1.6 1.1 %fusion.3 = bf16[128,1,512]{2,0,1:T(8,128)(2,1)S(1)} fusion(bf16[32,512]{1,0:T(8,128)(2,1)} %param.19, s32[32]{0:T(128)S(1)} %get-tuple-element.92, pred[32]{0:T(512)(128)(4,1)S(1)} %get-tuple-element.91), kind=kOutput, calls=%fused_computation.6 | convolution fusion | flops 4268032 | bytes 164000 | tf_op jit(solution)/shard_map/dot_general | solution.py:230
  3.8 0.8 reduce.14
  4.6 1.0 %reshape.506 = bf16[128,2,576]{2,1,0:T(2,128)(2,1)} reshape(bf16[128,1152]{1,0:T(8,128)(2,1)S(1)} %reduce.14) | data formatting | bytes 589824
  5.7 20.8 %all-to-all-start = ((bf16[128,2,576]{2,1,0:T(2,128)(2,1)}), bf16[128,2,576]{2,1,0:T(2,128)(2,1)S(1)}, u32[]{:S(2)}, u32[]{:S(2)}) async-start(bf16[128,2,576]{2,1,0:T(2,128)(2,1)} %reshape.506), calls=%async_computation | async-start | bytes 655360 | tf_op jit(solution)/shard_map/all_to_all | solution.py:236
  26.5 0.6 copy-done.19
  27.2 0.6 select_reduce_fusion.13
  28.6 1.0 %select_reduce_fusion.3 = (bf16[128,128]{1,0:T(8,128)(2,1)S(1)}, bf16[128,128]{1,0:T(8,128)(2,1)S(1)}, bf16[128,128]{1,0:T(8,128)(2,1)S(1)}, bf16[128,128]{1,0:T(8,128)(2,1)S(1)}) fusion(bf16[32,128,128]{2,1,0:T(8,128)(2,1)S(1)} %copy-done.1, pred[32]{0:T(512)(128)(4,1)S(1)} %get-tuple-element.54, pred[32]{0:T(512)(128)(4,1)S(1)} %get-tuple-element.53, ...), kind=kLoop, calls=%fused_computation.25 | loop fusion | flops 4128768 | bytes 2228288 | tf_op jit(solution)/shard_map/reduce_sum | solution.py:191
  29.8 4.0 %collective-permute-start.1 = (bf16[272,128]{1,0:T(8,128)(2,1)S(1)}, bf16[272,128]{1,0:T(8,128)(2,1)S(1)}, u32[]{:S(2)}, u32[]{:S(2)}) collective-permute-start(bf16[272,128]{1,0:T(8,128)(2,1)S(1)} %concatenate.28), channel_id=1, source_target_pairs={{0,1},{1,2},{2,3},{3,4},{4,5},{5,6},{6,7},{7,8},{8,9},{9,10},{10,1... | collective-permute-start | bytes 208904 | tf_op jit(solution)/shard_map/ppermute | solution.py:210
  34.5 7.0 %collective-permute-start = (bf16[272,128]{1,0:T(8,128)(2,1)S(1)}, bf16[272,128]{1,0:T(8,128)(2,1)S(1)}, u32[]{:S(2)}, u32[]{:S(2)}) collective-permute-start(bf16[272,128]{1,0:T(8,128)(2,1)S(1)} %concatenate.27), channel_id=1, source_target_pairs={{0,127},{1,0},{2,1},{3,2},{4,3},{5,4},{6,5},{7,6},{8,7},{9,8},{10,... | collective-permute-start | bytes 208904 | tf_op jit(solution)/shard_map/ppermute | solution.py:213
  41.6 0.6 copy-done.15
  43.5 0.6 select_reduce_fusion.9.src_ref
  44.1 0.5 slice.123
  45.3 0.5 slice.121
  46.5 0.6 select_select_fusion.3.take_ref
  47.1 3.3 %shard_map.218 = (bf16[32,128,128]{2,1,0:T(8,128)(2,1)}, bf16[32,128,128]{2,1,0:T(8,128)(2,1)}) custom-call(s32[32]{0:T(128)} %select_reduce_fusion.9.src_ref, s32[32]{0:T(128)} %select_select_fusion.3.take_ref, bf16[32,128,128]{2,1,0:T(8,128)(2,1)} %keys_ref.1, bf16[32,128,128]{2,1,0:T(8,128)(2,1)} %values_ref.1, bf16[272,128]{1,0:T(8,128)(2,1)} %copy-done.9, ...), custom_call_target="tpu_custom_call" | custom-call | bytes 4194304 | tf_op jit(solution)/shard_map/pallas_call | solution.py:136
  50.4 0.8 slice_bitcast_fusion.3
  51.2 0.7 slice_bitcast_fusion.4
  53.9 0.7 copy-done.17
  56.2 0.7 fusion.166
  58.6 2.2 %collective-permute-start.2 = (bf16[64,512]{1,0:T(8,128)(2,1)S(1)}, bf16[64,512]{1,0:T(8,128)(2,1)S(1)}, u32[]{:S(2)}, u32[]{:S(2)}) collective-permute-start(bf16[64,512]{1,0:T(8,128)(2,1)S(1)} %convolution_convert_fusion.3), channel_id=1, source_target_pairs={{0,256},{128,384},{256,0},{384,128},{1,257},{129,385},{257,1},{385... | collective-permute-start | bytes 196616 | tf_op jit(solution)/shard_map/ppermute | solution.py:101
  61.1 2.4 %collective-permute-done.2 = bf16[64,512]{1,0:T(8,128)(2,1)S(1)} collective-permute-done((bf16[64,512]{1,0:T(8,128)(2,1)S(1)}, bf16[64,512]{1,0:T(8,128)(2,1)S(1)}, u32[]{:S(2)}, u32[]{:S(2)}) %collective-permute-start.2) | collective-permute-done | bytes 65568 | tf_op jit(solution)/shard_map/ppermute | solution.py:101
  63.6 4.6 %collective-permute-start.3 = (f32[64,512]{1,0:T(8,128)S(1)}, f32[64,512]{1,0:T(8,128)S(1)}, u32[]{:S(2)}, u32[]{:S(2)}) collective-permute-start(f32[64,512]{1,0:T(8,128)S(1)} %convert_add_fusion.1), channel_id=1, source_target_pairs={{0,128},{128,0},{256,384},{384,256},{1,129},{129,1},{257,385},{385... | collective-permute-start | bytes 393224 | tf_op jit(solution)/shard_map/ppermute | solution.py:101
  68.2 0.9 %collective-permute-done.3 = f32[64,512]{1,0:T(8,128)S(1)} collective-permute-done((f32[64,512]{1,0:T(8,128)S(1)}, f32[64,512]{1,0:T(8,128)S(1)}, u32[]{:S(2)}, u32[]{:S(2)}) %collective-permute-start.3) | collective-permute-done | bytes 131104 | tf_op jit(solution)/shard_map/ppermute | solution.py:101
  70.0 1.7 %convolution_convert_fusion.2 = bf16[64,512]{1,0:T(8,128)(2,1)S(1)} fusion(bf16[512,512]{1,0:T(8,128)(2,1)S(1)} %copy-done, bf16[512,512]{1,0:T(8,128)(2,1)} %param.33, f32[64,512]{1,0:T(8,128)S(1)} %get-tuple-element.48, f32[512]{0:T(512)S(1)} %copy-done.21, f32[64]{0:T(128)S(1)} %add_rsqrt_fusion.1, f32[64]{0:T(128)S(1)} %broadcast_multiply_fusion.1), kind=kOutput, calls=%fused_computation.7 | convolution fusion | flops 69402624 | bytes 1247744 | tf_op jit(solution)/shard_map/dot_general | solution.py:307
  71.7 2.2 %collective-permute-start.4 = (bf16[64,512]{1,0:T(8,128)(2,1)S(1)}, bf16[64,512]{1,0:T(8,128)(2,1)S(1)}, u32[]{:S(2)}, u32[]{:S(2)}) collective-permute-start(bf16[64,512]{1,0:T(8,128)(2,1)S(1)} %convolution_convert_fusion.2), channel_id=1, source_target_pairs={{0,256},{128,384},{256,0},{384,128},{1,257},{129,385},{257,1},{385... | collective-permute-start | bytes 196616 | tf_op jit(solution)/shard_map/ppermute | solution.py:101
  74.1 2.6 %collective-permute-done.4 = bf16[64,512]{1,0:T(8,128)(2,1)S(1)} collective-permute-done((bf16[64,512]{1,0:T(8,128)(2,1)S(1)}, bf16[64,512]{1,0:T(8,128)(2,1)S(1)}, u32[]{:S(2)}, u32[]{:S(2)}) %collective-permute-start.4) | collective-permute-done | bytes 65568 | tf_op jit(solution)/shard_map/ppermute | solution.py:101
  76.7 3.4 %collective-permute-start.5 = (f32[64,512]{1,0:T(8,128)S(1)}, f32[64,512]{1,0:T(8,128)S(1)}, u32[]{:S(2)}, u32[]{:S(2)}) collective-permute-start(f32[64,512]{1,0:T(8,128)S(1)} %convert_add_fusion), channel_id=1, source_target_pairs={{0,128},{128,0},{256,384},{384,256},{1,129},{129,1},{257,385},{385... | collective-permute-start | bytes 393224 | tf_op jit(solution)/shard_map/ppermute | solution.py:101
  80.2 2.6 %select_select_fusion = (bf16[32,128,128]{2,1,0:T(8,128)(2,1)}, bf16[32,128,128]{2,1,0:T(8,128)(2,1)}) fusion(bf16[32,128,128]{2,1,0:T(8,128)(2,1)S(1)} %copy-done.5, pred[32,128]{1,0:T(8,128)(4,1)S(1)} %get-tuple-element.100, pred[32,128]{1,0:T(8,128)(4,1)S(1)} %get-tuple-element.101, bf16[32,128]{1,0:T(8,128)(2,1)S(1)} %get-tuple-element.76, ...), kind=kLoop, calls=%fused_computation.20 | loop fusion | flops 2097152 | bytes 4235264 | tf_op jit(solution)/shard_map/jit(_where)/select_n | solution.py:329
  83.1 0.6 slice_bitcast_fusion
  84.4 0.7 copy-done.20
  85.6 0.8 copy.91
  (130 shorter events, 10.6 us)
Async XLA Ops:
  0.6 68.9 %copy-start = (bf16[512,512]{1,0:T(8,128)(2,1)S(1)}, bf16[512,512]{1,0:T(8,128)(2,1)}, u32[]{:S(2)}) copy-start(bf16[512,512]{1,0:T(8,128)(2,1)} %param.34) | copy-start | bytes 1572868
  0.6 0.7 copy-start.22
  1.6 1.1 %copy-start.7 = (bf16[32,512]{1,0:T(8,128)(2,1)S(1)}, bf16[32,512]{1,0:T(8,128)(2,1)}, u32[]{:S(2)}) copy-start(bf16[32,512]{1,0:T(8,128)(2,1)} %param.19) | copy-start | bytes 98308
  3.2 25.3 %copy-start.2 = (bf16[32,128,128]{2,1,0:T(8,128)(2,1)S(1)}, bf16[32,128,128]{2,1,0:T(8,128)(2,1)}, u32[]{:S(2)}) copy-start(bf16[32,128,128]{2,1,0:T(8,128)(2,1)} %values_ref.1) | copy-start | bytes 3145732
  3.3 25.3 %copy-start.1 = (bf16[32,128,128]{2,1,0:T(8,128)(2,1)S(1)}, bf16[32,128,128]{2,1,0:T(8,128)(2,1)}, u32[]{:S(2)}) copy-start(bf16[32,128,128]{2,1,0:T(8,128)(2,1)} %keys_ref.1) | copy-start | bytes 3145732
  5.7 46.3 %all-to-all-start = ((bf16[128,2,576]{2,1,0:T(2,128)(2,1)}), bf16[128,2,576]{2,1,0:T(2,128)(2,1)S(1)}, u32[]{:S(2)}, u32[]{:S(2)}) async-start(bf16[128,2,576]{2,1,0:T(2,128)(2,1)} %reshape.506), calls=%async_computation | async-start | bytes 655360 | tf_op jit(solution)/shard_map/all_to_all | solution.py:236
  26.5 0.7 copy-start.19
  28.5 1.0 %copy-start.12 = (bf16[32,512]{1,0:T(8,128)(2,1)S(1)}, bf16[32,512]{1,0:T(8,128)(2,1)}, u32[]{:S(2)}) copy-start(bf16[32,512]{1,0:T(8,128)(2,1)} %param.23) | copy-start | bytes 98308
  28.6 1.0 %copy-start.13 = (bf16[32,512]{1,0:T(8,128)(2,1)S(1)}, bf16[32,512]{1,0:T(8,128)(2,1)}, u32[]{:S(2)}) copy-start(bf16[32,512]{1,0:T(8,128)(2,1)} %param.24) | copy-start | bytes 98308
  29.8 14.3 %collective-permute-start.1 = (bf16[272,128]{1,0:T(8,128)(2,1)S(1)}, bf16[272,128]{1,0:T(8,128)(2,1)S(1)}, u32[]{:S(2)}, u32[]{:S(2)}) collective-permute-start(bf16[272,128]{1,0:T(8,128)(2,1)S(1)} %concatenate.28), channel_id=1, source_target_pairs={{0,1},{1,2},{2,3},{3,4},{4,5},{5,6},{6,7},{7,8},{8,9},{9,10},{10,1... | collective-permute-start | bytes 208904 | tf_op jit(solution)/shard_map/ppermute | solution.py:210
  34.5 10.8 %collective-permute-start = (bf16[272,128]{1,0:T(8,128)(2,1)S(1)}, bf16[272,128]{1,0:T(8,128)(2,1)S(1)}, u32[]{:S(2)}, u32[]{:S(2)}) collective-permute-start(bf16[272,128]{1,0:T(8,128)(2,1)S(1)} %concatenate.27), channel_id=1, source_target_pairs={{0,127},{1,0},{2,1},{3,2},{4,3},{5,4},{6,5},{7,6},{8,7},{9,8},{10,... | collective-permute-start | bytes 208904 | tf_op jit(solution)/shard_map/ppermute | solution.py:213
  41.5 0.7 copy-start.15
  42.2 0.7 copy-start.16
  44.1 3.0 %copy-start.9 = (bf16[272,128]{1,0:T(8,128)(2,1)}, bf16[272,128]{1,0:T(8,128)(2,1)S(1)}, u32[]{:S(2)}) copy-start(bf16[272,128]{1,0:T(8,128)(2,1)S(1)} %collective-permute-done.1.lbox_ref) | copy-start | bytes 208900
  45.3 1.8 %copy-start.10 = (bf16[272,128]{1,0:T(8,128)(2,1)}, bf16[272,128]{1,0:T(8,128)(2,1)S(1)}, u32[]{:S(2)}) copy-start(bf16[272,128]{1,0:T(8,128)(2,1)S(1)} %collective-permute-done.rbox_ref) | copy-start | bytes 208900
  52.8 1.1 %copy-start.6 = (bf16[3,512,128]{2,1,0:T(8,128)(2,1)S(1)}, bf16[3,512,128]{2,1,0:T(8,128)(2,1)}, u32[]{:S(2)}) copy-start(bf16[3,512,128]{2,1,0:T(8,128)(2,1)} %param.29) | copy-start | bytes 1179652
  53.0 0.6 copy-start.11
  53.9 0.7 copy-start.17
  54.8 1.4 %copy-start.3 = (bf16[32,128,128]{2,1,0:T(8,128)(2,1)S(1)}, bf16[32,128,128]{2,1,0:T(8,128)(2,1)}, u32[]{:S(2)}) copy-start(bf16[32,128,128]{2,1,0:T(8,128)(2,1)} %get-tuple-element.7) | copy-start | bytes 3145732
  55.9 1.6 %copy-start.5 = (bf16[32,128,128]{2,1,0:T(8,128)(2,1)S(1)}, bf16[32,128,128]{2,1,0:T(8,128)(2,1)}, u32[]{:S(2)}) copy-start(bf16[32,128,128]{2,1,0:T(8,128)(2,1)} %get-tuple-element.8) | copy-start | bytes 3145732
  57.5 0.9 %copy-start.8 = (bf16[128,512]{1,0:T(8,128)(2,1)S(1)}, bf16[128,512]{1,0:T(8,128)(2,1)}, u32[]{:S(2)}) copy-start(bf16[128,512]{1,0:T(8,128)(2,1)} %param.30) | copy-start | bytes 393220
  58.6 5.0 %collective-permute-start.2 = (bf16[64,512]{1,0:T(8,128)(2,1)S(1)}, bf16[64,512]{1,0:T(8,128)(2,1)S(1)}, u32[]{:S(2)}, u32[]{:S(2)}) collective-permute-start(bf16[64,512]{1,0:T(8,128)(2,1)S(1)} %convolution_convert_fusion.3), channel_id=1, source_target_pairs={{0,256},{128,384},{256,0},{384,128},{1,257},{129,385},{257,1},{385... | collective-permute-start | bytes 196616 | tf_op jit(solution)/shard_map/ppermute | solution.py:101
  63.6 5.6 %copy-start.14 = (f32[512]{0:T(512)S(1)}, f32[512]{0:T(512)}, u32[]{:S(2)}) copy-start(f32[512]{0:T(512)} %param.31) | copy-start | bytes 6148
  63.6 5.5 %collective-permute-start.3 = (f32[64,512]{1,0:T(8,128)S(1)}, f32[64,512]{1,0:T(8,128)S(1)}, u32[]{:S(2)}, u32[]{:S(2)}) collective-permute-start(f32[64,512]{1,0:T(8,128)S(1)} %convert_add_fusion.1), channel_id=1, source_target_pairs={{0,128},{128,0},{256,384},{384,256},{1,129},{129,1},{257,385},{385... | collective-permute-start | bytes 393224 | tf_op jit(solution)/shard_map/ppermute | solution.py:101
  69.3 0.7 copy-start.21
  71.7 5.0 %collective-permute-start.4 = (bf16[64,512]{1,0:T(8,128)(2,1)S(1)}, bf16[64,512]{1,0:T(8,128)(2,1)S(1)}, u32[]{:S(2)}, u32[]{:S(2)}) collective-permute-start(bf16[64,512]{1,0:T(8,128)(2,1)S(1)} %convolution_convert_fusion.2), channel_id=1, source_target_pairs={{0,256},{128,384},{256,0},{384,128},{1,257},{129,385},{257,1},{385... | collective-permute-start | bytes 196616 | tf_op jit(solution)/shard_map/ppermute | solution.py:101
  76.7 6.2 %collective-permute-start.5 = (f32[64,512]{1,0:T(8,128)S(1)}, f32[64,512]{1,0:T(8,128)S(1)}, u32[]{:S(2)}, u32[]{:S(2)}) collective-permute-start(f32[64,512]{1,0:T(8,128)S(1)} %convert_add_fusion), channel_id=1, source_target_pairs={{0,128},{128,0},{256,384},{384,256},{1,129},{129,1},{257,385},{385... | collective-permute-start | bytes 393224 | tf_op jit(solution)/shard_map/ppermute | solution.py:101
  80.2 2.8 %copy-start.18 = (f32[512]{0:T(512)S(1)}, f32[512]{0:T(512)}, u32[]{:S(2)}) copy-start(f32[512]{0:T(512)} %param.35) | copy-start | bytes 6148
  82.8 1.2 %copy-start.4 = (bf16[16,64,512]{2,1,0:T(8,128)(2,1)S(1)}, bf16[16,64,512]{2,1,0:T(8,128)(2,1)}, u32[]{:S(2)}) copy-start(bf16[16,64,512]{2,1,0:T(8,128)(2,1)} %param.36) | copy-start | bytes 3145732
  84.4 0.7 copy-start.20

commit v12 on v4

--- a/solution.py
+++ b/solution.py
@@ -104,14 +104,19 @@
     return total
 
 
-def cache_kernel(src_ref, take_ref, keys_ref, values_ref, lbox_ref, rbox_ref, ok_ref, ov_ref):
-    streams, window, _ = keys_ref.shape
-
-    def body(n, carry):
+def cache_kernel(src_ref, take_ref, keys_hbm, values_hbm, lbox_ref, rbox_ref, ok_ref, ov_ref, sems):
+    streams, window, _ = ok_ref.shape
+    copies = []
+    for n in range(streams):
         src = src_ref[n]
+        for which, (source, target) in enumerate(((keys_hbm, ok_ref), (values_hbm, ov_ref))):
+            copy = pltpu.make_async_copy(source.at[src], target.at[n], sems.at[which, n])
+            copy.start()
+            copies.append(copy)
+    for copy in copies:
+        copy.wait()
+    for n in range(streams):
         take = take_ref[n]
-        ok_ref[n] = keys_ref[src]
-        ov_ref[n] = values_ref[src]
 
         @pl.when(take == 1)
         def _():
@@ -123,21 +128,19 @@
             ok_ref[n] = rbox_ref[0:window]
             ov_ref[n] = rbox_ref[window : 2 * window]
 
-        return carry
-
-    lax.fori_loop(0, streams, body, 0)
-
 
 def route_caches(src, take, keys, values, lbox, rbox):
     smem = pl.BlockSpec(memory_space=pltpu.SMEM)
     vmem = pl.BlockSpec(memory_space=pltpu.VMEM)
+    hbm = pl.BlockSpec(memory_space=pl.ANY)
     shape = jax.ShapeDtypeStruct(keys.shape, keys.dtype)
     moved = 4 * keys.size * keys.dtype.itemsize
     return pl.pallas_call(
         cache_kernel,
         out_shape=(shape, shape),
-        in_specs=[smem] * 2 + [vmem] * 4,
+        in_specs=[smem, smem, hbm, hbm, vmem, vmem],
         out_specs=(vmem, vmem),
+        scratch_shapes=[pltpu.SemaphoreType.DMA((2, keys.shape[0]))],
         cost_estimate=pl.CostEstimate(flops=0, transcendentals=0, bytes_accessed=moved),
     )(src, take, keys, values, lbox, rbox)
 

time: 87 us -> 88.3 us (1.015)
  Pallas kernels: 3.5 us -> 4.62 us
    pallas_call x1, Pallas kernels: 3.5 us -> 4.62 us  [route_caches(): pl.pallas_call(cache_kernel, out_shape=(shape, shape), in_specs=[smem, sm...]
  transfers between devices with their start and end apart: 7 -> 7, of which waited for: 3 -> 3; matrix products, arithmetic and copies ran while one was open for 11% -> 11% of each run, Pallas kernels for 4% -> 5%
where the time goes in v12:
time: 88.3 us; the launch traced here: 87.4 us
  starting transfers between devices  44.2 us (50%)
  local copies, waits for them, and re-layouts  13.5 us (15%)
  other arithmetic  9.77 us (11%)
  waiting for transfers between devices  6.02 us (7%)
  matrix products  5.24 us (6%)
  Pallas kernels  4.62 us (5%)
  between operations  3.98 us (5%)
    all_to_all x1, starting transfers between devices, local(): got = lax.all_to_all(send, 'batch', split_axis=0, concat_axis=0, tiled=True)  20.8 us
    ppermute x4, starting transfers between devices, section_sum(): other = lax.ppermute(total, 'section', route)  12.4 us
    unnamed x49, local copies, waits for them, and re-layouts  8.12 us
    ppermute x1, starting transfers between devices, local(): lax.ppermute(pack(left_owner), 'batch', [(i, (i - 1) % owners) for i in r...  7.01 us
    ppermute x4, waiting for transfers between devices, section_sum(): other = lax.ppermute(total, 'section', route)  6.01 us
    pallas_call x1, Pallas kernels, route_caches(): pl.pallas_call(cache_kernel, out_shape=(shape, shape), in_specs=[smem, sm...  4.62 us
    ppermute x1, starting transfers between devices, local(): lax.ppermute(pack(right_owner), 'batch', [(i, (i + 1) % owners) for i in...  3.97 us
    select_n x1, other arithmetic, local(): jnp.where(hit_second, fresh_values[:, 1][:, None, :], jnp.where(hit_first...  2.63 us
  transfers between devices with their start and end apart: 7, of which 3 were waited for; matrix products, arithmetic and copies ran while one was open for 11% of the time, Pallas kernels for 5%

profile of v12, /device:TPU:1, one launch (start us, length us, event | category | flops | bytes accessed | tf_op | source)
XLA Modules:
  0.0 87.4 jit_solution(1199722236432465382)
XLA Ops:
  0.6 0.7 fusion.111
  1.8 0.9 copy.100
  3.5 0.8 reduce.10
  4.4 1.0 %reshape.391 = bf16[128,2,576]{2,1,0:T(2,128)(2,1)} reshape(bf16[128,1152]{1,0:T(8,128)(2,1)S(1)} %reduce.10) | data formatting | bytes 589824
  5.4 20.8 %all-to-all-start = ((bf16[128,2,576]{2,1,0:T(2,128)(2,1)}), bf16[128,2,576]{2,1,0:T(2,128)(2,1)S(1)}, u32[]{:S(2)}, u32[]{:S(2)}) async-start(bf16[128,2,576]{2,1,0:T(2,128)(2,1)} %reshape.391), calls=%async_computation | async-start | bytes 655360 | tf_op jit(solution)/shard_map/all_to_all | solution.py:239
  26.3 0.6 copy-done.19
  27.0 0.6 select_reduce_fusion.11
  28.3 1.0 %select_reduce_fusion.3 = (bf16[128,128]{1,0:T(8,128)(2,1)S(1)}, bf16[128,128]{1,0:T(8,128)(2,1)S(1)}, bf16[128,128]{1,0:T(8,128)(2,1)S(1)}, bf16[128,128]{1,0:T(8,128)(2,1)S(1)}) fusion(bf16[32,128,128]{2,1,0:T(8,128)(2,1)S(1)} %copy-done.1, pred[32]{0:T(512)(128)(4,1)S(1)} %get-tuple-element.50, pred[32]{0:T(512)(128)(4,1)S(1)} %get-tuple-element.49, ...), kind=kLoop, calls=%fused_computation.22 | loop fusion | flops 4128768 | bytes 2228288 | tf_op jit(solution)/shard_map/reduce_sum | solution.py:194
  29.5 4.0 %collective-permute-start.1 = (bf16[272,128]{1,0:T(8,128)(2,1)S(1)}, bf16[272,128]{1,0:T(8,128)(2,1)S(1)}, u32[]{:S(2)}, u32[]{:S(2)}) collective-permute-start(bf16[272,128]{1,0:T(8,128)(2,1)S(1)} %concatenate.11), channel_id=1, source_target_pairs={{0,1},{1,2},{2,3},{3,4},{4,5},{5,6},{6,7},{7,8},{8,9},{9,10},{10,1... | collective-permute-start | bytes 208904 | tf_op jit(solution)/shard_map/ppermute | solution.py:213
  34.2 7.0 %collective-permute-start = (bf16[272,128]{1,0:T(8,128)(2,1)S(1)}, bf16[272,128]{1,0:T(8,128)(2,1)S(1)}, u32[]{:S(2)}, u32[]{:S(2)}) collective-permute-start(bf16[272,128]{1,0:T(8,128)(2,1)S(1)} %concatenate.10), channel_id=1, source_target_pairs={{0,127},{1,0},{2,1},{3,2},{4,3},{5,4},{6,5},{7,6},{8,7},{9,8},{10,... | collective-permute-start | bytes 208904 | tf_op jit(solution)/shard_map/ppermute | solution.py:216
  41.3 0.6 copy-done.15
  43.2 0.6 select_reduce_fusion.9.src_ref
  43.8 0.5 slice.118
  45.1 0.5 slice.116
  46.2 0.6 select_select_fusion.3.take_ref
  46.9 4.6 %shard_map.218 = (bf16[32,128,128]{2,1,0:T(8,128)(2,1)}, bf16[32,128,128]{2,1,0:T(8,128)(2,1)}) custom-call(s32[32]{0:T(128)} %select_reduce_fusion.9.src_ref, s32[32]{0:T(128)} %select_select_fusion.3.take_ref, bf16[32,128,128]{2,1,0:T(8,128)(2,1)} %keys_hbm.1, bf16[32,128,128]{2,1,0:T(8,128)(2,1)} %values_hbm.1, bf16[272,128]{1,0:T(8,128)(2,1)} %copy-done.8, ...), custom_call_target="tpu_custom_call" | custom-call | bytes 4194304 | tf_op jit(solution)/shard_map/pallas_call | solution.py:138
  51.5 0.8 slice_bitcast_fusion.3
  52.3 0.7 slice_bitcast_fusion.4
  55.0 0.6 copy-done.17
  57.3 0.7 fusion.157
  59.6 2.2 %collective-permute-start.2 = (bf16[64,512]{1,0:T(8,128)(2,1)S(1)}, bf16[64,512]{1,0:T(8,128)(2,1)S(1)}, u32[]{:S(2)}, u32[]{:S(2)}) collective-permute-start(bf16[64,512]{1,0:T(8,128)(2,1)S(1)} %convolution_convert_fusion.3), channel_id=1, source_target_pairs={{0,256},{128,384},{256,0},{384,128},{1,257},{129,385},{257,1},{385... | collective-permute-start | bytes 196616 | tf_op jit(solution)/shard_map/ppermute | solution.py:101
  62.2 2.4 %collective-permute-done.2 = bf16[64,512]{1,0:T(8,128)(2,1)S(1)} collective-permute-done((bf16[64,512]{1,0:T(8,128)(2,1)S(1)}, bf16[64,512]{1,0:T(8,128)(2,1)S(1)}, u32[]{:S(2)}, u32[]{:S(2)}) %collective-permute-start.2) | collective-permute-done | bytes 65568 | tf_op jit(solution)/shard_map/ppermute | solution.py:101
  64.7 4.6 %collective-permute-start.3 = (f32[64,512]{1,0:T(8,128)S(1)}, f32[64,512]{1,0:T(8,128)S(1)}, u32[]{:S(2)}, u32[]{:S(2)}) collective-permute-start(f32[64,512]{1,0:T(8,128)S(1)} %convert_add_fusion.1), channel_id=1, source_target_pairs={{0,128},{128,0},{256,384},{384,256},{1,129},{129,1},{257,385},{385... | collective-permute-start | bytes 393224 | tf_op jit(solution)/shard_map/ppermute | solution.py:101
  69.2 0.9 %collective-permute-done.3 = f32[64,512]{1,0:T(8,128)S(1)} collective-permute-done((f32[64,512]{1,0:T(8,128)S(1)}, f32[64,512]{1,0:T(8,128)S(1)}, u32[]{:S(2)}, u32[]{:S(2)}) %collective-permute-start.3) | collective-permute-done | bytes 131104 | tf_op jit(solution)/shard_map/ppermute | solution.py:101
  71.0 1.7 %convolution_convert_fusion.1 = bf16[64,512]{1,0:T(8,128)(2,1)S(1)} fusion(bf16[512,512]{1,0:T(8,128)(2,1)S(1)} %copy-done, bf16[512,512]{1,0:T(8,128)(2,1)} %param.33, f32[64,512]{1,0:T(8,128)S(1)} %get-tuple-element.44, f32[512]{0:T(512)S(1)} %copy-done.21, f32[64]{0:T(128)S(1)} %add_rsqrt_fusion.1, f32[64]{0:T(128)S(1)} %broadcast_multiply_fusion.1), kind=kOutput, calls=%fused_computation.4 | convolution fusion | flops 69402624 | bytes 1247744 | tf_op jit(solution)/shard_map/dot_general | solution.py:307
  72.7 2.2 %collective-permute-start.4 = (bf16[64,512]{1,0:T(8,128)(2,1)S(1)}, bf16[64,512]{1,0:T(8,128)(2,1)S(1)}, u32[]{:S(2)}, u32[]{:S(2)}) collective-permute-start(bf16[64,512]{1,0:T(8,128)(2,1)S(1)} %convolution_convert_fusion.1), channel_id=1, source_target_pairs={{0,256},{128,384},{256,0},{384,128},{1,257},{129,385},{257,1},{385... | collective-permute-start | bytes 196616 | tf_op jit(solution)/shard_map/ppermute | solution.py:101
  75.1 2.6 %collective-permute-done.4 = bf16[64,512]{1,0:T(8,128)(2,1)S(1)} collective-permute-done((bf16[64,512]{1,0:T(8,128)(2,1)S(1)}, bf16[64,512]{1,0:T(8,128)(2,1)S(1)}, u32[]{:S(2)}, u32[]{:S(2)}) %collective-permute-start.4) | collective-permute-done | bytes 65568 | tf_op jit(solution)/shard_map/ppermute | solution.py:101
  77.8 3.4 %collective-permute-start.5 = (f32[64,512]{1,0:T(8,128)S(1)}, f32[64,512]{1,0:T(8,128)S(1)}, u32[]{:S(2)}, u32[]{:S(2)}) collective-permute-start(f32[64,512]{1,0:T(8,128)S(1)} %convert_add_fusion), channel_id=1, source_target_pairs={{0,128},{128,0},{256,384},{384,256},{1,129},{129,1},{257,385},{385... | collective-permute-start | bytes 393224 | tf_op jit(solution)/shard_map/ppermute | solution.py:101
  81.2 2.6 %select_select_fusion = (bf16[32,128,128]{2,1,0:T(8,128)(2,1)}, bf16[32,128,128]{2,1,0:T(8,128)(2,1)}) fusion(bf16[32,128,128]{2,1,0:T(8,128)(2,1)S(1)} %copy-done.5, pred[32,128]{1,0:T(8,128)(4,1)S(1)} %get-tuple-element.94, pred[32,128]{1,0:T(8,128)(4,1)S(1)} %get-tuple-element.95, bf16[32,128]{1,0:T(8,128)(2,1)S(1)} %get-tuple-element.72, ...), kind=kLoop, calls=%fused_computation.17 | loop fusion | flops 2097152 | bytes 4235264 | tf_op jit(solution)/shard_map/jit(_where)/select_n | solution.py:329
  84.1 0.6 slice_bitcast_fusion
  85.4 0.7 copy-done.20
  86.6 0.8 copy.95
  (128 shorter events, 10.7 us)
Async XLA Ops:
  0.6 69.9 %copy-start = (bf16[512,512]{1,0:T(8,128)(2,1)S(1)}, bf16[512,512]{1,0:T(8,128)(2,1)}, u32[]{:S(2)}) copy-start(bf16[512,512]{1,0:T(8,128)(2,1)} %param.34) | copy-start | bytes 1572868
  1.8 0.9 %copy-start.10 = (bf16[32,512]{1,0:T(8,128)(2,1)S(1)}, bf16[32,512]{1,0:T(8,128)(2,1)}, u32[]{:S(2)}) copy-start(bf16[32,512]{1,0:T(8,128)(2,1)} %param.19) | copy-start | bytes 98308
  3.0 25.3 %copy-start.2 = (bf16[32,128,128]{2,1,0:T(8,128)(2,1)S(1)}, bf16[32,128,128]{2,1,0:T(8,128)(2,1)}, u32[]{:S(2)}) copy-start(bf16[32,128,128]{2,1,0:T(8,128)(2,1)} %values_hbm.1) | copy-start | bytes 3145732
  3.0 25.3 %copy-start.1 = (bf16[32,128,128]{2,1,0:T(8,128)(2,1)S(1)}, bf16[32,128,128]{2,1,0:T(8,128)(2,1)}, u32[]{:S(2)}) copy-start(bf16[32,128,128]{2,1,0:T(8,128)(2,1)} %keys_hbm.1) | copy-start | bytes 3145732
  5.4 47.6 %all-to-all-start = ((bf16[128,2,576]{2,1,0:T(2,128)(2,1)}), bf16[128,2,576]{2,1,0:T(2,128)(2,1)S(1)}, u32[]{:S(2)}, u32[]{:S(2)}) async-start(bf16[128,2,576]{2,1,0:T(2,128)(2,1)} %reshape.391), calls=%async_computation | async-start | bytes 655360 | tf_op jit(solution)/shard_map/all_to_all | solution.py:239
  26.3 0.7 copy-start.19
  28.3 1.0 %copy-start.12 = (bf16[32,512]{1,0:T(8,128)(2,1)S(1)}, bf16[32,512]{1,0:T(8,128)(2,1)}, u32[]{:S(2)}) copy-start(bf16[32,512]{1,0:T(8,128)(2,1)} %param.23) | copy-start | bytes 98308
  28.3 1.0 %copy-start.13 = (bf16[32,512]{1,0:T(8,128)(2,1)S(1)}, bf16[32,512]{1,0:T(8,128)(2,1)}, u32[]{:S(2)}) copy-start(bf16[32,512]{1,0:T(8,128)(2,1)} %param.24) | copy-start | bytes 98308
  29.5 14.3 %collective-permute-start.1 = (bf16[272,128]{1,0:T(8,128)(2,1)S(1)}, bf16[272,128]{1,0:T(8,128)(2,1)S(1)}, u32[]{:S(2)}, u32[]{:S(2)}) collective-permute-start(bf16[272,128]{1,0:T(8,128)(2,1)S(1)} %concatenate.11), channel_id=1, source_target_pairs={{0,1},{1,2},{2,3},{3,4},{4,5},{5,6},{6,7},{7,8},{8,9},{9,10},{10,1... | collective-permute-start | bytes 208904 | tf_op jit(solution)/shard_map/ppermute | solution.py:213
  34.2 10.8 %collective-permute-start = (bf16[272,128]{1,0:T(8,128)(2,1)S(1)}, bf16[272,128]{1,0:T(8,128)(2,1)S(1)}, u32[]{:S(2)}, u32[]{:S(2)}) collective-permute-start(bf16[272,128]{1,0:T(8,128)(2,1)S(1)} %concatenate.10), channel_id=1, source_target_pairs={{0,127},{1,0},{2,1},{3,2},{4,3},{5,4},{6,5},{7,6},{8,7},{9,8},{10,... | collective-permute-start | bytes 208904 | tf_op jit(solution)/shard_map/ppermute | solution.py:216
  41.3 0.7 copy-start.15
  41.9 0.7 copy-start.16
  43.8 3.0 %copy-start.8 = (bf16[272,128]{1,0:T(8,128)(2,1)}, bf16[272,128]{1,0:T(8,128)(2,1)S(1)}, u32[]{:S(2)}) copy-start(bf16[272,128]{1,0:T(8,128)(2,1)S(1)} %collective-permute-done.1.lbox_ref) | copy-start | bytes 208900
  45.1 1.8 %copy-start.9 = (bf16[272,128]{1,0:T(8,128)(2,1)}, bf16[272,128]{1,0:T(8,128)(2,1)S(1)}, u32[]{:S(2)}) copy-start(bf16[272,128]{1,0:T(8,128)(2,1)S(1)} %collective-permute-done.rbox_ref) | copy-start | bytes 208900
  54.0 0.6 copy-start.11
  54.0 1.0 %copy-start.6 = (bf16[3,512,128]{2,1,0:T(8,128)(2,1)S(1)}, bf16[3,512,128]{2,1,0:T(8,128)(2,1)}, u32[]{:S(2)}) copy-start(bf16[3,512,128]{2,1,0:T(8,128)(2,1)} %param.29) | copy-start | bytes 1179652
  54.9 0.7 copy-start.17
  55.9 1.4 %copy-start.3 = (bf16[32,128,128]{2,1,0:T(8,128)(2,1)S(1)}, bf16[32,128,128]{2,1,0:T(8,128)(2,1)}, u32[]{:S(2)}) copy-start(bf16[32,128,128]{2,1,0:T(8,128)(2,1)} %get-tuple-element.7) | copy-start | bytes 3145732
  56.9 1.6 %copy-start.5 = (bf16[32,128,128]{2,1,0:T(8,128)(2,1)S(1)}, bf16[32,128,128]{2,1,0:T(8,128)(2,1)}, u32[]{:S(2)}) copy-start(bf16[32,128,128]{2,1,0:T(8,128)(2,1)} %get-tuple-element.8) | copy-start | bytes 3145732
  58.6 0.9 %copy-start.7 = (bf16[128,512]{1,0:T(8,128)(2,1)S(1)}, bf16[128,512]{1,0:T(8,128)(2,1)}, u32[]{:S(2)}) copy-start(bf16[128,512]{1,0:T(8,128)(2,1)} %param.30) | copy-start | bytes 393220
  59.6 5.0 %collective-permute-start.2 = (bf16[64,512]{1,0:T(8,128)(2,1)S(1)}, bf16[64,512]{1,0:T(8,128)(2,1)S(1)}, u32[]{:S(2)}, u32[]{:S(2)}) collective-permute-start(bf16[64,512]{1,0:T(8,128)(2,1)S(1)} %convolution_convert_fusion.3), channel_id=1, source_target_pairs={{0,256},{128,384},{256,0},{384,128},{1,257},{129,385},{257,1},{385... | collective-permute-start | bytes 196616 | tf_op jit(solution)/shard_map/ppermute | solution.py:101
  64.6 5.6 %copy-start.14 = (f32[512]{0:T(512)S(1)}, f32[512]{0:T(512)}, u32[]{:S(2)}) copy-start(f32[512]{0:T(512)} %param.31) | copy-start | bytes 6148
  64.7 5.5 %collective-permute-start.3 = (f32[64,512]{1,0:T(8,128)S(1)}, f32[64,512]{1,0:T(8,128)S(1)}, u32[]{:S(2)}, u32[]{:S(2)}) collective-permute-start(f32[64,512]{1,0:T(8,128)S(1)} %convert_add_fusion.1), channel_id=1, source_target_pairs={{0,128},{128,0},{256,384},{384,256},{1,129},{129,1},{257,385},{385... | collective-permute-start | bytes 393224 | tf_op jit(solution)/shard_map/ppermute | solution.py:101
  70.3 0.7 copy-start.21
  72.7 5.0 %collective-permute-start.4 = (bf16[64,512]{1,0:T(8,128)(2,1)S(1)}, bf16[64,512]{1,0:T(8,128)(2,1)S(1)}, u32[]{:S(2)}, u32[]{:S(2)}) collective-permute-start(bf16[64,512]{1,0:T(8,128)(2,1)S(1)} %convolution_convert_fusion.1), channel_id=1, source_target_pairs={{0,256},{128,384},{256,0},{384,128},{1,257},{129,385},{257,1},{385... | collective-permute-start | bytes 196616 | tf_op jit(solution)/shard_map/ppermute | solution.py:101
  77.8 6.2 %collective-permute-start.5 = (f32[64,512]{1,0:T(8,128)S(1)}, f32[64,512]{1,0:T(8,128)S(1)}, u32[]{:S(2)}, u32[]{:S(2)}) collective-permute-start(f32[64,512]{1,0:T(8,128)S(1)} %convert_add_fusion), channel_id=1, source_target_pairs={{0,128},{128,0},{256,384},{384,256},{1,129},{129,1},{257,385},{385... | collective-permute-start | bytes 393224 | tf_op jit(solution)/shard_map/ppermute | solution.py:101
  81.2 2.8 %copy-start.18 = (f32[512]{0:T(512)S(1)}, f32[512]{0:T(512)}, u32[]{:S(2)}) copy-start(f32[512]{0:T(512)} %param.35) | copy-start | bytes 6148
  83.8 1.2 %copy-start.4 = (bf16[16,64,512]{2,1,0:T(8,128)(2,1)S(1)}, bf16[16,64,512]{2,1,0:T(8,128)(2,1)}, u32[]{:S(2)}) copy-start(bf16[16,64,512]{2,1,0:T(8,128)(2,1)} %param.36) | copy-start | bytes 3145732
  85.4 0.7 copy-start.20

commit v13 on v4

--- a/solution.py
+++ b/solution.py
@@ -95,12 +95,12 @@
     if size & (size - 1):
         return lax.psum(partial.astype(jnp.bfloat16), "section").astype(jnp.float32)
     total = partial.astype(jnp.bfloat16)
-    bit = size // 2
-    while bit >= 1:
+    bit = 1
+    while bit < size:
         route = [(i, i ^ bit) for i in range(size)]
         other = lax.ppermute(total, "section", route)
         total = total.astype(jnp.float32) + other.astype(jnp.float32)
-        bit //= 2
+        bit *= 2
     return total
 
 

time: 87 us -> 86.5 us (level)
  starting transfers between devices: 44.2 us -> 42.8 us
  waiting for transfers between devices: 6.02 us -> 7.31 us
    ppermute x4, starting transfers between devices: 12.4 us -> 11 us  [section_sum(): other = lax.ppermute(total, 'section', route)]
    ppermute x4, waiting for transfers between devices: 6.01 us -> 7.3 us  [section_sum(): other = lax.ppermute(total, 'section', route)]
  transfers between devices with their start and end apart: 7 -> 7, of which waited for: 3 -> 4; matrix products, arithmetic and copies ran while one was open for 11% -> 11% of each run, Pallas kernels for 4% -> 4%
where the time goes in v13:
time: 86.5 us; the launch traced here: 85.8 us
  starting transfers between devices  42.8 us (49%)
  local copies, waits for them, and re-layouts  13.2 us (15%)
  other arithmetic  9.77 us (11%)
  waiting for transfers between devices  7.31 us (8%)
  matrix products  5.24 us (6%)
  between operations  3.95 us (5%)
  Pallas kernels  3.5 us (4%)
    all_to_all x1, starting transfers between devices, local(): got = lax.all_to_all(send, 'batch', split_axis=0, concat_axis=0, tiled=True)  20.8 us
    ppermute x4, starting transfers between devices, section_sum(): other = lax.ppermute(total, 'section', route)  11 us
    unnamed x49, local copies, waits for them, and re-layouts  7.82 us
    ppermute x4, waiting for transfers between devices, section_sum(): other = lax.ppermute(total, 'section', route)  7.3 us
    ppermute x1, starting transfers between devices, local(): lax.ppermute(pack(left_owner), 'batch', [(i, (i - 1) % owners) for i in r...  7.01 us
    ppermute x1, starting transfers between devices, local(): lax.ppermute(pack(right_owner), 'batch', [(i, (i + 1) % owners) for i in...  3.97 us
    pallas_call x1, Pallas kernels, route_caches(): pl.pallas_call(cache_kernel, out_shape=(shape, shape), in_specs=[smem] *...  3.5 us
    select_n x1, other arithmetic, local(): jnp.where(hit_second, fresh_values[:, 1][:, None, :], jnp.where(hit_first...  2.63 us
  transfers between devices with their start and end apart: 7, of which 4 were waited for; matrix products, arithmetic and copies ran while one was open for 11% of the time, Pallas kernels for 4%

profile of v13, /device:TPU:1, one launch (start us, length us, event | category | flops | bytes accessed | tf_op | source)
XLA Modules:
  0.0 85.8 jit_solution(576879266718543017)
XLA Ops:
  0.6 0.7 fusion.111
  1.8 0.9 %copy.100 = bf16[128,2,1]{1,0,2:T(8,128)(2,1)S(1)} copy(bf16[128,2,1]{2,1,0:T(2,128)(2,1)S(1)} %bitcast.105) | data formatting | bytes 1024
  3.5 0.8 reduce.10
  4.4 1.0 %reshape.391 = bf16[128,2,576]{2,1,0:T(2,128)(2,1)} reshape(bf16[128,1152]{1,0:T(8,128)(2,1)S(1)} %reduce.10) | data formatting | bytes 589824
  5.4 20.8 %all-to-all-start = ((bf16[128,2,576]{2,1,0:T(2,128)(2,1)}), bf16[128,2,576]{2,1,0:T(2,128)(2,1)S(1)}, u32[]{:S(2)}, u32[]{:S(2)}) async-start(bf16[128,2,576]{2,1,0:T(2,128)(2,1)} %reshape.391), calls=%async_computation | async-start | bytes 655360 | tf_op jit(solution)/shard_map/all_to_all | solution.py:236
  26.3 0.6 copy-done.19
  27.0 0.6 select_reduce_fusion.11
  28.3 1.0 %select_reduce_fusion.3 = (bf16[128,128]{1,0:T(8,128)(2,1)S(1)}, bf16[128,128]{1,0:T(8,128)(2,1)S(1)}, bf16[128,128]{1,0:T(8,128)(2,1)S(1)}, bf16[128,128]{1,0:T(8,128)(2,1)S(1)}) fusion(bf16[32,128,128]{2,1,0:T(8,128)(2,1)S(1)} %copy-done.1, pred[32]{0:T(512)(128)(4,1)S(1)} %get-tuple-element.50, pred[32]{0:T(512)(128)(4,1)S(1)} %get-tuple-element.49, ...), kind=kLoop, calls=%fused_computation.22 | loop fusion | flops 4128768 | bytes 2228288 | tf_op jit(solution)/shard_map/reduce_sum | solution.py:191
  29.5 4.0 %collective-permute-start.1 = (bf16[272,128]{1,0:T(8,128)(2,1)S(1)}, bf16[272,128]{1,0:T(8,128)(2,1)S(1)}, u32[]{:S(2)}, u32[]{:S(2)}) collective-permute-start(bf16[272,128]{1,0:T(8,128)(2,1)S(1)} %concatenate.11), channel_id=1, source_target_pairs={{0,1},{1,2},{2,3},{3,4},{4,5},{5,6},{6,7},{7,8},{8,9},{9,10},{10,1... | collective-permute-start | bytes 208904 | tf_op jit(solution)/shard_map/ppermute | solution.py:210
  34.2 7.0 %collective-permute-start = (bf16[272,128]{1,0:T(8,128)(2,1)S(1)}, bf16[272,128]{1,0:T(8,128)(2,1)S(1)}, u32[]{:S(2)}, u32[]{:S(2)}) collective-permute-start(bf16[272,128]{1,0:T(8,128)(2,1)S(1)} %concatenate.10), channel_id=1, source_target_pairs={{0,127},{1,0},{2,1},{3,2},{4,3},{5,4},{6,5},{7,6},{8,7},{9,8},{10,... | collective-permute-start | bytes 208904 | tf_op jit(solution)/shard_map/ppermute | solution.py:213
  41.3 0.6 copy-done.15
  43.2 0.6 select_reduce_fusion.9.src_ref
  43.8 0.5 slice.118
  46.2 0.6 select_select_fusion.3.take_ref
  46.9 3.5 %shard_map.218 = (bf16[32,128,128]{2,1,0:T(8,128)(2,1)}, bf16[32,128,128]{2,1,0:T(8,128)(2,1)}) custom-call(s32[32]{0:T(128)} %select_reduce_fusion.9.src_ref, s32[32]{0:T(128)} %select_select_fusion.3.take_ref, bf16[32,128,128]{2,1,0:T(8,128)(2,1)} %keys_ref.1, bf16[32,128,128]{2,1,0:T(8,128)(2,1)} %values_ref.1, bf16[272,128]{1,0:T(8,128)(2,1)} %copy-done.8, ...), custom_call_target="tpu_custom_call" | custom-call | bytes 4194304 | tf_op jit(solution)/shard_map/pallas_call | solution.py:136
  50.4 0.8 slice_bitcast_fusion.3
  51.1 0.7 slice_bitcast_fusion.4
  53.9 0.6 copy-done.17
  56.1 0.7 fusion.157
  58.5 3.4 %collective-permute-start.2 = (bf16[64,512]{1,0:T(8,128)(2,1)S(1)}, bf16[64,512]{1,0:T(8,128)(2,1)S(1)}, u32[]{:S(2)}, u32[]{:S(2)}) collective-permute-start(bf16[64,512]{1,0:T(8,128)(2,1)S(1)} %convolution_convert_fusion.3), channel_id=1, source_target_pairs={{0,128},{128,0},{256,384},{384,256},{1,129},{129,1},{257,385},{385... | collective-permute-start | bytes 196616 | tf_op jit(solution)/shard_map/ppermute | solution.py:101
  62.2 0.5 collective-permute-done.2
  62.8 2.2 %collective-permute-start.3 = (f32[64,512]{1,0:T(8,128)S(1)}, f32[64,512]{1,0:T(8,128)S(1)}, u32[]{:S(2)}, u32[]{:S(2)}) collective-permute-start(f32[64,512]{1,0:T(8,128)S(1)} %convert_add_fusion.1), channel_id=1, source_target_pairs={{0,256},{128,384},{256,0},{384,128},{1,257},{129,385},{257,1},{385... | collective-permute-start | bytes 393224 | tf_op jit(solution)/shard_map/ppermute | solution.py:101
  65.1 4.4 %collective-permute-done.3 = f32[64,512]{1,0:T(8,128)S(1)} collective-permute-done((f32[64,512]{1,0:T(8,128)S(1)}, f32[64,512]{1,0:T(8,128)S(1)}, u32[]{:S(2)}, u32[]{:S(2)}) %collective-permute-start.3) | collective-permute-done | bytes 131104 | tf_op jit(solution)/shard_map/ppermute | solution.py:101
  70.3 1.7 %convolution_convert_fusion.1 = bf16[64,512]{1,0:T(8,128)(2,1)S(1)} fusion(bf16[512,512]{1,0:T(8,128)(2,1)S(1)} %copy-done, bf16[512,512]{1,0:T(8,128)(2,1)} %param.33, f32[64,512]{1,0:T(8,128)S(1)} %get-tuple-element.44, f32[512]{0:T(512)S(1)} %copy-done.21, f32[64]{0:T(128)S(1)} %add_rsqrt_fusion.1, f32[64]{0:T(128)S(1)} %broadcast_multiply_fusion.1), kind=kOutput, calls=%fused_computation.4 | convolution fusion | flops 69402624 | bytes 1247744 | tf_op jit(solution)/shard_map/dot_general | solution.py:304
  72.0 3.1 %collective-permute-start.4 = (bf16[64,512]{1,0:T(8,128)(2,1)S(1)}, bf16[64,512]{1,0:T(8,128)(2,1)S(1)}, u32[]{:S(2)}, u32[]{:S(2)}) collective-permute-start(bf16[64,512]{1,0:T(8,128)(2,1)S(1)} %convolution_convert_fusion.1), channel_id=1, source_target_pairs={{0,128},{128,0},{256,384},{384,256},{1,129},{129,1},{257,385},{385... | collective-permute-start | bytes 196616 | tf_op jit(solution)/shard_map/ppermute | solution.py:101
  75.2 0.7 collective-permute-done.4
  76.0 2.2 %collective-permute-start.5 = (f32[64,512]{1,0:T(8,128)S(1)}, f32[64,512]{1,0:T(8,128)S(1)}, u32[]{:S(2)}, u32[]{:S(2)}) collective-permute-start(f32[64,512]{1,0:T(8,128)S(1)} %convert_add_fusion), channel_id=1, source_target_pairs={{0,256},{128,384},{256,0},{384,128},{1,257},{129,385},{257,1},{385... | collective-permute-start | bytes 393224 | tf_op jit(solution)/shard_map/ppermute | solution.py:101
  78.2 2.6 %select_select_fusion = (bf16[32,128,128]{2,1,0:T(8,128)(2,1)}, bf16[32,128,128]{2,1,0:T(8,128)(2,1)}) fusion(bf16[32,128,128]{2,1,0:T(8,128)(2,1)S(1)} %copy-done.5, pred[32,128]{1,0:T(8,128)(4,1)S(1)} %get-tuple-element.94, pred[32,128]{1,0:T(8,128)(4,1)S(1)} %get-tuple-element.95, bf16[32,128]{1,0:T(8,128)(2,1)S(1)} %get-tuple-element.72, ...), kind=kLoop, calls=%fused_computation.17 | loop fusion | flops 2097152 | bytes 4235264 | tf_op jit(solution)/shard_map/jit(_where)/select_n | solution.py:326
  80.9 1.7 %collective-permute-done.5 = f32[64,512]{1,0:T(8,128)S(1)} collective-permute-done((f32[64,512]{1,0:T(8,128)S(1)}, f32[64,512]{1,0:T(8,128)S(1)}, u32[]{:S(2)}, u32[]{:S(2)}) %collective-permute-start.5) | collective-permute-done | bytes 131104 | tf_op jit(solution)/shard_map/ppermute | solution.py:101
  82.8 0.6 slice_bitcast_fusion
  83.8 0.7 copy-done.20
  85.0 0.8 copy.95
  (128 shorter events, 10.9 us)
Async XLA Ops:
  0.6 69.1 %copy-start = (bf16[512,512]{1,0:T(8,128)(2,1)S(1)}, bf16[512,512]{1,0:T(8,128)(2,1)}, u32[]{:S(2)}) copy-start(bf16[512,512]{1,0:T(8,128)(2,1)} %param.34) | copy-start | bytes 1572868
  1.8 0.9 %copy-start.10 = (bf16[32,512]{1,0:T(8,128)(2,1)S(1)}, bf16[32,512]{1,0:T(8,128)(2,1)}, u32[]{:S(2)}) copy-start(bf16[32,512]{1,0:T(8,128)(2,1)} %param.19) | copy-start | bytes 98308
  3.0 25.3 %copy-start.2 = (bf16[32,128,128]{2,1,0:T(8,128)(2,1)S(1)}, bf16[32,128,128]{2,1,0:T(8,128)(2,1)}, u32[]{:S(2)}) copy-start(bf16[32,128,128]{2,1,0:T(8,128)(2,1)} %values_ref.1) | copy-start | bytes 3145732
  3.0 25.3 %copy-start.1 = (bf16[32,128,128]{2,1,0:T(8,128)(2,1)S(1)}, bf16[32,128,128]{2,1,0:T(8,128)(2,1)}, u32[]{:S(2)}) copy-start(bf16[32,128,128]{2,1,0:T(8,128)(2,1)} %keys_ref.1) | copy-start | bytes 3145732
  5.4 46.4 %all-to-all-start = ((bf16[128,2,576]{2,1,0:T(2,128)(2,1)}), bf16[128,2,576]{2,1,0:T(2,128)(2,1)S(1)}, u32[]{:S(2)}, u32[]{:S(2)}) async-start(bf16[128,2,576]{2,1,0:T(2,128)(2,1)} %reshape.391), calls=%async_computation | async-start | bytes 655360 | tf_op jit(solution)/shard_map/all_to_all | solution.py:236
  26.3 0.7 copy-start.19
  28.3 1.0 %copy-start.12 = (bf16[32,512]{1,0:T(8,128)(2,1)S(1)}, bf16[32,512]{1,0:T(8,128)(2,1)}, u32[]{:S(2)}) copy-start(bf16[32,512]{1,0:T(8,128)(2,1)} %param.23) | copy-start | bytes 98308
  28.3 1.0 %copy-start.13 = (bf16[32,512]{1,0:T(8,128)(2,1)S(1)}, bf16[32,512]{1,0:T(8,128)(2,1)}, u32[]{:S(2)}) copy-start(bf16[32,512]{1,0:T(8,128)(2,1)} %param.24) | copy-start | bytes 98308
  29.5 14.3 %collective-permute-start.1 = (bf16[272,128]{1,0:T(8,128)(2,1)S(1)}, bf16[272,128]{1,0:T(8,128)(2,1)S(1)}, u32[]{:S(2)}, u32[]{:S(2)}) collective-permute-start(bf16[272,128]{1,0:T(8,128)(2,1)S(1)} %concatenate.11), channel_id=1, source_target_pairs={{0,1},{1,2},{2,3},{3,4},{4,5},{5,6},{6,7},{7,8},{8,9},{9,10},{10,1... | collective-permute-start | bytes 208904 | tf_op jit(solution)/shard_map/ppermute | solution.py:210
  34.2 10.8 %collective-permute-start = (bf16[272,128]{1,0:T(8,128)(2,1)S(1)}, bf16[272,128]{1,0:T(8,128)(2,1)S(1)}, u32[]{:S(2)}, u32[]{:S(2)}) collective-permute-start(bf16[272,128]{1,0:T(8,128)(2,1)S(1)} %concatenate.10), channel_id=1, source_target_pairs={{0,127},{1,0},{2,1},{3,2},{4,3},{5,4},{6,5},{7,6},{8,7},{9,8},{10,... | collective-permute-start | bytes 208904 | tf_op jit(solution)/shard_map/ppermute | solution.py:213
  41.3 0.7 copy-start.15
  41.9 0.7 copy-start.16
  43.8 3.0 %copy-start.8 = (bf16[272,128]{1,0:T(8,128)(2,1)}, bf16[272,128]{1,0:T(8,128)(2,1)S(1)}, u32[]{:S(2)}) copy-start(bf16[272,128]{1,0:T(8,128)(2,1)S(1)} %collective-permute-done.1.lbox_ref) | copy-start | bytes 208900
  45.1 1.8 %copy-start.9 = (bf16[272,128]{1,0:T(8,128)(2,1)}, bf16[272,128]{1,0:T(8,128)(2,1)S(1)}, u32[]{:S(2)}) copy-start(bf16[272,128]{1,0:T(8,128)(2,1)S(1)} %collective-permute-done.rbox_ref) | copy-start | bytes 208900
  52.8 0.6 copy-start.11
  52.8 1.0 %copy-start.6 = (bf16[3,512,128]{2,1,0:T(8,128)(2,1)S(1)}, bf16[3,512,128]{2,1,0:T(8,128)(2,1)}, u32[]{:S(2)}) copy-start(bf16[3,512,128]{2,1,0:T(8,128)(2,1)} %param.29) | copy-start | bytes 1179652
  53.7 0.7 copy-start.17
  54.7 1.4 %copy-start.3 = (bf16[32,128,128]{2,1,0:T(8,128)(2,1)S(1)}, bf16[32,128,128]{2,1,0:T(8,128)(2,1)}, u32[]{:S(2)}) copy-start(bf16[32,128,128]{2,1,0:T(8,128)(2,1)} %get-tuple-element.7) | copy-start | bytes 3145732
  55.8 1.6 %copy-start.5 = (bf16[32,128,128]{2,1,0:T(8,128)(2,1)S(1)}, bf16[32,128,128]{2,1,0:T(8,128)(2,1)}, u32[]{:S(2)}) copy-start(bf16[32,128,128]{2,1,0:T(8,128)(2,1)} %get-tuple-element.8) | copy-start | bytes 3145732
  57.4 0.9 %copy-start.7 = (bf16[128,512]{1,0:T(8,128)(2,1)S(1)}, bf16[128,512]{1,0:T(8,128)(2,1)}, u32[]{:S(2)}) copy-start(bf16[128,512]{1,0:T(8,128)(2,1)} %param.30) | copy-start | bytes 393220
  58.5 4.3 %collective-permute-start.2 = (bf16[64,512]{1,0:T(8,128)(2,1)S(1)}, bf16[64,512]{1,0:T(8,128)(2,1)S(1)}, u32[]{:S(2)}, u32[]{:S(2)}) collective-permute-start(bf16[64,512]{1,0:T(8,128)(2,1)S(1)} %convolution_convert_fusion.3), channel_id=1, source_target_pairs={{0,128},{128,0},{256,384},{384,256},{1,129},{129,1},{257,385},{385... | collective-permute-start | bytes 196616 | tf_op jit(solution)/shard_map/ppermute | solution.py:101
  62.8 6.6 %copy-start.14 = (f32[512]{0:T(512)S(1)}, f32[512]{0:T(512)}, u32[]{:S(2)}) copy-start(f32[512]{0:T(512)} %param.31) | copy-start | bytes 6148
  62.8 6.6 %collective-permute-start.3 = (f32[64,512]{1,0:T(8,128)S(1)}, f32[64,512]{1,0:T(8,128)S(1)}, u32[]{:S(2)}, u32[]{:S(2)}) collective-permute-start(f32[64,512]{1,0:T(8,128)S(1)} %convert_add_fusion.1), channel_id=1, source_target_pairs={{0,256},{128,384},{256,0},{384,128},{1,257},{129,385},{257,1},{385... | collective-permute-start | bytes 393224 | tf_op jit(solution)/shard_map/ppermute | solution.py:101
  69.6 0.7 copy-start.21
  72.0 4.0 %collective-permute-start.4 = (bf16[64,512]{1,0:T(8,128)(2,1)S(1)}, bf16[64,512]{1,0:T(8,128)(2,1)S(1)}, u32[]{:S(2)}, u32[]{:S(2)}) collective-permute-start(bf16[64,512]{1,0:T(8,128)(2,1)S(1)} %convolution_convert_fusion.1), channel_id=1, source_target_pairs={{0,128},{128,0},{256,384},{384,256},{1,129},{129,1},{257,385},{385... | collective-permute-start | bytes 196616 | tf_op jit(solution)/shard_map/ppermute | solution.py:101
  76.0 6.6 %collective-permute-start.5 = (f32[64,512]{1,0:T(8,128)S(1)}, f32[64,512]{1,0:T(8,128)S(1)}, u32[]{:S(2)}, u32[]{:S(2)}) collective-permute-start(f32[64,512]{1,0:T(8,128)S(1)} %convert_add_fusion), channel_id=1, source_target_pairs={{0,256},{128,384},{256,0},{384,128},{1,257},{129,385},{257,1},{385... | collective-permute-start | bytes 393224 | tf_op jit(solution)/shard_map/ppermute | solution.py:101
  78.2 4.5 %copy-start.18 = (f32[512]{0:T(512)S(1)}, f32[512]{0:T(512)}, u32[]{:S(2)}) copy-start(f32[512]{0:T(512)} %param.35) | copy-start | bytes 6148
  80.8 2.6 %copy-start.4 = (bf16[16,64,512]{2,1,0:T(8,128)(2,1)S(1)}, bf16[16,64,512]{2,1,0:T(8,128)(2,1)}, u32[]{:S(2)}) copy-start(bf16[16,64,512]{2,1,0:T(8,128)(2,1)} %param.36) | copy-start | bytes 3145732
  83.8 0.7 copy-start.20

commit v14 on v13

--- a/solution.py
+++ b/solution.py
@@ -98,6 +98,7 @@
     bit = 1
     while bit < size:
         route = [(i, i ^ bit) for i in range(size)]
+        total = total.astype(jnp.bfloat16)
         other = lax.ppermute(total, "section", route)
         total = total.astype(jnp.float32) + other.astype(jnp.float32)
         bit *= 2

time: 86.5 us -> 83.8 us (0.969)
  waiting for transfers between devices: 7.31 us -> 4.08 us
    ppermute x4, waiting for transfers between devices: 7.3 us -> 4.07 us  [section_sum(): other = lax.ppermute(total, 'section', route)]
  transfers between devices with their start and end apart: 7 -> 7, of which waited for: 4 -> 4; matrix products, arithmetic and copies ran while one was open for 11% -> 12% of each run, Pallas kernels for 4% -> 4%
where the time goes in v14:
time: 83.8 us; the launch traced here: 83.1 us
  starting transfers between devices  43.1 us (51%)
  local copies, waits for them, and re-layouts  13.5 us (16%)
  other arithmetic  9.77 us (12%)
  matrix products  5.24 us (6%)
  waiting for transfers between devices  4.08 us (5%)
  between operations  3.95 us (5%)
  Pallas kernels  3.5 us (4%)
    all_to_all x1, starting transfers between devices, local(): got = lax.all_to_all(send, 'batch', split_axis=0, concat_axis=0, tiled=True)  20.8 us
    ppermute x4, starting transfers between devices, section_sum(): other = lax.ppermute(total, 'section', route)  11.3 us
    unnamed x49, local copies, waits for them, and re-layouts  8.08 us
    ppermute x1, starting transfers between devices, local(): lax.ppermute(pack(left_owner), 'batch', [(i, (i - 1) % owners) for i in r...  7.01 us
    ppermute x4, waiting for transfers between devices, section_sum(): other = lax.ppermute(total, 'section', route)  4.07 us
    ppermute x1, starting transfers between devices, local(): lax.ppermute(pack(right_owner), 'batch', [(i, (i + 1) % owners) for i in...  3.97 us
    pallas_call x1, Pallas kernels, route_caches(): pl.pallas_call(cache_kernel, out_shape=(shape, shape), in_specs=[smem] *...  3.5 us
    select_n x1, other arithmetic, local(): jnp.where(hit_second, fresh_values[:, 1][:, None, :], jnp.where(hit_first...  2.63 us
  transfers between devices with their start and end apart: 7, of which 4 were waited for; matrix products, arithmetic and copies ran while one was open for 12% of the time, Pallas kernels for 4%

profile of v14, /device:TPU:1, one launch (start us, length us, event | category | flops | bytes accessed | tf_op | source)
XLA Modules:
  0.0 83.1 jit_solution(2917600553326573956)
XLA Ops:
  0.6 0.7 fusion.111
  1.8 0.9 %copy.100 = bf16[128,2,1]{1,0,2:T(8,128)(2,1)S(1)} copy(bf16[128,2,1]{2,1,0:T(2,128)(2,1)S(1)} %bitcast.105) | data formatting | bytes 1024
  3.5 0.8 %reduce.10 = bf16[128,1152]{1,0:T(8,128)(2,1)S(1)} reduce(bf16[128,1,1152]{2,0,1:T(8,128)(2,1)S(1)} %fusion.13, bf16[]{:T(256)} %broadcast.446), dimensions={1}, to_apply=%copy.80.reduce_sub_computation | reduce | bytes 589826 | tf_op jit(solution)/shard_map/all_to_all | solution.py:237
  4.4 1.0 %reshape.391 = bf16[128,2,576]{2,1,0:T(2,128)(2,1)} reshape(bf16[128,1152]{1,0:T(8,128)(2,1)S(1)} %reduce.10) | data formatting | bytes 589824
  5.4 20.8 %all-to-all-start = ((bf16[128,2,576]{2,1,0:T(2,128)(2,1)}), bf16[128,2,576]{2,1,0:T(2,128)(2,1)S(1)}, u32[]{:S(2)}, u32[]{:S(2)}) async-start(bf16[128,2,576]{2,1,0:T(2,128)(2,1)} %reshape.391), calls=%async_computation | async-start | bytes 655360 | tf_op jit(solution)/shard_map/all_to_all | solution.py:237
  26.3 0.6 copy-done.19
  27.0 0.6 select_reduce_fusion.11
  28.3 1.0 %select_reduce_fusion.3 = (bf16[128,128]{1,0:T(8,128)(2,1)S(1)}, bf16[128,128]{1,0:T(8,128)(2,1)S(1)}, bf16[128,128]{1,0:T(8,128)(2,1)S(1)}, bf16[128,128]{1,0:T(8,128)(2,1)S(1)}) fusion(bf16[32,128,128]{2,1,0:T(8,128)(2,1)S(1)} %copy-done.1, pred[32]{0:T(512)(128)(4,1)S(1)} %get-tuple-element.49, pred[32]{0:T(512)(128)(4,1)S(1)} %get-tuple-element.48, ...), kind=kLoop, calls=%fused_computation.22 | loop fusion | flops 4128768 | bytes 2228288 | tf_op jit(solution)/shard_map/reduce_sum | solution.py:192
  29.5 4.0 %collective-permute-start.1 = (bf16[272,128]{1,0:T(8,128)(2,1)S(1)}, bf16[272,128]{1,0:T(8,128)(2,1)S(1)}, u32[]{:S(2)}, u32[]{:S(2)}) collective-permute-start(bf16[272,128]{1,0:T(8,128)(2,1)S(1)} %concatenate.11), channel_id=1, source_target_pairs={{0,1},{1,2},{2,3},{3,4},{4,5},{5,6},{6,7},{7,8},{8,9},{9,10},{10,1... | collective-permute-start | bytes 208904 | tf_op jit(solution)/shard_map/ppermute | solution.py:211
  34.2 7.0 %collective-permute-start = (bf16[272,128]{1,0:T(8,128)(2,1)S(1)}, bf16[272,128]{1,0:T(8,128)(2,1)S(1)}, u32[]{:S(2)}, u32[]{:S(2)}) collective-permute-start(bf16[272,128]{1,0:T(8,128)(2,1)S(1)} %concatenate.10), channel_id=1, source_target_pairs={{0,127},{1,0},{2,1},{3,2},{4,3},{5,4},{6,5},{7,6},{8,7},{9,8},{10,... | collective-permute-start | bytes 208904 | tf_op jit(solution)/shard_map/ppermute | solution.py:214
  41.3 0.6 copy-done.15
  43.2 0.6 select_reduce_fusion.9.src_ref
  43.8 0.5 slice.118
  45.1 0.5 slice.116
  46.2 0.6 select_select_fusion.3.take_ref
  46.9 3.5 %shard_map.218 = (bf16[32,128,128]{2,1,0:T(8,128)(2,1)}, bf16[32,128,128]{2,1,0:T(8,128)(2,1)}) custom-call(s32[32]{0:T(128)} %select_reduce_fusion.9.src_ref, s32[32]{0:T(128)} %select_select_fusion.3.take_ref, bf16[32,128,128]{2,1,0:T(8,128)(2,1)} %keys_ref.1, bf16[32,128,128]{2,1,0:T(8,128)(2,1)} %values_ref.1, bf16[272,128]{1,0:T(8,128)(2,1)} %copy-done.8, ...), custom_call_target="tpu_custom_call" | custom-call | bytes 4194304 | tf_op jit(solution)/shard_map/pallas_call | solution.py:137
  50.4 0.8 slice_bitcast_fusion.3
  51.1 0.7 slice_bitcast_fusion.4
  53.9 0.6 copy-done.17
  56.1 0.7 fusion.154
  58.5 3.4 %collective-permute-start.2 = (bf16[64,512]{1,0:T(8,128)(2,1)S(1)}, bf16[64,512]{1,0:T(8,128)(2,1)S(1)}, u32[]{:S(2)}, u32[]{:S(2)}) collective-permute-start(bf16[64,512]{1,0:T(8,128)(2,1)S(1)} %convolution_convert_fusion.3), channel_id=1, source_target_pairs={{0,128},{128,0},{256,384},{384,256},{1,129},{129,1},{257,385},{385... | collective-permute-start | bytes 196616 | tf_op jit(solution)/shard_map/ppermute | solution.py:102
  62.0 0.8 collective-permute-done.2
  62.8 2.2 %collective-permute-start.3 = (bf16[64,512]{1,0:T(8,128)(2,1)S(1)}, bf16[64,512]{1,0:T(8,128)(2,1)S(1)}, u32[]{:S(2)}, u32[]{:S(2)}) collective-permute-start(bf16[64,512]{1,0:T(8,128)(2,1)S(1)} %add_convert_fusion.1), channel_id=1, source_target_pairs={{0,256},{128,384},{256,0},{384,128},{1,257},{129,385},{257,1},{385... | collective-permute-start | bytes 196616 | tf_op jit(solution)/shard_map/ppermute | solution.py:102
  65.3 2.5 %collective-permute-done.3 = bf16[64,512]{1,0:T(8,128)(2,1)S(1)} collective-permute-done((bf16[64,512]{1,0:T(8,128)(2,1)S(1)}, bf16[64,512]{1,0:T(8,128)(2,1)S(1)}, u32[]{:S(2)}, u32[]{:S(2)}) %collective-permute-start.3) | collective-permute-done | bytes 65568 | tf_op jit(solution)/shard_map/ppermute | solution.py:102
  68.6 1.7 %convolution_convert_fusion.1 = bf16[64,512]{1,0:T(8,128)(2,1)S(1)} fusion(bf16[512,512]{1,0:T(8,128)(2,1)S(1)} %copy-done, bf16[512,512]{1,0:T(8,128)(2,1)} %param.33, f32[64,512]{1,0:T(8,128)S(1)} %get-tuple-element.44, f32[512]{0:T(512)S(1)} %copy-done.21, f32[64]{0:T(128)S(1)} %add_rsqrt_fusion.1, f32[64]{0:T(128)S(1)} %broadcast_multiply_fusion.1), kind=kOutput, calls=%fused_computation.4 | convolution fusion | flops 69402624 | bytes 1247744 | tf_op jit(solution)/shard_map/dot_general | solution.py:305
  70.3 3.4 %collective-permute-start.4 = (bf16[64,512]{1,0:T(8,128)(2,1)S(1)}, bf16[64,512]{1,0:T(8,128)(2,1)S(1)}, u32[]{:S(2)}, u32[]{:S(2)}) collective-permute-start(bf16[64,512]{1,0:T(8,128)(2,1)S(1)} %convolution_convert_fusion.1), channel_id=1, source_target_pairs={{0,128},{128,0},{256,384},{384,256},{1,129},{129,1},{257,385},{385... | collective-permute-start | bytes 196616 | tf_op jit(solution)/shard_map/ppermute | solution.py:102
  73.9 0.7 collective-permute-done.4
  74.7 2.2 %collective-permute-start.5 = (bf16[64,512]{1,0:T(8,128)(2,1)S(1)}, bf16[64,512]{1,0:T(8,128)(2,1)S(1)}, u32[]{:S(2)}, u32[]{:S(2)}) collective-permute-start(bf16[64,512]{1,0:T(8,128)(2,1)S(1)} %add_convert_fusion), channel_id=1, source_target_pairs={{0,256},{128,384},{256,0},{384,128},{1,257},{129,385},{257,1},{385... | collective-permute-start | bytes 196616 | tf_op jit(solution)/shard_map/ppermute | solution.py:102
  76.9 2.6 %select_select_fusion = (bf16[32,128,128]{2,1,0:T(8,128)(2,1)}, bf16[32,128,128]{2,1,0:T(8,128)(2,1)}) fusion(bf16[32,128,128]{2,1,0:T(8,128)(2,1)S(1)} %copy-done.5, pred[32,128]{1,0:T(8,128)(4,1)S(1)} %get-tuple-element.94, pred[32,128]{1,0:T(8,128)(4,1)S(1)} %get-tuple-element.95, bf16[32,128]{1,0:T(8,128)(2,1)S(1)} %get-tuple-element.72, ...), kind=kLoop, calls=%fused_computation.17 | loop fusion | flops 2097152 | bytes 4235264 | tf_op jit(solution)/shard_map/jit(_where)/select_n | solution.py:327
  79.9 0.6 slice_bitcast_fusion
  81.1 0.7 copy-done.20
  82.3 0.8 copy.95
  (128 shorter events, 10.7 us)
Async XLA Ops:
  0.6 67.5 %copy-start = (bf16[512,512]{1,0:T(8,128)(2,1)S(1)}, bf16[512,512]{1,0:T(8,128)(2,1)}, u32[]{:S(2)}) copy-start(bf16[512,512]{1,0:T(8,128)(2,1)} %param.34) | copy-start | bytes 1572868
  1.8 0.9 %copy-start.10 = (bf16[32,512]{1,0:T(8,128)(2,1)S(1)}, bf16[32,512]{1,0:T(8,128)(2,1)}, u32[]{:S(2)}) copy-start(bf16[32,512]{1,0:T(8,128)(2,1)} %param.19) | copy-start | bytes 98308
  3.0 25.3 %copy-start.2 = (bf16[32,128,128]{2,1,0:T(8,128)(2,1)S(1)}, bf16[32,128,128]{2,1,0:T(8,128)(2,1)}, u32[]{:S(2)}) copy-start(bf16[32,128,128]{2,1,0:T(8,128)(2,1)} %values_ref.1) | copy-start | bytes 3145732
  3.0 25.3 %copy-start.1 = (bf16[32,128,128]{2,1,0:T(8,128)(2,1)S(1)}, bf16[32,128,128]{2,1,0:T(8,128)(2,1)}, u32[]{:S(2)}) copy-start(bf16[32,128,128]{2,1,0:T(8,128)(2,1)} %keys_ref.1) | copy-start | bytes 3145732
  5.4 46.4 %all-to-all-start = ((bf16[128,2,576]{2,1,0:T(2,128)(2,1)}), bf16[128,2,576]{2,1,0:T(2,128)(2,1)S(1)}, u32[]{:S(2)}, u32[]{:S(2)}) async-start(bf16[128,2,576]{2,1,0:T(2,128)(2,1)} %reshape.391), calls=%async_computation | async-start | bytes 655360 | tf_op jit(solution)/shard_map/all_to_all | solution.py:237
  26.3 0.7 copy-start.19
  28.3 1.0 %copy-start.12 = (bf16[32,512]{1,0:T(8,128)(2,1)S(1)}, bf16[32,512]{1,0:T(8,128)(2,1)}, u32[]{:S(2)}) copy-start(bf16[32,512]{1,0:T(8,128)(2,1)} %param.23) | copy-start | bytes 98308
  28.3 1.0 %copy-start.13 = (bf16[32,512]{1,0:T(8,128)(2,1)S(1)}, bf16[32,512]{1,0:T(8,128)(2,1)}, u32[]{:S(2)}) copy-start(bf16[32,512]{1,0:T(8,128)(2,1)} %param.24) | copy-start | bytes 98308
  29.5 14.3 %collective-permute-start.1 = (bf16[272,128]{1,0:T(8,128)(2,1)S(1)}, bf16[272,128]{1,0:T(8,128)(2,1)S(1)}, u32[]{:S(2)}, u32[]{:S(2)}) collective-permute-start(bf16[272,128]{1,0:T(8,128)(2,1)S(1)} %concatenate.11), channel_id=1, source_target_pairs={{0,1},{1,2},{2,3},{3,4},{4,5},{5,6},{6,7},{7,8},{8,9},{9,10},{10,1... | collective-permute-start | bytes 208904 | tf_op jit(solution)/shard_map/ppermute | solution.py:211
  34.2 10.8 %collective-permute-start = (bf16[272,128]{1,0:T(8,128)(2,1)S(1)}, bf16[272,128]{1,0:T(8,128)(2,1)S(1)}, u32[]{:S(2)}, u32[]{:S(2)}) collective-permute-start(bf16[272,128]{1,0:T(8,128)(2,1)S(1)} %concatenate.10), channel_id=1, source_target_pairs={{0,127},{1,0},{2,1},{3,2},{4,3},{5,4},{6,5},{7,6},{8,7},{9,8},{10,... | collective-permute-start | bytes 208904 | tf_op jit(solution)/shard_map/ppermute | solution.py:214
  41.3 0.7 copy-start.15
  41.9 0.7 copy-start.16
  43.8 3.0 %copy-start.8 = (bf16[272,128]{1,0:T(8,128)(2,1)}, bf16[272,128]{1,0:T(8,128)(2,1)S(1)}, u32[]{:S(2)}) copy-start(bf16[272,128]{1,0:T(8,128)(2,1)S(1)} %collective-permute-done.1.lbox_ref) | copy-start | bytes 208900
  45.1 1.8 %copy-start.9 = (bf16[272,128]{1,0:T(8,128)(2,1)}, bf16[272,128]{1,0:T(8,128)(2,1)S(1)}, u32[]{:S(2)}) copy-start(bf16[272,128]{1,0:T(8,128)(2,1)S(1)} %collective-permute-done.rbox_ref) | copy-start | bytes 208900
  52.8 0.6 copy-start.11
  52.8 1.0 %copy-start.6 = (bf16[3,512,128]{2,1,0:T(8,128)(2,1)S(1)}, bf16[3,512,128]{2,1,0:T(8,128)(2,1)}, u32[]{:S(2)}) copy-start(bf16[3,512,128]{2,1,0:T(8,128)(2,1)} %param.29) | copy-start | bytes 1179652
  53.7 0.7 copy-start.17
  54.7 1.4 %copy-start.3 = (bf16[32,128,128]{2,1,0:T(8,128)(2,1)S(1)}, bf16[32,128,128]{2,1,0:T(8,128)(2,1)}, u32[]{:S(2)}) copy-start(bf16[32,128,128]{2,1,0:T(8,128)(2,1)} %get-tuple-element.7) | copy-start | bytes 3145732
  55.8 1.6 %copy-start.5 = (bf16[32,128,128]{2,1,0:T(8,128)(2,1)S(1)}, bf16[32,128,128]{2,1,0:T(8,128)(2,1)}, u32[]{:S(2)}) copy-start(bf16[32,128,128]{2,1,0:T(8,128)(2,1)} %get-tuple-element.8) | copy-start | bytes 3145732
  57.4 0.9 %copy-start.7 = (bf16[128,512]{1,0:T(8,128)(2,1)S(1)}, bf16[128,512]{1,0:T(8,128)(2,1)}, u32[]{:S(2)}) copy-start(bf16[128,512]{1,0:T(8,128)(2,1)} %param.30) | copy-start | bytes 393220
  58.5 4.3 %collective-permute-start.2 = (bf16[64,512]{1,0:T(8,128)(2,1)S(1)}, bf16[64,512]{1,0:T(8,128)(2,1)S(1)}, u32[]{:S(2)}, u32[]{:S(2)}) collective-permute-start(bf16[64,512]{1,0:T(8,128)(2,1)S(1)} %convolution_convert_fusion.3), channel_id=1, source_target_pairs={{0,128},{128,0},{256,384},{384,256},{1,129},{129,1},{257,385},{385... | collective-permute-start | bytes 196616 | tf_op jit(solution)/shard_map/ppermute | solution.py:102
  62.8 5.0 %collective-permute-start.3 = (bf16[64,512]{1,0:T(8,128)(2,1)S(1)}, bf16[64,512]{1,0:T(8,128)(2,1)S(1)}, u32[]{:S(2)}, u32[]{:S(2)}) collective-permute-start(bf16[64,512]{1,0:T(8,128)(2,1)S(1)} %add_convert_fusion.1), channel_id=1, source_target_pairs={{0,256},{128,384},{256,0},{384,128},{1,257},{129,385},{257,1},{385... | collective-permute-start | bytes 196616 | tf_op jit(solution)/shard_map/ppermute | solution.py:102
  65.2 2.7 %copy-start.14 = (f32[512]{0:T(512)S(1)}, f32[512]{0:T(512)}, u32[]{:S(2)}) copy-start(f32[512]{0:T(512)} %param.31) | copy-start | bytes 6148
  67.9 0.7 copy-start.21
  70.3 4.3 %collective-permute-start.4 = (bf16[64,512]{1,0:T(8,128)(2,1)S(1)}, bf16[64,512]{1,0:T(8,128)(2,1)S(1)}, u32[]{:S(2)}, u32[]{:S(2)}) collective-permute-start(bf16[64,512]{1,0:T(8,128)(2,1)S(1)} %convolution_convert_fusion.1), channel_id=1, source_target_pairs={{0,128},{128,0},{256,384},{384,256},{1,129},{129,1},{257,385},{385... | collective-permute-start | bytes 196616 | tf_op jit(solution)/shard_map/ppermute | solution.py:102
  74.7 5.0 %collective-permute-start.5 = (bf16[64,512]{1,0:T(8,128)(2,1)S(1)}, bf16[64,512]{1,0:T(8,128)(2,1)S(1)}, u32[]{:S(2)}, u32[]{:S(2)}) collective-permute-start(bf16[64,512]{1,0:T(8,128)(2,1)S(1)} %add_convert_fusion), channel_id=1, source_target_pairs={{0,256},{128,384},{256,0},{384,128},{1,257},{129,385},{257,1},{385... | collective-permute-start | bytes 196616 | tf_op jit(solution)/shard_map/ppermute | solution.py:102
  76.9 2.9 %copy-start.18 = (f32[512]{0:T(512)S(1)}, f32[512]{0:T(512)}, u32[]{:S(2)}) copy-start(f32[512]{0:T(512)} %param.35) | copy-start | bytes 6148
  79.5 1.2 %copy-start.4 = (bf16[16,64,512]{2,1,0:T(8,128)(2,1)S(1)}, bf16[16,64,512]{2,1,0:T(8,128)(2,1)}, u32[]{:S(2)}) copy-start(bf16[16,64,512]{2,1,0:T(8,128)(2,1)} %param.36) | copy-start | bytes 3145732
  81.1 0.7 copy-start.20

commit v15 on v14

--- a/solution.py
+++ b/solution.py
@@ -126,7 +126,7 @@
 
         return carry
 
-    lax.fori_loop(0, streams, body, 0)
+    lax.fori_loop(0, streams, body, 0, unroll=True)
 
 
 def route_caches(src, take, keys, values, lbox, rbox):

time: 83.8 us -> 83.6 us (level)
  no operation moved by 1% of the time
where the time goes in v15:
time: 83.6 us; the launch traced here: 82.9 us
  starting transfers between devices  43.1 us (52%)
  local copies, waits for them, and re-layouts  13.5 us (16%)
  other arithmetic  9.77 us (12%)
  matrix products  5.24 us (6%)
  waiting for transfers between devices  4.08 us (5%)
  between operations  3.95 us (5%)
  Pallas kernels  3.31 us (4%)
    all_to_all x1, starting transfers between devices, local(): got = lax.all_to_all(send, 'batch', split_axis=0, concat_axis=0, tiled=True)  20.8 us
    ppermute x4, starting transfers between devices, section_sum(): other = lax.ppermute(total, 'section', route)  11.3 us
    unnamed x49, local copies, waits for them, and re-layouts  8.08 us
    ppermute x1, starting transfers between devices, local(): lax.ppermute(pack(left_owner), 'batch', [(i, (i - 1) % owners) for i in r...  7.01 us
    ppermute x4, waiting for transfers between devices, section_sum(): other = lax.ppermute(total, 'section', route)  4.07 us
    ppermute x1, starting transfers between devices, local(): lax.ppermute(pack(right_owner), 'batch', [(i, (i + 1) % owners) for i in...  3.97 us
    pallas_call x1, Pallas kernels, route_caches(): pl.pallas_call(cache_kernel, out_shape=(shape, shape), in_specs=[smem] *...  3.31 us
    select_n x1, other arithmetic, local(): jnp.where(hit_second, fresh_values[:, 1][:, None, :], jnp.where(hit_first...  2.63 us
  transfers between devices with their start and end apart: 7, of which 4 were waited for; matrix products, arithmetic and copies ran while one was open for 12% of the time, Pallas kernels for 4%

profile of v15, /device:TPU:1, one launch (start us, length us, event | category | flops | bytes accessed | tf_op | source)
XLA Modules:
  0.0 82.9 jit_solution(5066884844212373941)
XLA Ops:
  0.6 0.7 fusion.111
  1.8 0.9 %copy.100 = bf16[128,2,1]{1,0,2:T(8,128)(2,1)S(1)} copy(bf16[128,2,1]{2,1,0:T(2,128)(2,1)S(1)} %bitcast.105) | data formatting | bytes 1024
  3.5 0.8 %reduce.10 = bf16[128,1152]{1,0:T(8,128)(2,1)S(1)} reduce(bf16[128,1,1152]{2,0,1:T(8,128)(2,1)S(1)} %fusion.13, bf16[]{:T(256)} %broadcast.446), dimensions={1}, to_apply=%copy.80.reduce_sub_computation | reduce | bytes 589826 | tf_op jit(solution)/shard_map/all_to_all | solution.py:237
  4.4 1.0 %reshape.391 = bf16[128,2,576]{2,1,0:T(2,128)(2,1)} reshape(bf16[128,1152]{1,0:T(8,128)(2,1)S(1)} %reduce.10) | data formatting | bytes 589824
  5.4 20.8 %all-to-all-start = ((bf16[128,2,576]{2,1,0:T(2,128)(2,1)}), bf16[128,2,576]{2,1,0:T(2,128)(2,1)S(1)}, u32[]{:S(2)}, u32[]{:S(2)}) async-start(bf16[128,2,576]{2,1,0:T(2,128)(2,1)} %reshape.391), calls=%async_computation | async-start | bytes 655360 | tf_op jit(solution)/shard_map/all_to_all | solution.py:237
  26.3 0.6 copy-done.19
  27.0 0.6 select_reduce_fusion.11
  28.3 1.0 %select_reduce_fusion.3 = (bf16[128,128]{1,0:T(8,128)(2,1)S(1)}, bf16[128,128]{1,0:T(8,128)(2,1)S(1)}, bf16[128,128]{1,0:T(8,128)(2,1)S(1)}, bf16[128,128]{1,0:T(8,128)(2,1)S(1)}) fusion(bf16[32,128,128]{2,1,0:T(8,128)(2,1)S(1)} %copy-done.1, pred[32]{0:T(512)(128)(4,1)S(1)} %get-tuple-element.49, pred[32]{0:T(512)(128)(4,1)S(1)} %get-tuple-element.48, ...), kind=kLoop, calls=%fused_computation.22 | loop fusion | flops 4128768 | bytes 2228288 | tf_op jit(solution)/shard_map/reduce_sum | solution.py:192
  29.5 4.0 %collective-permute-start.1 = (bf16[272,128]{1,0:T(8,128)(2,1)S(1)}, bf16[272,128]{1,0:T(8,128)(2,1)S(1)}, u32[]{:S(2)}, u32[]{:S(2)}) collective-permute-start(bf16[272,128]{1,0:T(8,128)(2,1)S(1)} %concatenate.11), channel_id=1, source_target_pairs={{0,1},{1,2},{2,3},{3,4},{4,5},{5,6},{6,7},{7,8},{8,9},{9,10},{10,1... | collective-permute-start | bytes 208904 | tf_op jit(solution)/shard_map/ppermute | solution.py:211
  34.2 7.0 %collective-permute-start = (bf16[272,128]{1,0:T(8,128)(2,1)S(1)}, bf16[272,128]{1,0:T(8,128)(2,1)S(1)}, u32[]{:S(2)}, u32[]{:S(2)}) collective-permute-start(bf16[272,128]{1,0:T(8,128)(2,1)S(1)} %concatenate.10), channel_id=1, source_target_pairs={{0,127},{1,0},{2,1},{3,2},{4,3},{5,4},{6,5},{7,6},{8,7},{9,8},{10,... | collective-permute-start | bytes 208904 | tf_op jit(solution)/shard_map/ppermute | solution.py:214
  41.3 0.6 copy-done.15
  43.2 0.6 select_reduce_fusion.9.src_ref
  43.8 0.5 slice.118
  45.1 0.5 slice.116
  46.2 0.6 select_select_fusion.3.take_ref
  46.9 3.3 %shard_map.218 = (bf16[32,128,128]{2,1,0:T(8,128)(2,1)}, bf16[32,128,128]{2,1,0:T(8,128)(2,1)}) custom-call(s32[32]{0:T(128)} %select_reduce_fusion.9.src_ref, s32[32]{0:T(128)} %select_select_fusion.3.take_ref, bf16[32,128,128]{2,1,0:T(8,128)(2,1)} %keys_ref.1, bf16[32,128,128]{2,1,0:T(8,128)(2,1)} %values_ref.1, bf16[272,128]{1,0:T(8,128)(2,1)} %copy-done.8, ...), custom_call_target="tpu_custom_call" | custom-call | bytes 4194304 | tf_op jit(solution)/shard_map/pallas_call | solution.py:137
  50.2 0.8 slice_bitcast_fusion.3
  50.9 0.7 slice_bitcast_fusion.4
  53.7 0.6 copy-done.17
  56.0 0.7 fusion.154
  58.3 3.4 %collective-permute-start.2 = (bf16[64,512]{1,0:T(8,128)(2,1)S(1)}, bf16[64,512]{1,0:T(8,128)(2,1)S(1)}, u32[]{:S(2)}, u32[]{:S(2)}) collective-permute-start(bf16[64,512]{1,0:T(8,128)(2,1)S(1)} %convolution_convert_fusion.3), channel_id=1, source_target_pairs={{0,128},{128,0},{256,384},{384,256},{1,129},{129,1},{257,385},{385... | collective-permute-start | bytes 196616 | tf_op jit(solution)/shard_map/ppermute | solution.py:102
  61.8 0.8 collective-permute-done.2
  62.6 2.2 %collective-permute-start.3 = (bf16[64,512]{1,0:T(8,128)(2,1)S(1)}, bf16[64,512]{1,0:T(8,128)(2,1)S(1)}, u32[]{:S(2)}, u32[]{:S(2)}) collective-permute-start(bf16[64,512]{1,0:T(8,128)(2,1)S(1)} %add_convert_fusion.1), channel_id=1, source_target_pairs={{0,256},{128,384},{256,0},{384,128},{1,257},{129,385},{257,1},{385... | collective-permute-start | bytes 196616 | tf_op jit(solution)/shard_map/ppermute | solution.py:102
  65.1 2.5 %collective-permute-done.3 = bf16[64,512]{1,0:T(8,128)(2,1)S(1)} collective-permute-done((bf16[64,512]{1,0:T(8,128)(2,1)S(1)}, bf16[64,512]{1,0:T(8,128)(2,1)S(1)}, u32[]{:S(2)}, u32[]{:S(2)}) %collective-permute-start.3) | collective-permute-done | bytes 65568 | tf_op jit(solution)/shard_map/ppermute | solution.py:102
  68.4 1.7 %convolution_convert_fusion.1 = bf16[64,512]{1,0:T(8,128)(2,1)S(1)} fusion(bf16[512,512]{1,0:T(8,128)(2,1)S(1)} %copy-done, bf16[512,512]{1,0:T(8,128)(2,1)} %param.33, f32[64,512]{1,0:T(8,128)S(1)} %get-tuple-element.44, f32[512]{0:T(512)S(1)} %copy-done.21, f32[64]{0:T(128)S(1)} %add_rsqrt_fusion.1, f32[64]{0:T(128)S(1)} %broadcast_multiply_fusion.1), kind=kOutput, calls=%fused_computation.4 | convolution fusion | flops 69402624 | bytes 1247744 | tf_op jit(solution)/shard_map/dot_general | solution.py:305
  70.2 3.4 %collective-permute-start.4 = (bf16[64,512]{1,0:T(8,128)(2,1)S(1)}, bf16[64,512]{1,0:T(8,128)(2,1)S(1)}, u32[]{:S(2)}, u32[]{:S(2)}) collective-permute-start(bf16[64,512]{1,0:T(8,128)(2,1)S(1)} %convolution_convert_fusion.1), channel_id=1, source_target_pairs={{0,128},{128,0},{256,384},{384,256},{1,129},{129,1},{257,385},{385... | collective-permute-start | bytes 196616 | tf_op jit(solution)/shard_map/ppermute | solution.py:102
  73.7 0.7 collective-permute-done.4
  74.5 2.2 %collective-permute-start.5 = (bf16[64,512]{1,0:T(8,128)(2,1)S(1)}, bf16[64,512]{1,0:T(8,128)(2,1)S(1)}, u32[]{:S(2)}, u32[]{:S(2)}) collective-permute-start(bf16[64,512]{1,0:T(8,128)(2,1)S(1)} %add_convert_fusion), channel_id=1, source_target_pairs={{0,256},{128,384},{256,0},{384,128},{1,257},{129,385},{257,1},{385... | collective-permute-start | bytes 196616 | tf_op jit(solution)/shard_map/ppermute | solution.py:102
  76.7 2.6 %select_select_fusion = (bf16[32,128,128]{2,1,0:T(8,128)(2,1)}, bf16[32,128,128]{2,1,0:T(8,128)(2,1)}) fusion(bf16[32,128,128]{2,1,0:T(8,128)(2,1)S(1)} %copy-done.5, pred[32,128]{1,0:T(8,128)(4,1)S(1)} %get-tuple-element.94, pred[32,128]{1,0:T(8,128)(4,1)S(1)} %get-tuple-element.95, bf16[32,128]{1,0:T(8,128)(2,1)S(1)} %get-tuple-element.72, ...), kind=kLoop, calls=%fused_computation.17 | loop fusion | flops 2097152 | bytes 4235264 | tf_op jit(solution)/shard_map/jit(_where)/select_n | solution.py:327
  79.7 0.6 slice_bitcast_fusion
  81.0 0.7 copy-done.20
  82.2 0.8 copy.95
  (128 shorter events, 10.7 us)
Async XLA Ops:
  0.6 67.3 %copy-start = (bf16[512,512]{1,0:T(8,128)(2,1)S(1)}, bf16[512,512]{1,0:T(8,128)(2,1)}, u32[]{:S(2)}) copy-start(bf16[512,512]{1,0:T(8,128)(2,1)} %param.34) | copy-start | bytes 1572868
  1.8 0.9 %copy-start.10 = (bf16[32,512]{1,0:T(8,128)(2,1)S(1)}, bf16[32,512]{1,0:T(8,128)(2,1)}, u32[]{:S(2)}) copy-start(bf16[32,512]{1,0:T(8,128)(2,1)} %param.19) | copy-start | bytes 98308
  3.0 25.3 %copy-start.2 = (bf16[32,128,128]{2,1,0:T(8,128)(2,1)S(1)}, bf16[32,128,128]{2,1,0:T(8,128)(2,1)}, u32[]{:S(2)}) copy-start(bf16[32,128,128]{2,1,0:T(8,128)(2,1)} %values_ref.1) | copy-start | bytes 3145732
  3.0 25.3 %copy-start.1 = (bf16[32,128,128]{2,1,0:T(8,128)(2,1)S(1)}, bf16[32,128,128]{2,1,0:T(8,128)(2,1)}, u32[]{:S(2)}) copy-start(bf16[32,128,128]{2,1,0:T(8,128)(2,1)} %keys_ref.1) | copy-start | bytes 3145732
  5.4 46.3 %all-to-all-start = ((bf16[128,2,576]{2,1,0:T(2,128)(2,1)}), bf16[128,2,576]{2,1,0:T(2,128)(2,1)S(1)}, u32[]{:S(2)}, u32[]{:S(2)}) async-start(bf16[128,2,576]{2,1,0:T(2,128)(2,1)} %reshape.391), calls=%async_computation | async-start | bytes 655360 | tf_op jit(solution)/shard_map/all_to_all | solution.py:237
  26.3 0.7 copy-start.19
  28.3 1.0 %copy-start.12 = (bf16[32,512]{1,0:T(8,128)(2,1)S(1)}, bf16[32,512]{1,0:T(8,128)(2,1)}, u32[]{:S(2)}) copy-start(bf16[32,512]{1,0:T(8,128)(2,1)} %param.23) | copy-start | bytes 98308
  28.3 1.0 %copy-start.13 = (bf16[32,512]{1,0:T(8,128)(2,1)S(1)}, bf16[32,512]{1,0:T(8,128)(2,1)}, u32[]{:S(2)}) copy-start(bf16[32,512]{1,0:T(8,128)(2,1)} %param.24) | copy-start | bytes 98308
  29.5 14.3 %collective-permute-start.1 = (bf16[272,128]{1,0:T(8,128)(2,1)S(1)}, bf16[272,128]{1,0:T(8,128)(2,1)S(1)}, u32[]{:S(2)}, u32[]{:S(2)}) collective-permute-start(bf16[272,128]{1,0:T(8,128)(2,1)S(1)} %concatenate.11), channel_id=1, source_target_pairs={{0,1},{1,2},{2,3},{3,4},{4,5},{5,6},{6,7},{7,8},{8,9},{9,10},{10,1... | collective-permute-start | bytes 208904 | tf_op jit(solution)/shard_map/ppermute | solution.py:211
  34.2 10.8 %collective-permute-start = (bf16[272,128]{1,0:T(8,128)(2,1)S(1)}, bf16[272,128]{1,0:T(8,128)(2,1)S(1)}, u32[]{:S(2)}, u32[]{:S(2)}) collective-permute-start(bf16[272,128]{1,0:T(8,128)(2,1)S(1)} %concatenate.10), channel_id=1, source_target_pairs={{0,127},{1,0},{2,1},{3,2},{4,3},{5,4},{6,5},{7,6},{8,7},{9,8},{10,... | collective-permute-start | bytes 208904 | tf_op jit(solution)/shard_map/ppermute | solution.py:214
  41.3 0.7 copy-start.15
  41.9 0.7 copy-start.16
  43.8 3.0 %copy-start.8 = (bf16[272,128]{1,0:T(8,128)(2,1)}, bf16[272,128]{1,0:T(8,128)(2,1)S(1)}, u32[]{:S(2)}) copy-start(bf16[272,128]{1,0:T(8,128)(2,1)S(1)} %collective-permute-done.1.lbox_ref) | copy-start | bytes 208900
  45.1 1.8 %copy-start.9 = (bf16[272,128]{1,0:T(8,128)(2,1)}, bf16[272,128]{1,0:T(8,128)(2,1)S(1)}, u32[]{:S(2)}) copy-start(bf16[272,128]{1,0:T(8,128)(2,1)S(1)} %collective-permute-done.rbox_ref) | copy-start | bytes 208900
  52.7 0.6 copy-start.11
  52.7 1.0 %copy-start.6 = (bf16[3,512,128]{2,1,0:T(8,128)(2,1)S(1)}, bf16[3,512,128]{2,1,0:T(8,128)(2,1)}, u32[]{:S(2)}) copy-start(bf16[3,512,128]{2,1,0:T(8,128)(2,1)} %param.29) | copy-start | bytes 1179652
  53.6 0.7 copy-start.17
  54.5 1.4 %copy-start.3 = (bf16[32,128,128]{2,1,0:T(8,128)(2,1)S(1)}, bf16[32,128,128]{2,1,0:T(8,128)(2,1)}, u32[]{:S(2)}) copy-start(bf16[32,128,128]{2,1,0:T(8,128)(2,1)} %get-tuple-element.7) | copy-start | bytes 3145732
  55.6 1.6 %copy-start.5 = (bf16[32,128,128]{2,1,0:T(8,128)(2,1)S(1)}, bf16[32,128,128]{2,1,0:T(8,128)(2,1)}, u32[]{:S(2)}) copy-start(bf16[32,128,128]{2,1,0:T(8,128)(2,1)} %get-tuple-element.8) | copy-start | bytes 3145732
  57.2 0.9 %copy-start.7 = (bf16[128,512]{1,0:T(8,128)(2,1)S(1)}, bf16[128,512]{1,0:T(8,128)(2,1)}, u32[]{:S(2)}) copy-start(bf16[128,512]{1,0:T(8,128)(2,1)} %param.30) | copy-start | bytes 393220
  58.3 4.3 %collective-permute-start.2 = (bf16[64,512]{1,0:T(8,128)(2,1)S(1)}, bf16[64,512]{1,0:T(8,128)(2,1)S(1)}, u32[]{:S(2)}, u32[]{:S(2)}) collective-permute-start(bf16[64,512]{1,0:T(8,128)(2,1)S(1)} %convolution_convert_fusion.3), channel_id=1, source_target_pairs={{0,128},{128,0},{256,384},{384,256},{1,129},{129,1},{257,385},{385... | collective-permute-start | bytes 196616 | tf_op jit(solution)/shard_map/ppermute | solution.py:102
  62.6 5.0 %collective-permute-start.3 = (bf16[64,512]{1,0:T(8,128)(2,1)S(1)}, bf16[64,512]{1,0:T(8,128)(2,1)S(1)}, u32[]{:S(2)}, u32[]{:S(2)}) collective-permute-start(bf16[64,512]{1,0:T(8,128)(2,1)S(1)} %add_convert_fusion.1), channel_id=1, source_target_pairs={{0,256},{128,384},{256,0},{384,128},{1,257},{129,385},{257,1},{385... | collective-permute-start | bytes 196616 | tf_op jit(solution)/shard_map/ppermute | solution.py:102
  65.0 2.7 %copy-start.14 = (f32[512]{0:T(512)S(1)}, f32[512]{0:T(512)}, u32[]{:S(2)}) copy-start(f32[512]{0:T(512)} %param.31) | copy-start | bytes 6148
  67.8 0.7 copy-start.21
  70.2 4.3 %collective-permute-start.4 = (bf16[64,512]{1,0:T(8,128)(2,1)S(1)}, bf16[64,512]{1,0:T(8,128)(2,1)S(1)}, u32[]{:S(2)}, u32[]{:S(2)}) collective-permute-start(bf16[64,512]{1,0:T(8,128)(2,1)S(1)} %convolution_convert_fusion.1), channel_id=1, source_target_pairs={{0,128},{128,0},{256,384},{384,256},{1,129},{129,1},{257,385},{385... | collective-permute-start | bytes 196616 | tf_op jit(solution)/shard_map/ppermute | solution.py:102
  74.5 5.0 %collective-permute-start.5 = (bf16[64,512]{1,0:T(8,128)(2,1)S(1)}, bf16[64,512]{1,0:T(8,128)(2,1)S(1)}, u32[]{:S(2)}, u32[]{:S(2)}) collective-permute-start(bf16[64,512]{1,0:T(8,128)(2,1)S(1)} %add_convert_fusion), channel_id=1, source_target_pairs={{0,256},{128,384},{256,0},{384,128},{1,257},{129,385},{257,1},{385... | collective-permute-start | bytes 196616 | tf_op jit(solution)/shard_map/ppermute | solution.py:102
  76.7 2.9 %copy-start.18 = (f32[512]{0:T(512)S(1)}, f32[512]{0:T(512)}, u32[]{:S(2)}) copy-start(f32[512]{0:T(512)} %param.35) | copy-start | bytes 6148
  79.4 1.2 %copy-start.4 = (bf16[16,64,512]{2,1,0:T(8,128)(2,1)S(1)}, bf16[16,64,512]{2,1,0:T(8,128)(2,1)}, u32[]{:S(2)}) copy-start(bf16[16,64,512]{2,1,0:T(8,128)(2,1)} %param.36) | copy-start | bytes 3145732
  81.0 0.7 copy-start.20
